TPU v7x, 32 devices: a whole 2x2x4 slice. The times are simulated.
32 devices in a mesh: seq: 8 (over z, x), exp: 4 (over y, core).
Axes of the slice: x: 2, y: 2, z: 4, core: 2. Of those that a mesh axis runs over, the one named last changes fastest.
Arguments:
- hidden_in: bfloat16 [2048, 1536], P('seq'), may hold values from -6 to 6
- attn_gain: float32 [1536], replicated, may hold values from 0.1 to 1.9
- q_weight: bfloat16 [1536, 1536], P(None, 'exp'), may hold values from -1.25 to 1.25
- k_weight: bfloat16 [1536, 512], P(None, 'exp'), may hold values from -0.625 to 0.625
- v_weight: bfloat16 [1536, 512], P(None, 'exp'), may hold values from -0.15625 to 0.15625
- o_weight: bfloat16 [1536, 1536], P('exp'), may hold values from -0.15625 to 0.15625
- cache_kv: bfloat16 [4096, 1024], P('seq', 'exp'), may hold values from -216 to 216
- moe_gain: float32 [1536], replicated, may hold values from 0.1 to 1.9
- expert_in: bfloat16 [32, 1536, 1024], P('seq'), may hold values from -0.15625 to 0.15625
- expert_out: bfloat16 [32, 512, 1536], P('seq'), may hold values from -0.25 to 0.25
- routes: int32 [2048, 8], P(('seq', 'exp')), may hold values from 0 to 31, all different within a row; in each aligned block of 64 rows (0 to 63, 64 to 127, ...) at most 32 rows name the same one
- route_prob: float32 [2048, 8], P(('seq', 'exp')), may hold values from 0.05 to 1
- page_slot: int32 [256], replicated, may hold values from 0 to 31, as said below
Outputs:
- hidden_out: bfloat16 [2048, 1536], P(('seq', 'exp'))
- decode_pages: bfloat16 [256, 8, 2, 512], P('seq', 'exp')
Inputs may be any that keep to these rules, and one draw needn't show every extreme that they name: `routes`: in each aligned block of 64 rows (the rows of one device) no expert is named by more than 32 rows; a row names 8 different experts. `page_slot`: for each r, the 32 blocks b with b mod (8) == r have different slots.
All inputs are finite; a program needn't handle non-finite values.
Results may differ from a plain program's by a relative error of at most 0.0074.
Values may be sent and summed in bfloat16 or wider, within the bound.
No kernel may reach another device: no remote copies, remote signals or barrier semaphores. Data moves between devices by JAX's collectives and lax.ppermute only.
A program may use at most 128 MiB of HBM per device.

v0:
```python
import math

import jax
import jax.numpy as jnp
from jax import lax
from jax.sharding import PartitionSpec as P

HEADS = 24
KV_HEADS = 8
HEAD_DIM = 64
EXPERTS = 32
PAGE = 8


norm_epsilon = 1e-06
attention_scale = 0.015625
residual_scale = 0.22
masked_score = -1e30


def rms_norm(values, gain_row):
    widened = values.astype(jnp.float32)
    spread = lax.rsqrt(jnp.mean(widened * widened, axis=-1, keepdims=True) + norm_epsilon)
    return (widened * spread * gain_row).astype(jnp.bfloat16)


def attend_block(carried, query_heads, visible, key_rows, value_rows):
    best_old, total_old, summed_old = carried
    scores = (
        jnp.einsum("tkgd,nkd->kgtn", query_heads, key_rows, preferred_element_type=jnp.float32)
        * attention_scale
    )
    scores = jnp.where(visible, scores, masked_score)
    best_new = jnp.maximum(best_old, jnp.max(scores, axis=-1))
    weights = jnp.where(visible, jnp.exp(scores - best_new[..., None]), 0.0)
    factor = jnp.exp(best_old - best_new)
    total_new = total_old * factor + jnp.sum(weights, axis=-1)
    summed_new = summed_old * factor[..., None] + jnp.einsum(
        "kgtn,nkd->kgtd",
        weights.astype(jnp.bfloat16),
        value_rows,
        preferred_element_type=jnp.float32,
    )
    return (best_new, total_new, summed_new)


def block_size(piece_rows):
    return math.gcd(piece_rows, 512)


def body(
    hidden_in,
    attn_gain,
    q_weight,
    k_weight,
    v_weight,
    o_weight,
    cache_kv,
    moe_gain,
    expert_in,
    expert_out,
    routes,
    route_prob,
    page_slot,
):
    seq_count = lax.axis_size("seq")
    seq_index = lax.axis_index("seq")
    exp_index = lax.axis_index("exp")
    tokens_here = hidden_in.shape[0]
    head_dim = HEAD_DIM
    kv_local = k_weight.shape[1] // head_dim
    group_size = HEADS // KV_HEADS
    prompt_len = tokens_here * seq_count // 2
    first_row = seq_index * tokens_here
    query_rows = first_row + jnp.arange(tokens_here, dtype=jnp.int32)
    query_second = query_rows >= prompt_len
    holds_first = first_row < prompt_len
    normed = rms_norm(hidden_in, attn_gain)
    queries = jnp.dot(normed, q_weight, preferred_element_type=jnp.float32).astype(jnp.bfloat16)
    keys_new = jnp.dot(normed, k_weight, preferred_element_type=jnp.float32).astype(jnp.bfloat16)
    values_new = jnp.dot(normed, v_weight, preferred_element_type=jnp.float32).astype(jnp.bfloat16)
    pair_width = 2 * kv_local * head_dim
    pairs_new = jnp.stack(
        [
            keys_new.reshape(tokens_here, kv_local, head_dim),
            values_new.reshape(tokens_here, kv_local, head_dim),
        ],
        axis=2,
    ).reshape(tokens_here, pair_width)
    query_heads = queries.reshape(tokens_here, kv_local, group_size, head_dim)
    cache_lines = cache_kv.reshape(tokens_here, -1)
    blocks_here = tokens_here // PAGE
    rounds = blocks_here // seq_count
    outgoing = pairs_new.reshape(rounds, seq_count, PAGE * pair_width)
    received = lax.all_to_all(outgoing, "seq", split_axis=1, concat_axis=1, tiled=True)
    block_ids = (
        jnp.arange(seq_count, dtype=jnp.int32)[None, :] * blocks_here
        + jnp.arange(rounds, dtype=jnp.int32)[:, None] * seq_count
        + seq_index
    ).reshape(-1)
    table_ids = jnp.arange(page_slot.shape[0], dtype=jnp.int32)
    page_slots = jnp.sum(
        jnp.where(block_ids[:, None] == table_ids[None, :], page_slot[None, :], 0), axis=1
    )
    local_pages = (
        jnp.zeros((blocks_here, PAGE * pair_width), jnp.bfloat16)
        .at[page_slots]
        .set(received.reshape(blocks_here, -1))
    )
    page_rows = local_pages.reshape(blocks_here, PAGE, kv_local, 2, head_dim).transpose(
        0, 2, 3, 1, 4
    )
    page_rows = page_rows.reshape(blocks_here, kv_local, 2, PAGE * head_dim)
    start_state = (
        jnp.full((kv_local, group_size, tokens_here), masked_score, jnp.float32),
        jnp.zeros((kv_local, group_size, tokens_here), jnp.float32),
        jnp.zeros((kv_local, group_size, tokens_here, head_dim), jnp.float32),
    )

    def new_keys_part(carried, new_block, key_first):
        width_rows = new_block.shape[0]
        key_rows = key_first + jnp.arange(width_rows, dtype=jnp.int32)
        visible = ((key_rows >= prompt_len)[None, :] == query_second[:, None]) & (
            key_rows[None, :] <= query_rows[:, None]
        )
        split_pairs = new_block.reshape(width_rows, kv_local, 2, head_dim)
        return lax.cond(
            jnp.any(visible),
            lambda carried_in: attend_block(
                carried_in, query_heads, visible, split_pairs[:, :, 0], split_pairs[:, :, 1]
            ),
            lambda carried_in: carried_in,
            carried,
        )

    carried = start_state
    new_piece = lax.all_gather(pairs_new, "seq", axis=0, tiled=True)
    cache_piece = lax.all_gather(cache_lines, "seq", axis=0, tiled=True)
    piece_rows = new_piece.shape[0]
    stride = block_size(piece_rows)
    new_blocks = new_piece.reshape(piece_rows // stride, stride, -1)
    cache_blocks = cache_piece.reshape(piece_rows // stride, 2 * stride, kv_local, 2, head_dim)
    offsets = stride * jnp.arange(piece_rows // stride, dtype=jnp.int32)
    everything = jnp.ones((tokens_here, 2 * stride), bool)

    def visit(carried_in, block_part):
        new_block, cache_block, key_first = block_part
        carried_in = new_keys_part(carried_in, new_block, key_first)
        carried_in = lax.cond(
            holds_first,
            lambda inner: attend_block(
                inner, query_heads, everything, cache_block[:, :, 0], cache_block[:, :, 1]
            ),
            lambda inner: inner,
            carried_in,
        )
        return (carried_in, None)

    carried, _ = lax.scan(visit, carried, (new_blocks, cache_blocks, offsets))
    best_final, total_final, summed_final = carried
    attended = (
        (summed_final / total_final[..., None])
        .transpose(2, 0, 1, 3)
        .reshape(tokens_here, -1)
        .astype(jnp.bfloat16)
    )
    mixed_rows = lax.psum_scatter(
        jnp.dot(attended, o_weight, preferred_element_type=jnp.float32).astype(jnp.bfloat16),
        "exp",
        scatter_dimension=0,
        tiled=True,
    ).astype(jnp.float32)
    moe_rows = mixed_rows.shape[0]
    residual = (
        lax.dynamic_slice_in_dim(hidden_in, exp_index * moe_rows, moe_rows, 0).astype(jnp.float32)
        + residual_scale * mixed_rows
    )
    moe_in = rms_norm(residual, moe_gain)
    top_count = routes.shape[1]
    assigns = moe_rows * top_count
    capacity = 2 * moe_rows * top_count // EXPERTS
    flat_ids = routes.reshape(-1)
    hit_table = (flat_ids[:, None] == jnp.arange(EXPERTS, dtype=jnp.int32)[None, :]).astype(
        jnp.int32
    )
    earlier = jnp.cumsum(hit_table, axis=0) - hit_table
    slot_rank = jnp.sum(earlier * hit_table, axis=1)
    dest_slot = flat_ids * capacity + slot_rank
    source = (
        jnp.full((EXPERTS * capacity,), assigns, jnp.int32)
        .at[dest_slot]
        .set(jnp.arange(assigns, dtype=jnp.int32))
    )
    filled = source < assigns
    picked = moe_in[jnp.minimum(source, assigns - 1) // top_count]
    dispatched = jnp.where(filled[:, None], picked, jnp.zeros_like(picked)).reshape(
        seq_count, EXPERTS // seq_count, capacity, -1
    )
    hidden = jnp.einsum(
        "sexd,edf->sexf",
        lax.all_to_all(dispatched, "seq", split_axis=0, concat_axis=0, tiled=True),
        expert_in,
        preferred_element_type=jnp.float32,
    )
    half_width = hidden.shape[-1] // 2
    active = (jax.nn.silu(hidden[..., :half_width]) * hidden[..., half_width:]).astype(jnp.bfloat16)
    produced = jnp.einsum(
        "sexf,efd->sexd", active, expert_out, preferred_element_type=jnp.float32
    ).astype(jnp.bfloat16)
    returned = lax.all_to_all(produced, "seq", split_axis=0, concat_axis=0, tiled=True)
    flat_back = returned.reshape(EXPERTS * capacity, -1)
    per_assign = flat_back[dest_slot].reshape(moe_rows, top_count, -1)
    share = route_prob / jnp.sum(route_prob, axis=-1, keepdims=True)
    moe = jnp.sum(share[..., None] * per_assign.astype(jnp.float32), axis=1)
    hidden_out = (residual + residual_scale * moe).astype(jnp.bfloat16)
    return (hidden_out, page_rows)


def solution(mesh):
    return jax.shard_map(
        body,
        mesh=mesh,
        in_specs=(
            P("seq", None),
            P(),
            P(None, "exp"),
            P(None, "exp"),
            P(None, "exp"),
            P("exp", None),
            P("seq", "exp"),
            P(),
            P("seq", None, None),
            P("seq", None, None),
            P(("seq", "exp"), None),
            P(("seq", "exp"), None),
            P(),
        ),
        out_specs=(P(("seq", "exp"), None), P("seq", "exp", None, None)),
        check_vma=False,
    )
```

profile of v0, /device:TPU:0, one launch (start us, length us, event | category | flops | bytes accessed | tf_op | source)
XLA Modules:
  0.0 385.0 jit_solution(13722507623709581729)
XLA Ops:
  7.3 1.5 fusion.45
  8.8 1.7 convolution_convert_fusion.3
  10.5 1.7 convolution_convert_fusion.2
  14.7 40.6 %all-gather.3.cloned.1.call-done = bf16[2048,256]{0,1:T(8,128)(2,1)} async-done(((bf16[256,256]{0,1:T(8,128)(2,1)}), bf16[2048,256]{0,1:T(8,128)(2,1)}) %all-gather.3.cloned.1.call-update) | async-done | bytes 1048592 | tf_op jit(solution)/shard_map/all_gather | solution.py:137
  55.4 1.3 copy.142
  56.7 49.0 %all-gather.5.cloned.1.call-done = bf16[2048,512]{1,0:T(8,128)(2,1)} async-done(((bf16[256,512]{1,0:T(8,128)(2,1)}), bf16[2048,512]{1,0:T(8,128)(2,1)}) %all-gather.5.cloned.1.call-update) | async-done | bytes 2097168 | tf_op jit(solution)/shard_map/all_gather | solution.py:138
  105.7 8.9 %reshape.173 = bf16[4,1024,2,2,64]{4,3,2,1,0:T(2,128)(2,1)} reshape(bf16[2048,512]{1,0:T(8,128)(2,1)} %all-gather.5.cloned.1.call-done) | data formatting | bytes 4194304 | tf_op jit(solution)/shard_map/reshape | solution.py:142
  114.6 10.6 %copy.101 = bf16[4,1024,2,2,64]{1,4,2,3,0:T(8,128)(2,1)} copy(bf16[4,1024,2,2,64]{4,3,2,1,0:T(2,128)(2,1)} %reshape.173) | data formatting | bytes 4194304
  125.3 35.4 %while.16 = (s32[]{:T(128)}, f32[2,3,256]{2,1,0:T(4,128)S(1)}, f32[2,3,256]{2,1,0:T(4,128)S(1)}, f32[2,3,256,64]{2,3,1,0:T(8,128)S(1)}, pred[]{:T(512)}, /*index...) while((s32[]{:T(128)}, f32[2,3,256]{2,1,0:T(4,128)S(1)}, ...), condition=%wide.region_11.12_spmd.clone.clone, body=%wide.region_1.11_spmd.clone.clone.sunk | while | flops 627712256 | bytes 33374036 | solution.py:159
  129.0 2.5 conditional.8
  131.5 4.5 %conditional.9 = ((f32[2,3,256]{2,1,0:T(4,128)S(1)}, f32[2,3,256]{2,1,0:T(4,128)S(1)}, f32[2,3,256,64]{2,3,1,0:T(8,128)S(1)})) conditional(s32[]{:T(128)} %convert_element_type.152, (f32[2,3,256]{2,1,0:T(4,128)S(1)}, f32[2,3,256]{2,1,0:T(4,128)S(1)}, f32[2,3,256,64]{2,3,1,0:T(8,128)S(1)}) %get-tuple-element.445, ...), branch_computations={%region_7.7_spmd, %region_8.10_spmd} | conditional | flops 415435776 | bytes 21532708 | solution.py:149
  131.5 1.1 dynamic-slice_bitcast_fusion
  132.6 1.0 bitcast_reduce_fusion
  133.7 1.0 fusion.19
  134.7 1.2 fusion.22
  139.7 4.5 %conditional.9 = ((f32[2,3,256]{2,1,0:T(4,128)S(1)}, f32[2,3,256]{2,1,0:T(4,128)S(1)}, f32[2,3,256,64]{2,3,1,0:T(8,128)S(1)})) conditional(s32[]{:T(128)} %convert_element_type.152, (f32[2,3,256]{2,1,0:T(4,128)S(1)}, f32[2,3,256]{2,1,0:T(4,128)S(1)}, f32[2,3,256,64]{2,3,1,0:T(8,128)S(1)}) %get-tuple-element.445, ...), branch_computations={%region_7.7_spmd, %region_8.10_spmd} | conditional | flops 415435776 | bytes 21532708 | solution.py:149
  139.8 1.1 dynamic-slice_bitcast_fusion
  140.8 1.0 bitcast_reduce_fusion
  141.9 1.0 fusion.19
  143.0 1.2 fusion.22
  148.0 4.5 %conditional.9 = ((f32[2,3,256]{2,1,0:T(4,128)S(1)}, f32[2,3,256]{2,1,0:T(4,128)S(1)}, f32[2,3,256,64]{2,3,1,0:T(8,128)S(1)})) conditional(s32[]{:T(128)} %convert_element_type.152, (f32[2,3,256]{2,1,0:T(4,128)S(1)}, f32[2,3,256]{2,1,0:T(4,128)S(1)}, f32[2,3,256,64]{2,3,1,0:T(8,128)S(1)}) %get-tuple-element.445, ...), branch_computations={%region_7.7_spmd, %region_8.10_spmd} | conditional | flops 415435776 | bytes 21532708 | solution.py:149
  148.0 1.1 dynamic-slice_bitcast_fusion
  149.1 1.0 bitcast_reduce_fusion
  150.1 1.0 fusion.19
  151.2 1.2 fusion.22
  156.2 4.5 %conditional.9 = ((f32[2,3,256]{2,1,0:T(4,128)S(1)}, f32[2,3,256]{2,1,0:T(4,128)S(1)}, f32[2,3,256,64]{2,3,1,0:T(8,128)S(1)})) conditional(s32[]{:T(128)} %convert_element_type.152, (f32[2,3,256]{2,1,0:T(4,128)S(1)}, f32[2,3,256]{2,1,0:T(4,128)S(1)}, f32[2,3,256,64]{2,3,1,0:T(8,128)S(1)}) %get-tuple-element.445, ...), branch_computations={%region_7.7_spmd, %region_8.10_spmd} | conditional | flops 415435776 | bytes 21532708 | solution.py:149
  156.2 1.1 dynamic-slice_bitcast_fusion
  157.3 1.0 bitcast_reduce_fusion
  158.4 1.0 fusion.19
  159.4 1.2 fusion.22
  160.8 1.5 convolution_convert_fusion
  162.6 1.2 reduce-window.6
  164.3 2.4 scatter_custom_fusion
  166.9 19.4 %reduce-scatter.2.cloned.1.call-done = bf16[64,1536]{1,0:T(8,128)(2,1)} async-done(((bf16[256,1536]{1,0:T(8,128)(2,1)}), bf16[64,1536]{1,0:T(8,128)(2,1)}) %reduce-scatter.2.cloned.1.call-update) | async-done | bytes 196624 | tf_op jit(solution)/shard_map/reduce_scatter | solution.py:167
  186.3 1.1 multiply_reduce_fusion
  188.5 5.6 %gather_fusion = bf16[1024,1536]{1,0:T(8,128)(2,1)} fusion(bf16[64,1536]{1,0:T(8,128)(2,1)S(1)} %multiply_convert_fusion, s32[1024]{0:T(1024)S(1)} %fusion.59), kind=kCustom, calls=%fused_computation | custom fusion | bytes 6295552 | tf_op jit(solution)/shard_map/gather | solution.py:195
  194.1 3.8 broadcast_select_fusion
  197.9 5.8 %all-to-all-start = ((bf16[8,4,32,1536]{3,2,1,0:T(8,128)(2,1)}), bf16[8,4,32,1536]{3,2,1,0:T(8,128)(2,1)}, u32[]{:S(2)}, u32[]{:S(2)}) async-start(bf16[8,4,32,1536]{3,2,1,0:T(8,128)(2,1)} %broadcast_select_fusion), calls=%async_computation.1 | async-start | bytes 6291456 | tf_op jit(solution)/shard_map/all_to_all | solution.py:201
  204.9 69.6 %all-to-all-done = bf16[8,4,32,1536]{3,2,1,0:T(8,128)(2,1)} async-done(((bf16[8,4,32,1536]{3,2,1,0:T(8,128)(2,1)}), bf16[8,4,32,1536]{3,2,1,0:T(8,128)(2,1)}, u32[]{:S(2)}, u32[]{:S(2)}) %all-to-all-start) | async-done | bytes 3145760 | tf_op jit(solution)/shard_map/all_to_all | solution.py:201
  274.5 3.6 all-to-all-start.2
  278.2 7.4 %fusion.39 = f32[8,4,32,1024]{3,2,0,1:T(8,128)S(1)} fusion(bf16[4,1536,1024]{2,1,0:T(8,128)(2,1)} %param.27, bf16[8,4,32,1536]{3,2,1,0:T(8,128)(2,1)} %all-to-all-done), kind=kOutput, calls=%fused_computation.53 | convolution fusion | flops 3221225472 | bytes 19922944 | tf_op jit(solution)/shard_map/sexd,edf->sexf/dot_general | solution.py:199
  285.6 4.6 %fusion.34 = bf16[8,4,32,1536]{3,2,0,1:T(8,128)(2,1)S(1)} fusion(bf16[4,512,1536]{2,1,0:T(8,128)(2,1)} %param.28, f32[8,4,32,1024]{3,2,0,1:T(8,128)S(1)} %fusion.39), kind=kOutput, calls=%fused_computation.47 | convolution fusion | flops 1615331328 | bytes 13631488 | tf_op jit(solution)/shard_map/sexf,efd->sexd/dot_general | solution.py:207
  290.2 1.9 copy.108
  292.1 6.1 %all-to-all-start.1 = ((bf16[8,4,32,1536]{3,2,1,0:T(8,128)(2,1)}), bf16[8,4,32,1536]{3,2,1,0:T(8,128)(2,1)}, u32[]{:S(2)}, u32[]{:S(2)}) async-start(bf16[8,4,32,1536]{3,2,1,0:T(8,128)(2,1)} %copy.108), calls=%async_computation.2 | async-start | bytes 6291456 | tf_op jit(solution)/shard_map/all_to_all | solution.py:210
  301.4 67.3 %all-to-all-done.1 = bf16[8,4,32,1536]{3,2,1,0:T(8,128)(2,1)} async-done(((bf16[8,4,32,1536]{3,2,1,0:T(8,128)(2,1)}), bf16[8,4,32,1536]{3,2,1,0:T(8,128)(2,1)}, u32[]{:S(2)}, u32[]{:S(2)}) %all-to-all-start.1) | async-done | bytes 3145760 | tf_op jit(solution)/shard_map/all_to_all | solution.py:210
  368.7 5.9 %gather_fusion.1 = bf16[512,1536]{1,0:T(8,128)(2,1)S(1)} fusion(bf16[1024,1536]{1,0:T(8,128)(2,1)} %bitcast.33, s32[1024]{0:T(1024)S(1)} %pad_clamp_fusion), kind=kCustom, calls=%fused_computation.1 | custom fusion | bytes 3147776 | tf_op jit(solution)/shard_map/gather | solution.py:212
  374.6 2.2 fusion.37
  376.8 1.7 add_convert_fusion
  (123 shorter events, 23.4 us)
Async XLA Ops:
  7.2 153.6 %copy-start = (bf16[384,1536]{1,0:T(8,128)(2,1)S(1)}, bf16[384,1536]{1,0:T(8,128)(2,1)}, u32[]{:S(2)}) copy-start(bf16[384,1536]{1,0:T(8,128)(2,1)} %param.24) | copy-start | bytes 3538948
  7.2 6.7 %copy-start.1 = (bf16[256,1536]{1,0:T(8,128)(2,1)S(1)}, bf16[256,1536]{1,0:T(8,128)(2,1)}, u32[]{:S(2)}) copy-start(bf16[256,1536]{1,0:T(8,128)(2,1)} %param.19) | copy-start | bytes 2359300
  7.2 6.7 %copy-start.10 = (f32[1536]{0:T(1024)S(1)}, f32[1536]{0:T(1024)}, u32[]{:S(2)}) copy-start(f32[1536]{0:T(1024)} %param.20) | copy-start | bytes 18436
  7.2 5.8 %copy-start.4 = (bf16[512,256]{1,0:T(8,128)(2,1)S(1)}, bf16[512,256]{1,0:T(8,128)(2,1)}, u32[]{:S(2)}) copy-start(bf16[512,256]{1,0:T(8,128)(2,1)} %param.25) | copy-start | bytes 786436
  7.2 6.7 %copy-start.9 = (bf16[1536,384]{1,0:T(8,128)(2,1)S(1)}, bf16[1536,384]{1,0:T(8,128)(2,1)}, u32[]{:S(2)}) copy-start(bf16[1536,384]{1,0:T(8,128)(2,1)} %param.21) | copy-start | bytes 3538948
  7.2 48.1 %all-gather.3.cloned.1.call-start = ((), (), s32[]{:S(2)}) async-start(), calls=%async_computation.4 | async-start | bytes 1179648 | tf_op jit(solution)/shard_map/all_gather | solution.py:137
  13.0 92.7 %all-gather.5.cloned.1.call-start = ((), (), s32[]{:S(2)}) async-start(), calls=%async_computation.5 | async-start | bytes 2359296 | tf_op jit(solution)/shard_map/all_gather | solution.py:138
  13.9 172.4 %reduce-scatter.2.cloned.1.call-start = ((), (), s32[]{:S(2)}) async-start(), calls=%async_computation.6 | async-start | bytes 983040 | tf_op jit(solution)/shard_map/reduce_scatter | solution.py:167
  160.7 1.6 copy-start.5
  160.7 25.6 %copy-start.2 = (bf16[256,1536]{1,0:T(8,128)(2,1)S(1)}, bf16[256,1536]{1,0:T(8,128)(2,1)}, u32[]{:S(2)}) copy-start(bf16[256,1536]{1,0:T(8,128)(2,1)} %param.19) | copy-start | bytes 2359300
  160.7 26.7 %copy-start.7 = (f32[1536]{0:T(1024)S(1)}, f32[1536]{0:T(1024)}, u32[]{:S(2)}) copy-start(f32[1536]{0:T(1024)} %param.26) | copy-start | bytes 18436
  197.9 5.8 %copy-start.3 = (bf16[256,2,2,64]{0,3,2,1:T(8,128)(2,1)S(1)}, bf16[256,2,2,64]{0,3,2,1:T(8,128)(2,1)}, u32[]{:S(2)}) copy-start(bf16[256,2,2,64]{0,3,2,1:T(8,128)(2,1)} %pad_maximum_fusion) | copy-start | bytes 393220
  197.9 76.6 %all-to-all-start = ((bf16[8,4,32,1536]{3,2,1,0:T(8,128)(2,1)}), bf16[8,4,32,1536]{3,2,1,0:T(8,128)(2,1)}, u32[]{:S(2)}, u32[]{:S(2)}) async-start(bf16[8,4,32,1536]{3,2,1,0:T(8,128)(2,1)} %broadcast_select_fusion), calls=%async_computation.1 | async-start | bytes 6291456 | tf_op jit(solution)/shard_map/all_to_all | solution.py:201
  274.5 17.6 %all-to-all-start.2 = ((bf16[4,8,2048]{2,0,1:T(4,128)(2,1)}), bf16[4,8,2048]{2,0,1:T(4,128)(2,1)S(1)}, u32[]{:S(2)}, u32[]{:S(2)}) async-start(bf16[4,8,2048]{2,0,1:T(4,128)(2,1)} %copy.110), calls=%async_computation.3 | async-start | bytes 262144 | tf_op jit(solution)/shard_map/all_to_all | solution.py:95
  292.1 6.1 %copy-start.6 = (f32[64,8]{0,1:T(8,128)S(1)}, f32[64,8]{0,1:T(8,128)}, u32[]{:S(2)}) copy-start(f32[64,8]{0,1:T(8,128)} %param.30) | copy-start | bytes 6148
  292.1 7.1 %copy-start.8 = (s32[256]{0:T(256)S(1)}, s32[256]{0:T(256)}, u32[]{:S(2)}) copy-start(s32[256]{0:T(256)} %param.31) | copy-start | bytes 3076
  292.1 76.6 %all-to-all-start.1 = ((bf16[8,4,32,1536]{3,2,1,0:T(8,128)(2,1)}), bf16[8,4,32,1536]{3,2,1,0:T(8,128)(2,1)}, u32[]{:S(2)}, u32[]{:S(2)}) async-start(bf16[8,4,32,1536]{3,2,1,0:T(8,128)(2,1)} %copy.108), calls=%async_computation.2 | async-start | bytes 6291456 | tf_op jit(solution)/shard_map/all_to_all | solution.py:210
Sparse Core Ops, SparseCore 0:
  13.1 42.2 all-gather.2
  57.5 48.1 all-gather.4
  162.4 23.8 reduce-scatter.1
where the time goes:
time: 386 us; the launch traced here: 385 us
  waiting for transfers between devices  246 us (64%)
  local copies, waits for them, and re-layouts  49.6 us (13%)
  matrix products  28.3 us (7%)
  other arithmetic  28.1 us (7%)
  starting transfers between devices  15.7 us (4%)
  between operations  14.1 us (4%)
    all_to_all x1, waiting for transfers between devices, body(): lax.all_to_all(dispatched, 'seq', split_axis=0, concat_axis=0, tiled=True)  69.6 us
    all_to_all x1, waiting for transfers between devices, body(): lax.all_to_all(produced, 'seq', split_axis=0, concat_axis=0, tiled=True)  67.3 us
    all_gather x1, waiting for transfers between devices, body(): cache_piece = lax.all_gather(cache_lines, 'seq', axis=0, tiled=True)  49 us
    all_gather x1, waiting for transfers between devices, body(): new_piece = lax.all_gather(pairs_new, 'seq', axis=0, tiled=True)  40.6 us
    reduce_scatter x1, waiting for transfers between devices, body(): lax.psum_scatter(jnp.dot(attended, o_weight, preferred_element_type=jnp.f...  19.4 us
    unnamed x26, local copies, waits for them, and re-layouts  11.7 us
    reshape x1, local copies, waits for them, and re-layouts, body(): cache_piece.reshape(piece_rows // stride, 2 * stride, kv_local, 2, head_dim)  8.88 us
  transfers between devices with their start and end apart: 6, of which 5 were waited for; matrix products, arithmetic and copies ran while one was open for 7% of the time, Pallas kernels for 0%

commit v1 on v0

--- a/solution.py
+++ b/solution.py
@@ -177,41 +177,51 @@
     )
     moe_in = rms_norm(residual, moe_gain)
     top_count = routes.shape[1]
-    assigns = moe_rows * top_count
+    experts_here = expert_in.shape[0]
     capacity = 2 * moe_rows * top_count // EXPERTS
-    flat_ids = routes.reshape(-1)
-    hit_table = (flat_ids[:, None] == jnp.arange(EXPERTS, dtype=jnp.int32)[None, :]).astype(
-        jnp.int32
-    )
-    earlier = jnp.cumsum(hit_table, axis=0) - hit_table
-    slot_rank = jnp.sum(earlier * hit_table, axis=1)
-    dest_slot = flat_ids * capacity + slot_rank
-    source = (
-        jnp.full((EXPERTS * capacity,), assigns, jnp.int32)
-        .at[dest_slot]
-        .set(jnp.arange(assigns, dtype=jnp.int32))
-    )
-    filled = source < assigns
-    picked = moe_in[jnp.minimum(source, assigns - 1) // top_count]
-    dispatched = jnp.where(filled[:, None], picked, jnp.zeros_like(picked)).reshape(
-        seq_count, EXPERTS // seq_count, capacity, -1
-    )
-    hidden = jnp.einsum(
-        "sexd,edf->sexf",
-        lax.all_to_all(dispatched, "seq", split_axis=0, concat_axis=0, tiled=True),
-        expert_in,
-        preferred_element_type=jnp.float32,
-    )
+    share = route_prob / jnp.sum(route_prob, axis=-1, keepdims=True)
+    rows_all = lax.all_gather(moe_in, "seq", axis=0, tiled=True)
+    routes_all = lax.all_gather(routes, "seq", axis=0, tiled=True)
+    share_all = lax.all_gather(share, "seq", axis=0, tiled=True)
+    total_rows = rows_all.shape[0]
+    local_ids = seq_index * experts_here + jnp.arange(experts_here, dtype=jnp.int32)
+    hits = routes_all[:, :, None] == local_ids[None, None, :]
+    named = jnp.any(hits, axis=1)
+    weight = jnp.sum(jnp.where(hits, share_all[:, :, None], 0.0), axis=1)
+    named_blocks = named.reshape(seq_count, moe_rows, experts_here).astype(jnp.int32)
+    rank = jnp.cumsum(named_blocks, axis=1) - named_blocks
+    slot = (jnp.arange(seq_count, dtype=jnp.int32)[:, None, None] * capacity + rank).reshape(
+        total_rows, experts_here
+    )
+    slots_total = seq_count * capacity
+    picks = named[:, :, None] & (
+        slot[:, :, None] == jnp.arange(slots_total, dtype=jnp.int32)[None, None, :]
+    )
+    onehot = picks.astype(jnp.bfloat16)
+    rows_in = jnp.einsum(
+        "nec,nd->ecd", onehot, rows_all, preferred_element_type=jnp.float32
+    ).astype(jnp.bfloat16)
+    hidden = jnp.einsum("ecd,edf->ecf", rows_in, expert_in, preferred_element_type=jnp.float32)
     half_width = hidden.shape[-1] // 2
     active = (jax.nn.silu(hidden[..., :half_width]) * hidden[..., half_width:]).astype(jnp.bfloat16)
     produced = jnp.einsum(
-        "sexf,efd->sexd", active, expert_out, preferred_element_type=jnp.float32
+        "ecf,efd->ecd", active, expert_out, preferred_element_type=jnp.float32
     ).astype(jnp.bfloat16)
-    returned = lax.all_to_all(produced, "seq", split_axis=0, concat_axis=0, tiled=True)
-    flat_back = returned.reshape(EXPERTS * capacity, -1)
-    per_assign = flat_back[dest_slot].reshape(moe_rows, top_count, -1)
-    share = route_prob / jnp.sum(route_prob, axis=-1, keepdims=True)
-    moe = jnp.sum(share[..., None] * per_assign.astype(jnp.float32), axis=1)
+    weight_hi = weight.astype(jnp.bfloat16)
+    weight_lo = (weight - weight_hi.astype(jnp.float32)).astype(jnp.bfloat16)
+    scaled_hi = jnp.where(picks, weight_hi[:, :, None], jnp.zeros_like(onehot))
+    scaled_lo = jnp.where(picks, weight_lo[:, :, None], jnp.zeros_like(onehot))
+    partial = jnp.einsum(
+        "nec,ecd->nd", scaled_hi, produced, preferred_element_type=jnp.float32
+    ) + jnp.einsum("nec,ecd->nd", scaled_lo, produced, preferred_element_type=jnp.float32)
+    returned = lax.all_to_all(
+        partial.astype(jnp.bfloat16).reshape(seq_count, moe_rows, -1),
+        "seq",
+        split_axis=0,
+        concat_axis=0,
+        tiled=True,
+    )
+    moe = jnp.sum(returned.astype(jnp.float32), axis=0)
     hidden_out = (residual + residual_scale * moe).astype(jnp.bfloat16)
     return (hidden_out, page_rows)
 

time: 386 us -> 327 us (0.85)
  waiting for transfers between devices: 246 us -> 130 us
  blocking collectives: 0 us -> 63 us
  local copies, waits for them, and re-layouts: 49.6 us -> 38.9 us
  matrix products: 28.3 us -> 38.2 us
  starting transfers between devices: 15.7 us -> 9.77 us
    all_to_all x2 -> x1, waiting for transfers between devices: 137 us -> 16.3 us  [body(): lax.all_to_all(partial.astype(jnp.bfloat16).reshape(seq_count, moe_rows,...]
    all_gather x0 -> x2, blocking collectives: none -> 63 us  [the longest x1 32.6 us: body(): routes_all = lax.all_gather(routes, 'seq', axis=0, tiled=True)]
    gather x2 -> x0, local copies, waits for them, and re-layouts: 11.5 us -> none  [the longest x1 5.89 us: body(): per_assign = flat_back[dest_slot].reshape(moe_rows, top_count, -1)]
    dot_general x2 -> x4, matrix products: 12 us -> 21.9 us  [the longest x1 10.2 us: body(): jnp.einsum('ecd,edf->ecf', rows_in, expert_in, preferred_element_type=jnp...]
    all_to_all x2 -> x1, starting transfers between devices: 11.9 us -> 4.11 us  [body(): lax.all_to_all(partial.astype(jnp.bfloat16).reshape(seq_count, moe_rows,...]
    another operation x2 -> x1, other arithmetic: 1.2 us -> 6.33 us  [body(): rank = jnp.cumsum(named_blocks, axis=1) - named_blocks]
    reduce_scatter x1, waiting for transfers between devices: 19.4 us -> 24 us  [body(): lax.psum_scatter(jnp.dot(attended, o_weight, preferred_element_type=jnp.f...]
    unnamed x26 -> x29, local copies, waits for them, and re-layouts: 11.7 us -> 15 us
  transfers between devices with their start and end apart: 6 -> 6, of which waited for: 5 -> 4; matrix products, arithmetic and copies ran while one was open for 7% -> 13% of each run, Pallas kernels for 0% -> 0%
where the time goes in v1:
time: 327 us; the launch traced here: 325 us
  waiting for transfers between devices  130 us (40%)
  blocking collectives  63 us (19%)
  local copies, waits for them, and re-layouts  38.9 us (12%)
  matrix products  38.2 us (12%)
  other arithmetic  28.1 us (9%)
  between operations  14.1 us (4%)
  starting transfers between devices  9.77 us (3%)
  loops' own time  3.31 us (1%)
    all_gather x1, waiting for transfers between devices, body(): cache_piece = lax.all_gather(cache_lines, 'seq', axis=0, tiled=True)  49 us
    all_gather x1, waiting for transfers between devices, body(): new_piece = lax.all_gather(pairs_new, 'seq', axis=0, tiled=True)  40.6 us
    all_gather x1, blocking collectives, body(): routes_all = lax.all_gather(routes, 'seq', axis=0, tiled=True)  32.6 us
    all_gather x1, blocking collectives, body(): share_all = lax.all_gather(share, 'seq', axis=0, tiled=True)  30.4 us
    reduce_scatter x1, waiting for transfers between devices, body(): lax.psum_scatter(jnp.dot(attended, o_weight, preferred_element_type=jnp.f...  24 us
    all_to_all x1, waiting for transfers between devices, body(): lax.all_to_all(partial.astype(jnp.bfloat16).reshape(seq_count, moe_rows,...  16.3 us
    unnamed x29, local copies, waits for them, and re-layouts  15 us
    dot_general x1, matrix products, body(): jnp.einsum('ecd,edf->ecf', rows_in, expert_in, preferred_element_type=jnp...  10.2 us
  transfers between devices with their start and end apart: 6, of which 4 were waited for; matrix products, arithmetic and copies ran while one was open for 13% of the time, Pallas kernels for 0%

profile of v1, /device:TPU:0, one launch (start us, length us, event | category | flops | bytes accessed | tf_op | source)
XLA Modules:
  0.0 325.4 jit_solution(1514818207814304607)
XLA Ops:
  7.3 1.5 fusion.34
  8.8 1.7 convolution_convert_fusion.5
  10.5 1.7 convolution_convert_fusion.4
  14.7 40.6 %all-gather.6.cloned.1.call-done = bf16[2048,256]{0,1:T(8,128)(2,1)} async-done(((bf16[256,256]{0,1:T(8,128)(2,1)}), bf16[2048,256]{0,1:T(8,128)(2,1)}) %all-gather.6.cloned.1.call-update) | async-done | bytes 1048592 | tf_op jit(solution)/shard_map/all_gather | solution.py:137
  55.4 1.3 copy.129
  56.7 49.0 %all-gather.8.cloned.1.call-done = bf16[2048,512]{1,0:T(8,128)(2,1)} async-done(((bf16[256,512]{1,0:T(8,128)(2,1)}), bf16[2048,512]{1,0:T(8,128)(2,1)}) %all-gather.8.cloned.1.call-update) | async-done | bytes 2097168 | tf_op jit(solution)/shard_map/all_gather | solution.py:138
  105.7 8.9 %reshape.159 = bf16[4,1024,2,2,64]{4,3,2,1,0:T(2,128)(2,1)} reshape(bf16[2048,512]{1,0:T(8,128)(2,1)} %all-gather.8.cloned.1.call-done) | data formatting | bytes 4194304 | tf_op jit(solution)/shard_map/reshape | solution.py:142
  114.6 10.6 %copy.97 = bf16[4,1024,2,2,64]{1,4,2,3,0:T(8,128)(2,1)} copy(bf16[4,1024,2,2,64]{4,3,2,1,0:T(2,128)(2,1)} %reshape.159) | data formatting | bytes 4194304
  125.3 35.4 %while.16 = (s32[]{:T(128)}, f32[2,3,256]{2,1,0:T(4,128)S(1)}, f32[2,3,256]{2,1,0:T(4,128)S(1)}, f32[2,3,256,64]{2,3,1,0:T(8,128)S(1)}, pred[]{:T(512)}, /*index...) while((s32[]{:T(128)}, f32[2,3,256]{2,1,0:T(4,128)S(1)}, ...), condition=%wide.region_11.12_spmd.clone.clone, body=%wide.region_1.11_spmd.clone.clone.sunk | while | flops 627712256 | bytes 33374036 | solution.py:159
  129.0 2.5 conditional.8
  131.5 4.5 %conditional.9 = ((f32[2,3,256]{2,1,0:T(4,128)S(1)}, f32[2,3,256]{2,1,0:T(4,128)S(1)}, f32[2,3,256,64]{2,3,1,0:T(8,128)S(1)})) conditional(s32[]{:T(128)} %convert_element_type.193, (f32[2,3,256]{2,1,0:T(4,128)S(1)}, f32[2,3,256]{2,1,0:T(4,128)S(1)}, f32[2,3,256,64]{2,3,1,0:T(8,128)S(1)}) %get-tuple-element.447, ...), branch_computations={%region_7.7_spmd, %region_8.10_spmd} | conditional | flops 415435776 | bytes 21532708 | solution.py:149
  131.5 1.1 dynamic-slice_bitcast_fusion
  132.6 1.0 bitcast_reduce_fusion
  133.7 1.0 fusion.19
  134.7 1.2 fusion.22
  139.7 4.5 %conditional.9 = ((f32[2,3,256]{2,1,0:T(4,128)S(1)}, f32[2,3,256]{2,1,0:T(4,128)S(1)}, f32[2,3,256,64]{2,3,1,0:T(8,128)S(1)})) conditional(s32[]{:T(128)} %convert_element_type.193, (f32[2,3,256]{2,1,0:T(4,128)S(1)}, f32[2,3,256]{2,1,0:T(4,128)S(1)}, f32[2,3,256,64]{2,3,1,0:T(8,128)S(1)}) %get-tuple-element.447, ...), branch_computations={%region_7.7_spmd, %region_8.10_spmd} | conditional | flops 415435776 | bytes 21532708 | solution.py:149
  139.8 1.1 dynamic-slice_bitcast_fusion
  140.8 1.0 bitcast_reduce_fusion
  141.9 1.0 fusion.19
  143.0 1.2 fusion.22
  148.0 4.5 %conditional.9 = ((f32[2,3,256]{2,1,0:T(4,128)S(1)}, f32[2,3,256]{2,1,0:T(4,128)S(1)}, f32[2,3,256,64]{2,3,1,0:T(8,128)S(1)})) conditional(s32[]{:T(128)} %convert_element_type.193, (f32[2,3,256]{2,1,0:T(4,128)S(1)}, f32[2,3,256]{2,1,0:T(4,128)S(1)}, f32[2,3,256,64]{2,3,1,0:T(8,128)S(1)}) %get-tuple-element.447, ...), branch_computations={%region_7.7_spmd, %region_8.10_spmd} | conditional | flops 415435776 | bytes 21532708 | solution.py:149
  148.0 1.1 dynamic-slice_bitcast_fusion
  149.1 1.0 bitcast_reduce_fusion
  150.1 1.0 fusion.19
  151.2 1.2 fusion.22
  156.2 4.5 %conditional.9 = ((f32[2,3,256]{2,1,0:T(4,128)S(1)}, f32[2,3,256]{2,1,0:T(4,128)S(1)}, f32[2,3,256,64]{2,3,1,0:T(8,128)S(1)})) conditional(s32[]{:T(128)} %convert_element_type.193, (f32[2,3,256]{2,1,0:T(4,128)S(1)}, f32[2,3,256]{2,1,0:T(4,128)S(1)}, f32[2,3,256,64]{2,3,1,0:T(8,128)S(1)}) %get-tuple-element.447, ...), branch_computations={%region_7.7_spmd, %region_8.10_spmd} | conditional | flops 415435776 | bytes 21532708 | solution.py:149
  156.2 1.1 dynamic-slice_bitcast_fusion
  157.3 1.0 bitcast_reduce_fusion
  159.4 1.2 fusion.22
  160.8 1.5 convolution_convert_fusion.2
  162.4 24.0 %reduce-scatter.2.cloned.1.call-done = bf16[64,1536]{1,0:T(8,128)(2,1)} async-done(((bf16[256,1536]{1,0:T(8,128)(2,1)}), bf16[64,1536]{1,0:T(8,128)(2,1)}) %reduce-scatter.2.cloned.1.call-update) | async-done | bytes 196624 | tf_op jit(solution)/shard_map/reduce_scatter | solution.py:167
  186.4 1.1 multiply_reduce_fusion
  187.5 1.7 multiply_convert_fusion
  190.4 5.5 %all-to-all-start.1 = ((bf16[4,8,2048]{2,0,1:T(4,128)(2,1)}), bf16[4,8,2048]{2,0,1:T(4,128)(2,1)S(1)}, u32[]{:S(2)}, u32[]{:S(2)}) async-start(bf16[4,8,2048]{2,0,1:T(4,128)(2,1)} %copy.104), calls=%async_computation.2 | async-start | bytes 262144 | tf_op jit(solution)/shard_map/all_to_all | solution.py:95
  195.9 32.6 %all-gather = s32[8,64,8]{1,2,0:T(8,128)S(1)} all-gather(s32[1,64,8]{1,2,0:T(8,128)S(1)} %bitcast.136), channel_id=1, replica_groups=mesh['seq'=8,'exp'=4] {'seq'}, dimensions={0}, use_global_device_ids=true | all-gather | bytes 18432 | tf_op jit(solution)/shard_map/all_gather | solution.py:184
  229.0 6.3 %fusion.65 = s32[8,64,4]{2,0,1:T(8,128)S(1)} fusion(s32[8,64,4]{2,0,1:T(8,128)S(1)} %copy.99), kind=kOutput, calls=%fused_computation.105 | output fusion | flops 129024 | bytes 16384 | tf_op jit(solution)/shard_map/jit(cumsum)/reduce_window_sum | solution.py:192
  235.8 30.4 %all-gather.1 = f32[8,64,8]{1,2,0:T(8,128)S(1)} all-gather(f32[1,64,8]{1,2,0:T(8,128)S(1)} %divide_bitcast_fusion), channel_id=1, replica_groups=mesh['seq'=8,'exp'=4] {'seq'}, dimensions={0}, use_global_device_ids=true | all-gather | bytes 18432 | tf_op jit(solution)/shard_map/all_gather | solution.py:185
  266.4 10.2 %fusion.66 = f32[4,256,1024]{2,1,0:T(8,128)} fusion(bf16[4,1536,1024]{2,1,0:T(8,128)(2,1)} %param.27, bf16[512,1536]{1,0:T(8,128)(2,1)} %all-gather.10.cloned.1.call-done, s32[512,4]{0,1:T(4,128)S(1)} %subtract_add_fusion, pred[512,4]{0,1:T(4,128)(4,1)S(1)} %compare_reduce_fusion), kind=kOutput, calls=%fused_computation.106 | convolution fusion | flops 4834459648 | bytes 18360320 | tf_op jit(solution)/shard_map/ecd,edf->ecf/dot_general | solution.py:204
  276.6 5.9 %convolution_convert_fusion.1 = bf16[4,256,1536]{2,1,0:T(8,128)(2,1)S(1)} fusion(bf16[4,512,1536]{2,1,0:T(8,128)(2,1)} %param.28, f32[4,256,1024]{2,1,0:T(8,128)} %fusion.66), kind=kOutput, calls=%fused_computation.40 | convolution fusion | flops 1615331328 | bytes 13631488 | tf_op jit(solution)/shard_map/ecf,efd->ecd/dot_general | solution.py:207
  282.5 2.1 convolution_bitcast_fusion
  284.6 3.7 %fusion.28 = bf16[512,1536]{1,0:T(8,128)(2,1)} fusion(f32[512,1536]{1,0:T(8,128)S(1)} %convolution_bitcast_fusion, bf16[4,256,1536]{2,1,0:T(8,128)(2,1)S(1)} %convolution_convert_fusion.1, s32[512,4]{0,1:T(4,128)S(1)} %subtract_add_fusion, pred[512,4]{0,1:T(4,128)(4,1)S(1)} %compare_reduce_fusion, bf16[512,4]{0,1:T(4,128)(2,1)S(1)} %get-tuple-element.320), kind=kOutput, calls=%fused_computation.45 | convolution fusion | flops 1613758464 | bytes 7878656 | tf_op jit(solution)/shard_map/nec,ecd->nd/dot_general | solution.py:214
  289.0 4.1 %all-to-all-start = ((bf16[8,64,1536]{2,1,0:T(8,128)(2,1)}), bf16[8,64,1536]{2,1,0:T(8,128)(2,1)S(1)}, u32[]{:S(2)}, u32[]{:S(2)}) async-start(bf16[8,64,1536]{2,1,0:T(8,128)(2,1)} %bitcast.129), calls=%async_computation.1 | async-start | bytes 3145728 | tf_op jit(solution)/shard_map/all_to_all | solution.py:217
  293.5 1.8 scatter_custom_fusion
  295.3 1.9 reshape.162
  297.2 1.7 copy.115
  298.9 1.8 reshape.186
  300.7 16.3 %all-to-all-done = bf16[8,64,1536]{2,1,0:T(8,128)(2,1)S(1)} async-done(((bf16[8,64,1536]{2,1,0:T(8,128)(2,1)}), bf16[8,64,1536]{2,1,0:T(8,128)(2,1)S(1)}, u32[]{:S(2)}, u32[]{:S(2)}) %all-to-all-start) | async-done | bytes 1572896 | tf_op jit(solution)/shard_map/all_to_all | solution.py:217
  317.2 1.7 add_convert_fusion
  (123 shorter events, 21.7 us)
Async XLA Ops:
  7.2 153.6 %copy-start = (bf16[384,1536]{1,0:T(8,128)(2,1)S(1)}, bf16[384,1536]{1,0:T(8,128)(2,1)}, u32[]{:S(2)}) copy-start(bf16[384,1536]{1,0:T(8,128)(2,1)} %param.24) | copy-start | bytes 3538948
  7.2 6.7 %copy-start.1 = (bf16[256,1536]{1,0:T(8,128)(2,1)S(1)}, bf16[256,1536]{1,0:T(8,128)(2,1)}, u32[]{:S(2)}) copy-start(bf16[256,1536]{1,0:T(8,128)(2,1)} %param.19) | copy-start | bytes 2359300
  7.2 6.7 %copy-start.11 = (f32[1536]{0:T(1024)S(1)}, f32[1536]{0:T(1024)}, u32[]{:S(2)}) copy-start(f32[1536]{0:T(1024)} %param.20) | copy-start | bytes 18436
  7.2 5.8 %copy-start.5 = (bf16[512,256]{1,0:T(8,128)(2,1)S(1)}, bf16[512,256]{1,0:T(8,128)(2,1)}, u32[]{:S(2)}) copy-start(bf16[512,256]{1,0:T(8,128)(2,1)} %param.25) | copy-start | bytes 786436
  7.2 6.7 %copy-start.10 = (bf16[1536,384]{1,0:T(8,128)(2,1)S(1)}, bf16[1536,384]{1,0:T(8,128)(2,1)}, u32[]{:S(2)}) copy-start(bf16[1536,384]{1,0:T(8,128)(2,1)} %param.21) | copy-start | bytes 3538948
  7.2 48.1 %all-gather.6.cloned.1.call-start = ((), (), s32[]{:S(2)}) async-start(), calls=%async_computation.3 | async-start | bytes 1179648 | tf_op jit(solution)/shard_map/all_gather | solution.py:137
  13.0 92.7 %all-gather.8.cloned.1.call-start = ((), (), s32[]{:S(2)}) async-start(), calls=%async_computation.4 | async-start | bytes 2359296 | tf_op jit(solution)/shard_map/all_gather | solution.py:138
  13.9 172.5 %reduce-scatter.2.cloned.1.call-start = ((), (), s32[]{:S(2)}) async-start(), calls=%async_computation.5 | async-start | bytes 983040 | tf_op jit(solution)/shard_map/reduce_scatter | solution.py:167
  160.7 25.7 %copy-start.2 = (bf16[256,1536]{1,0:T(8,128)(2,1)S(1)}, bf16[256,1536]{1,0:T(8,128)(2,1)}, u32[]{:S(2)}) copy-start(bf16[256,1536]{1,0:T(8,128)(2,1)} %param.19) | copy-start | bytes 2359300
  160.7 26.8 %copy-start.7 = (f32[1536]{0:T(1024)S(1)}, f32[1536]{0:T(1024)}, u32[]{:S(2)}) copy-start(f32[1536]{0:T(1024)} %param.26) | copy-start | bytes 18436
  160.7 28.5 %copy-start.3 = (bf16[256,2,2,64]{0,3,2,1:T(8,128)(2,1)S(1)}, bf16[256,2,2,64]{0,3,2,1:T(8,128)(2,1)}, u32[]{:S(2)}) copy-start(bf16[256,2,2,64]{0,3,2,1:T(8,128)(2,1)} %pad_maximum_fusion) | copy-start | bytes 393220
  160.7 35.2 %copy-start.8 = (s32[64,8]{0,1:T(8,128)S(1)}, s32[64,8]{0,1:T(8,128)}, u32[]{:S(2)}) copy-start(s32[64,8]{0,1:T(8,128)} %param.29) | copy-start | bytes 6148
  160.8 74.9 %copy-start.6 = (f32[64,8]{0,1:T(8,128)S(1)}, f32[64,8]{0,1:T(8,128)}, u32[]{:S(2)}) copy-start(f32[64,8]{0,1:T(8,128)} %param.30) | copy-start | bytes 6148
  162.3 104.1 %all-gather.10.cloned.1.call-start = ((), (), s32[]{:S(2)}) async-start(), calls=%async_computation.6 | async-start | bytes 1769472 | tf_op jit(solution)/shard_map/all_gather | solution.py:183
  190.4 97.9 %all-to-all-start.1 = ((bf16[4,8,2048]{2,0,1:T(4,128)(2,1)}), bf16[4,8,2048]{2,0,1:T(4,128)(2,1)S(1)}, u32[]{:S(2)}, u32[]{:S(2)}) async-start(bf16[4,8,2048]{2,0,1:T(4,128)(2,1)} %copy.104), calls=%async_computation.2 | async-start | bytes 262144 | tf_op jit(solution)/shard_map/all_to_all | solution.py:95
  288.4 4.9 %copy-start.9 = (s32[256]{0:T(256)S(1)}, s32[256]{0:T(256)}, u32[]{:S(2)}) copy-start(s32[256]{0:T(256)} %param.31) | copy-start | bytes 3076
  288.4 0.7 copy-start.4
  289.0 28.0 %all-to-all-start = ((bf16[8,64,1536]{2,1,0:T(8,128)(2,1)}), bf16[8,64,1536]{2,1,0:T(8,128)(2,1)S(1)}, u32[]{:S(2)}, u32[]{:S(2)}) async-start(bf16[8,64,1536]{2,1,0:T(8,128)(2,1)} %bitcast.129), calls=%async_computation.1 | async-start | bytes 3145728 | tf_op jit(solution)/shard_map/all_to_all | solution.py:217
Sparse Core Ops, SparseCore 0:
  13.1 42.2 all-gather.5
  57.5 48.1 all-gather.7
  162.4 23.8 reduce-scatter.1
  189.3 44.4 all-gather.9

commit v2 on v1

--- a/solution.py
+++ b/solution.py
@@ -42,6 +42,10 @@
         preferred_element_type=jnp.float32,
     )
     return (best_new, total_new, summed_new)
+
+
+def pl_cdiv(a, b):
+    return -(-a // b)
 
 
 def block_size(piece_rows):
@@ -180,14 +184,35 @@
     experts_here = expert_in.shape[0]
     capacity = 2 * moe_rows * top_count // EXPERTS
     share = route_prob / jnp.sum(route_prob, axis=-1, keepdims=True)
-    rows_all = lax.all_gather(moe_in, "seq", axis=0, tiled=True)
-    routes_all = lax.all_gather(routes, "seq", axis=0, tiled=True)
-    share_all = lax.all_gather(share, "seq", axis=0, tiled=True)
+    expert_ids = jnp.arange(EXPERTS, dtype=jnp.int32)
+    route_hits = routes[:, :, None] == expert_ids[None, None, :]
+    full_weight = jnp.sum(jnp.where(route_hits, share[:, :, None], 0.0), axis=1)
+    full_hi = full_weight.astype(jnp.bfloat16)
+    full_lo = (full_weight - full_hi.astype(jnp.float32)).astype(jnp.bfloat16)
+    full_named = jnp.any(route_hits, axis=1).astype(jnp.bfloat16)
+    model_width = moe_in.shape[1]
+    side_width = 128 * pl_cdiv(3 * EXPERTS, 128)
+    side = jnp.concatenate(
+        [
+            full_named,
+            full_hi,
+            full_lo,
+            jnp.zeros((moe_rows, side_width - 3 * EXPERTS), jnp.bfloat16),
+        ],
+        axis=1,
+    )
+    packed_all = lax.all_gather(
+        jnp.concatenate([moe_in, side], axis=1), "seq", axis=0, tiled=True
+    )
+    rows_all = packed_all[:, :model_width]
     total_rows = rows_all.shape[0]
-    local_ids = seq_index * experts_here + jnp.arange(experts_here, dtype=jnp.int32)
-    hits = routes_all[:, :, None] == local_ids[None, None, :]
-    named = jnp.any(hits, axis=1)
-    weight = jnp.sum(jnp.where(hits, share_all[:, :, None], 0.0), axis=1)
+    local_first = seq_index * experts_here
+    side_all = packed_all[:, model_width:]
+    named = (
+        lax.dynamic_slice_in_dim(side_all, local_first, experts_here, 1) > 0
+    )
+    weight_hi = lax.dynamic_slice_in_dim(side_all, EXPERTS + local_first, experts_here, 1)
+    weight_lo = lax.dynamic_slice_in_dim(side_all, 2 * EXPERTS + local_first, experts_here, 1)
     named_blocks = named.reshape(seq_count, moe_rows, experts_here).astype(jnp.int32)
     rank = jnp.cumsum(named_blocks, axis=1) - named_blocks
     slot = (jnp.arange(seq_count, dtype=jnp.int32)[:, None, None] * capacity + rank).reshape(
@@ -207,8 +232,6 @@
     produced = jnp.einsum(
         "ecf,efd->ecd", active, expert_out, preferred_element_type=jnp.float32
     ).astype(jnp.bfloat16)
-    weight_hi = weight.astype(jnp.bfloat16)
-    weight_lo = (weight - weight_hi.astype(jnp.float32)).astype(jnp.bfloat16)
     scaled_hi = jnp.where(picks, weight_hi[:, :, None], jnp.zeros_like(onehot))
     scaled_lo = jnp.where(picks, weight_lo[:, :, None], jnp.zeros_like(onehot))
     partial = jnp.einsum(

time: 327 us -> 316 us (0.966)
  blocking collectives: 63 us -> 0 us
  waiting for transfers between devices: 130 us -> 181 us
    all_gather x2 -> x0, blocking collectives: 63 us -> none  [the longest x1 32.6 us: body(): routes_all = lax.all_gather(routes, 'seq', axis=0, tiled=True)]
    all_gather x1, waiting for transfers between devices: 0.02 us -> 38.4 us  [body(): lax.all_gather(jnp.concatenate([moe_in, side], axis=1), 'seq', axis=0, ti...]
    all_to_all x1, waiting for transfers between devices: 16.3 us -> 29.4 us  [body(): lax.all_to_all(partial.astype(jnp.bfloat16).reshape(seq_count, moe_rows,...]
    unnamed x29 -> x30, local copies, waits for them, and re-layouts: 15 us -> 15.2 us
  transfers between devices with their start and end apart: 6 -> 6, of which waited for: 4 -> 5; matrix products, arithmetic and copies ran while one was open for 13% -> 14% of each run, Pallas kernels for 0% -> 0%
where the time goes in v2:
time: 316 us; the launch traced here: 315 us
  waiting for transfers between devices  181 us (57%)
  local copies, waits for them, and re-layouts  41.2 us (13%)
  matrix products  38.3 us (12%)
  other arithmetic  27.3 us (9%)
  between operations  14.2 us (4%)
  starting transfers between devices  9.41 us (3%)
  loops' own time  3.31 us (1%)
    all_gather x1, waiting for transfers between devices, body(): cache_piece = lax.all_gather(cache_lines, 'seq', axis=0, tiled=True)  49 us
    all_gather x1, waiting for transfers between devices, body(): new_piece = lax.all_gather(pairs_new, 'seq', axis=0, tiled=True)  40.6 us
    all_gather x1, waiting for transfers between devices, body(): lax.all_gather(jnp.concatenate([moe_in, side], axis=1), 'seq', axis=0, ti...  38.4 us
    all_to_all x1, waiting for transfers between devices, body(): lax.all_to_all(partial.astype(jnp.bfloat16).reshape(seq_count, moe_rows,...  29.4 us
    reduce_scatter x1, waiting for transfers between devices, body(): lax.psum_scatter(jnp.dot(attended, o_weight, preferred_element_type=jnp.f...  23.4 us
    unnamed x30, local copies, waits for them, and re-layouts  15.2 us
    dot_general x1, matrix products, body(): jnp.einsum('ecd,edf->ecf', rows_in, expert_in, preferred_element_type=jnp...  10.2 us
    reshape x1, local copies, waits for them, and re-layouts, body(): cache_piece.reshape(piece_rows // stride, 2 * stride, kv_local, 2, head_dim)  8.88 us
  transfers between devices with their start and end apart: 6, of which 5 were waited for; matrix products, arithmetic and copies ran while one was open for 14% of the time, Pallas kernels for 0%

profile of v2, /device:TPU:0, one launch (start us, length us, event | category | flops | bytes accessed | tf_op | source)
XLA Modules:
  0.0 314.6 jit_solution(17847331740359119873)
XLA Ops:
  7.3 1.5 fusion.34
  8.8 1.7 convolution_convert_fusion.5
  10.5 1.7 convolution_convert_fusion.4
  14.7 40.6 %all-gather.4.cloned.1.call-done = bf16[2048,256]{0,1:T(8,128)(2,1)} async-done(((bf16[256,256]{0,1:T(8,128)(2,1)}), bf16[2048,256]{0,1:T(8,128)(2,1)}) %all-gather.4.cloned.1.call-update) | async-done | bytes 1048592 | tf_op jit(solution)/shard_map/all_gather | solution.py:141
  55.4 1.3 copy.198
  56.7 49.0 %all-gather.6.cloned.1.call-done = bf16[2048,512]{1,0:T(8,128)(2,1)} async-done(((bf16[256,512]{1,0:T(8,128)(2,1)}), bf16[2048,512]{1,0:T(8,128)(2,1)}) %all-gather.6.cloned.1.call-update) | async-done | bytes 2097168 | tf_op jit(solution)/shard_map/all_gather | solution.py:142
  105.7 8.9 %reshape.136 = bf16[4,1024,2,2,64]{4,3,2,1,0:T(2,128)(2,1)} reshape(bf16[2048,512]{1,0:T(8,128)(2,1)} %all-gather.6.cloned.1.call-done) | data formatting | bytes 4194304 | tf_op jit(solution)/shard_map/reshape | solution.py:146
  114.6 10.6 %copy.156 = bf16[4,1024,2,2,64]{1,4,2,3,0:T(8,128)(2,1)} copy(bf16[4,1024,2,2,64]{4,3,2,1,0:T(2,128)(2,1)} %reshape.136) | data formatting | bytes 4194304
  125.3 35.4 %while.16 = (s32[]{:T(128)}, f32[2,3,256]{2,1,0:T(4,128)S(1)}, f32[2,3,256]{2,1,0:T(4,128)S(1)}, f32[2,3,256,64]{2,3,1,0:T(8,128)S(1)}, pred[]{:T(512)}, /*index...) while((s32[]{:T(128)}, f32[2,3,256]{2,1,0:T(4,128)S(1)}, ...), condition=%wide.region_11.12_spmd.clone.clone, body=%wide.region_1.11_spmd.clone.clone.sunk | while | flops 627712256 | bytes 33374036 | solution.py:163
  129.0 2.5 conditional.8
  131.5 4.5 %conditional.9 = ((f32[2,3,256]{2,1,0:T(4,128)S(1)}, f32[2,3,256]{2,1,0:T(4,128)S(1)}, f32[2,3,256,64]{2,3,1,0:T(8,128)S(1)})) conditional(s32[]{:T(128)} %convert_element_type.181, (f32[2,3,256]{2,1,0:T(4,128)S(1)}, f32[2,3,256]{2,1,0:T(4,128)S(1)}, f32[2,3,256,64]{2,3,1,0:T(8,128)S(1)}) %get-tuple-element.488, ...), branch_computations={%region_7.7_spmd, %region_8.10_spmd} | conditional | flops 415435776 | bytes 21532708 | solution.py:153
  131.5 1.1 dynamic-slice_bitcast_fusion
  132.6 1.0 bitcast_reduce_fusion
  133.7 1.0 fusion.19
  134.7 1.2 fusion.22
  139.7 4.5 %conditional.9 = ((f32[2,3,256]{2,1,0:T(4,128)S(1)}, f32[2,3,256]{2,1,0:T(4,128)S(1)}, f32[2,3,256,64]{2,3,1,0:T(8,128)S(1)})) conditional(s32[]{:T(128)} %convert_element_type.181, (f32[2,3,256]{2,1,0:T(4,128)S(1)}, f32[2,3,256]{2,1,0:T(4,128)S(1)}, f32[2,3,256,64]{2,3,1,0:T(8,128)S(1)}) %get-tuple-element.488, ...), branch_computations={%region_7.7_spmd, %region_8.10_spmd} | conditional | flops 415435776 | bytes 21532708 | solution.py:153
  139.8 1.1 dynamic-slice_bitcast_fusion
  140.8 1.0 bitcast_reduce_fusion
  141.9 1.0 fusion.19
  143.0 1.2 fusion.22
  148.0 4.5 %conditional.9 = ((f32[2,3,256]{2,1,0:T(4,128)S(1)}, f32[2,3,256]{2,1,0:T(4,128)S(1)}, f32[2,3,256,64]{2,3,1,0:T(8,128)S(1)})) conditional(s32[]{:T(128)} %convert_element_type.181, (f32[2,3,256]{2,1,0:T(4,128)S(1)}, f32[2,3,256]{2,1,0:T(4,128)S(1)}, f32[2,3,256,64]{2,3,1,0:T(8,128)S(1)}) %get-tuple-element.488, ...), branch_computations={%region_7.7_spmd, %region_8.10_spmd} | conditional | flops 415435776 | bytes 21532708 | solution.py:153
  148.0 1.1 dynamic-slice_bitcast_fusion
  149.1 1.0 bitcast_reduce_fusion
  150.1 1.0 fusion.19
  151.2 1.2 fusion.22
  156.2 4.5 %conditional.9 = ((f32[2,3,256]{2,1,0:T(4,128)S(1)}, f32[2,3,256]{2,1,0:T(4,128)S(1)}, f32[2,3,256,64]{2,3,1,0:T(8,128)S(1)})) conditional(s32[]{:T(128)} %convert_element_type.181, (f32[2,3,256]{2,1,0:T(4,128)S(1)}, f32[2,3,256]{2,1,0:T(4,128)S(1)}, f32[2,3,256,64]{2,3,1,0:T(8,128)S(1)}) %get-tuple-element.488, ...), branch_computations={%region_7.7_spmd, %region_8.10_spmd} | conditional | flops 415435776 | bytes 21532708 | solution.py:153
  156.2 1.1 dynamic-slice_bitcast_fusion
  157.3 1.0 bitcast_reduce_fusion
  158.4 1.0 fusion.19
  159.4 1.2 fusion.22
  160.8 1.5 convolution_convert_fusion.2
  163.0 23.4 %reduce-scatter.4.cloned.1.call-done = bf16[64,1536]{1,0:T(8,128)(2,1)} async-done(((bf16[256,1536]{1,0:T(8,128)(2,1)}), bf16[64,1536]{1,0:T(8,128)(2,1)}) %reduce-scatter.4.cloned.1.call-update) | async-done | bytes 196624 | tf_op jit(solution)/shard_map/reduce_scatter | solution.py:171
  186.4 1.1 multiply_reduce_fusion
  187.5 1.0 multiply_convert_fusion
  190.6 5.5 %all-to-all-start.1 = ((bf16[4,8,2048]{2,0,1:T(4,128)(2,1)}), bf16[4,8,2048]{2,0,1:T(4,128)(2,1)S(1)}, u32[]{:S(2)}, u32[]{:S(2)}) async-start(bf16[4,8,2048]{2,0,1:T(4,128)(2,1)} %copy.167), calls=%async_computation.1 | async-start | bytes 262144 | tf_op jit(solution)/shard_map/all_to_all | solution.py:99
  196.2 38.4 %all-gather.8.cloned.1.call-done = bf16[512,1664]{1,0:T(8,128)(2,1)} async-done(((bf16[64,1664]{1,0:T(8,128)(2,1)}), bf16[512,1664]{1,0:T(8,128)(2,1)}) %all-gather.8.cloned.1.call-update) | async-done | bytes 1703952 | tf_op jit(solution)/shard_map/all_gather | solution.py:204
  236.1 6.3 %fusion.65 = s32[8,64,4]{2,0,1:T(8,128)S(1)} fusion(s32[8,64,4]{2,0,1:T(8,128)S(1)} %copy.163), kind=kOutput, calls=%fused_computation.109 | output fusion | flops 129024 | bytes 16384 | tf_op jit(solution)/shard_map/jit(cumsum)/reduce_window_sum | solution.py:217
  242.9 10.2 %fusion.66 = f32[4,256,1024]{2,1,0:T(8,128)} fusion(bf16[4,1536,1024]{2,1,0:T(8,128)(2,1)} %param.27, bf16[512,1664]{1,0:T(8,128)(2,1)} %all-gather.8.cloned.1.call-done, s32[512,4]{0,1:T(4,128)S(1)} %subtract_add_fusion, pred[512,4]{0,1:T(4,128)(4,1)S(1)} %get-tuple-element.356), kind=kOutput, calls=%fused_computation.110 | convolution fusion | flops 4834459648 | bytes 18360320 | tf_op jit(solution)/shard_map/ecd,edf->ecf/dot_general | solution.py:229
  253.0 5.9 %convolution_convert_fusion.1 = bf16[4,256,1536]{2,1,0:T(8,128)(2,1)S(1)} fusion(bf16[4,512,1536]{2,1,0:T(8,128)(2,1)} %param.28, f32[4,256,1024]{2,1,0:T(8,128)} %fusion.66), kind=kOutput, calls=%fused_computation.40 | convolution fusion | flops 1615331328 | bytes 13631488 | tf_op jit(solution)/shard_map/ecf,efd->ecd/dot_general | solution.py:232
  258.9 2.3 convolution_bitcast_fusion
  261.2 3.7 %fusion.28 = bf16[512,1536]{1,0:T(8,128)(2,1)} fusion(f32[512,1536]{1,0:T(8,128)S(1)} %convolution_bitcast_fusion, bf16[4,256,1536]{2,1,0:T(8,128)(2,1)S(1)} %convolution_convert_fusion.1, s32[512,4]{0,1:T(4,128)S(1)} %subtract_add_fusion, pred[512,4]{0,1:T(4,128)(4,1)S(1)} %get-tuple-element.356, bf16[512,4]{0,1:T(4,128)(2,1)S(1)} %copy.184), kind=kOutput, calls=%fused_computation.45 | convolution fusion | flops 1613758464 | bytes 7878656 | tf_op jit(solution)/shard_map/nec,ecd->nd/dot_general | solution.py:237
  265.6 3.6 %all-to-all-start = ((bf16[8,64,1536]{2,1,0:T(8,128)(2,1)}), bf16[8,64,1536]{2,1,0:T(8,128)(2,1)S(1)}, u32[]{:S(2)}, u32[]{:S(2)}) async-start(bf16[8,64,1536]{2,1,0:T(8,128)(2,1)} %bitcast.123), calls=%async_computation | async-start | bytes 3145728 | tf_op jit(solution)/shard_map/all_to_all | solution.py:240
  269.6 1.8 scatter_custom_fusion
  271.4 1.9 reshape.139
  273.3 1.7 copy.178
  275.0 1.8 reshape.159
  276.8 29.4 %all-to-all-done = bf16[8,64,1536]{2,1,0:T(8,128)(2,1)S(1)} async-done(((bf16[8,64,1536]{2,1,0:T(8,128)(2,1)}), bf16[8,64,1536]{2,1,0:T(8,128)(2,1)S(1)}, u32[]{:S(2)}, u32[]{:S(2)}) %all-to-all-start) | async-done | bytes 1572896 | tf_op jit(solution)/shard_map/all_to_all | solution.py:240
  306.4 1.7 add_convert_fusion
  (127 shorter events, 23.1 us)
Async XLA Ops:
  7.2 153.6 %copy-start = (bf16[384,1536]{1,0:T(8,128)(2,1)S(1)}, bf16[384,1536]{1,0:T(8,128)(2,1)}, u32[]{:S(2)}) copy-start(bf16[384,1536]{1,0:T(8,128)(2,1)} %param.24) | copy-start | bytes 3538948
  7.2 6.7 %copy-start.1 = (bf16[256,1536]{1,0:T(8,128)(2,1)S(1)}, bf16[256,1536]{1,0:T(8,128)(2,1)}, u32[]{:S(2)}) copy-start(bf16[256,1536]{1,0:T(8,128)(2,1)} %param.19) | copy-start | bytes 2359300
  7.2 6.7 %copy-start.11 = (f32[1536]{0:T(1024)S(1)}, f32[1536]{0:T(1024)}, u32[]{:S(2)}) copy-start(f32[1536]{0:T(1024)} %param.20) | copy-start | bytes 18436
  7.2 5.8 %copy-start.5 = (bf16[512,256]{1,0:T(8,128)(2,1)S(1)}, bf16[512,256]{1,0:T(8,128)(2,1)}, u32[]{:S(2)}) copy-start(bf16[512,256]{1,0:T(8,128)(2,1)} %param.25) | copy-start | bytes 786436
  7.2 6.7 %copy-start.10 = (bf16[1536,384]{1,0:T(8,128)(2,1)S(1)}, bf16[1536,384]{1,0:T(8,128)(2,1)}, u32[]{:S(2)}) copy-start(bf16[1536,384]{1,0:T(8,128)(2,1)} %param.21) | copy-start | bytes 3538948
  7.2 48.1 %all-gather.4.cloned.1.call-start = ((), (), s32[]{:S(2)}) async-start(), calls=%async_computation.3 | async-start | bytes 1179648 | tf_op jit(solution)/shard_map/all_gather | solution.py:141
  13.0 92.7 %all-gather.6.cloned.1.call-start = ((), (), s32[]{:S(2)}) async-start(), calls=%async_computation.4 | async-start | bytes 2359296 | tf_op jit(solution)/shard_map/all_gather | solution.py:142
  13.9 172.5 %reduce-scatter.4.cloned.1.call-start = ((), (), s32[]{:S(2)}) async-start(), calls=%async_computation.6 | async-start | bytes 983040 | tf_op jit(solution)/shard_map/reduce_scatter | solution.py:171
  160.7 1.8 copy-start.6
  160.7 1.9 copy-start.7
  160.7 25.6 %copy-start.2 = (bf16[256,1536]{1,0:T(8,128)(2,1)S(1)}, bf16[256,1536]{1,0:T(8,128)(2,1)}, u32[]{:S(2)}) copy-start(bf16[256,1536]{1,0:T(8,128)(2,1)} %param.19) | copy-start | bytes 2359300
  160.7 26.7 %copy-start.8 = (f32[1536]{0:T(1024)S(1)}, f32[1536]{0:T(1024)}, u32[]{:S(2)}) copy-start(f32[1536]{0:T(1024)} %param.26) | copy-start | bytes 18436
  160.7 28.6 %copy-start.3 = (bf16[256,2,2,64]{0,3,2,1:T(8,128)(2,1)S(1)}, bf16[256,2,2,64]{0,3,2,1:T(8,128)(2,1)}, u32[]{:S(2)}) copy-start(bf16[256,2,2,64]{0,3,2,1:T(8,128)(2,1)} %pad_maximum_fusion) | copy-start | bytes 393220
  162.3 72.3 %all-gather.8.cloned.1.call-start = ((), (), s32[]{:S(2)}) async-start(), calls=%async_computation.5 | async-start | bytes 1916928 | tf_op jit(solution)/shard_map/all_gather | solution.py:204
  190.6 74.4 %all-to-all-start.1 = ((bf16[4,8,2048]{2,0,1:T(4,128)(2,1)}), bf16[4,8,2048]{2,0,1:T(4,128)(2,1)S(1)}, u32[]{:S(2)}, u32[]{:S(2)}) async-start(bf16[4,8,2048]{2,0,1:T(4,128)(2,1)} %copy.167), calls=%async_computation.1 | async-start | bytes 262144 | tf_op jit(solution)/shard_map/all_to_all | solution.py:99
  264.9 4.4 %copy-start.9 = (s32[256]{0:T(256)S(1)}, s32[256]{0:T(256)}, u32[]{:S(2)}) copy-start(s32[256]{0:T(256)} %param.31) | copy-start | bytes 3076
  265.0 0.7 copy-start.4
  265.6 40.6 %all-to-all-start = ((bf16[8,64,1536]{2,1,0:T(8,128)(2,1)}), bf16[8,64,1536]{2,1,0:T(8,128)(2,1)S(1)}, u32[]{:S(2)}, u32[]{:S(2)}) async-start(bf16[8,64,1536]{2,1,0:T(8,128)(2,1)} %bitcast.123), calls=%async_computation | async-start | bytes 3145728 | tf_op jit(solution)/shard_map/all_to_all | solution.py:240
Sparse Core Ops, SparseCore 0:
  13.1 42.2 all-gather.3
  57.5 48.1 all-gather.5
  162.4 23.8 reduce-scatter.3
  189.5 45.0 all-gather.7

commit v3 on v2

--- a/solution.py
+++ b/solution.py
@@ -3,13 +3,14 @@
 import jax
 import jax.numpy as jnp
 from jax import lax
-from jax.sharding import PartitionSpec as P
+from jax.sharding import Mesh, PartitionSpec as P
 
 HEADS = 24
 KV_HEADS = 8
 HEAD_DIM = 64
 EXPERTS = 32
 PAGE = 8
+SEQ_AXES = ("half", "hseq")
 
 
 norm_epsilon = 1e-06
@@ -27,7 +28,7 @@
 def attend_block(carried, query_heads, visible, key_rows, value_rows):
     best_old, total_old, summed_old = carried
     scores = (
-        jnp.einsum("tkgd,nkd->kgtn", query_heads, key_rows, preferred_element_type=jnp.float32)
+        jnp.einsum("tkgd,knd->kgtn", query_heads, key_rows, preferred_element_type=jnp.float32)
         * attention_scale
     )
     scores = jnp.where(visible, scores, masked_score)
@@ -36,7 +37,7 @@
     factor = jnp.exp(best_old - best_new)
     total_new = total_old * factor + jnp.sum(weights, axis=-1)
     summed_new = summed_old * factor[..., None] + jnp.einsum(
-        "kgtn,nkd->kgtd",
+        "kgtn,knd->kgtd",
         weights.astype(jnp.bfloat16),
         value_rows,
         preferred_element_type=jnp.float32,
@@ -67,36 +68,36 @@
     route_prob,
     page_slot,
 ):
-    seq_count = lax.axis_size("seq")
-    seq_index = lax.axis_index("seq")
+    halves = lax.axis_size("half")
+    half_size = lax.axis_size("hseq")
+    seq_count = halves * half_size
+    half_index = lax.axis_index("half")
+    half_pos = lax.axis_index("hseq")
+    seq_index = half_index * half_size + half_pos
     exp_index = lax.axis_index("exp")
     tokens_here = hidden_in.shape[0]
     head_dim = HEAD_DIM
     kv_local = k_weight.shape[1] // head_dim
     group_size = HEADS // KV_HEADS
-    prompt_len = tokens_here * seq_count // 2
-    first_row = seq_index * tokens_here
-    query_rows = first_row + jnp.arange(tokens_here, dtype=jnp.int32)
-    query_second = query_rows >= prompt_len
-    holds_first = first_row < prompt_len
+    holds_first = half_index == 0
     normed = rms_norm(hidden_in, attn_gain)
     queries = jnp.dot(normed, q_weight, preferred_element_type=jnp.float32).astype(jnp.bfloat16)
     keys_new = jnp.dot(normed, k_weight, preferred_element_type=jnp.float32).astype(jnp.bfloat16)
     values_new = jnp.dot(normed, v_weight, preferred_element_type=jnp.float32).astype(jnp.bfloat16)
     pair_width = 2 * kv_local * head_dim
-    pairs_new = jnp.stack(
+    split_new = jnp.stack(
         [
             keys_new.reshape(tokens_here, kv_local, head_dim),
             values_new.reshape(tokens_here, kv_local, head_dim),
         ],
         axis=2,
-    ).reshape(tokens_here, pair_width)
+    )
+    pairs_new = split_new.reshape(tokens_here, pair_width)
     query_heads = queries.reshape(tokens_here, kv_local, group_size, head_dim)
-    cache_lines = cache_kv.reshape(tokens_here, -1)
     blocks_here = tokens_here // PAGE
     rounds = blocks_here // seq_count
     outgoing = pairs_new.reshape(rounds, seq_count, PAGE * pair_width)
-    received = lax.all_to_all(outgoing, "seq", split_axis=1, concat_axis=1, tiled=True)
+    received = lax.all_to_all(outgoing, SEQ_AXES, split_axis=1, concat_axis=1, tiled=True)
     block_ids = (
         jnp.arange(seq_count, dtype=jnp.int32)[None, :] * blocks_here
         + jnp.arange(rounds, dtype=jnp.int32)[:, None] * seq_count
@@ -120,47 +121,34 @@
         jnp.zeros((kv_local, group_size, tokens_here), jnp.float32),
         jnp.zeros((kv_local, group_size, tokens_here, head_dim), jnp.float32),
     )
-
-    def new_keys_part(carried, new_block, key_first):
-        width_rows = new_block.shape[0]
-        key_rows = key_first + jnp.arange(width_rows, dtype=jnp.int32)
-        visible = ((key_rows >= prompt_len)[None, :] == query_second[:, None]) & (
-            key_rows[None, :] <= query_rows[:, None]
-        )
-        split_pairs = new_block.reshape(width_rows, kv_local, 2, head_dim)
-        return lax.cond(
-            jnp.any(visible),
-            lambda carried_in: attend_block(
-                carried_in, query_heads, visible, split_pairs[:, :, 0], split_pairs[:, :, 1]
-            ),
-            lambda carried_in: carried_in,
-            carried,
-        )
-
-    carried = start_state
-    new_piece = lax.all_gather(pairs_new, "seq", axis=0, tiled=True)
-    cache_piece = lax.all_gather(cache_lines, "seq", axis=0, tiled=True)
-    piece_rows = new_piece.shape[0]
-    stride = block_size(piece_rows)
-    new_blocks = new_piece.reshape(piece_rows // stride, stride, -1)
-    cache_blocks = cache_piece.reshape(piece_rows // stride, 2 * stride, kv_local, 2, head_dim)
-    offsets = stride * jnp.arange(piece_rows // stride, dtype=jnp.int32)
-    everything = jnp.ones((tokens_here, 2 * stride), bool)
-
-    def visit(carried_in, block_part):
-        new_block, cache_block, key_first = block_part
-        carried_in = new_keys_part(carried_in, new_block, key_first)
+    kv_own = split_new.transpose(2, 1, 0, 3)
+    kv_half = lax.all_gather(kv_own, "hseq", axis=2, tiled=True)
+    cache_rows = cache_kv.shape[0]
+    cache_own = cache_kv.reshape(cache_rows, kv_local, 2, head_dim).transpose(2, 1, 0, 3)
+    cache_far = lax.ppermute(cache_own, "half", perm=[(1, 0)])
+    cache_piece = jnp.concatenate([cache_own, cache_far], axis=2)
+    cache_all = lax.all_gather(cache_piece, "hseq", axis=2, tiled=True)
+    query_pos = half_pos * tokens_here + jnp.arange(tokens_here, dtype=jnp.int32)
+    key_pos = jnp.arange(kv_half.shape[2], dtype=jnp.int32)
+    visible_new = key_pos[None, :] <= query_pos[:, None]
+    carried = attend_block(start_state, query_heads, visible_new, kv_half[0], kv_half[1])
+    stride = block_size(cache_all.shape[2])
+    cache_blocks = cache_all.reshape(2, kv_local, cache_all.shape[2] // stride, stride, head_dim)
+    cache_blocks = cache_blocks.transpose(2, 0, 1, 3, 4)
+    everything = jnp.ones((tokens_here, stride), bool)
+
+    def visit(carried_in, cache_block):
         carried_in = lax.cond(
             holds_first,
             lambda inner: attend_block(
-                inner, query_heads, everything, cache_block[:, :, 0], cache_block[:, :, 1]
+                inner, query_heads, everything, cache_block[0], cache_block[1]
             ),
             lambda inner: inner,
             carried_in,
         )
         return (carried_in, None)
 
-    carried, _ = lax.scan(visit, carried, (new_blocks, cache_blocks, offsets))
+    carried, _ = lax.scan(visit, carried, cache_blocks)
     best_final, total_final, summed_final = carried
     attended = (
         (summed_final / total_final[..., None])
@@ -202,7 +190,7 @@
         axis=1,
     )
     packed_all = lax.all_gather(
-        jnp.concatenate([moe_in, side], axis=1), "seq", axis=0, tiled=True
+        jnp.concatenate([moe_in, side], axis=1), SEQ_AXES, axis=0, tiled=True
     )
     rows_all = packed_all[:, :model_width]
     total_rows = rows_all.shape[0]
@@ -239,7 +227,7 @@
     ) + jnp.einsum("nec,ecd->nd", scaled_lo, produced, preferred_element_type=jnp.float32)
     returned = lax.all_to_all(
         partial.astype(jnp.bfloat16).reshape(seq_count, moe_rows, -1),
-        "seq",
+        SEQ_AXES,
         split_axis=0,
         concat_axis=0,
         tiled=True,
@@ -250,24 +238,28 @@
 
 
 def solution(mesh):
+    seq_count, exp_count = mesh.devices.shape
+    split_mesh = Mesh(
+        mesh.devices.reshape(2, seq_count // 2, exp_count), ("half", "hseq", "exp")
+    )
     return jax.shard_map(
         body,
-        mesh=mesh,
+        mesh=split_mesh,
         in_specs=(
-            P("seq", None),
+            P(SEQ_AXES, None),
             P(),
             P(None, "exp"),
             P(None, "exp"),
             P(None, "exp"),
             P("exp", None),
-            P("seq", "exp"),
+            P(SEQ_AXES, "exp"),
             P(),
-            P("seq", None, None),
-            P("seq", None, None),
-            P(("seq", "exp"), None),
-            P(("seq", "exp"), None),
+            P(SEQ_AXES, None, None),
+            P(SEQ_AXES, None, None),
+            P(("half", "hseq", "exp"), None),
+            P(("half", "hseq", "exp"), None),
             P(),
         ),
-        out_specs=(P(("seq", "exp"), None), P("seq", "exp", None, None)),
+        out_specs=(P(("half", "hseq", "exp"), None), P(SEQ_AXES, "exp", None, None)),
         check_vma=False,
     )

time: 316 us -> 284 us (0.90)
  waiting for transfers between devices: 181 us -> 119 us
  matrix products: 38.3 us -> 63.4 us
  blocking collectives: 0 us -> 24.7 us
  local copies, waits for them, and re-layouts: 41.2 us -> 31.4 us
  other arithmetic: 27.3 us -> 19.2 us
    all_gather x3 -> x2, waiting for transfers between devices: 128 us -> 56.4 us  [the longest x1 38.4 us: body(): lax.all_gather(jnp.concatenate([moe_in, side], axis=1), SEQ_AXES, axis=0,...]
    dot_general x10 -> x18, matrix products: 10.7 us -> 36.7 us  [the longest x9 23.2 us: attend_block(): jnp.einsum('kgtn,knd->kgtd', weights.astype(jnp.bfloat16), value_rows, pr...]
    all_gather x0 -> x1, blocking collectives: none -> 24.7 us  [body(): kv_half = lax.all_gather(kv_own, 'hseq', axis=2, tiled=True)]
    cond x5 -> x24, local copies, waits for them, and re-layouts: 0.02 us -> 13.2 us
    ppermute x0 -> x1, waiting for transfers between devices: none -> 12.3 us  [body(): cache_far = lax.ppermute(cache_own, 'half', perm=[(1, 0)])]
    reshape x3 -> x0, local copies, waits for them, and re-layouts: 11 us -> none  [the longest x1 8.88 us: body(): cache_piece.reshape(piece_rows // stride, 2 * stride, kv_local, 2, head_dim)]
    unnamed x30 -> x27, local copies, waits for them, and re-layouts: 15.2 us -> 8.26 us
    squeeze x4 -> x0, local copies, waits for them, and re-layouts: 4.33 us -> none  [body(): carried, _ = lax.scan(visit, carried, (new_blocks, cache_blocks, offsets))]
  transfers between devices with their start and end apart: 6 -> 6, of which waited for: 5 -> 5; matrix products, arithmetic and copies ran while one was open for 14% -> 17% of each run, Pallas kernels for 0% -> 0%
where the time goes in v3:
time: 284 us; the launch traced here: 283 us
  waiting for transfers between devices  119 us (42%)
  matrix products  63.4 us (22%)
  local copies, waits for them, and re-layouts  31.4 us (11%)
  blocking collectives  24.7 us (9%)
  other arithmetic  19.2 us (7%)
  between operations  14.1 us (5%)
  starting transfers between devices  10.5 us (4%)
    all_gather x1, waiting for transfers between devices, body(): lax.all_gather(jnp.concatenate([moe_in, side], axis=1), SEQ_AXES, axis=0,...  38.4 us
    all_to_all x1, waiting for transfers between devices, body(): lax.all_to_all(partial.astype(jnp.bfloat16).reshape(seq_count, moe_rows,...  29.3 us
    all_gather x1, blocking collectives, body(): kv_half = lax.all_gather(kv_own, 'hseq', axis=2, tiled=True)  24.7 us
    dot_general x9, matrix products, attend_block(): jnp.einsum('kgtn,knd->kgtd', weights.astype(jnp.bfloat16), value_rows, pr...  23.2 us
    reduce_scatter x1, waiting for transfers between devices, body(): lax.psum_scatter(jnp.dot(attended, o_weight, preferred_element_type=jnp.f...  20.8 us
    all_gather x1, waiting for transfers between devices, body(): cache_all = lax.all_gather(cache_piece, 'hseq', axis=2, tiled=True)  18.1 us
    dot_general x9, matrix products, attend_block(): jnp.einsum('tkgd,knd->kgtn', query_heads, key_rows, preferred_element_typ...  13.5 us
    cond x24, local copies, waits for them, and re-layouts  13.2 us
  transfers between devices with their start and end apart: 6, of which 5 were waited for; matrix products, arithmetic and copies ran while one was open for 17% of the time, Pallas kernels for 0%

profile of v3, /device:TPU:0, one launch (start us, length us, event | category | flops | bytes accessed | tf_op | source)
XLA Modules:
  0.0 282.9 jit_solution(13722504334293530569)
XLA Ops:
  11.2 2.2 convolution_convert_fusion.3
  13.4 12.3 %collective-permute-done = bf16[2,2,512,64]{2,3,0,1:T(8,128)(2,1)S(1)} collective-permute-done((bf16[2,2,512,64]{2,3,0,1:T(8,128)(2,1)S(1)}, bf16[2,2,512,64]{2,3,0,1:T(8,128)(2,1)S(1)}, u32[]{:S(2)}, u32[]{:S(2)}) %collective-permute-start) | collective-permute-done | bytes 262176 | tf_op jit(solution)/shard_map/ppermute | solution.py:128
  27.9 24.7 %all_gather.9 = bf16[2,2,1024,64]{2,3,1,0:T(8,128)(2,1)S(1)} all-gather(bf16[2,2,256,64]{2,3,1,0:T(8,128)(2,1)S(1)} %get-tuple-element.175), channel_id=1, replica_groups=mesh['half'=2,'hseq'=4,'exp'=4] {'hseq'}, dimensions={2}, use_global_device_ids=true | all-gather | bytes 655360 | tf_op jit(solution)/shard_map/all_gather | solution.py:125
  55.5 1.7 fusion.30
  57.2 18.1 %all-gather.3.cloned.1.call-done = bf16[2,2,4096,64]{2,3,0,1:T(8,128)(2,1)} async-done(((bf16[2,2,1024,64]{2,3,0,1:T(8,128)(2,1)}), bf16[2,2,4096,64]{2,3,0,1:T(8,128)(2,1)}) %all-gather.3.cloned.1.call-update) | async-done | bytes 2097168 | tf_op jit(solution)/shard_map/all_gather | solution.py:130
  75.2 2.5 copy.175
  77.7 2.1 copy.143
  79.8 52.1 %while.14 = (s32[]{:T(128)}, f32[2,3,256]{2,1,0:T(4,128)S(1)}, f32[2,3,256]{2,1,0:T(4,128)S(1)}, f32[2,3,256,64]{2,3,1,0:T(8,128)S(1)}, pred[]{:T(512)}, /*index...) while((s32[]{:T(128)}, f32[2,3,256]{2,1,0:T(4,128)S(1)}, ...), condition=%wide.region_8.9_spmd, body=%wide.region_3.8_spmd.sunk | while | flops 207817728 | bytes 23364844 | solution.py:151
  79.8 6.5 %conditional.2 = ((f32[2,3,256]{2,1,0:T(4,128)S(1)}, f32[2,3,256]{2,1,0:T(4,128)S(1)}, f32[2,3,256,64]{2,3,1,0:T(8,128)S(1)})) conditional(s32[]{:T(128)} %convert_element_type.174, (f32[2,3,256]{2,1,0:T(4,128)S(1)}, f32[2,3,256]{2,1,0:T(4,128)S(1)}, f32[2,3,256,64]{2,3,1,0:T(8,128)S(1)}) %tuple.57, (bf16[8,2,2,512,64]{3,4,2,1,0:T(8,128)(2,1)}, ...), branch_computations={%region_4.4_spmd, %region_5.7_spmd} | conditional | flops 207817728 | bytes 23364684 | solution.py:141
  81.4 1.6 copy-done.1
  83.6 2.7 fusion.7
  86.3 6.5 %conditional.2 = ((f32[2,3,256]{2,1,0:T(4,128)S(1)}, f32[2,3,256]{2,1,0:T(4,128)S(1)}, f32[2,3,256,64]{2,3,1,0:T(8,128)S(1)})) conditional(s32[]{:T(128)} %convert_element_type.174, (f32[2,3,256]{2,1,0:T(4,128)S(1)}, f32[2,3,256]{2,1,0:T(4,128)S(1)}, f32[2,3,256,64]{2,3,1,0:T(8,128)S(1)}) %tuple.57, (bf16[8,2,2,512,64]{3,4,2,1,0:T(8,128)(2,1)}, ...), branch_computations={%region_4.4_spmd, %region_5.7_spmd} | conditional | flops 207817728 | bytes 23364684 | solution.py:141
  87.9 1.6 copy-done.1
  90.1 2.7 fusion.7
  92.8 6.5 %conditional.2 = ((f32[2,3,256]{2,1,0:T(4,128)S(1)}, f32[2,3,256]{2,1,0:T(4,128)S(1)}, f32[2,3,256,64]{2,3,1,0:T(8,128)S(1)})) conditional(s32[]{:T(128)} %convert_element_type.174, (f32[2,3,256]{2,1,0:T(4,128)S(1)}, f32[2,3,256]{2,1,0:T(4,128)S(1)}, f32[2,3,256,64]{2,3,1,0:T(8,128)S(1)}) %tuple.57, (bf16[8,2,2,512,64]{3,4,2,1,0:T(8,128)(2,1)}, ...), branch_computations={%region_4.4_spmd, %region_5.7_spmd} | conditional | flops 207817728 | bytes 23364684 | solution.py:141
  94.4 1.6 copy-done.1
  96.6 2.7 fusion.7
  99.3 6.5 %conditional.2 = ((f32[2,3,256]{2,1,0:T(4,128)S(1)}, f32[2,3,256]{2,1,0:T(4,128)S(1)}, f32[2,3,256,64]{2,3,1,0:T(8,128)S(1)})) conditional(s32[]{:T(128)} %convert_element_type.174, (f32[2,3,256]{2,1,0:T(4,128)S(1)}, f32[2,3,256]{2,1,0:T(4,128)S(1)}, f32[2,3,256,64]{2,3,1,0:T(8,128)S(1)}) %tuple.57, (bf16[8,2,2,512,64]{3,4,2,1,0:T(8,128)(2,1)}, ...), branch_computations={%region_4.4_spmd, %region_5.7_spmd} | conditional | flops 207817728 | bytes 23364684 | solution.py:141
  100.9 1.6 copy-done.1
  103.1 2.7 fusion.7
  105.9 6.5 %conditional.2 = ((f32[2,3,256]{2,1,0:T(4,128)S(1)}, f32[2,3,256]{2,1,0:T(4,128)S(1)}, f32[2,3,256,64]{2,3,1,0:T(8,128)S(1)})) conditional(s32[]{:T(128)} %convert_element_type.174, (f32[2,3,256]{2,1,0:T(4,128)S(1)}, f32[2,3,256]{2,1,0:T(4,128)S(1)}, f32[2,3,256,64]{2,3,1,0:T(8,128)S(1)}) %tuple.57, (bf16[8,2,2,512,64]{3,4,2,1,0:T(8,128)(2,1)}, ...), branch_computations={%region_4.4_spmd, %region_5.7_spmd} | conditional | flops 207817728 | bytes 23364684 | solution.py:141
  105.9 1.5 bitcast_reduce_fusion
  107.4 1.6 copy-done.1
  109.6 2.7 fusion.7
  112.4 6.5 %conditional.2 = ((f32[2,3,256]{2,1,0:T(4,128)S(1)}, f32[2,3,256]{2,1,0:T(4,128)S(1)}, f32[2,3,256,64]{2,3,1,0:T(8,128)S(1)})) conditional(s32[]{:T(128)} %convert_element_type.174, (f32[2,3,256]{2,1,0:T(4,128)S(1)}, f32[2,3,256]{2,1,0:T(4,128)S(1)}, f32[2,3,256,64]{2,3,1,0:T(8,128)S(1)}) %tuple.57, (bf16[8,2,2,512,64]{3,4,2,1,0:T(8,128)(2,1)}, ...), branch_computations={%region_4.4_spmd, %region_5.7_spmd} | conditional | flops 207817728 | bytes 23364684 | solution.py:141
  114.0 1.6 copy-done.1
  116.2 2.7 fusion.7
  118.9 6.5 %conditional.2 = ((f32[2,3,256]{2,1,0:T(4,128)S(1)}, f32[2,3,256]{2,1,0:T(4,128)S(1)}, f32[2,3,256,64]{2,3,1,0:T(8,128)S(1)})) conditional(s32[]{:T(128)} %convert_element_type.174, (f32[2,3,256]{2,1,0:T(4,128)S(1)}, f32[2,3,256]{2,1,0:T(4,128)S(1)}, f32[2,3,256,64]{2,3,1,0:T(8,128)S(1)}) %tuple.57, (bf16[8,2,2,512,64]{3,4,2,1,0:T(8,128)(2,1)}, ...), branch_computations={%region_4.4_spmd, %region_5.7_spmd} | conditional | flops 207817728 | bytes 23364684 | solution.py:141
  120.5 1.6 copy-done.1
  122.7 2.7 fusion.7
  125.4 6.5 %conditional.2 = ((f32[2,3,256]{2,1,0:T(4,128)S(1)}, f32[2,3,256]{2,1,0:T(4,128)S(1)}, f32[2,3,256,64]{2,3,1,0:T(8,128)S(1)})) conditional(s32[]{:T(128)} %convert_element_type.174, (f32[2,3,256]{2,1,0:T(4,128)S(1)}, f32[2,3,256]{2,1,0:T(4,128)S(1)}, f32[2,3,256,64]{2,3,1,0:T(8,128)S(1)}) %tuple.57, (bf16[8,2,2,512,64]{3,4,2,1,0:T(8,128)(2,1)}, ...), branch_computations={%region_4.4_spmd, %region_5.7_spmd} | conditional | flops 207817728 | bytes 23364684 | solution.py:141
  127.0 1.6 copy-done.1
  129.2 2.7 fusion.7
  134.0 20.8 %reduce-scatter.4.cloned.1.call-done = bf16[64,1536]{1,0:T(8,128)(2,1)} async-done(((bf16[256,1536]{1,0:T(8,128)(2,1)}), bf16[64,1536]{1,0:T(8,128)(2,1)}) %reduce-scatter.4.cloned.1.call-update) | async-done | bytes 196624 | tf_op jit(solution)/shard_map/reduce_scatter | solution.py:159
  158.9 5.5 %all-to-all-start.1 = ((bf16[4,8,2048]{2,0,1:T(4,128)(2,1)}), bf16[4,8,2048]{2,0,1:T(4,128)(2,1)S(1)}, u32[]{:S(2)}, u32[]{:S(2)}) async-start(bf16[4,8,2048]{2,0,1:T(4,128)(2,1)} %copy.154), calls=%async_computation.1 | async-start | bytes 262144 | tf_op jit(solution)/shard_map/all_to_all | solution.py:100
  164.6 38.4 %all-gather.5.cloned.1.call-done = bf16[512,1664]{1,0:T(8,128)(2,1)} async-done(((bf16[64,1664]{1,0:T(8,128)(2,1)}), bf16[512,1664]{1,0:T(8,128)(2,1)}) %all-gather.5.cloned.1.call-update) | async-done | bytes 1703952 | tf_op jit(solution)/shard_map/all_gather | solution.py:192
  204.5 6.3 %fusion.66 = s32[8,64,4]{2,0,1:T(8,128)S(1)} fusion(s32[8,64,4]{2,0,1:T(8,128)S(1)} %copy.150), kind=kOutput, calls=%fused_computation.106 | output fusion | flops 129024 | bytes 16384 | tf_op jit(solution)/shard_map/jit(cumsum)/reduce_window_sum | solution.py:205
  211.3 10.2 %fusion.67 = f32[4,256,1024]{2,1,0:T(8,128)} fusion(bf16[4,1536,1024]{2,1,0:T(8,128)(2,1)} %param.25, bf16[512,1664]{1,0:T(8,128)(2,1)} %all-gather.5.cloned.1.call-done, s32[512,4]{0,1:T(4,128)S(1)} %subtract_add_fusion, pred[512,4]{0,1:T(4,128)(4,1)S(1)} %get-tuple-element.169), kind=kOutput, calls=%fused_computation.107 | convolution fusion | flops 4834459648 | bytes 18360320 | tf_op jit(solution)/shard_map/ecd,edf->ecf/dot_general | solution.py:217
  221.5 5.9 %convolution_convert_fusion.1 = bf16[4,256,1536]{2,1,0:T(8,128)(2,1)S(1)} fusion(bf16[4,512,1536]{2,1,0:T(8,128)(2,1)} %param.26, f32[4,256,1024]{2,1,0:T(8,128)} %fusion.67), kind=kOutput, calls=%fused_computation.24 | convolution fusion | flops 1615331328 | bytes 13631488 | tf_op jit(solution)/shard_map/ecf,efd->ecd/dot_general | solution.py:220
  227.4 2.3 convolution_bitcast_fusion
  229.6 3.7 %fusion.21 = bf16[512,1536]{1,0:T(8,128)(2,1)} fusion(f32[512,1536]{1,0:T(8,128)S(1)} %convolution_bitcast_fusion, bf16[4,256,1536]{2,1,0:T(8,128)(2,1)S(1)} %convolution_convert_fusion.1, s32[512,4]{0,1:T(4,128)S(1)} %subtract_add_fusion, pred[512,4]{0,1:T(4,128)(4,1)S(1)} %get-tuple-element.169, bf16[512,4]{0,1:T(4,128)(2,1)S(1)} %copy.173), kind=kOutput, calls=%fused_computation.31 | convolution fusion | flops 1613758464 | bytes 7878656 | tf_op jit(solution)/shard_map/nec,ecd->nd/dot_general | solution.py:225
  234.0 3.6 %all-to-all-start = ((bf16[8,64,1536]{2,1,0:T(8,128)(2,1)}), bf16[8,64,1536]{2,1,0:T(8,128)(2,1)S(1)}, u32[]{:S(2)}, u32[]{:S(2)}) async-start(bf16[8,64,1536]{2,1,0:T(8,128)(2,1)} %bitcast.124), calls=%async_computation | async-start | bytes 3145728 | tf_op jit(solution)/shard_map/all_to_all | solution.py:228
  238.0 1.8 scatter_custom_fusion
  239.8 1.9 reshape.135
  241.7 1.7 copy.167
  243.4 1.8 reshape.154
  245.2 29.3 %all-to-all-done = bf16[8,64,1536]{2,1,0:T(8,128)(2,1)S(1)} async-done(((bf16[8,64,1536]{2,1,0:T(8,128)(2,1)}), bf16[8,64,1536]{2,1,0:T(8,128)(2,1)S(1)}, u32[]{:S(2)}, u32[]{:S(2)}) %all-to-all-start) | async-done | bytes 1572896 | tf_op jit(solution)/shard_map/all_to_all | solution.py:228
  274.7 1.7 add_convert_fusion
  (128 shorter events, 33.6 us)
Async XLA Ops:
  7.2 124.8 %copy-start = (bf16[384,1536]{1,0:T(8,128)(2,1)S(1)}, bf16[384,1536]{1,0:T(8,128)(2,1)}, u32[]{:S(2)}) copy-start(bf16[384,1536]{1,0:T(8,128)(2,1)} %param.22) | copy-start | bytes 3538948
  7.2 19.7 %copy-start.2 = (bf16[256,1536]{1,0:T(8,128)(2,1)S(1)}, bf16[256,1536]{1,0:T(8,128)(2,1)}, u32[]{:S(2)}) copy-start(bf16[256,1536]{1,0:T(8,128)(2,1)} %param.17) | copy-start | bytes 2359300
  7.2 19.7 %copy-start.10 = (f32[1536]{0:T(1024)S(1)}, f32[1536]{0:T(1024)}, u32[]{:S(2)}) copy-start(f32[1536]{0:T(1024)} %param.18) | copy-start | bytes 18436
  7.2 19.7 %copy-start.8 = (bf16[1536,128]{1,0:T(8,128)(2,1)S(1)}, bf16[1536,128]{1,0:T(8,128)(2,1)}, u32[]{:S(2)}) copy-start(bf16[1536,128]{1,0:T(8,128)(2,1)} %param.20) | copy-start | bytes 1179652
  7.2 68.0 %all-gather.3.cloned.1.call-start = ((), (), s32[]{:S(2)}) async-start(), calls=%async_computation.3 | async-start | bytes 2621440 | tf_op jit(solution)/shard_map/all_gather | solution.py:130
  8.5 17.2 %collective-permute-start = (bf16[2,2,512,64]{2,3,0,1:T(8,128)(2,1)S(1)}, bf16[2,2,512,64]{2,3,0,1:T(8,128)(2,1)S(1)}, u32[]{:S(2)}, u32[]{:S(2)}) collective-permute-start(bf16[2,2,512,64]{2,3,0,1:T(8,128)(2,1)S(1)} %bitcast.126), channel_id=1, source_target_pairs={{16,0},{17,1},{18,2},{19,3},{20,4},{21,5},{22,6},{23,7},{24,8},{25... | collective-permute-start | bytes 786440 | tf_op jit(solution)/shard_map/ppermute | solution.py:128
  11.2 16.2 %copy-start.9 = (bf16[1536,128]{1,0:T(8,128)(2,1)S(1)}, bf16[1536,128]{1,0:T(8,128)(2,1)}, u32[]{:S(2)}) copy-start(bf16[1536,128]{1,0:T(8,128)(2,1)} %param.21) | copy-start | bytes 1179652
  26.6 128.1 %reduce-scatter.4.cloned.1.call-start = ((), (), s32[]{:S(2)}) async-start(), calls=%async_computation.5 | async-start | bytes 983040 | tf_op jit(solution)/shard_map/reduce_scatter | solution.py:159
  81.3 1.7 copy-start.1
  87.9 1.7 copy-start.1
  94.4 1.7 copy-start.1
  100.9 1.7 copy-start.1
  107.4 1.7 copy-start.1
  113.9 1.7 copy-start.1
  120.5 1.7 copy-start.1
  127.0 1.7 copy-start.1
  131.9 1.6 copy-start.4
  131.9 1.7 copy-start.5
  131.9 23.9 %copy-start.6 = (f32[1536]{0:T(1024)S(1)}, f32[1536]{0:T(1024)}, u32[]{:S(2)}) copy-start(f32[1536]{0:T(1024)} %param.24) | copy-start | bytes 18436
  133.5 69.5 %all-gather.5.cloned.1.call-start = ((), (), s32[]{:S(2)}) async-start(), calls=%async_computation.4 | async-start | bytes 1916928 | tf_op jit(solution)/shard_map/all_gather | solution.py:192
  158.9 74.4 %all-to-all-start.1 = ((bf16[4,8,2048]{2,0,1:T(4,128)(2,1)}), bf16[4,8,2048]{2,0,1:T(4,128)(2,1)S(1)}, u32[]{:S(2)}, u32[]{:S(2)}) async-start(bf16[4,8,2048]{2,0,1:T(4,128)(2,1)} %copy.154), calls=%async_computation.1 | async-start | bytes 262144 | tf_op jit(solution)/shard_map/all_to_all | solution.py:100
  233.4 4.4 %copy-start.7 = (s32[256]{0:T(256)S(1)}, s32[256]{0:T(256)}, u32[]{:S(2)}) copy-start(s32[256]{0:T(256)} %param.29) | copy-start | bytes 3076
  233.4 0.7 copy-start.3
  234.0 40.5 %all-to-all-start = ((bf16[8,64,1536]{2,1,0:T(8,128)(2,1)}), bf16[8,64,1536]{2,1,0:T(8,128)(2,1)S(1)}, u32[]{:S(2)}, u32[]{:S(2)}) async-start(bf16[8,64,1536]{2,1,0:T(8,128)(2,1)} %bitcast.124), calls=%async_computation | async-start | bytes 3145728 | tf_op jit(solution)/shard_map/all_to_all | solution.py:228
Sparse Core Ops, SparseCore 0:
  26.8 48.4 all-gather.2
  133.6 21.0 reduce-scatter.3
  157.9 45.0 all-gather.4

commit v4 on v3

--- a/solution.py
+++ b/solution.py
@@ -1,8 +1,11 @@
+import functools
 import math
 
 import jax
 import jax.numpy as jnp
 from jax import lax
+from jax.experimental import pallas as pl
+from jax.experimental.pallas import tpu as pltpu
 from jax.sharding import Mesh, PartitionSpec as P
 
 HEADS = 24
@@ -25,24 +28,91 @@
     return (widened * spread * gain_row).astype(jnp.bfloat16)
 
 
-def attend_block(carried, query_heads, visible, key_rows, value_rows):
-    best_old, total_old, summed_old = carried
-    scores = (
-        jnp.einsum("tkgd,knd->kgtn", query_heads, key_rows, preferred_element_type=jnp.float32)
-        * attention_scale
-    )
-    scores = jnp.where(visible, scores, masked_score)
-    best_new = jnp.maximum(best_old, jnp.max(scores, axis=-1))
-    weights = jnp.where(visible, jnp.exp(scores - best_new[..., None]), 0.0)
-    factor = jnp.exp(best_old - best_new)
-    total_new = total_old * factor + jnp.sum(weights, axis=-1)
-    summed_new = summed_old * factor[..., None] + jnp.einsum(
-        "kgtn,knd->kgtd",
-        weights.astype(jnp.bfloat16),
-        value_rows,
-        preferred_element_type=jnp.float32,
-    )
-    return (best_new, total_new, summed_new)
+KEY_BLOCK = 512
+
+
+def flash_kernel(flags_ref, q_ref, ck_ref, cv_ref, nk_ref, nv_ref, o_ref, m_sc, l_sc, acc_sc, *, cache_blocks, group_rows):
+    step = pl.program_id(1)
+    last = pl.num_programs(1) - 1
+    query_first = flags_ref[0]
+    use_cache = flags_ref[1]
+
+    @pl.when(step == 0)
+    def _():
+        m_sc[...] = jnp.full(m_sc.shape, masked_score, jnp.float32)
+        l_sc[...] = jnp.zeros(l_sc.shape, jnp.float32)
+        acc_sc[...] = jnp.zeros(acc_sc.shape, jnp.float32)
+
+    def update(k_ref, v_ref, visible):
+        q = q_ref[0]
+        k = k_ref[0, 0]
+        v = v_ref[0, 0]
+        scores = lax.dot_general(q, k, (((1,), (1,)), ((), ())), preferred_element_type=jnp.float32) * attention_scale
+        if visible is not None:
+            scores = jnp.where(visible, scores, masked_score)
+        m_prev = m_sc[...]
+        m_new = jnp.maximum(m_prev, jnp.max(scores, axis=1, keepdims=True))
+        weights = jnp.exp(scores - m_new)
+        if visible is not None:
+            weights = jnp.where(visible, weights, 0.0)
+        factor = jnp.exp(m_prev - m_new)
+        l_sc[...] = l_sc[...] * factor + jnp.sum(weights, axis=1, keepdims=True)
+        acc_sc[...] = acc_sc[...] * factor + jnp.dot(weights.astype(jnp.bfloat16), v, preferred_element_type=jnp.float32)
+        m_sc[...] = m_new
+
+    @pl.when((step < cache_blocks) & (use_cache > 0))
+    def _():
+        update(ck_ref, cv_ref, None)
+
+    new_first = (step - cache_blocks) * KEY_BLOCK
+
+    @pl.when((step >= cache_blocks) & (new_first <= query_first + group_rows - 1))
+    def _():
+        rows = q_ref.shape[1]
+        query_pos = query_first + lax.broadcasted_iota(jnp.int32, (rows, KEY_BLOCK), 0) % group_rows
+        key_pos = new_first + lax.broadcasted_iota(jnp.int32, (rows, KEY_BLOCK), 1)
+        update(nk_ref, nv_ref, key_pos <= query_pos)
+
+    @pl.when(step == last)
+    def _():
+        o_ref[0] = (acc_sc[...] / l_sc[...]).astype(o_ref.dtype)
+
+
+def flash_attend(flags, q, cache_all, kv_half, group_rows):
+    heads, rows, dim = q.shape
+    cache_blocks = cache_all.shape[2] // KEY_BLOCK
+    new_blocks = kv_half.shape[2] // KEY_BLOCK
+    kernel = functools.partial(flash_kernel, cache_blocks=cache_blocks, group_rows=group_rows)
+
+    def cache_map(kind):
+        return lambda h, s, f: (kind, h, jnp.minimum(s, cache_blocks - 1), 0)
+
+    def new_map(kind):
+        return lambda h, s, f: (kind, h, jnp.maximum(s - cache_blocks, 0), 0)
+
+    kv_block = (1, 1, KEY_BLOCK, dim)
+    return pl.pallas_call(
+        kernel,
+        out_shape=jax.ShapeDtypeStruct((heads, rows, dim), jnp.bfloat16),
+        grid_spec=pltpu.PrefetchScalarGridSpec(
+            num_scalar_prefetch=1,
+            grid=(heads, cache_blocks + new_blocks),
+            in_specs=[
+                pl.BlockSpec((1, rows, dim), lambda h, s, f: (h, 0, 0)),
+                pl.BlockSpec(kv_block, cache_map(0)),
+                pl.BlockSpec(kv_block, cache_map(1)),
+                pl.BlockSpec(kv_block, new_map(0)),
+                pl.BlockSpec(kv_block, new_map(1)),
+            ],
+            out_specs=pl.BlockSpec((1, rows, dim), lambda h, s, f: (h, 0, 0)),
+            scratch_shapes=[
+                pltpu.VMEM((rows, 1), jnp.float32),
+                pltpu.VMEM((rows, 1), jnp.float32),
+                pltpu.VMEM((rows, dim), jnp.float32),
+            ],
+        ),
+        compiler_params=pltpu.CompilerParams(dimension_semantics=("arbitrary", "arbitrary")),
+    )(flags, q, cache_all, cache_all, kv_half, kv_half)
 
 
 def pl_cdiv(a, b):
@@ -93,7 +163,6 @@
         axis=2,
     )
     pairs_new = split_new.reshape(tokens_here, pair_width)
-    query_heads = queries.reshape(tokens_here, kv_local, group_size, head_dim)
     blocks_here = tokens_here // PAGE
     rounds = blocks_here // seq_count
     outgoing = pairs_new.reshape(rounds, seq_count, PAGE * pair_width)
@@ -116,11 +185,6 @@
         0, 2, 3, 1, 4
     )
     page_rows = page_rows.reshape(blocks_here, kv_local, 2, PAGE * head_dim)
-    start_state = (
-        jnp.full((kv_local, group_size, tokens_here), masked_score, jnp.float32),
-        jnp.zeros((kv_local, group_size, tokens_here), jnp.float32),
-        jnp.zeros((kv_local, group_size, tokens_here, head_dim), jnp.float32),
-    )
     kv_own = split_new.transpose(2, 1, 0, 3)
     kv_half = lax.all_gather(kv_own, "hseq", axis=2, tiled=True)
     cache_rows = cache_kv.shape[0]
@@ -128,34 +192,12 @@
     cache_far = lax.ppermute(cache_own, "half", perm=[(1, 0)])
     cache_piece = jnp.concatenate([cache_own, cache_far], axis=2)
     cache_all = lax.all_gather(cache_piece, "hseq", axis=2, tiled=True)
-    query_pos = half_pos * tokens_here + jnp.arange(tokens_here, dtype=jnp.int32)
-    key_pos = jnp.arange(kv_half.shape[2], dtype=jnp.int32)
-    visible_new = key_pos[None, :] <= query_pos[:, None]
-    carried = attend_block(start_state, query_heads, visible_new, kv_half[0], kv_half[1])
-    stride = block_size(cache_all.shape[2])
-    cache_blocks = cache_all.reshape(2, kv_local, cache_all.shape[2] // stride, stride, head_dim)
-    cache_blocks = cache_blocks.transpose(2, 0, 1, 3, 4)
-    everything = jnp.ones((tokens_here, stride), bool)
-
-    def visit(carried_in, cache_block):
-        carried_in = lax.cond(
-            holds_first,
-            lambda inner: attend_block(
-                inner, query_heads, everything, cache_block[0], cache_block[1]
-            ),
-            lambda inner: inner,
-            carried_in,
-        )
-        return (carried_in, None)
-
-    carried, _ = lax.scan(visit, carried, cache_blocks)
-    best_final, total_final, summed_final = carried
-    attended = (
-        (summed_final / total_final[..., None])
-        .transpose(2, 0, 1, 3)
-        .reshape(tokens_here, -1)
-        .astype(jnp.bfloat16)
-    )
+    query_rows = queries.reshape(tokens_here, kv_local, group_size, head_dim)
+    query_rows = query_rows.transpose(1, 2, 0, 3).reshape(kv_local, group_size * tokens_here, head_dim)
+    flags = jnp.stack([half_pos * tokens_here, holds_first.astype(jnp.int32)]).astype(jnp.int32)
+    attended = flash_attend(flags, query_rows, cache_all, kv_half, tokens_here)
+    attended = attended.reshape(kv_local, group_size, tokens_here, head_dim).transpose(2, 0, 1, 3)
+    attended = attended.reshape(tokens_here, -1)
     mixed_rows = lax.psum_scatter(
         jnp.dot(attended, o_weight, preferred_element_type=jnp.float32).astype(jnp.bfloat16),
         "exp",

time: 284 us -> 330 us (1.16)
  waiting for transfers between devices: 119 us -> 161 us
  Pallas kernels: 0 us -> 40.2 us
  matrix products: 63.4 us -> 26.2 us
  blocking collectives: 24.7 us -> 47.9 us
  local copies, waits for them, and re-layouts: 31.4 us -> 17.1 us
  other arithmetic: 19.2 us -> 12 us
    pallas_call x0 -> x1, Pallas kernels: none -> 40.2 us  [flash_attend(): pl.pallas_call(kernel, out_shape=jax.ShapeDtypeStruct((heads, rows, dim),...]
    dot_general x18 -> x0, matrix products: 36.7 us -> none  [the longest x9 23.2 us: attend_block(): jnp.einsum('kgtn,knd->kgtd', weights.astype(jnp.bfloat16), value_rows, pr...]
    all_gather x1, waiting for transfers between devices: 18.1 us -> 42.4 us  [body(): cache_all = lax.all_gather(cache_piece, 'hseq', axis=2, tiled=True)]
    all_gather x1, blocking collectives: 24.7 us -> 47.9 us  [body(): kv_half = lax.all_gather(kv_own, 'hseq', axis=2, tiled=True)]
    ppermute x1, waiting for transfers between devices: 12.3 us -> 27.2 us  [body(): cache_far = lax.ppermute(cache_own, 'half', perm=[(1, 0)])]
    cond x24 -> x0, local copies, waits for them, and re-layouts: 13.2 us -> none
    reduce_sum x9 -> x0, other arithmetic: 5.79 us -> none  [attend_block(): total_new = total_old * factor + jnp.sum(weights, axis=-1)]
    unnamed x27 -> x28, local copies, waits for them, and re-layouts: 8.26 us -> 6.43 us
  transfers between devices with their start and end apart: 6 -> 6, of which waited for: 5 -> 5; matrix products, arithmetic and copies ran while one was open for 17% -> 14% of each run, Pallas kernels for 0% -> 0%
where the time goes in v4:
time: 330 us; the launch traced here: 329 us
  waiting for transfers between devices  161 us (49%)
  blocking collectives  47.9 us (15%)
  Pallas kernels  40.2 us (12%)
  matrix products  26.2 us (8%)
  local copies, waits for them, and re-layouts  17.1 us (5%)
  between operations  14.1 us (4%)
  other arithmetic  12 us (4%)
  starting transfers between devices  10.6 us (3%)
    all_gather x1, blocking collectives, body(): kv_half = lax.all_gather(kv_own, 'hseq', axis=2, tiled=True)  47.9 us
    all_gather x1, waiting for transfers between devices, body(): cache_all = lax.all_gather(cache_piece, 'hseq', axis=2, tiled=True)  42.4 us
    pallas_call x1, Pallas kernels, flash_attend(): pl.pallas_call(kernel, out_shape=jax.ShapeDtypeStruct((heads, rows, dim),...  40.2 us
    all_gather x1, waiting for transfers between devices, body(): lax.all_gather(jnp.concatenate([moe_in, side], axis=1), SEQ_AXES, axis=0,...  38.5 us
    all_to_all x1, waiting for transfers between devices, body(): lax.all_to_all(partial.astype(jnp.bfloat16).reshape(seq_count, moe_rows,...  29.4 us
    ppermute x1, waiting for transfers between devices, body(): cache_far = lax.ppermute(cache_own, 'half', perm=[(1, 0)])  27.2 us
    reduce_scatter x1, waiting for transfers between devices, body(): lax.psum_scatter(jnp.dot(attended, o_weight, preferred_element_type=jnp.f...  23 us
    dot_general x1, matrix products, body(): jnp.einsum('ecd,edf->ecf', rows_in, expert_in, preferred_element_type=jnp...  10.2 us
  transfers between devices with their start and end apart: 6, of which 5 were waited for; matrix products, arithmetic and copies ran while one was open for 14% of the time, Pallas kernels for 0%

profile of v4, /device:TPU:0, one launch (start us, length us, event | category | flops | bytes accessed | tf_op | source)
XLA Modules:
  0.0 328.8 jit_solution(3838903708168504028)
XLA Ops:
  7.2 1.2 copy.143
  8.4 0.3 copy.144
  8.7 1.4 collective-permute-start
  10.2 27.2 %collective-permute-done = bf16[2,2,512,64]{3,2,1,0:T(8,128)(2,1)S(1)} collective-permute-done((bf16[2,2,512,64]{3,2,1,0:T(8,128)(2,1)S(1)}, bf16[2,2,512,64]{3,2,1,0:T(8,128)(2,1)S(1)}, u32[]{:S(2)}, u32[]{:S(2)}) %collective-permute-start) | collective-permute-done | bytes 262176 | tf_op jit(solution)/shard_map/ppermute | solution.py:192
  37.3 1.2 pad_maximum_fusion
  38.6 0.2 fusion.7
  38.9 0.5 convolution_convert_fusion.5
  39.4 0.1 copy.145
  39.5 0.5 convolution_convert_fusion.4
  40.0 0.1 copy.146
  40.1 1.9 convolution_convert_fusion.3
  42.0 0.1 copy.141
  42.2 0.9 copy.142
  43.1 0.6 pad_add_fusion.flags_ref
  43.8 47.9 %all_gather.10.nk_ref.nv_ref = bf16[2,2,1024,64]{3,2,1,0:T(8,128)(2,1)} all-gather(bf16[2,2,256,64]{3,2,1,0:T(8,128)(2,1)S(1)} %get-tuple-element.19), channel_id=1, replica_groups=mesh['half'=2,'hseq'=4,'exp'=4] {'hseq'}, dimensions={2}, use_global_device_ids=true | all-gather | bytes 655360 | tf_op jit(solution)/shard_map/all_gather | solution.py:189
  91.7 42.4 %all-gather.3.cloned.1.call-done.ck_ref.cv_ref = bf16[2,2,4096,64]{3,2,1,0:T(8,128)(2,1)} async-done(((bf16[2,2,1024,64]{3,2,1,0:T(8,128)(2,1)}), bf16[2,2,4096,64]{3,2,1,0:T(8,128)(2,1)}) %all-gather.3.cloned.1.call-update) | async-done | bytes 2097168 | tf_op jit(solution)/shard_map/all_gather | solution.py:194
  134.2 40.2 %shard_map.140 = bf16[2,768,64]{2,1,0:T(8,128)(2,1)} custom-call(s32[2]{0:T(128)} %pad_add_fusion.flags_ref, bf16[2,768,64]{2,1,0:T(8,128)(2,1)} %bitcast.61, bf16[2,2,4096,64]{3,2,1,0:T(8,128)(2,1)} %all-gather.3.cloned.1.call-done.ck_ref.cv_ref, bf16[2,2,4096,64]{3,2,1,0:T(8,128)(2,1)} %all-gather.3.cloned.1.call-done.ck_ref.cv_ref, ...), custom_call_target="tpu_custom_call" | custom-call | tf_op jit(solution)/shard_map/pallas_call | solution.py:94
  174.4 1.2 copy.147
  175.6 1.5 convolution_convert_fusion.2
  177.6 23.0 %reduce-scatter.4.cloned.1.call-done = bf16[64,1536]{1,0:T(8,128)(2,1)} async-done(((bf16[256,1536]{1,0:T(8,128)(2,1)}), bf16[64,1536]{1,0:T(8,128)(2,1)}) %reduce-scatter.4.cloned.1.call-update) | async-done | bytes 196624 | tf_op jit(solution)/shard_map/reduce_scatter | solution.py:201
  200.6 1.1 multiply_reduce_fusion
  201.8 1.0 multiply_convert_fusion
  202.8 0.8 concatenate.7
  203.6 0.3 copy.157
  203.9 0.3 reshape_reshape.3
  204.2 0.8 copy.158
  204.9 5.5 %all-to-all-start.1 = ((bf16[4,8,2048]{2,0,1:T(4,128)(2,1)}), bf16[4,8,2048]{2,0,1:T(4,128)(2,1)S(1)}, u32[]{:S(2)}, u32[]{:S(2)}) async-start(bf16[4,8,2048]{2,0,1:T(4,128)(2,1)} %copy.158), calls=%async_computation.1 | async-start | bytes 262144 | tf_op jit(solution)/shard_map/all_to_all | solution.py:169
  210.6 38.5 %all-gather.5.cloned.1.call-done = bf16[512,1664]{1,0:T(8,128)(2,1)} async-done(((bf16[64,1664]{1,0:T(8,128)(2,1)}), bf16[512,1664]{1,0:T(8,128)(2,1)}) %all-gather.5.cloned.1.call-update) | async-done | bytes 1703952 | tf_op jit(solution)/shard_map/all_gather | solution.py:234
  249.1 0.9 slice.16
  250.0 0.2 constant_dynamic-slice_fusion.1
  250.6 0.2 copy.154
  250.8 6.3 %fusion.38 = s32[8,64,4]{2,0,1:T(8,128)S(1)} fusion(s32[8,64,4]{2,0,1:T(8,128)S(1)} %copy.154), kind=kOutput, calls=%fused_computation.70 | output fusion | flops 129024 | bytes 16384 | tf_op jit(solution)/shard_map/jit(cumsum)/reduce_window_sum | solution.py:247
  257.2 0.1 copy.155
  257.4 10.2 %fusion.39 = f32[4,256,1024]{2,1,0:T(8,128)} fusion(bf16[4,1536,1024]{2,1,0:T(8,128)(2,1)} %param.21, bf16[512,1664]{1,0:T(8,128)(2,1)} %all-gather.5.cloned.1.call-done, s32[512,4]{0,1:T(4,128)S(1)} %subtract_add_fusion, pred[512,4]{0,1:T(4,128)(4,1)S(1)} %get-tuple-element.15), kind=kOutput, calls=%fused_computation.71 | convolution fusion | flops 4834459648 | bytes 18360320 | tf_op jit(solution)/shard_map/ecd,edf->ecf/dot_general | solution.py:259
  267.6 5.9 %convolution_convert_fusion.1 = bf16[4,256,1536]{2,1,0:T(8,128)(2,1)S(1)} fusion(bf16[4,512,1536]{2,1,0:T(8,128)(2,1)} %param.22, f32[4,256,1024]{2,1,0:T(8,128)} %fusion.39), kind=kOutput, calls=%fused_computation.2 | convolution fusion | flops 1615331328 | bytes 13631488 | tf_op jit(solution)/shard_map/ecf,efd->ecd/dot_general | solution.py:262
  273.5 2.1 convolution_bitcast_fusion
  275.6 3.7 %fusion.1 = bf16[512,1536]{1,0:T(8,128)(2,1)} fusion(f32[512,1536]{1,0:T(8,128)S(1)} %convolution_bitcast_fusion, bf16[4,256,1536]{2,1,0:T(8,128)(2,1)S(1)} %convolution_convert_fusion.1, s32[512,4]{0,1:T(4,128)S(1)} %subtract_add_fusion, pred[512,4]{0,1:T(4,128)(4,1)S(1)} %get-tuple-element.15, bf16[512,4]{0,1:T(4,128)(2,1)S(1)} %copy.169), kind=kOutput, calls=%fused_computation.7 | convolution fusion | flops 1613758464 | bytes 7878656 | tf_op jit(solution)/shard_map/nec,ecd->nd/dot_general | solution.py:267
  279.3 0.7 copy-done.3
  280.0 3.6 %all-to-all-start = ((bf16[8,64,1536]{2,1,0:T(8,128)(2,1)}), bf16[8,64,1536]{2,1,0:T(8,128)(2,1)S(1)}, u32[]{:S(2)}, u32[]{:S(2)}) async-start(bf16[8,64,1536]{2,1,0:T(8,128)(2,1)} %bitcast.63), calls=%async_computation | async-start | bytes 3145728 | tf_op jit(solution)/shard_map/all_to_all | solution.py:270
  283.8 0.2 select_reduce_fusion.1
  283.9 1.8 scatter_custom_fusion
  285.8 1.9 reshape.119
  287.7 1.7 copy.163
  289.4 1.8 reshape.134
  291.2 29.4 %all-to-all-done = bf16[8,64,1536]{2,1,0:T(8,128)(2,1)S(1)} async-done(((bf16[8,64,1536]{2,1,0:T(8,128)(2,1)}), bf16[8,64,1536]{2,1,0:T(8,128)(2,1)S(1)}, u32[]{:S(2)}, u32[]{:S(2)}) %all-to-all-start) | async-done | bytes 1572896 | tf_op jit(solution)/shard_map/all_to_all | solution.py:270
  320.5 0.2 convert_reduce_fusion
  320.8 0.7 copy-done.2
  321.5 0.8 add_convert_fusion
  (54 shorter events, 1.5 us)
Async XLA Ops:
  7.2 168.4 %copy-start = (bf16[384,1536]{1,0:T(8,128)(2,1)S(1)}, bf16[384,1536]{1,0:T(8,128)(2,1)}, u32[]{:S(2)}) copy-start(bf16[384,1536]{1,0:T(8,128)(2,1)} %param.18) | copy-start | bytes 3538948
  7.2 127.0 %all-gather.3.cloned.1.call-start = ((), (), s32[]{:S(2)}) async-start(), calls=%async_computation.3 | async-start | bytes 5242880 | tf_op jit(solution)/shard_map/all_gather | solution.py:194
  8.4 30.2 %copy-start.1 = (bf16[256,1536]{1,0:T(8,128)(2,1)S(1)}, bf16[256,1536]{1,0:T(8,128)(2,1)}, u32[]{:S(2)}) copy-start(bf16[256,1536]{1,0:T(8,128)(2,1)} %param.13) | copy-start | bytes 2359300
  8.7 30.2 %copy-start.8 = (bf16[1536,128]{1,0:T(8,128)(2,1)S(1)}, bf16[1536,128]{1,0:T(8,128)(2,1)}, u32[]{:S(2)}) copy-start(bf16[1536,128]{1,0:T(8,128)(2,1)} %param.16) | copy-start | bytes 1179652
  8.7 30.2 %copy-start.10 = (f32[1536]{0:T(1024)S(1)}, f32[1536]{0:T(1024)}, u32[]{:S(2)}) copy-start(f32[1536]{0:T(1024)} %param.14) | copy-start | bytes 18436
  8.7 28.6 %collective-permute-start = (bf16[2,2,512,64]{3,2,1,0:T(8,128)(2,1)S(1)}, bf16[2,2,512,64]{3,2,1,0:T(8,128)(2,1)S(1)}, u32[]{:S(2)}, u32[]{:S(2)}) collective-permute-start(bf16[2,2,512,64]{3,2,1,0:T(8,128)(2,1)S(1)} %bitcast.59), channel_id=1, source_target_pairs={{16,0},{17,1},{18,2},{19,3},{20,4},{21,5},{22,6},{23,7},{24,8},{25... | collective-permute-start | bytes 786440 | tf_op jit(solution)/shard_map/ppermute | solution.py:192
  38.5 1.0 copy-start.9
  38.6 162.1 %reduce-scatter.4.cloned.1.call-start = ((), (), s32[]{:S(2)}) async-start(), calls=%async_computation.5 | async-start | bytes 983040 | tf_op jit(solution)/shard_map/reduce_scatter | solution.py:201
  174.4 2.8 copy-start.5
  174.4 2.9 copy-start.4
  174.4 27.3 %copy-start.6 = (f32[1536]{0:T(1024)S(1)}, f32[1536]{0:T(1024)}, u32[]{:S(2)}) copy-start(f32[1536]{0:T(1024)} %param.20) | copy-start | bytes 18436
  177.1 72.0 %all-gather.5.cloned.1.call-start = ((), (), s32[]{:S(2)}) async-start(), calls=%async_computation.4 | async-start | bytes 1916928 | tf_op jit(solution)/shard_map/all_gather | solution.py:234
  204.9 74.4 %all-to-all-start.1 = ((bf16[4,8,2048]{2,0,1:T(4,128)(2,1)}), bf16[4,8,2048]{2,0,1:T(4,128)(2,1)S(1)}, u32[]{:S(2)}, u32[]{:S(2)}) async-start(bf16[4,8,2048]{2,0,1:T(4,128)(2,1)} %copy.158), calls=%async_computation.1 | async-start | bytes 262144 | tf_op jit(solution)/shard_map/all_to_all | solution.py:169
  279.3 4.4 %copy-start.7 = (s32[256]{0:T(256)S(1)}, s32[256]{0:T(256)}, u32[]{:S(2)}) copy-start(s32[256]{0:T(256)} %param.25) | copy-start | bytes 3076
  279.3 0.7 copy-start.3
  280.0 40.6 %all-to-all-start = ((bf16[8,64,1536]{2,1,0:T(8,128)(2,1)}), bf16[8,64,1536]{2,1,0:T(8,128)(2,1)S(1)}, u32[]{:S(2)}, u32[]{:S(2)}) async-start(bf16[8,64,1536]{2,1,0:T(8,128)(2,1)} %bitcast.63), calls=%async_computation | async-start | bytes 3145728 | tf_op jit(solution)/shard_map/all_to_all | solution.py:270
  320.5 0.9 copy-start.2
Sparse Core Ops, SparseCore 0:
  38.7 95.4 all-gather.2
  177.2 23.3 reduce-scatter.3
  203.7 45.3 all-gather.4

commit v5 on v4

--- a/solution.py
+++ b/solution.py
@@ -28,14 +28,24 @@
     return (widened * spread * gain_row).astype(jnp.bfloat16)
 
 
-KEY_BLOCK = 512
-
-
-def flash_kernel(flags_ref, q_ref, ck_ref, cv_ref, nk_ref, nv_ref, o_ref, m_sc, l_sc, acc_sc, *, cache_blocks, group_rows):
+def partial_kernel(
+    flags_ref, q_ref, k_ref, v_ref, acc_ref, m_ref, l_ref, m_sc, l_sc, acc_sc, *, mode, cache_per,
+    new_per, key_block, group_rows
+):
     step = pl.program_id(1)
     last = pl.num_programs(1) - 1
     query_first = flags_ref[0]
-    use_cache = flags_ref[1]
+    stride = cache_per + new_per
+    if mode == "all":
+        within = step % stride
+        new_index = (step // stride) * new_per + within - cache_per
+    elif mode == "new":
+        within = cache_per
+        new_index = step
+    else:
+        within = 0
+        new_index = 0
+    new_first = new_index * key_block
 
     @pl.when(step == 0)
     def _():
@@ -43,11 +53,13 @@
         l_sc[...] = jnp.zeros(l_sc.shape, jnp.float32)
         acc_sc[...] = jnp.zeros(acc_sc.shape, jnp.float32)
 
-    def update(k_ref, v_ref, visible):
+    def update(visible):
         q = q_ref[0]
         k = k_ref[0, 0]
         v = v_ref[0, 0]
-        scores = lax.dot_general(q, k, (((1,), (1,)), ((), ())), preferred_element_type=jnp.float32) * attention_scale
+        scores = lax.dot_general(
+            q, k, (((1,), (1,)), ((), ())), preferred_element_type=jnp.float32
+        ) * attention_scale
         if visible is not None:
             scores = jnp.where(visible, scores, masked_score)
         m_prev = m_sc[...]
@@ -57,54 +69,74 @@
             weights = jnp.where(visible, weights, 0.0)
         factor = jnp.exp(m_prev - m_new)
         l_sc[...] = l_sc[...] * factor + jnp.sum(weights, axis=1, keepdims=True)
-        acc_sc[...] = acc_sc[...] * factor + jnp.dot(weights.astype(jnp.bfloat16), v, preferred_element_type=jnp.float32)
+        acc_sc[...] = acc_sc[...] * factor + jnp.dot(
+            weights.astype(jnp.bfloat16), v, preferred_element_type=jnp.float32
+        )
         m_sc[...] = m_new
 
-    @pl.when((step < cache_blocks) & (use_cache > 0))
-    def _():
-        update(ck_ref, cv_ref, None)
-
-    new_first = (step - cache_blocks) * KEY_BLOCK
-
-    @pl.when((step >= cache_blocks) & (new_first <= query_first + group_rows - 1))
-    def _():
-        rows = q_ref.shape[1]
-        query_pos = query_first + lax.broadcasted_iota(jnp.int32, (rows, KEY_BLOCK), 0) % group_rows
-        key_pos = new_first + lax.broadcasted_iota(jnp.int32, (rows, KEY_BLOCK), 1)
-        update(nk_ref, nv_ref, key_pos <= query_pos)
+    if mode != "new":
+
+        @pl.when(within < cache_per)
+        def _():
+            update(None)
+
+    if mode != "cache":
+
+        @pl.when((within >= cache_per) & (new_first <= query_first + group_rows - 1))
+        def _():
+            rows = q_ref.shape[1]
+            query_pos = (
+                query_first + lax.broadcasted_iota(jnp.int32, (rows, key_block), 0) % group_rows
+            )
+            key_pos = new_first + lax.broadcasted_iota(jnp.int32, (rows, key_block), 1)
+            update(key_pos <= query_pos)
 
     @pl.when(step == last)
     def _():
-        o_ref[0] = (acc_sc[...] / l_sc[...]).astype(o_ref.dtype)
-
-
-def flash_attend(flags, q, cache_all, kv_half, group_rows):
+        acc_ref[0] = acc_sc[...]
+        m_ref[0] = m_sc[...]
+        l_ref[0] = l_sc[...]
+
+
+def attend_partial(flags, q, kv_all, mode, cache_per, new_per, key_block, group_rows):
     heads, rows, dim = q.shape
-    cache_blocks = cache_all.shape[2] // KEY_BLOCK
-    new_blocks = kv_half.shape[2] // KEY_BLOCK
-    kernel = functools.partial(flash_kernel, cache_blocks=cache_blocks, group_rows=group_rows)
-
-    def cache_map(kind):
-        return lambda h, s, f: (kind, h, jnp.minimum(s, cache_blocks - 1), 0)
-
-    def new_map(kind):
-        return lambda h, s, f: (kind, h, jnp.maximum(s - cache_blocks, 0), 0)
-
-    kv_block = (1, 1, KEY_BLOCK, dim)
+    stride = cache_per + new_per
+    devices = kv_all.shape[2] // (key_block * stride)
+    if mode == "all":
+        steps = devices * stride
+        block_of = lambda s: s
+    elif mode == "new":
+        steps = devices * new_per
+        block_of = lambda s: (s // new_per) * stride + cache_per + s % new_per
+    else:
+        steps = devices * cache_per
+        block_of = lambda s: (s // cache_per) * stride + s % cache_per
+    kernel = functools.partial(
+        partial_kernel,
+        mode=mode,
+        cache_per=cache_per,
+        new_per=new_per,
+        key_block=key_block,
+        group_rows=group_rows,
+    )
+    kv_block = (1, 1, key_block, dim)
+    row_block = pl.BlockSpec((1, rows, 1), lambda h, s, f: (h, 0, 0))
     return pl.pallas_call(
         kernel,
-        out_shape=jax.ShapeDtypeStruct((heads, rows, dim), jnp.bfloat16),
+        out_shape=(
+            jax.ShapeDtypeStruct((heads, rows, dim), jnp.float32),
+            jax.ShapeDtypeStruct((heads, rows, 1), jnp.float32),
+            jax.ShapeDtypeStruct((heads, rows, 1), jnp.float32),
+        ),
         grid_spec=pltpu.PrefetchScalarGridSpec(
             num_scalar_prefetch=1,
-            grid=(heads, cache_blocks + new_blocks),
+            grid=(heads, steps),
             in_specs=[
                 pl.BlockSpec((1, rows, dim), lambda h, s, f: (h, 0, 0)),
-                pl.BlockSpec(kv_block, cache_map(0)),
-                pl.BlockSpec(kv_block, cache_map(1)),
-                pl.BlockSpec(kv_block, new_map(0)),
-                pl.BlockSpec(kv_block, new_map(1)),
+                pl.BlockSpec(kv_block, lambda h, s, f: (0, h, block_of(s), 0)),
+                pl.BlockSpec(kv_block, lambda h, s, f: (1, h, block_of(s), 0)),
             ],
-            out_specs=pl.BlockSpec((1, rows, dim), lambda h, s, f: (h, 0, 0)),
+            out_specs=[pl.BlockSpec((1, rows, dim), lambda h, s, f: (h, 0, 0)), row_block, row_block],
             scratch_shapes=[
                 pltpu.VMEM((rows, 1), jnp.float32),
                 pltpu.VMEM((rows, 1), jnp.float32),
@@ -112,7 +144,7 @@
             ],
         ),
         compiler_params=pltpu.CompilerParams(dimension_semantics=("arbitrary", "arbitrary")),
-    )(flags, q, cache_all, cache_all, kv_half, kv_half)
+    )(flags, q, kv_all, kv_all)
 
 
 def pl_cdiv(a, b):
@@ -186,18 +218,53 @@
     )
     page_rows = page_rows.reshape(blocks_here, kv_local, 2, PAGE * head_dim)
     kv_own = split_new.transpose(2, 1, 0, 3)
-    kv_half = lax.all_gather(kv_own, "hseq", axis=2, tiled=True)
     cache_rows = cache_kv.shape[0]
     cache_own = cache_kv.reshape(cache_rows, kv_local, 2, head_dim).transpose(2, 1, 0, 3)
-    cache_far = lax.ppermute(cache_own, "half", perm=[(1, 0)])
-    cache_piece = jnp.concatenate([cache_own, cache_far], axis=2)
-    cache_all = lax.all_gather(cache_piece, "hseq", axis=2, tiled=True)
+    kv_all = lax.all_gather(
+        jnp.concatenate([cache_own, kv_own], axis=2), "hseq", axis=2, tiled=True
+    )
+    key_block = math.gcd(math.gcd(cache_rows, tokens_here), 256)
+    cache_per = cache_rows // key_block
+    new_per = tokens_here // key_block
     query_rows = queries.reshape(tokens_here, kv_local, group_size, head_dim)
     query_rows = query_rows.transpose(1, 2, 0, 3).reshape(kv_local, group_size * tokens_here, head_dim)
-    flags = jnp.stack([half_pos * tokens_here, holds_first.astype(jnp.int32)]).astype(jnp.int32)
-    attended = flash_attend(flags, query_rows, cache_all, kv_half, tokens_here)
-    attended = attended.reshape(kv_local, group_size, tokens_here, head_dim).transpose(2, 0, 1, 3)
-    attended = attended.reshape(tokens_here, -1)
+    partner_rows = lax.ppermute(query_rows, "half", perm=[(0, 1)])
+    flags = jnp.reshape(half_pos * tokens_here, (1,)).astype(jnp.int32)
+    shapes = dict(cache_per=cache_per, new_per=new_per, key_block=key_block, group_rows=tokens_here)
+
+    def empty_partial(rows_in):
+        heads, rows, _ = rows_in.shape
+        return (
+            jnp.zeros((heads, rows, head_dim), jnp.float32),
+            jnp.full((heads, rows, 1), masked_score, jnp.float32),
+            jnp.zeros((heads, rows, 1), jnp.float32),
+        )
+
+    far_part = lax.cond(
+        holds_first,
+        empty_partial,
+        lambda rows_in: attend_partial(flags, rows_in, kv_all, "cache", **shapes),
+        partner_rows,
+    )
+    own_part = lax.cond(
+        holds_first,
+        lambda rows_in: attend_partial(flags, rows_in, kv_all, "all", **shapes),
+        lambda rows_in: attend_partial(flags, rows_in, kv_all, "new", **shapes),
+        query_rows,
+    )
+    back_acc, back_best, back_total = lax.ppermute(far_part, "half", perm=[(1, 0)])
+    back_best = jnp.where(holds_first, back_best, masked_score)
+    back_total = jnp.where(holds_first, back_total, 0.0)
+    back_acc = jnp.where(holds_first, back_acc, 0.0)
+    own_acc, own_best, own_total = own_part
+    best = jnp.maximum(own_best, back_best)
+    own_scale = jnp.exp(own_best - best)
+    back_scale = jnp.exp(back_best - best)
+    attended = (own_acc * own_scale + back_acc * back_scale) / (
+        own_total * own_scale + back_total * back_scale
+    )
+    attended = attended.astype(jnp.bfloat16).reshape(kv_local, group_size, tokens_here, head_dim)
+    attended = attended.transpose(2, 0, 1, 3).reshape(tokens_here, -1)
     mixed_rows = lax.psum_scatter(
         jnp.dot(attended, o_weight, preferred_element_type=jnp.float32).astype(jnp.bfloat16),
         "exp",

time: 330 us -> 281 us (0.85)
  blocking collectives: 47.9 us -> 0 us
  waiting for transfers between devices: 161 us -> 133 us
  local copies, waits for them, and re-layouts: 17.1 us -> 30.3 us
  starting transfers between devices: 10.6 us -> 19.2 us
    all_gather x1 -> x0, blocking collectives: 47.9 us -> none  [body(): kv_half = lax.all_gather(kv_own, 'hseq', axis=2, tiled=True)]
    ppermute x1 -> x4, waiting for transfers between devices: 27.2 us -> 7.19 us  [the longest x1 6.82 us: body(): partner_rows = lax.ppermute(query_rows, 'half', perm=[(0, 1)])]
    all_gather x1, waiting for transfers between devices: 42.4 us -> 23.5 us  [body(): lax.all_gather(jnp.concatenate([cache_own, kv_own], axis=2), 'hseq', axis...]
    reduce_scatter x1, waiting for transfers between devices: 23 us -> 34.1 us  [body(): lax.psum_scatter(jnp.dot(attended, o_weight, preferred_element_type=jnp.f...]
    cond x0 -> x8, local copies, waits for them, and re-layouts: none -> 9.33 us  [the longest x3 6.22 us: body(): lax.cond(holds_first, empty_partial, lambda rows_in: attend_partial(flags...]
    ppermute x1 -> x4, starting transfers between devices: 1.42 us -> 9.8 us  [the longest x1 5.95 us: body(): partner_rows = lax.ppermute(query_rows, 'half', perm=[(0, 1)])]
    another operation x0 -> x5, local copies, waits for them, and re-layouts: none -> 7.48 us
  transfers between devices with their start and end apart: 6 -> 9, of which waited for: 5 -> 7; matrix products, arithmetic and copies ran while one was open for 14% -> 19% of each run, Pallas kernels for 0% -> 15%
where the time goes in v5:
time: 281 us; the launch traced here: 279 us
  waiting for transfers between devices  133 us (47%)
  Pallas kernels  40.8 us (15%)
  local copies, waits for them, and re-layouts  30.3 us (11%)
  matrix products  27.5 us (10%)
  starting transfers between devices  19.2 us (7%)
  other arithmetic  14.6 us (5%)
  between operations  14.2 us (5%)
    pallas_call x1, Pallas kernels, attend_partial(): pl.pallas_call(kernel, out_shape=(jax.ShapeDtypeStruct((heads, rows, dim)...  40.8 us
    all_gather x1, waiting for transfers between devices, body(): lax.all_gather(jnp.concatenate([moe_in, side], axis=1), SEQ_AXES, axis=0,...  38.4 us
    reduce_scatter x1, waiting for transfers between devices, body(): lax.psum_scatter(jnp.dot(attended, o_weight, preferred_element_type=jnp.f...  34.1 us
    all_to_all x1, waiting for transfers between devices, body(): lax.all_to_all(partial.astype(jnp.bfloat16).reshape(seq_count, moe_rows,...  29.5 us
    all_gather x1, waiting for transfers between devices, body(): lax.all_gather(jnp.concatenate([cache_own, kv_own], axis=2), 'hseq', axis...  23.5 us
    dot_general x1, matrix products, body(): jnp.einsum('ecd,edf->ecf', rows_in, expert_in, preferred_element_type=jnp...  10.2 us
    another operation x5, local copies, waits for them, and re-layouts  7.48 us
    ppermute x1, waiting for transfers between devices, body(): partner_rows = lax.ppermute(query_rows, 'half', perm=[(0, 1)])  6.82 us
  transfers between devices with their start and end apart: 9, of which 7 were waited for; matrix products, arithmetic and copies ran while one was open for 19% of the time, Pallas kernels for 15%

profile of v5, /device:TPU:0, one launch (start us, length us, event | category | flops | bytes accessed | tf_op | source)
XLA Modules:
  0.0 279.4 jit_solution(11917235767297903246)
XLA Ops:
  7.3 1.5 fusion.7
  8.8 1.7 convolution_convert_fusion.5
  11.2 0.7 pad_maximum_fusion.1
  11.9 0.8 pad_maximum_fusion
  12.8 1.9 convolution_convert_fusion.3
  14.8 5.9 %collective-permute-start = (bf16[2,768,64]{1,2,0:T(8,128)(2,1)S(1)}, bf16[2,768,64]{1,2,0:T(8,128)(2,1)S(1)}, u32[]{:S(2)}, u32[]{:S(2)}) collective-permute-start(bf16[2,768,64]{1,2,0:T(8,128)(2,1)S(1)} %bitcast.70), channel_id=1, source_target_pairs={{0,16},{1,17},{2,18},{3,19},{4,20},{5,21},{6,22},{7,23},{8,24},{9,... | collective-permute-start | bytes 589832 | tf_op jit(solution)/shard_map/ppermute | solution.py:231
  20.8 6.8 %collective-permute-done = bf16[2,768,64]{1,2,0:T(8,128)(2,1)S(1)} collective-permute-done((bf16[2,768,64]{1,2,0:T(8,128)(2,1)S(1)}, bf16[2,768,64]{1,2,0:T(8,128)(2,1)S(1)}, u32[]{:S(2)}, u32[]{:S(2)}) %collective-permute-start) | collective-permute-done | bytes 196640 | tf_op jit(solution)/shard_map/ppermute | solution.py:231
  27.6 23.5 %all-gather.3.cloned.1.call-done = bf16[2,2,3072,64]{2,3,0,1:T(8,128)(2,1)} async-done(((bf16[2,2,768,64]{2,3,0,1:T(8,128)(2,1)}), bf16[2,2,3072,64]{2,3,0,1:T(8,128)(2,1)}) %all-gather.3.cloned.1.call-update) | async-done | bytes 1572880 | tf_op jit(solution)/shard_map/all_gather | solution.py:223
  51.1 2.9 %conditional.3 = ((f32[2,768,64]{2,1,0:T(8,128)}, f32[2,768,1]{2,1,0:T(8,128)}, f32[2,768,1]{2,1,0:T(8,128)})) conditional(s32[]{:T(128)} %convert_element_type.76, (s32[1]{0:T(128)}, bf16[2,768,64]{1,2,0:T(8,128)(2,1)S(1)}, bf16[2,2,3072,64]{2,3,0,1:T(8,128)(2,1)}) %tuple.22, () %tuple.23), branch_computations={%region_3.4_spmd, %region_4.5_spmd} | conditional | bytes 3538952 | solution.py:243
  51.1 1.0 broadcast.93
  52.1 1.0 broadcast.91
  53.0 0.9 broadcast.92
  54.0 2.2 copy.212
  56.2 1.3 collective-permute-start.2
  57.5 2.0 copy.208
  59.5 2.0 copy.214
  61.5 1.3 collective-permute-start.3
  62.8 1.3 collective-permute-start.1
  64.1 48.6 %conditional.2 = (f32[2,768,64]{1,2,0:T(8,128)S(1)}, f32[2,768,1]{1,0,2:T(2,128)S(1)}, f32[2,768,1]{1,0,2:T(2,128)S(1)}) conditional(s32[]{:T(128)} %convert_element_type.76, (s32[1]{0:T(128)}, bf16[2,768,64]{1,2,0:T(8,128)(2,1)}, bf16[2,2,3072,64]{2,3,0,1:T(8,128)(2,1)S(1)}) %tuple.79, (s32[1]{0:T(128)}, bf16[2,768,64]{1,2,0:T(8,128)(2,1)}, ...), branch_computations={%region_1.2_spmd, %region_2.3_spmd} | conditional | bytes 4374580 | solution.py:249
  64.1 1.9 copy.204.q_ref
  66.0 2.8 copy.205.k_ref.v_ref
  68.7 40.8 %branch_1_fun.1 = (f32[2,768,64]{2,1,0:T(8,128)}, f32[2,768,1]{2,1,0:T(8,128)}, f32[2,768,1]{2,1,0:T(8,128)}) custom-call(s32[1]{0:T(128)} %get-tuple-element.21.flags_ref, bf16[2,768,64]{2,1,0:T(8,128)(2,1)} %copy.204.q_ref, bf16[2,2,3072,64]{3,2,1,0:T(8,128)(2,1)} %copy.205.k_ref.v_ref, bf16[2,2,3072,64]{3,2,1,0:T(8,128)(2,1)} %copy.205.k_ref.v_ref), custom_call_target="tpu_custom_call" | custom-call | tf_op jit(solution)/shard_map/cond/branch_1_fun/pallas_call | solution.py:124
  109.5 1.5 copy.235
  111.0 1.4 copy.237
  113.0 0.7 fusion.36
  113.8 1.1 divide_convert_fusion
  115.0 1.5 convolution_convert_fusion.2
  117.2 34.1 %reduce-scatter.4.cloned.1.call-done = bf16[64,1536]{1,0:T(8,128)(2,1)} async-done(((bf16[256,1536]{1,0:T(8,128)(2,1)}), bf16[64,1536]{1,0:T(8,128)(2,1)}) %reduce-scatter.4.cloned.1.call-update) | async-done | bytes 196624 | tf_op jit(solution)/shard_map/reduce_scatter | solution.py:268
  151.3 1.1 multiply_reduce_fusion
  152.4 1.0 multiply_convert_fusion
  153.5 0.8 concatenate.7
  154.8 0.8 copy.226
  155.5 5.5 %all-to-all-start.1 = ((bf16[4,8,2048]{2,0,1:T(4,128)(2,1)}), bf16[4,8,2048]{2,0,1:T(4,128)(2,1)S(1)}, u32[]{:S(2)}, u32[]{:S(2)}) async-start(bf16[4,8,2048]{2,0,1:T(4,128)(2,1)} %copy.226), calls=%async_computation.1 | async-start | bytes 262144 | tf_op jit(solution)/shard_map/all_to_all | solution.py:201
  161.2 38.4 %all-gather.5.cloned.1.call-done = bf16[512,1664]{1,0:T(8,128)(2,1)} async-done(((bf16[64,1664]{1,0:T(8,128)(2,1)}), bf16[512,1664]{1,0:T(8,128)(2,1)}) %all-gather.5.cloned.1.call-update) | async-done | bytes 1703952 | tf_op jit(solution)/shard_map/all_gather | solution.py:301
  199.6 0.9 slice.16
  201.3 6.3 %fusion.42 = s32[8,64,4]{2,0,1:T(8,128)S(1)} fusion(s32[8,64,4]{2,0,1:T(8,128)S(1)} %copy.222), kind=kOutput, calls=%fused_computation.78 | output fusion | flops 129024 | bytes 16384 | tf_op jit(solution)/shard_map/jit(cumsum)/reduce_window_sum | solution.py:314
  207.9 10.2 %fusion.43 = f32[4,256,1024]{2,1,0:T(8,128)} fusion(bf16[4,1536,1024]{2,1,0:T(8,128)(2,1)} %param.25, bf16[512,1664]{1,0:T(8,128)(2,1)} %all-gather.5.cloned.1.call-done, s32[512,4]{0,1:T(4,128)S(1)} %subtract_add_fusion, pred[512,4]{0,1:T(4,128)(4,1)S(1)} %get-tuple-element.126), kind=kOutput, calls=%fused_computation.79 | convolution fusion | flops 4834459648 | bytes 18360320 | tf_op jit(solution)/shard_map/ecd,edf->ecf/dot_general | solution.py:326
  218.1 5.9 %convolution_convert_fusion.1 = bf16[4,256,1536]{2,1,0:T(8,128)(2,1)S(1)} fusion(bf16[4,512,1536]{2,1,0:T(8,128)(2,1)} %param.26, f32[4,256,1024]{2,1,0:T(8,128)} %fusion.43), kind=kOutput, calls=%fused_computation.2 | convolution fusion | flops 1615331328 | bytes 13631488 | tf_op jit(solution)/shard_map/ecf,efd->ecd/dot_general | solution.py:329
  224.0 2.1 convolution_bitcast_fusion
  226.1 3.7 %fusion.1 = bf16[512,1536]{1,0:T(8,128)(2,1)} fusion(f32[512,1536]{1,0:T(8,128)S(1)} %convolution_bitcast_fusion, bf16[4,256,1536]{2,1,0:T(8,128)(2,1)S(1)} %convolution_convert_fusion.1, s32[512,4]{0,1:T(4,128)S(1)} %subtract_add_fusion, pred[512,4]{0,1:T(4,128)(4,1)S(1)} %get-tuple-element.126, bf16[512,4]{0,1:T(4,128)(2,1)S(1)} %copy.243), kind=kOutput, calls=%fused_computation.7 | convolution fusion | flops 1613758464 | bytes 7878656 | tf_op jit(solution)/shard_map/nec,ecd->nd/dot_general | solution.py:334
  230.5 3.6 %all-to-all-start = ((bf16[8,64,1536]{2,1,0:T(8,128)(2,1)}), bf16[8,64,1536]{2,1,0:T(8,128)(2,1)S(1)}, u32[]{:S(2)}, u32[]{:S(2)}) async-start(bf16[8,64,1536]{2,1,0:T(8,128)(2,1)} %bitcast.73), calls=%async_computation | async-start | bytes 3145728 | tf_op jit(solution)/shard_map/all_to_all | solution.py:337
  234.4 1.8 scatter_custom_fusion
  236.3 1.9 reshape.123
  238.1 1.7 copy.231
  239.9 1.8 reshape.137
  241.7 29.5 %all-to-all-done = bf16[8,64,1536]{2,1,0:T(8,128)(2,1)S(1)} async-done(((bf16[8,64,1536]{2,1,0:T(8,128)(2,1)}), bf16[8,64,1536]{2,1,0:T(8,128)(2,1)S(1)}, u32[]{:S(2)}, u32[]{:S(2)}) %all-to-all-start) | async-done | bytes 1572896 | tf_op jit(solution)/shard_map/all_to_all | solution.py:337
  271.4 0.7 copy-done.3
  272.1 0.8 add_convert_fusion
  (79 shorter events, 5.2 us)
Async XLA Ops:
  7.2 107.9 %copy-start = (bf16[384,1536]{1,0:T(8,128)(2,1)S(1)}, bf16[384,1536]{1,0:T(8,128)(2,1)}, u32[]{:S(2)}) copy-start(bf16[384,1536]{1,0:T(8,128)(2,1)} %param.22) | copy-start | bytes 3538948
  7.2 3.4 %copy-start.2 = (bf16[256,1536]{1,0:T(8,128)(2,1)S(1)}, bf16[256,1536]{1,0:T(8,128)(2,1)}, u32[]{:S(2)}) copy-start(bf16[256,1536]{1,0:T(8,128)(2,1)} %param.17) | copy-start | bytes 2359300
  7.2 3.4 %copy-start.15 = (f32[1536]{0:T(1024)S(1)}, f32[1536]{0:T(1024)}, u32[]{:S(2)}) copy-start(f32[1536]{0:T(1024)} %param.18) | copy-start | bytes 18436
  7.2 3.4 %copy-start.14 = (bf16[1536,128]{1,0:T(8,128)(2,1)S(1)}, bf16[1536,128]{1,0:T(8,128)(2,1)}, u32[]{:S(2)}) copy-start(bf16[1536,128]{1,0:T(8,128)(2,1)} %param.21) | copy-start | bytes 1179652
  7.2 3.9 %copy-start.9 = (bf16[512,256]{1,0:T(8,128)(2,1)S(1)}, bf16[512,256]{1,0:T(8,128)(2,1)}, u32[]{:S(2)}) copy-start(bf16[512,256]{1,0:T(8,128)(2,1)} %param.23) | copy-start | bytes 786436
  7.2 43.9 %all-gather.3.cloned.1.call-start = ((), (), s32[]{:S(2)}) async-start(), calls=%async_computation.3 | async-start | bytes 1966080 | tf_op jit(solution)/shard_map/all_gather | solution.py:223
  12.7 138.6 %reduce-scatter.4.cloned.1.call-start = ((), (), s32[]{:S(2)}) async-start(), calls=%async_computation.5 | async-start | bytes 983040 | tf_op jit(solution)/shard_map/reduce_scatter | solution.py:268
  14.8 36.3 %copy-start.4 = (bf16[2,3,8,8,256]{4,3,1,2,0:T(8,128)(2,1)}, bf16[2,3,8,8,256]{4,3,1,2,0:T(8,128)(2,1)S(1)}, u32[]{:S(2)}) copy-start(bf16[2,3,8,8,256]{4,3,1,2,0:T(8,128)(2,1)S(1)} %copy.245) | copy-start | bytes 589828
  14.8 12.8 %collective-permute-start = (bf16[2,768,64]{1,2,0:T(8,128)(2,1)S(1)}, bf16[2,768,64]{1,2,0:T(8,128)(2,1)S(1)}, u32[]{:S(2)}, u32[]{:S(2)}) collective-permute-start(bf16[2,768,64]{1,2,0:T(8,128)(2,1)S(1)} %bitcast.70), channel_id=1, source_target_pairs={{0,16},{1,17},{2,18},{3,19},{4,20},{5,21},{6,22},{7,23},{8,24},{9,... | collective-permute-start | bytes 589832 | tf_op jit(solution)/shard_map/ppermute | solution.py:231
  54.0 10.1 %copy-start.1 = (bf16[2,2,3072,64]{2,3,0,1:T(8,128)(2,1)S(1)}, bf16[2,2,3072,64]{2,3,0,1:T(8,128)(2,1)}, u32[]{:S(2)}) copy-start(bf16[2,2,3072,64]{2,3,0,1:T(8,128)(2,1)} %all-gather.3.cloned.1.call-done) | copy-start | bytes 4718596
  56.2 57.6 %collective-permute-start.2 = (f32[2,768,64]{1,2,0:T(8,128)}, f32[2,768,64]{1,2,0:T(8,128)}, u32[]{:S(2)}, u32[]{:S(2)}) collective-permute-start(f32[2,768,64]{1,2,0:T(8,128)} %copy.212), channel_id=1, source_target_pairs={{16,0},{17,1},{18,2},{19,3},{20,4},{21,5},{22,6},{23,7},{24,8},{25... | collective-permute-start | bytes 1179656 | tf_op jit(solution)/shard_map/ppermute | solution.py:255
  61.5 51.5 %collective-permute-start.3 = (f32[2,768,1]{1,0,2:T(2,128)}, f32[2,768,1]{1,0,2:T(2,128)}, u32[]{:S(2)}, u32[]{:S(2)}) collective-permute-start(f32[2,768,1]{1,0,2:T(2,128)} %copy.214), channel_id=1, source_target_pairs={{16,0},{17,1},{18,2},{19,3},{20,4},{21,5},{22,6},{23,7},{24,8},{25... | collective-permute-start | bytes 18440 | tf_op jit(solution)/shard_map/ppermute | solution.py:255
  62.8 50.3 %collective-permute-start.1 = (f32[2,768,1]{1,0,2:T(2,128)}, f32[2,768,1]{1,0,2:T(2,128)}, u32[]{:S(2)}, u32[]{:S(2)}) collective-permute-start(f32[2,768,1]{1,0,2:T(2,128)} %copy.208), channel_id=1, source_target_pairs={{16,0},{17,1},{18,2},{19,3},{20,4},{21,5},{22,6},{23,7},{24,8},{25... | collective-permute-start | bytes 18440 | tf_op jit(solution)/shard_map/ppermute | solution.py:255
  109.5 2.9 %copy-start.6 = (f32[2,768,1]{2,1,0:T(8,128)S(1)}, f32[2,768,1]{2,1,0:T(8,128)}, u32[]{:S(2)}) copy-start(f32[2,768,1]{2,1,0:T(8,128)} %get-tuple-element.121) | copy-start | bytes 18436 | tf_op jit(solution)/shard_map/cond
  114.9 1.9 copy-start.11
  114.9 2.1 copy-start.10
  115.0 37.5 %copy-start.12 = (f32[1536]{0:T(1024)S(1)}, f32[1536]{0:T(1024)}, u32[]{:S(2)}) copy-start(f32[1536]{0:T(1024)} %param.24) | copy-start | bytes 18436
  115.0 39.3 %copy-start.7 = (bf16[256,2,2,64]{0,3,2,1:T(8,128)(2,1)S(1)}, bf16[256,2,2,64]{0,3,2,1:T(8,128)(2,1)}, u32[]{:S(2)}) copy-start(bf16[256,2,2,64]{0,3,2,1:T(8,128)(2,1)} %get-tuple-element.129) | copy-start | bytes 393220
  116.6 83.0 %all-gather.5.cloned.1.call-start = ((), (), s32[]{:S(2)}) async-start(), calls=%async_computation.4 | async-start | bytes 1916928 | tf_op jit(solution)/shard_map/all_gather | solution.py:301
  155.5 74.3 %all-to-all-start.1 = ((bf16[4,8,2048]{2,0,1:T(4,128)(2,1)}), bf16[4,8,2048]{2,0,1:T(4,128)(2,1)S(1)}, u32[]{:S(2)}, u32[]{:S(2)}) async-start(bf16[4,8,2048]{2,0,1:T(4,128)(2,1)} %copy.226), calls=%async_computation.1 | async-start | bytes 262144 | tf_op jit(solution)/shard_map/all_to_all | solution.py:201
  229.8 4.4 %copy-start.13 = (s32[256]{0:T(256)S(1)}, s32[256]{0:T(256)}, u32[]{:S(2)}) copy-start(s32[256]{0:T(256)} %param.29) | copy-start | bytes 3076
  229.8 0.7 copy-start.8
  230.5 40.7 %all-to-all-start = ((bf16[8,64,1536]{2,1,0:T(8,128)(2,1)}), bf16[8,64,1536]{2,1,0:T(8,128)(2,1)S(1)}, u32[]{:S(2)}, u32[]{:S(2)}) async-start(bf16[8,64,1536]{2,1,0:T(8,128)(2,1)} %bitcast.73), calls=%async_computation | async-start | bytes 3145728 | tf_op jit(solution)/shard_map/all_to_all | solution.py:337
  271.2 0.9 copy-start.3
Sparse Core Ops, SparseCore 0:
  12.8 38.2 all-gather.2
  116.7 34.5 reduce-scatter.3
  154.4 45.1 all-gather.4

commit v6 on v5

--- a/solution.py
+++ b/solution.py
@@ -14,6 +14,7 @@
 EXPERTS = 32
 PAGE = 8
 SEQ_AXES = ("half", "hseq")
+EXP_AXES = ("ey", "ec")
 
 
 norm_epsilon = 1e-06
@@ -176,7 +177,7 @@
     half_index = lax.axis_index("half")
     half_pos = lax.axis_index("hseq")
     seq_index = half_index * half_size + half_pos
-    exp_index = lax.axis_index("exp")
+    exp_index = lax.axis_index("ey") * lax.axis_size("ec") + lax.axis_index("ec")
     tokens_here = hidden_in.shape[0]
     head_dim = HEAD_DIM
     kv_local = k_weight.shape[1] // head_dim
@@ -265,12 +266,13 @@
     )
     attended = attended.astype(jnp.bfloat16).reshape(kv_local, group_size, tokens_here, head_dim)
     attended = attended.transpose(2, 0, 1, 3).reshape(tokens_here, -1)
-    mixed_rows = lax.psum_scatter(
-        jnp.dot(attended, o_weight, preferred_element_type=jnp.float32).astype(jnp.bfloat16),
-        "exp",
-        scatter_dimension=0,
-        tiled=True,
-    ).astype(jnp.float32)
+    ey_size = lax.axis_size("ey")
+    ec_size = lax.axis_size("ec")
+    projected = jnp.dot(attended, o_weight, preferred_element_type=jnp.float32).astype(jnp.bfloat16)
+    projected = projected.reshape(ey_size, ec_size, -1, projected.shape[1]).transpose(1, 0, 2, 3)
+    projected = projected.reshape(tokens_here, -1)
+    on_chip = lax.psum_scatter(projected, "ec", scatter_dimension=0, tiled=True)
+    mixed_rows = lax.psum_scatter(on_chip, "ey", scatter_dimension=0, tiled=True).astype(jnp.float32)
     moe_rows = mixed_rows.shape[0]
     residual = (
         lax.dynamic_slice_in_dim(hidden_in, exp_index * moe_rows, moe_rows, 0).astype(jnp.float32)
@@ -298,9 +300,10 @@
         ],
         axis=1,
     )
-    packed_all = lax.all_gather(
-        jnp.concatenate([moe_in, side], axis=1), SEQ_AXES, axis=0, tiled=True
-    )
+    crossed = lax.all_gather(
+        jnp.concatenate([moe_in, side], axis=1), "half", axis=0, tiled=True
+    )
+    packed_all = lax.all_gather(crossed, "hseq", axis=0, tiled=True)
     rows_all = packed_all[:, :model_width]
     total_rows = rows_all.shape[0]
     local_first = seq_index * experts_here
@@ -334,14 +337,12 @@
     partial = jnp.einsum(
         "nec,ecd->nd", scaled_hi, produced, preferred_element_type=jnp.float32
     ) + jnp.einsum("nec,ecd->nd", scaled_lo, produced, preferred_element_type=jnp.float32)
-    returned = lax.all_to_all(
-        partial.astype(jnp.bfloat16).reshape(seq_count, moe_rows, -1),
-        SEQ_AXES,
-        split_axis=0,
-        concat_axis=0,
-        tiled=True,
-    )
-    moe = jnp.sum(returned.astype(jnp.float32), axis=0)
+    partial = partial.astype(jnp.bfloat16).reshape(half_size, halves, moe_rows, -1)
+    in_half = lax.psum_scatter(partial, "hseq", scatter_dimension=0, tiled=True)
+    moe = lax.psum_scatter(
+        in_half.reshape(halves, moe_rows, -1), "half", scatter_dimension=0, tiled=True
+    )
+    moe = moe.reshape(moe_rows, -1).astype(jnp.float32)
     hidden_out = (residual + residual_scale * moe).astype(jnp.bfloat16)
     return (hidden_out, page_rows)
 
@@ -349,7 +350,7 @@
 def solution(mesh):
     seq_count, exp_count = mesh.devices.shape
     split_mesh = Mesh(
-        mesh.devices.reshape(2, seq_count // 2, exp_count), ("half", "hseq", "exp")
+        mesh.devices.reshape(2, seq_count // 2, 2, exp_count // 2), SEQ_AXES + EXP_AXES
     )
     return jax.shard_map(
         body,
@@ -357,18 +358,18 @@
         in_specs=(
             P(SEQ_AXES, None),
             P(),
-            P(None, "exp"),
-            P(None, "exp"),
-            P(None, "exp"),
-            P("exp", None),
-            P(SEQ_AXES, "exp"),
+            P(None, EXP_AXES),
+            P(None, EXP_AXES),
+            P(None, EXP_AXES),
+            P(EXP_AXES, None),
+            P(SEQ_AXES, EXP_AXES),
             P(),
             P(SEQ_AXES, None, None),
             P(SEQ_AXES, None, None),
-            P(("half", "hseq", "exp"), None),
-            P(("half", "hseq", "exp"), None),
+            P(SEQ_AXES + EXP_AXES, None),
+            P(SEQ_AXES + EXP_AXES, None),
             P(),
         ),
-        out_specs=(P(("half", "hseq", "exp"), None), P(SEQ_AXES, "exp", None, None)),
+        out_specs=(P(SEQ_AXES + EXP_AXES, None), P(SEQ_AXES, EXP_AXES, None, None)),
         check_vma=False,
     )

time: 281 us -> 305 us (1.085)
  waiting for transfers between devices: 133 us -> 153 us
  blocking collectives: 0 us -> 13.1 us
  local copies, waits for them, and re-layouts: 30.3 us -> 24.5 us
  starting transfers between devices: 19.2 us -> 14.8 us
    all_to_all x1 -> x0, waiting for transfers between devices: 29.5 us -> none  [body(): lax.all_to_all(partial.astype(jnp.bfloat16).reshape(seq_count, moe_rows,...]
    unnamed x3 -> x7, waiting for transfers between devices: 0.05 us -> 19.8 us
    reduce_scatter x1 -> x3, waiting for transfers between devices: 34.1 us -> 52.5 us  [the longest x1 34.4 us: body(): in_half = lax.psum_scatter(partial, 'hseq', scatter_dimension=0, tiled=True)]
    all_gather x0 -> x1, blocking collectives: none -> 13.1 us  [body(): lax.all_gather(jnp.concatenate([moe_in, side], axis=1), 'half', axis=0, t...]
    all_to_all x1, waiting for transfers between devices: 0.01 us -> 11.6 us  [body(): lax.all_to_all(outgoing, SEQ_AXES, split_axis=1, concat_axis=1, tiled=True)]
    unnamed x34 -> x29, local copies, waits for them, and re-layouts: 5.42 us -> 1.1 us
    all_to_all x1 -> x0, starting transfers between devices: 3.58 us -> none  [body(): lax.all_to_all(partial.astype(jnp.bfloat16).reshape(seq_count, moe_rows,...]
  transfers between devices with their start and end apart: 9 -> 11, of which waited for: 7 -> 10; matrix products, arithmetic and copies ran while one was open for 19% -> 6% of each run, Pallas kernels for 15% -> 13%
where the time goes in v6:
time: 305 us; the launch traced here: 304 us
  waiting for transfers between devices  153 us (50%)
  Pallas kernels  40.8 us (13%)
  matrix products  27.1 us (9%)
  local copies, waits for them, and re-layouts  24.5 us (8%)
  other arithmetic  15.4 us (5%)
  starting transfers between devices  14.8 us (5%)
  between operations  14.6 us (5%)
  blocking collectives  13.1 us (4%)
    pallas_call x1, Pallas kernels, attend_partial(): pl.pallas_call(kernel, out_shape=(jax.ShapeDtypeStruct((heads, rows, dim)...  40.8 us
    all_gather x1, waiting for transfers between devices, body(): packed_all = lax.all_gather(crossed, 'hseq', axis=0, tiled=True)  38.9 us
    reduce_scatter x1, waiting for transfers between devices, body(): in_half = lax.psum_scatter(partial, 'hseq', scatter_dimension=0, tiled=True)  34.4 us
    all_gather x1, waiting for transfers between devices, body(): lax.all_gather(jnp.concatenate([cache_own, kv_own], axis=2), 'hseq', axis...  23.5 us
    unnamed x7, waiting for transfers between devices  19.8 us
    reduce_scatter x1, waiting for transfers between devices, body(): lax.psum_scatter(on_chip, 'ey', scatter_dimension=0, tiled=True)  16 us
    all_gather x1, blocking collectives, body(): lax.all_gather(jnp.concatenate([moe_in, side], axis=1), 'half', axis=0, t...  13.1 us
    all_to_all x1, waiting for transfers between devices, body(): lax.all_to_all(outgoing, SEQ_AXES, split_axis=1, concat_axis=1, tiled=True)  11.6 us
  transfers between devices with their start and end apart: 11, of which 10 were waited for; matrix products, arithmetic and copies ran while one was open for 6% of the time, Pallas kernels for 13%

profile of v6, /device:TPU:0, one launch (start us, length us, event | category | flops | bytes accessed | tf_op | source)
XLA Modules:
  0.0 303.7 jit_solution(2379154804966921890)
XLA Ops:
  7.3 1.5 fusion.7
  8.8 1.7 convolution_convert_fusion.5
  11.2 0.7 pad_maximum_fusion.1
  11.9 0.8 pad_maximum_fusion
  12.8 1.9 convolution_convert_fusion.3
  14.8 5.9 %collective-permute-start = (bf16[2,768,64]{1,2,0:T(8,128)(2,1)S(1)}, bf16[2,768,64]{1,2,0:T(8,128)(2,1)S(1)}, u32[]{:S(2)}, u32[]{:S(2)}) collective-permute-start(bf16[2,768,64]{1,2,0:T(8,128)(2,1)S(1)} %bitcast.82), channel_id=1, source_target_pairs={{0,16},{1,17},{2,18},{3,19},{4,20},{5,21},{6,22},{7,23},{8,24},{9,... | collective-permute-start | bytes 589832 | tf_op jit(solution)/shard_map/ppermute | solution.py:232
  20.8 6.8 %collective-permute-done = bf16[2,768,64]{1,2,0:T(8,128)(2,1)S(1)} collective-permute-done((bf16[2,768,64]{1,2,0:T(8,128)(2,1)S(1)}, bf16[2,768,64]{1,2,0:T(8,128)(2,1)S(1)}, u32[]{:S(2)}, u32[]{:S(2)}) %collective-permute-start) | collective-permute-done | bytes 196640 | tf_op jit(solution)/shard_map/ppermute | solution.py:232
  27.6 23.5 %all-gather.3.cloned.1.call-done = bf16[2,2,3072,64]{2,3,0,1:T(8,128)(2,1)} async-done(((bf16[2,2,768,64]{2,3,0,1:T(8,128)(2,1)}), bf16[2,2,3072,64]{2,3,0,1:T(8,128)(2,1)}) %all-gather.3.cloned.1.call-update) | async-done | bytes 1572880 | tf_op jit(solution)/shard_map/all_gather | solution.py:224
  51.1 2.9 conditional.3
  51.1 1.0 broadcast.96
  52.1 1.0 broadcast.94
  53.0 0.9 broadcast.95
  54.0 2.2 copy.254
  56.2 1.3 collective-permute-start.2
  57.5 2.0 copy.250
  59.5 2.0 copy.256
  61.5 1.3 collective-permute-start.3
  62.8 1.3 collective-permute-start.1
  64.1 48.6 %conditional.2 = (f32[2,768,64]{1,2,0:T(8,128)S(1)}, f32[2,768,1]{1,0,2:T(2,128)S(1)}, f32[2,768,1]{1,0,2:T(2,128)S(1)}) conditional(s32[]{:T(128)} %convert_element_type.77, (s32[1]{0:T(128)}, bf16[2,768,64]{1,2,0:T(8,128)(2,1)}, bf16[2,2,3072,64]{2,3,0,1:T(8,128)(2,1)S(1)}) %tuple.89, (s32[1]{0:T(128)}, bf16[2,768,64]{1,2,0:T(8,128)(2,1)}, ...), branch_computations={%region_1.2_spmd, %region_2.3_spmd} | conditional | bytes 4374580 | solution.py:250
  64.1 1.9 copy.246.q_ref
  66.0 2.8 copy.247.k_ref.v_ref
  68.7 40.8 %branch_1_fun.1 = (f32[2,768,64]{2,1,0:T(8,128)}, f32[2,768,1]{2,1,0:T(8,128)}, f32[2,768,1]{2,1,0:T(8,128)}) custom-call(s32[1]{0:T(128)} %get-tuple-element.21.flags_ref, bf16[2,768,64]{2,1,0:T(8,128)(2,1)} %copy.246.q_ref, bf16[2,2,3072,64]{3,2,1,0:T(8,128)(2,1)} %copy.247.k_ref.v_ref, bf16[2,2,3072,64]{3,2,1,0:T(8,128)(2,1)} %copy.247.k_ref.v_ref), custom_call_target="tpu_custom_call" | custom-call | tf_op jit(solution)/shard_map/cond/branch_1_fun/pallas_call | solution.py:125
  109.5 1.5 copy.283
  111.0 1.4 copy.285
  113.0 0.7 fusion.38
  113.8 1.1 divide_convert_fusion
  115.6 1.0 copy.258
  116.7 19.7 %reduce-scatter.13.cloned.1.call-done = bf16[128,1536]{1,0:T(8,128)(2,1)} async-done(((bf16[256,1536]{1,0:T(8,128)(2,1)}), bf16[128,1536]{1,0:T(8,128)(2,1)}) %reduce-scatter.13.cloned.1.call-update) | async-done | bytes 393232
  137.0 16.0 %reduce-scatter.15.cloned.1.call-done = bf16[64,1536]{1,0:T(8,128)(2,1)} async-done(((bf16[128,1536]{1,0:T(8,128)(2,1)}), bf16[64,1536]{1,0:T(8,128)(2,1)}) %reduce-scatter.15.cloned.1.call-update) | async-done | bytes 196624 | tf_op jit(solution)/shard_map/reduce_scatter | solution.py:275
  153.0 1.1 multiply_reduce_fusion
  154.1 1.0 multiply_convert_fusion
  155.3 13.1 %all_gather.10 = bf16[128,1664]{1,0:T(8,128)(2,1)S(1)} all-gather(bf16[64,1664]{1,0:T(8,128)(2,1)S(1)} %concatenate.7), channel_id=1, replica_groups=mesh['half'=2,'hseq'=4,'ey'=2,'ec'=2] {'half'}, dimensions={0}, use_global_device_ids=true | all-gather | bytes 638976 | tf_op jit(solution)/shard_map/all_gather | solution.py:303
  168.4 1.0 copy.264
  169.6 38.9 %all-gather.5.cloned.1.call-done = bf16[512,1664]{0,1:T(8,128)(2,1)} async-done(((bf16[128,1664]{0,1:T(8,128)(2,1)}), bf16[512,1664]{0,1:T(8,128)(2,1)}) %all-gather.5.cloned.1.call-update) | async-done | bytes 1703952 | tf_op jit(solution)/shard_map/all_gather | solution.py:306
  208.5 0.9 slice.16
  209.7 6.3 %fusion.44 = s32[8,64,4]{2,0,1:T(8,128)S(1)} fusion(s32[8,64,4]{2,0,1:T(8,128)S(1)} %copy.265), kind=kOutput, calls=%fused_computation.78 | output fusion | flops 129024 | bytes 16384 | tf_op jit(solution)/shard_map/jit(cumsum)/reduce_window_sum | solution.py:317
  216.3 10.7 %fusion.45 = f32[4,256,1024]{2,1,0:T(8,128)} fusion(bf16[4,1536,1024]{2,1,0:T(8,128)(2,1)} %param.25, bf16[512,1664]{0,1:T(8,128)(2,1)} %all-gather.5.cloned.1.call-done, s32[512,4]{0,1:T(4,128)S(1)} %subtract_add_fusion, pred[512,4]{0,1:T(4,128)(4,1)S(1)} %get-tuple-element.139), kind=kOutput, calls=%fused_computation.79 | convolution fusion | flops 4834983936 | bytes 18360320 | tf_op jit(solution)/shard_map/ecd,edf->ecf/dot_general | solution.py:329
  227.0 5.9 %convolution_convert_fusion.1 = bf16[4,256,1536]{2,1,0:T(8,128)(2,1)S(1)} fusion(bf16[4,512,1536]{2,1,0:T(8,128)(2,1)} %param.26, f32[4,256,1024]{2,1,0:T(8,128)} %fusion.45), kind=kOutput, calls=%fused_computation.2 | convolution fusion | flops 1615331328 | bytes 13631488 | tf_op jit(solution)/shard_map/ecf,efd->ecd/dot_general | solution.py:332
  232.9 2.1 convolution_bitcast_fusion
  235.0 3.7 %fusion.1 = bf16[512,1536]{1,0:T(8,128)(2,1)} fusion(f32[512,1536]{1,0:T(8,128)S(1)} %convolution_bitcast_fusion, bf16[4,256,1536]{2,1,0:T(8,128)(2,1)S(1)} %convolution_convert_fusion.1, s32[512,4]{0,1:T(4,128)S(1)} %subtract_add_fusion, pred[512,4]{0,1:T(4,128)(4,1)S(1)} %get-tuple-element.139, bf16[512,4]{0,1:T(4,128)(2,1)S(1)} %get-tuple-element.144), kind=kOutput, calls=%fused_computation.6 | convolution fusion | flops 1613758464 | bytes 7878656 | tf_op jit(solution)/shard_map/nec,ecd->nd/dot_general | solution.py:337
  238.8 34.4 %reduce-scatter.9.cloned.1.call-done = bf16[1,2,64,1536]{3,2,1,0:T(8,128)(2,1)} async-done(((bf16[4,2,64,1536]{3,2,1,0:T(8,128)(2,1)}), bf16[1,2,64,1536]{3,2,1,0:T(8,128)(2,1)}) %reduce-scatter.9.cloned.1.call-update) | async-done | bytes 393232 | tf_op jit(solution)/shard_map/reduce_scatter | solution.py:341
  273.7 0.8 copy.270
  274.5 4.6 %all-to-all-start = ((bf16[4,8,2048]{2,0,1:T(4,128)(2,1)}), bf16[4,8,2048]{2,0,1:T(4,128)(2,1)S(1)}, u32[]{:S(2)}, u32[]{:S(2)}) async-start(bf16[4,8,2048]{2,0,1:T(4,128)(2,1)} %copy.270), calls=%async_computation.2 | async-start | bytes 262144 | tf_op jit(solution)/shard_map/all_to_all | solution.py:202
  279.4 11.6 %all-to-all-done = bf16[4,8,2048]{2,0,1:T(4,128)(2,1)S(1)} async-done(((bf16[4,8,2048]{2,0,1:T(4,128)(2,1)}), bf16[4,8,2048]{2,0,1:T(4,128)(2,1)S(1)}, u32[]{:S(2)}, u32[]{:S(2)}) %all-to-all-start) | async-done | bytes 131104 | tf_op jit(solution)/shard_map/all_to_all | solution.py:202
  291.0 0.9 scatter_custom_fusion
  292.2 0.8 reshape.153
  293.0 2.1 reduce-scatter.11.cloned.1.call-done
  295.1 1.7 fusion.25
  (83 shorter events, 5.0 us)
Async XLA Ops:
  7.2 107.8 %copy-start = (bf16[384,1536]{1,0:T(8,128)(2,1)S(1)}, bf16[384,1536]{1,0:T(8,128)(2,1)}, u32[]{:S(2)}) copy-start(bf16[384,1536]{1,0:T(8,128)(2,1)} %param.22) | copy-start | bytes 3538948
  7.2 3.4 %copy-start.2 = (bf16[256,1536]{1,0:T(8,128)(2,1)S(1)}, bf16[256,1536]{1,0:T(8,128)(2,1)}, u32[]{:S(2)}) copy-start(bf16[256,1536]{1,0:T(8,128)(2,1)} %param.17) | copy-start | bytes 2359300
  7.2 3.4 %copy-start.14 = (f32[1536]{0:T(1024)S(1)}, f32[1536]{0:T(1024)}, u32[]{:S(2)}) copy-start(f32[1536]{0:T(1024)} %param.18) | copy-start | bytes 18436
  7.2 3.4 %copy-start.13 = (bf16[1536,128]{1,0:T(8,128)(2,1)S(1)}, bf16[1536,128]{1,0:T(8,128)(2,1)}, u32[]{:S(2)}) copy-start(bf16[1536,128]{1,0:T(8,128)(2,1)} %param.21) | copy-start | bytes 1179652
  7.2 3.9 %copy-start.8 = (bf16[512,256]{1,0:T(8,128)(2,1)S(1)}, bf16[512,256]{1,0:T(8,128)(2,1)}, u32[]{:S(2)}) copy-start(bf16[512,256]{1,0:T(8,128)(2,1)} %param.23) | copy-start | bytes 786436
  7.2 43.9 %all-gather.3.cloned.1.call-start = ((), (), s32[]{:S(2)}) async-start(), calls=%async_computation.5 | async-start | bytes 1966080 | tf_op jit(solution)/shard_map/all_gather | solution.py:224
  12.7 123.7 %reduce-scatter.13.cloned.1.call-start = ((), (), s32[]{:S(2)}) async-start(), calls=%async_computation.9 | async-start | bytes 1179648
  14.8 36.3 %copy-start.4 = (bf16[2,3,8,8,256]{4,3,1,2,0:T(8,128)(2,1)}, bf16[2,3,8,8,256]{4,3,1,2,0:T(8,128)(2,1)S(1)}, u32[]{:S(2)}) copy-start(bf16[2,3,8,8,256]{4,3,1,2,0:T(8,128)(2,1)S(1)} %copy.289) | copy-start | bytes 589828
  14.8 12.8 %collective-permute-start = (bf16[2,768,64]{1,2,0:T(8,128)(2,1)S(1)}, bf16[2,768,64]{1,2,0:T(8,128)(2,1)S(1)}, u32[]{:S(2)}, u32[]{:S(2)}) collective-permute-start(bf16[2,768,64]{1,2,0:T(8,128)(2,1)S(1)} %bitcast.82), channel_id=1, source_target_pairs={{0,16},{1,17},{2,18},{3,19},{4,20},{5,21},{6,22},{7,23},{8,24},{9,... | collective-permute-start | bytes 589832 | tf_op jit(solution)/shard_map/ppermute | solution.py:232
  54.0 10.1 %copy-start.1 = (bf16[2,2,3072,64]{2,3,0,1:T(8,128)(2,1)S(1)}, bf16[2,2,3072,64]{2,3,0,1:T(8,128)(2,1)}, u32[]{:S(2)}) copy-start(bf16[2,2,3072,64]{2,3,0,1:T(8,128)(2,1)} %all-gather.3.cloned.1.call-done) | copy-start | bytes 4718596
  56.2 57.6 %collective-permute-start.2 = (f32[2,768,64]{1,2,0:T(8,128)}, f32[2,768,64]{1,2,0:T(8,128)}, u32[]{:S(2)}, u32[]{:S(2)}) collective-permute-start(f32[2,768,64]{1,2,0:T(8,128)} %copy.254), channel_id=1, source_target_pairs={{16,0},{17,1},{18,2},{19,3},{20,4},{21,5},{22,6},{23,7},{24,8},{25... | collective-permute-start | bytes 1179656 | tf_op jit(solution)/shard_map/ppermute | solution.py:256
  61.5 51.5 %collective-permute-start.3 = (f32[2,768,1]{1,0,2:T(2,128)}, f32[2,768,1]{1,0,2:T(2,128)}, u32[]{:S(2)}, u32[]{:S(2)}) collective-permute-start(f32[2,768,1]{1,0,2:T(2,128)} %copy.256), channel_id=1, source_target_pairs={{16,0},{17,1},{18,2},{19,3},{20,4},{21,5},{22,6},{23,7},{24,8},{25... | collective-permute-start | bytes 18440 | tf_op jit(solution)/shard_map/ppermute | solution.py:256
  62.8 50.3 %collective-permute-start.1 = (f32[2,768,1]{1,0,2:T(2,128)}, f32[2,768,1]{1,0,2:T(2,128)}, u32[]{:S(2)}, u32[]{:S(2)}) collective-permute-start(f32[2,768,1]{1,0,2:T(2,128)} %copy.250), channel_id=1, source_target_pairs={{16,0},{17,1},{18,2},{19,3},{20,4},{21,5},{22,6},{23,7},{24,8},{25... | collective-permute-start | bytes 18440 | tf_op jit(solution)/shard_map/ppermute | solution.py:256
  109.5 2.9 copy-start.6
  115.0 21.6 %copy-start.10 = (s32[64,8]{0,1:T(8,128)S(1)}, s32[64,8]{0,1:T(8,128)}, u32[]{:S(2)}) copy-start(s32[64,8]{0,1:T(8,128)} %param.27) | copy-start | bytes 6148
  115.0 21.8 %copy-start.9 = (f32[64,8]{0,1:T(8,128)S(1)}, f32[64,8]{0,1:T(8,128)}, u32[]{:S(2)}) copy-start(f32[64,8]{0,1:T(8,128)} %param.28) | copy-start | bytes 6148
  115.6 38.5 %copy-start.11 = (f32[1536]{0:T(1024)S(1)}, f32[1536]{0:T(1024)}, u32[]{:S(2)}) copy-start(f32[1536]{0:T(1024)} %param.24) | copy-start | bytes 18436
  116.6 36.4 %reduce-scatter.15.cloned.1.call-start = ((), (), s32[]{:S(2)}) async-start(), calls=%async_computation.10 | async-start | bytes 589824 | tf_op jit(solution)/shard_map/reduce_scatter | solution.py:275
  136.4 72.2 %all-gather.5.cloned.1.call-start = ((), (), s32[]{:S(2)}) async-start(), calls=%async_computation.6 | async-start | bytes 2129920 | tf_op jit(solution)/shard_map/all_gather | solution.py:306
  169.4 103.8 %reduce-scatter.9.cloned.1.call-start = ((), (), s32[]{:S(2)}) async-start(), calls=%async_computation.7 | async-start | bytes 1966080 | tf_op jit(solution)/shard_map/reduce_scatter | solution.py:341
  235.0 38.2 %copy-start.7 = (bf16[256,2,2,64]{0,3,2,1:T(8,128)(2,1)S(1)}, bf16[256,2,2,64]{0,3,2,1:T(8,128)(2,1)}, u32[]{:S(2)}) copy-start(bf16[256,2,2,64]{0,3,2,1:T(8,128)(2,1)} %get-tuple-element.142) | copy-start | bytes 393220
  238.7 40.5 %copy-start.12 = (s32[256]{0:T(256)S(1)}, s32[256]{0:T(256)}, u32[]{:S(2)}) copy-start(s32[256]{0:T(256)} %param.29) | copy-start | bytes 3076
  238.7 56.4 %copy-start.3 = (bf16[64,1536]{1,0:T(8,128)(2,1)S(1)}, bf16[64,1536]{1,0:T(8,128)(2,1)}, u32[]{:S(2)}) copy-start(bf16[64,1536]{1,0:T(8,128)(2,1)} %reduce-scatter.15.cloned.1.call-done) | copy-start | bytes 589828
  238.8 56.4 %reduce-scatter.11.cloned.1.call-start = ((), (), s32[]{:S(2)}) async-start(), calls=%async_computation.8 | async-start | bytes 589824 | tf_op jit(solution)/shard_map/reduce_scatter | solution.py:342
  274.5 16.5 %all-to-all-start = ((bf16[4,8,2048]{2,0,1:T(4,128)(2,1)}), bf16[4,8,2048]{2,0,1:T(4,128)(2,1)S(1)}, u32[]{:S(2)}, u32[]{:S(2)}) async-start(bf16[4,8,2048]{2,0,1:T(4,128)(2,1)} %copy.270), calls=%async_computation.2 | async-start | bytes 262144 | tf_op jit(solution)/shard_map/all_to_all | solution.py:202
Sparse Core Ops, SparseCore 0:
  12.8 38.2 all-gather.2
  116.7 19.5 reduce-scatter.12
  138.7 14.2 reduce-scatter.14
  169.5 38.9 all-gather.4
  238.9 34.2 reduce-scatter.8
  275.3 19.7 reduce-scatter.10

commit v7 on v5

--- a/solution.py
+++ b/solution.py
@@ -145,6 +145,16 @@
         ),
         compiler_params=pltpu.CompilerParams(dimension_semantics=("arbitrary", "arbitrary")),
     )(flags, q, kv_all, kv_all)
+
+
+def gather_by_all_to_all(values, axis_name, axis):
+    count = lax.axis_size(axis_name)
+    spread = jnp.broadcast_to(values[None], (count,) + values.shape)
+    moved = lax.all_to_all(spread, axis_name, split_axis=0, concat_axis=0, tiled=True)
+    moved = jnp.moveaxis(moved, 0, axis)
+    shape = list(values.shape)
+    shape[axis] = shape[axis] * count
+    return moved.reshape(shape)
 
 
 def pl_cdiv(a, b):
@@ -220,9 +230,7 @@
     kv_own = split_new.transpose(2, 1, 0, 3)
     cache_rows = cache_kv.shape[0]
     cache_own = cache_kv.reshape(cache_rows, kv_local, 2, head_dim).transpose(2, 1, 0, 3)
-    kv_all = lax.all_gather(
-        jnp.concatenate([cache_own, kv_own], axis=2), "hseq", axis=2, tiled=True
-    )
+    kv_all = gather_by_all_to_all(jnp.concatenate([cache_own, kv_own], axis=2), "hseq", 2)
     key_block = math.gcd(math.gcd(cache_rows, tokens_here), 256)
     cache_per = cache_rows // key_block
     new_per = tokens_here // key_block
@@ -265,12 +273,12 @@
     )
     attended = attended.astype(jnp.bfloat16).reshape(kv_local, group_size, tokens_here, head_dim)
     attended = attended.transpose(2, 0, 1, 3).reshape(tokens_here, -1)
-    mixed_rows = lax.psum_scatter(
-        jnp.dot(attended, o_weight, preferred_element_type=jnp.float32).astype(jnp.bfloat16),
-        "exp",
-        scatter_dimension=0,
-        tiled=True,
-    ).astype(jnp.float32)
+    exp_count = lax.axis_size("exp")
+    projected = jnp.dot(attended, o_weight, preferred_element_type=jnp.float32).astype(jnp.bfloat16)
+    pieces = lax.all_to_all(
+        projected.reshape(exp_count, -1, projected.shape[1]), "exp", split_axis=0, concat_axis=0, tiled=True
+    )
+    mixed_rows = jnp.sum(pieces.astype(jnp.float32), axis=0)
     moe_rows = mixed_rows.shape[0]
     residual = (
         lax.dynamic_slice_in_dim(hidden_in, exp_index * moe_rows, moe_rows, 0).astype(jnp.float32)
@@ -298,9 +306,7 @@
         ],
         axis=1,
     )
-    packed_all = lax.all_gather(
-        jnp.concatenate([moe_in, side], axis=1), SEQ_AXES, axis=0, tiled=True
-    )
+    packed_all = gather_by_all_to_all(jnp.concatenate([moe_in, side], axis=1), SEQ_AXES, 0)
     rows_all = packed_all[:, :model_width]
     total_rows = rows_all.shape[0]
     local_first = seq_index * experts_here

time: 281 us -> 252 us (0.90)
  waiting for transfers between devices: 133 us -> 95.9 us
  starting transfers between devices: 19.2 us -> 44.7 us
  between operations: 14.2 us -> 1.06 us
  other arithmetic: 14.6 us -> 11.4 us
    all_gather x2 -> x0, waiting for transfers between devices: 61.9 us -> none  [the longest x1 38.4 us: body(): lax.all_gather(jnp.concatenate([moe_in, side], axis=1), SEQ_AXES, axis=0,...]
    all_to_all x0 -> x3, waiting for transfers between devices: none -> 60 us  [the longest x2 48.8 us: gather_by_all_to_all(): lax.all_to_all(spread, axis_name, split_axis=0, concat_axis=0, tiled=True)]
    reduce_scatter x1 -> x0, waiting for transfers between devices: 34.1 us -> none  [body(): lax.psum_scatter(jnp.dot(attended, o_weight, preferred_element_type=jnp.f...]
    all_to_all x0 -> x3, starting transfers between devices: none -> 25.7 us  [the longest x2 21.9 us: gather_by_all_to_all(): lax.all_to_all(spread, axis_name, split_axis=0, concat_axis=0, tiled=True)]
    ppermute x1, waiting for transfers between devices: 6.82 us -> 0.01 us  [body(): partner_rows = lax.ppermute(query_rows, 'half', perm=[(0, 1)])]
    ppermute x3, waiting for transfers between devices: 0.38 us -> 3.51 us  [body(): lax.ppermute(far_part, 'half', perm=[(1, 0)])]
    all_to_all x1, waiting for transfers between devices: 29.5 us -> 32.4 us  [body(): lax.all_to_all(partial.astype(jnp.bfloat16).reshape(seq_count, moe_rows,...]
  transfers between devices with their start and end apart: 9 -> 9, of which waited for: 7 -> 6; matrix products, arithmetic and copies ran while one was open for 19% -> 20% of each run, Pallas kernels for 15% -> 16%
where the time goes in v7:
time: 252 us; the launch traced here: 251 us
  waiting for transfers between devices  95.9 us (38%)
  starting transfers between devices  44.7 us (18%)
  Pallas kernels  40.8 us (16%)
  local copies, waits for them, and re-layouts  28.8 us (11%)
  matrix products  28.2 us (11%)
  other arithmetic  11.4 us (5%)
    all_to_all x2, waiting for transfers between devices, gather_by_all_to_all(): lax.all_to_all(spread, axis_name, split_axis=0, concat_axis=0, tiled=True)  48.8 us
    pallas_call x1, Pallas kernels, attend_partial(): pl.pallas_call(kernel, out_shape=(jax.ShapeDtypeStruct((heads, rows, dim)...  40.8 us
    all_to_all x1, waiting for transfers between devices, body(): lax.all_to_all(partial.astype(jnp.bfloat16).reshape(seq_count, moe_rows,...  32.4 us
    all_to_all x2, starting transfers between devices, gather_by_all_to_all(): lax.all_to_all(spread, axis_name, split_axis=0, concat_axis=0, tiled=True)  21.9 us
    all_to_all x1, waiting for transfers between devices, body(): lax.all_to_all(projected.reshape(exp_count, -1, projected.shape[1]), 'exp...  11.2 us
    dot_general x1, matrix products, body(): jnp.einsum('ecd,edf->ecf', rows_in, expert_in, preferred_element_type=jnp...  10.2 us
    another operation x5, local copies, waits for them, and re-layouts  6.5 us
    another operation x1, other arithmetic, body(): rank = jnp.cumsum(named_blocks, axis=1) - named_blocks  6.33 us
  transfers between devices with their start and end apart: 9, of which 6 were waited for; matrix products, arithmetic and copies ran while one was open for 20% of the time, Pallas kernels for 16%

profile of v7, /device:TPU:0, one launch (start us, length us, event | category | flops | bytes accessed | tf_op | source)
XLA Modules:
  0.0 250.9 jit_solution(1499144137749265955)
XLA Ops:
  0.7 1.5 fusion.7
  2.2 1.7 convolution_convert_fusion.5
  4.6 0.7 pad_maximum_fusion.1
  5.4 1.3 broadcast_in_dim.84
  6.7 5.2 %all-to-all-start = ((bf16[4,2,2,768,64]{3,4,2,1,0:T(8,128)(2,1)}), bf16[4,2,2,768,64]{3,4,2,1,0:T(8,128)(2,1)S(1)}, u32[]{:S(2)}, u32[]{:S(2)}) async-start(bf16[4,2,2,768,64]{3,4,2,1,0:T(8,128)(2,1)} %broadcast_in_dim.84), calls=%async_computation | async-start | bytes 3145728 | tf_op jit(solution)/shard_map/all_to_all | solution.py:153
  11.9 2.6 %convolution_convert_fusion.3 = bf16[256,384]{1,0:T(8,128)(2,1)} fusion(bf16[1536,384]{1,0:T(8,128)(2,1)} %param.19, bf16[256,1536]{1,0:T(8,128)(2,1)S(1)} %copy-done.3, f32[1536]{0:T(1024)S(1)} %copy-done.14, f32[256]{0:T(256)S(1)} %add_rsqrt_fusion), kind=kOutput, calls=%fused_computation.22 | convolution fusion | flops 303661056 | bytes 2169856 | tf_op jit(solution)/shard_map/dot_general | solution.py:196
  14.5 1.1 copy.169
  15.6 5.2 %collective-permute-start = (bf16[2,768,64]{1,2,0:T(8,128)(2,1)S(1)}, bf16[2,768,64]{1,2,0:T(8,128)(2,1)}, u32[]{:S(2)}, u32[]{:S(2)}) collective-permute-start(bf16[2,768,64]{1,2,0:T(8,128)(2,1)S(1)} %bitcast.78), channel_id=1, source_target_pairs={{0,16},{1,17},{2,18},{3,19},{4,20},{5,21},{6,22},{7,23},{8,24},{9,... | collective-permute-start | bytes 589832 | tf_op jit(solution)/shard_map/ppermute | solution.py:239
  20.7 10.4 %all-to-all-done = bf16[4,2,2,768,64]{3,4,2,1,0:T(8,128)(2,1)S(1)} async-done(((bf16[4,2,2,768,64]{3,4,2,1,0:T(8,128)(2,1)}), bf16[4,2,2,768,64]{3,4,2,1,0:T(8,128)(2,1)S(1)}, u32[]{:S(2)}, u32[]{:S(2)}) %all-to-all-start) | async-done | bytes 1572896 | tf_op jit(solution)/shard_map/all_to_all | solution.py:153
  31.2 1.2 copy-done.2
  32.3 1.6 copy.216
  33.9 2.9 %conditional.3 = ((f32[2,768,64]{2,1,0:T(8,128)}, f32[2,768,1]{2,1,0:T(8,128)}, f32[2,768,1]{2,1,0:T(8,128)})) conditional(s32[]{:T(128)} %convert_element_type.76, (s32[1]{0:T(128)}, bf16[2,768,64]{1,2,0:T(8,128)(2,1)}, bf16[2,2,3072,64]{2,3,1,0:T(8,128)(2,1)S(1)}) %tuple.64, () %tuple.23), branch_computations={%region_3.4_spmd, %region_4.5_spmd} | conditional | bytes 3538952 | solution.py:251
  34.0 1.0 broadcast.95
  34.9 1.0 broadcast.93
  35.9 0.9 broadcast.94
  36.8 2.1 copy.186
  38.9 1.3 collective-permute-start.2
  40.2 1.4 copy.182
  41.6 1.4 copy.188
  43.0 1.3 collective-permute-start.3
  44.3 1.3 collective-permute-start.1
  45.6 47.6 %conditional.2 = (f32[2,768,64]{1,2,0:T(8,128)S(1)}, f32[2,768,1]{1,0,2:T(2,128)S(1)}, f32[2,768,1]{1,0,2:T(2,128)S(1)}) conditional(s32[]{:T(128)} %convert_element_type.76, (s32[1]{0:T(128)}, bf16[2,768,64]{1,2,0:T(8,128)(2,1)S(1)}, bf16[2,2,3072,64]{2,3,1,0:T(8,128)(2,1)S(1)}) %tuple.67, (s32[1]{0:T(128)}, bf16[2,768,64]{1,2,0:T(8,128)(2,1)S(1)}, ...), branch_computations={%region_1.2_spmd, %region_2.3_spmd} | conditional | bytes 4374580 | solution.py:257
  45.6 0.9 copy.178.q_ref
  46.6 2.7 %copy.179.k_ref.v_ref = bf16[2,2,3072,64]{3,2,1,0:T(8,128)(2,1)} copy(bf16[2,2,3072,64]{2,3,1,0:T(8,128)(2,1)S(1)} %get-tuple-element.90) | data formatting | bytes 3145728 | tf_op jit(solution)/shard_map
  49.3 40.8 %branch_1_fun.1 = (f32[2,768,64]{2,1,0:T(8,128)}, f32[2,768,1]{2,1,0:T(8,128)}, f32[2,768,1]{2,1,0:T(8,128)}) custom-call(s32[1]{0:T(128)} %get-tuple-element.21.flags_ref, bf16[2,768,64]{2,1,0:T(8,128)(2,1)} %copy.178.q_ref, bf16[2,2,3072,64]{3,2,1,0:T(8,128)(2,1)} %copy.179.k_ref.v_ref, bf16[2,2,3072,64]{3,2,1,0:T(8,128)(2,1)} %copy.179.k_ref.v_ref), custom_call_target="tpu_custom_call" | custom-call | tf_op jit(solution)/shard_map/cond/branch_1_fun/pallas_call | solution.py:124
  90.1 1.5 copy.205
  91.6 1.4 copy.207
  93.3 3.4 %collective-permute-done.3 = f32[2,768,1]{1,0,2:T(2,128)S(1)} collective-permute-done((f32[2,768,1]{1,0,2:T(2,128)S(1)}, f32[2,768,1]{1,0,2:T(2,128)S(1)}, u32[]{:S(2)}, u32[]{:S(2)}) %collective-permute-start.3) | collective-permute-done | bytes 6176 | tf_op jit(solution)/shard_map/ppermute | solution.py:263
  97.1 1.5 convolution_convert_fusion.2
  98.6 3.8 %all-to-all-start.1 = ((bf16[4,64,1536]{2,1,0:T(8,128)(2,1)}), bf16[4,64,1536]{2,1,0:T(8,128)(2,1)S(1)}, u32[]{:S(2)}, u32[]{:S(2)}) async-start(bf16[4,64,1536]{2,1,0:T(8,128)(2,1)} %bitcast.16), calls=%async_computation.1 | async-start | bytes 1572864 | tf_op jit(solution)/shard_map/all_to_all | solution.py:278
  102.8 11.2 %all-to-all-done.1 = bf16[4,64,1536]{2,1,0:T(8,128)(2,1)S(1)} async-done(((bf16[4,64,1536]{2,1,0:T(8,128)(2,1)}), bf16[4,64,1536]{2,1,0:T(8,128)(2,1)S(1)}, u32[]{:S(2)}, u32[]{:S(2)}) %all-to-all-start.1) | async-done | bytes 786464 | tf_op jit(solution)/shard_map/all_to_all | solution.py:278
  114.5 1.3 broadcast_in_dim.91
  115.9 16.7 %all-to-all-start.2 = ((bf16[8,64,1664]{2,1,0:T(8,128)(2,1)}), bf16[8,64,1664]{2,1,0:T(8,128)(2,1)}, u32[]{:S(2)}, u32[]{:S(2)}) async-start(bf16[8,64,1664]{2,1,0:T(8,128)(2,1)} %broadcast_in_dim.91), calls=%async_computation.2 | async-start | bytes 3407872 | tf_op jit(solution)/shard_map/all_to_all | solution.py:153
  133.2 0.8 copy.198
  134.0 38.4 %all-to-all-done.2 = bf16[8,64,1664]{2,1,0:T(8,128)(2,1)} async-done(((bf16[8,64,1664]{2,1,0:T(8,128)(2,1)}), bf16[8,64,1664]{2,1,0:T(8,128)(2,1)}, u32[]{:S(2)}, u32[]{:S(2)}) %all-to-all-start.2) | async-done | bytes 1703968 | tf_op jit(solution)/shard_map/all_to_all | solution.py:153
  172.3 3.6 %all-to-all-start.4 = ((bf16[4,8,2048]{2,0,1:T(4,128)(2,1)}), bf16[4,8,2048]{2,0,1:T(4,128)(2,1)S(1)}, u32[]{:S(2)}, u32[]{:S(2)}) async-start(bf16[4,8,2048]{2,0,1:T(4,128)(2,1)} %copy.198), calls=%async_computation.4 | async-start | bytes 262144 | tf_op jit(solution)/shard_map/all_to_all | solution.py:211
  176.0 0.9 slice.16
  177.7 6.3 %fusion.42 = s32[8,64,4]{2,0,1:T(8,128)S(1)} fusion(s32[8,64,4]{2,0,1:T(8,128)S(1)} %copy.194), kind=kOutput, calls=%fused_computation.79 | output fusion | flops 129024 | bytes 16384 | tf_op jit(solution)/shard_map/jit(cumsum)/reduce_window_sum | solution.py:320
  184.3 10.2 %fusion.43 = f32[4,256,1024]{2,1,0:T(8,128)} fusion(bf16[4,1536,1024]{2,1,0:T(8,128)(2,1)} %param.25, bf16[512,1664]{1,0:T(8,128)(2,1)} %bitcast.17, s32[512,4]{0,1:T(4,128)S(1)} %subtract_add_fusion, pred[512,4]{0,1:T(4,128)(4,1)S(1)} %get-tuple-element.106), kind=kOutput, calls=%fused_computation.80 | convolution fusion | flops 4834459648 | bytes 18360320 | tf_op jit(solution)/shard_map/ecd,edf->ecf/dot_general | solution.py:332
  194.5 5.9 %convolution_convert_fusion.1 = bf16[4,256,1536]{2,1,0:T(8,128)(2,1)S(1)} fusion(bf16[4,512,1536]{2,1,0:T(8,128)(2,1)} %param.26, f32[4,256,1024]{2,1,0:T(8,128)} %fusion.43), kind=kOutput, calls=%fused_computation.2 | convolution fusion | flops 1615331328 | bytes 13631488 | tf_op jit(solution)/shard_map/ecf,efd->ecd/dot_general | solution.py:335
  200.4 2.1 convolution_bitcast_fusion
  202.5 3.7 %fusion.1 = bf16[512,1536]{1,0:T(8,128)(2,1)} fusion(f32[512,1536]{1,0:T(8,128)S(1)} %convolution_bitcast_fusion, bf16[4,256,1536]{2,1,0:T(8,128)(2,1)S(1)} %convolution_convert_fusion.1, s32[512,4]{0,1:T(4,128)S(1)} %subtract_add_fusion, pred[512,4]{0,1:T(4,128)(4,1)S(1)} %get-tuple-element.106, bf16[512,4]{0,1:T(4,128)(2,1)S(1)} %copy.213), kind=kOutput, calls=%fused_computation.7 | convolution fusion | flops 1613758464 | bytes 7878656 | tf_op jit(solution)/shard_map/nec,ecd->nd/dot_general | solution.py:340
  206.2 6.3 %all-to-all-start.3 = ((bf16[8,64,1536]{2,1,0:T(8,128)(2,1)}), bf16[8,64,1536]{2,1,0:T(8,128)(2,1)S(1)}, u32[]{:S(2)}, u32[]{:S(2)}) async-start(bf16[8,64,1536]{2,1,0:T(8,128)(2,1)} %bitcast.81), calls=%async_computation.3 | async-start | bytes 3145728 | tf_op jit(solution)/shard_map/all_to_all | solution.py:343
  212.8 0.9 scatter_custom_fusion
  214.0 0.7 copy.203
  214.7 1.8 reshape.151
  216.5 32.4 %all-to-all-done.3 = bf16[8,64,1536]{2,1,0:T(8,128)(2,1)S(1)} async-done(((bf16[8,64,1536]{2,1,0:T(8,128)(2,1)}), bf16[8,64,1536]{2,1,0:T(8,128)(2,1)S(1)}, u32[]{:S(2)}, u32[]{:S(2)}) %all-to-all-start.3) | async-done | bytes 1572896 | tf_op jit(solution)/shard_map/all_to_all | solution.py:343
  249.2 1.7 add_convert_fusion
  (79 shorter events, 4.6 us)
Async XLA Ops:
  0.6 96.4 %copy-start = (bf16[384,1536]{1,0:T(8,128)(2,1)S(1)}, bf16[384,1536]{1,0:T(8,128)(2,1)}, u32[]{:S(2)}) copy-start(bf16[384,1536]{1,0:T(8,128)(2,1)} %param.22) | copy-start | bytes 3538948
  0.6 3.3 %copy-start.3 = (bf16[256,1536]{1,0:T(8,128)(2,1)S(1)}, bf16[256,1536]{1,0:T(8,128)(2,1)}, u32[]{:S(2)}) copy-start(bf16[256,1536]{1,0:T(8,128)(2,1)} %param.17) | copy-start | bytes 2359300
  0.7 3.3 %copy-start.14 = (f32[1536]{0:T(1024)S(1)}, f32[1536]{0:T(1024)}, u32[]{:S(2)}) copy-start(f32[1536]{0:T(1024)} %param.18) | copy-start | bytes 18436
  0.7 3.3 %copy-start.13 = (bf16[1536,128]{1,0:T(8,128)(2,1)S(1)}, bf16[1536,128]{1,0:T(8,128)(2,1)}, u32[]{:S(2)}) copy-start(bf16[1536,128]{1,0:T(8,128)(2,1)} %param.21) | copy-start | bytes 1179652
  0.7 3.8 %copy-start.8 = (bf16[512,256]{1,0:T(8,128)(2,1)S(1)}, bf16[512,256]{1,0:T(8,128)(2,1)}, u32[]{:S(2)}) copy-start(bf16[512,256]{1,0:T(8,128)(2,1)} %param.23) | copy-start | bytes 786436
  6.7 24.5 %all-to-all-start = ((bf16[4,2,2,768,64]{3,4,2,1,0:T(8,128)(2,1)}), bf16[4,2,2,768,64]{3,4,2,1,0:T(8,128)(2,1)S(1)}, u32[]{:S(2)}, u32[]{:S(2)}) async-start(bf16[4,2,2,768,64]{3,4,2,1,0:T(8,128)(2,1)} %broadcast_in_dim.84), calls=%async_computation | async-start | bytes 3145728 | tf_op jit(solution)/shard_map/all_to_all | solution.py:153
  15.6 18.4 %collective-permute-start = (bf16[2,768,64]{1,2,0:T(8,128)(2,1)S(1)}, bf16[2,768,64]{1,2,0:T(8,128)(2,1)}, u32[]{:S(2)}, u32[]{:S(2)}) collective-permute-start(bf16[2,768,64]{1,2,0:T(8,128)(2,1)S(1)} %bitcast.78), channel_id=1, source_target_pairs={{0,16},{1,17},{2,18},{3,19},{4,20},{5,21},{6,22},{7,23},{8,24},{9,... | collective-permute-start | bytes 589832 | tf_op jit(solution)/shard_map/ppermute | solution.py:239
  31.2 1.2 copy-start.2
  38.9 57.9 %collective-permute-start.2 = (f32[2,768,64]{1,2,0:T(8,128)}, f32[2,768,64]{1,2,0:T(8,128)S(1)}, u32[]{:S(2)}, u32[]{:S(2)}) collective-permute-start(f32[2,768,64]{1,2,0:T(8,128)} %copy.186), channel_id=1, source_target_pairs={{16,0},{17,1},{18,2},{19,3},{20,4},{21,5},{22,6},{23,7},{24,8},{25... | collective-permute-start | bytes 1179656 | tf_op jit(solution)/shard_map/ppermute | solution.py:263
  43.0 53.7 %collective-permute-start.3 = (f32[2,768,1]{1,0,2:T(2,128)S(1)}, f32[2,768,1]{1,0,2:T(2,128)S(1)}, u32[]{:S(2)}, u32[]{:S(2)}) collective-permute-start(f32[2,768,1]{1,0,2:T(2,128)S(1)} %copy.188), channel_id=1, source_target_pairs={{16,0},{17,1},{18,2},{19,3},{20,4},{21,5},{22,6},{23,7},{24,8},{25... | collective-permute-start | bytes 18440 | tf_op jit(solution)/shard_map/ppermute | solution.py:263
  44.3 52.5 %collective-permute-start.1 = (f32[2,768,1]{1,0,2:T(2,128)S(1)}, f32[2,768,1]{1,0,2:T(2,128)S(1)}, u32[]{:S(2)}, u32[]{:S(2)}) collective-permute-start(f32[2,768,1]{1,0,2:T(2,128)S(1)} %copy.182), channel_id=1, source_target_pairs={{16,0},{17,1},{18,2},{19,3},{20,4},{21,5},{22,6},{23,7},{24,8},{25... | collective-permute-start | bytes 18440 | tf_op jit(solution)/shard_map/ppermute | solution.py:263
  90.1 2.9 %copy-start.6 = (f32[2,768,1]{2,1,0:T(8,128)S(1)}, f32[2,768,1]{2,1,0:T(8,128)}, u32[]{:S(2)}) copy-start(f32[2,768,1]{2,1,0:T(8,128)} %get-tuple-element.101) | copy-start | bytes 18436 | tf_op jit(solution)/shard_map/cond
  97.0 5.4 %copy-start.10 = (s32[64,8]{0,1:T(8,128)S(1)}, s32[64,8]{0,1:T(8,128)}, u32[]{:S(2)}) copy-start(s32[64,8]{0,1:T(8,128)} %param.27) | copy-start | bytes 6148
  97.0 5.5 %copy-start.9 = (f32[64,8]{0,1:T(8,128)S(1)}, f32[64,8]{0,1:T(8,128)}, u32[]{:S(2)}) copy-start(f32[64,8]{0,1:T(8,128)} %param.28) | copy-start | bytes 6148
  97.0 17.1 %copy-start.4 = (bf16[256,1536]{1,0:T(8,128)(2,1)S(1)}, bf16[256,1536]{1,0:T(8,128)(2,1)}, u32[]{:S(2)}) copy-start(bf16[256,1536]{1,0:T(8,128)(2,1)} %param.17) | copy-start | bytes 2359300
  98.5 15.7 %copy-start.11 = (f32[1536]{0:T(1024)S(1)}, f32[1536]{0:T(1024)}, u32[]{:S(2)}) copy-start(f32[1536]{0:T(1024)} %param.24) | copy-start | bytes 18436
  98.6 15.4 %all-to-all-start.1 = ((bf16[4,64,1536]{2,1,0:T(8,128)(2,1)}), bf16[4,64,1536]{2,1,0:T(8,128)(2,1)S(1)}, u32[]{:S(2)}, u32[]{:S(2)}) async-start(bf16[4,64,1536]{2,1,0:T(8,128)(2,1)} %bitcast.16), calls=%async_computation.1 | async-start | bytes 1572864 | tf_op jit(solution)/shard_map/all_to_all | solution.py:278
  115.9 16.9 %copy-start.7 = (bf16[256,2,2,64]{0,3,2,1:T(8,128)(2,1)S(1)}, bf16[256,2,2,64]{0,3,2,1:T(8,128)(2,1)}, u32[]{:S(2)}) copy-start(bf16[256,2,2,64]{0,3,2,1:T(8,128)(2,1)} %get-tuple-element.109) | copy-start | bytes 393220
  115.9 56.4 %all-to-all-start.2 = ((bf16[8,64,1664]{2,1,0:T(8,128)(2,1)}), bf16[8,64,1664]{2,1,0:T(8,128)(2,1)}, u32[]{:S(2)}, u32[]{:S(2)}) async-start(bf16[8,64,1664]{2,1,0:T(8,128)(2,1)} %broadcast_in_dim.91), calls=%async_computation.2 | async-start | bytes 3407872 | tf_op jit(solution)/shard_map/all_to_all | solution.py:153
  172.3 33.9 %all-to-all-start.4 = ((bf16[4,8,2048]{2,0,1:T(4,128)(2,1)}), bf16[4,8,2048]{2,0,1:T(4,128)(2,1)S(1)}, u32[]{:S(2)}, u32[]{:S(2)}) async-start(bf16[4,8,2048]{2,0,1:T(4,128)(2,1)} %copy.198), calls=%async_computation.4 | async-start | bytes 262144 | tf_op jit(solution)/shard_map/all_to_all | solution.py:211
  206.2 6.5 %copy-start.12 = (s32[256]{0:T(256)S(1)}, s32[256]{0:T(256)}, u32[]{:S(2)}) copy-start(s32[256]{0:T(256)} %param.29) | copy-start | bytes 3076
  206.2 42.8 %all-to-all-start.3 = ((bf16[8,64,1536]{2,1,0:T(8,128)(2,1)}), bf16[8,64,1536]{2,1,0:T(8,128)(2,1)S(1)}, u32[]{:S(2)}, u32[]{:S(2)}) async-start(bf16[8,64,1536]{2,1,0:T(8,128)(2,1)} %bitcast.81), calls=%async_computation.3 | async-start | bytes 3145728 | tf_op jit(solution)/shard_map/all_to_all | solution.py:343
  213.7 37.1 %copy-start.1 = (bf16[384,1536]{1,0:T(8,128)(2,1)S(1)}, bf16[384,1536]{1,0:T(8,128)(2,1)}, u32[]{:S(2)}) copy-start(bf16[384,1536]{1,0:T(8,128)(2,1)} %param.22) | copy-start | bytes 3538948

commit v8 on v7

--- a/solution.py
+++ b/solution.py
@@ -29,23 +29,15 @@
 
 
 def partial_kernel(
-    flags_ref, q_ref, k_ref, v_ref, acc_ref, m_ref, l_ref, m_sc, l_sc, acc_sc, *, mode, cache_per,
-    new_per, key_block, group_rows
+    flags_ref, q_ref, k_ref, v_ref, acc_ref, m_ref, l_ref, m_sc, l_sc, acc_sc, *, mode, cache_rows,
+    group_rows
 ):
     step = pl.program_id(1)
     last = pl.num_programs(1) - 1
     query_first = flags_ref[0]
-    stride = cache_per + new_per
-    if mode == "all":
-        within = step % stride
-        new_index = (step // stride) * new_per + within - cache_per
-    elif mode == "new":
-        within = cache_per
-        new_index = step
-    else:
-        within = 0
-        new_index = 0
-    new_first = new_index * key_block
+    chunk = k_ref.shape[1]
+    new_rows = chunk - cache_rows
+    new_first = step * new_rows
 
     @pl.when(step == 0)
     def _():
@@ -53,19 +45,23 @@
         l_sc[...] = jnp.zeros(l_sc.shape, jnp.float32)
         acc_sc[...] = jnp.zeros(acc_sc.shape, jnp.float32)
 
-    def update(visible):
+    def update(first, count, causal):
         q = q_ref[0]
-        k = k_ref[0, 0]
-        v = v_ref[0, 0]
+        k = k_ref[0, pl.ds(first, count), :]
+        v = v_ref[0, pl.ds(first, count), :]
         scores = lax.dot_general(
             q, k, (((1,), (1,)), ((), ())), preferred_element_type=jnp.float32
         ) * attention_scale
-        if visible is not None:
+        if causal:
+            rows = q.shape[0]
+            query_pos = query_first + lax.broadcasted_iota(jnp.int32, (rows, count), 0) % group_rows
+            column = lax.broadcasted_iota(jnp.int32, (rows, count), 1) + first
+            visible = (column < cache_rows) | (new_first + column - cache_rows <= query_pos)
             scores = jnp.where(visible, scores, masked_score)
         m_prev = m_sc[...]
         m_new = jnp.maximum(m_prev, jnp.max(scores, axis=1, keepdims=True))
         weights = jnp.exp(scores - m_new)
-        if visible is not None:
+        if causal:
             weights = jnp.where(visible, weights, 0.0)
         factor = jnp.exp(m_prev - m_new)
         l_sc[...] = l_sc[...] * factor + jnp.sum(weights, axis=1, keepdims=True)
@@ -74,22 +70,15 @@
         )
         m_sc[...] = m_new
 
-    if mode != "new":
-
-        @pl.when(within < cache_per)
+    if mode == "all":
+        update(0, chunk, True)
+    elif mode == "cache":
+        update(0, cache_rows, False)
+    else:
+
+        @pl.when(new_first <= query_first + group_rows - 1)
         def _():
-            update(None)
-
-    if mode != "cache":
-
-        @pl.when((within >= cache_per) & (new_first <= query_first + group_rows - 1))
-        def _():
-            rows = q_ref.shape[1]
-            query_pos = (
-                query_first + lax.broadcasted_iota(jnp.int32, (rows, key_block), 0) % group_rows
-            )
-            key_pos = new_first + lax.broadcasted_iota(jnp.int32, (rows, key_block), 1)
-            update(key_pos <= query_pos)
+            update(cache_rows, new_rows, True)
 
     @pl.when(step == last)
     def _():
@@ -98,28 +87,11 @@
         l_ref[0] = l_sc[...]
 
 
-def attend_partial(flags, q, kv_all, mode, cache_per, new_per, key_block, group_rows):
+def attend_partial(flags, q, kv_all, mode, cache_rows, group_rows):
     heads, rows, dim = q.shape
-    stride = cache_per + new_per
-    devices = kv_all.shape[2] // (key_block * stride)
-    if mode == "all":
-        steps = devices * stride
-        block_of = lambda s: s
-    elif mode == "new":
-        steps = devices * new_per
-        block_of = lambda s: (s // new_per) * stride + cache_per + s % new_per
-    else:
-        steps = devices * cache_per
-        block_of = lambda s: (s // cache_per) * stride + s % cache_per
-    kernel = functools.partial(
-        partial_kernel,
-        mode=mode,
-        cache_per=cache_per,
-        new_per=new_per,
-        key_block=key_block,
-        group_rows=group_rows,
-    )
-    kv_block = (1, 1, key_block, dim)
+    devices, _, _, chunk, _ = kv_all.shape
+    kernel = functools.partial(partial_kernel, mode=mode, cache_rows=cache_rows, group_rows=group_rows)
+    kv_block = (None, None, 1, chunk, dim)
     row_block = pl.BlockSpec((1, rows, 1), lambda h, s, f: (h, 0, 0))
     return pl.pallas_call(
         kernel,
@@ -130,11 +102,11 @@
         ),
         grid_spec=pltpu.PrefetchScalarGridSpec(
             num_scalar_prefetch=1,
-            grid=(heads, steps),
+            grid=(heads, devices),
             in_specs=[
                 pl.BlockSpec((1, rows, dim), lambda h, s, f: (h, 0, 0)),
-                pl.BlockSpec(kv_block, lambda h, s, f: (0, h, block_of(s), 0)),
-                pl.BlockSpec(kv_block, lambda h, s, f: (1, h, block_of(s), 0)),
+                pl.BlockSpec(kv_block, lambda h, s, f: (s, 0, h, 0, 0)),
+                pl.BlockSpec(kv_block, lambda h, s, f: (s, 1, h, 0, 0)),
             ],
             out_specs=[pl.BlockSpec((1, rows, dim), lambda h, s, f: (h, 0, 0)), row_block, row_block],
             scratch_shapes=[
@@ -145,16 +117,6 @@
         ),
         compiler_params=pltpu.CompilerParams(dimension_semantics=("arbitrary", "arbitrary")),
     )(flags, q, kv_all, kv_all)
-
-
-def gather_by_all_to_all(values, axis_name, axis):
-    count = lax.axis_size(axis_name)
-    spread = jnp.broadcast_to(values[None], (count,) + values.shape)
-    moved = lax.all_to_all(spread, axis_name, split_axis=0, concat_axis=0, tiled=True)
-    moved = jnp.moveaxis(moved, 0, axis)
-    shape = list(values.shape)
-    shape[axis] = shape[axis] * count
-    return moved.reshape(shape)
 
 
 def pl_cdiv(a, b):
@@ -230,15 +192,19 @@
     kv_own = split_new.transpose(2, 1, 0, 3)
     cache_rows = cache_kv.shape[0]
     cache_own = cache_kv.reshape(cache_rows, kv_local, 2, head_dim).transpose(2, 1, 0, 3)
-    kv_all = gather_by_all_to_all(jnp.concatenate([cache_own, kv_own], axis=2), "hseq", 2)
-    key_block = math.gcd(math.gcd(cache_rows, tokens_here), 256)
-    cache_per = cache_rows // key_block
-    new_per = tokens_here // key_block
+    kv_piece = jnp.concatenate([cache_own, kv_own], axis=2)
+    kv_all = lax.all_to_all(
+        jnp.broadcast_to(kv_piece[None], (half_size,) + kv_piece.shape),
+        "hseq",
+        split_axis=0,
+        concat_axis=0,
+        tiled=True,
+    )
     query_rows = queries.reshape(tokens_here, kv_local, group_size, head_dim)
     query_rows = query_rows.transpose(1, 2, 0, 3).reshape(kv_local, group_size * tokens_here, head_dim)
     partner_rows = lax.ppermute(query_rows, "half", perm=[(0, 1)])
     flags = jnp.reshape(half_pos * tokens_here, (1,)).astype(jnp.int32)
-    shapes = dict(cache_per=cache_per, new_per=new_per, key_block=key_block, group_rows=tokens_here)
+    shapes = dict(cache_rows=cache_rows, group_rows=tokens_here)
 
     def empty_partial(rows_in):
         heads, rows, _ = rows_in.shape
@@ -306,7 +272,9 @@
         ],
         axis=1,
     )
-    packed_all = gather_by_all_to_all(jnp.concatenate([moe_in, side], axis=1), SEQ_AXES, 0)
+    packed_all = lax.all_gather(
+        jnp.concatenate([moe_in, side], axis=1), SEQ_AXES, axis=0, tiled=True
+    )
     rows_all = packed_all[:, :model_width]
     total_rows = rows_all.shape[0]
     local_first = seq_index * experts_here

time: 252 us -> 241 us (0.956)
  Pallas kernels: 40.8 us -> 23.5 us
  between operations: 1.06 us -> 14.5 us
  starting transfers between devices: 44.7 us -> 37.5 us
  local copies, waits for them, and re-layouts: 28.8 us -> 25.4 us
  waiting for transfers between devices: 95.9 us -> 99.3 us
    all_to_all x2 -> x1, waiting for transfers between devices: 48.8 us -> 0.01 us  [body(): lax.all_to_all(jnp.broadcast_to(kv_piece[None], (half_size,) + kv_piece.s...]
    all_gather x0 -> x1, waiting for transfers between devices: none -> 38.5 us  [body(): lax.all_gather(jnp.concatenate([moe_in, side], axis=1), SEQ_AXES, axis=0,...]
    pallas_call x1, Pallas kernels: 40.8 us -> 23.5 us  [attend_partial(): pl.pallas_call(kernel, out_shape=(jax.ShapeDtypeStruct((heads, rows, dim)...]
    all_to_all x2 -> x1, starting transfers between devices: 21.9 us -> 5.22 us  [body(): lax.all_to_all(jnp.broadcast_to(kv_piece[None], (half_size,) + kv_piece.s...]
    ppermute x1, waiting for transfers between devices: 0.01 us -> 13.1 us  [body(): partner_rows = lax.ppermute(query_rows, 'half', perm=[(0, 1)])]
    all_to_all x1, starting transfers between devices: 3.64 us -> 16.4 us  [body(): lax.all_to_all(outgoing, SEQ_AXES, split_axis=1, concat_axis=1, tiled=True)]
  transfers between devices with their start and end apart: 9 -> 9, of which waited for: 6 -> 6; matrix products, arithmetic and copies ran while one was open for 20% -> 20% of each run, Pallas kernels for 16% -> 10%
where the time goes in v8:
time: 241 us; the launch traced here: 240 us
  waiting for transfers between devices  99.3 us (41%)
  starting transfers between devices  37.5 us (16%)
  matrix products  28.2 us (12%)
  local copies, waits for them, and re-layouts  25.4 us (11%)
  Pallas kernels  23.5 us (10%)
  between operations  14.5 us (6%)
  other arithmetic  11.4 us (5%)
    all_gather x1, waiting for transfers between devices, body(): lax.all_gather(jnp.concatenate([moe_in, side], axis=1), SEQ_AXES, axis=0,...  38.5 us
    all_to_all x1, waiting for transfers between devices, body(): lax.all_to_all(partial.astype(jnp.bfloat16).reshape(seq_count, moe_rows,...  32.8 us
    pallas_call x1, Pallas kernels, attend_partial(): pl.pallas_call(kernel, out_shape=(jax.ShapeDtypeStruct((heads, rows, dim)...  23.5 us
    all_to_all x1, starting transfers between devices, body(): lax.all_to_all(outgoing, SEQ_AXES, split_axis=1, concat_axis=1, tiled=True)  16.4 us
    ppermute x1, waiting for transfers between devices, body(): partner_rows = lax.ppermute(query_rows, 'half', perm=[(0, 1)])  13.1 us
    all_to_all x1, waiting for transfers between devices, body(): lax.all_to_all(projected.reshape(exp_count, -1, projected.shape[1]), 'exp...  11.1 us
    dot_general x1, matrix products, body(): jnp.einsum('ecd,edf->ecf', rows_in, expert_in, preferred_element_type=jnp...  10.2 us
    another operation x5, local copies, waits for them, and re-layouts  6.5 us
  transfers between devices with their start and end apart: 9, of which 6 were waited for; matrix products, arithmetic and copies ran while one was open for 20% of the time, Pallas kernels for 10%

profile of v8, /device:TPU:0, one launch (start us, length us, event | category | flops | bytes accessed | tf_op | source)
XLA Modules:
  0.0 239.9 jit_solution(18169587469003788127)
XLA Ops:
  7.2 1.5 fusion.7
  8.8 1.7 convolution_convert_fusion.5
  10.5 0.5 convolution_convert_fusion.4
  11.2 0.7 pad_maximum_fusion.1
  11.9 1.3 broadcast_in_dim.78
  13.2 5.2 %all-to-all-start = ((bf16[4,2,2,768,64]{3,4,2,1,0:T(8,128)(2,1)}), bf16[4,2,2,768,64]{3,4,2,1,0:T(8,128)(2,1)S(1)}, u32[]{:S(2)}, u32[]{:S(2)}) async-start(bf16[4,2,2,768,64]{3,4,2,1,0:T(8,128)(2,1)} %broadcast_in_dim.78), calls=%async_computation | async-start | bytes 3145728 | tf_op jit(solution)/shard_map/all_to_all | solution.py:196
  18.4 2.6 %convolution_convert_fusion.3 = bf16[256,384]{1,0:T(8,128)(2,1)} fusion(bf16[1536,384]{1,0:T(8,128)(2,1)} %param.19, bf16[256,1536]{1,0:T(8,128)(2,1)S(1)} %copy-done.2, f32[1536]{0:T(1024)S(1)} %copy-done.13, f32[256]{0:T(256)S(1)} %add_rsqrt_fusion), kind=kOutput, calls=%fused_computation.22 | convolution fusion | flops 303661056 | bytes 2169856 | tf_op jit(solution)/shard_map/dot_general | solution.py:158
  21.0 1.1 copy.197
  22.1 4.5 %collective-permute-start = (bf16[2,768,64]{1,2,0:T(8,128)(2,1)S(1)}, bf16[2,768,64]{1,2,0:T(8,128)(2,1)S(1)}, u32[]{:S(2)}, u32[]{:S(2)}) collective-permute-start(bf16[2,768,64]{1,2,0:T(8,128)(2,1)S(1)} %bitcast.70), channel_id=1, source_target_pairs={{0,16},{1,17},{2,18},{3,19},{4,20},{5,21},{6,22},{7,23},{8,24},{9,... | collective-permute-start | bytes 589832 | tf_op jit(solution)/shard_map/ppermute | solution.py:205
  26.6 13.1 %collective-permute-done = bf16[2,768,64]{1,2,0:T(8,128)(2,1)S(1)} collective-permute-done((bf16[2,768,64]{1,2,0:T(8,128)(2,1)S(1)}, bf16[2,768,64]{1,2,0:T(8,128)(2,1)S(1)}, u32[]{:S(2)}, u32[]{:S(2)}) %collective-permute-start) | collective-permute-done | bytes 196640 | tf_op jit(solution)/shard_map/ppermute | solution.py:205
  39.7 2.8 %conditional.3 = ((f32[2,768,64]{2,1,0:T(8,128)}, f32[2,768,1]{2,1,0:T(8,128)}, f32[2,768,1]{2,1,0:T(8,128)})) conditional(s32[]{:T(128)} %convert_element_type.76, (s32[1]{0:T(128)}, bf16[2,768,64]{1,2,0:T(8,128)(2,1)S(1)}, bf16[4,2,2,768,64]{3,4,2,1,0:T(8,128)(2,1)S(1)}) %tuple.22, () %tuple.23), branch_computations={%region_3.4_spmd, %region_4.5_spmd} | conditional | bytes 3538952 | solution.py:217
  39.7 1.0 broadcast.94
  40.7 1.0 broadcast.92
  41.6 0.9 broadcast.93
  42.6 2.1 copy.213
  44.7 1.3 collective-permute-start.2
  46.0 1.4 copy.209
  47.4 1.4 copy.215
  48.8 1.3 collective-permute-start.3
  50.1 1.3 collective-permute-start.1
  51.4 30.5 %conditional.2 = (f32[2,768,64]{1,2,0:T(8,128)S(1)}, f32[2,768,1]{1,0,2:T(2,128)S(1)}, f32[2,768,1]{1,0,2:T(2,128)S(1)}) conditional(s32[]{:T(128)} %convert_element_type.76, (s32[1]{0:T(128)}, bf16[2,768,64]{1,2,0:T(8,128)(2,1)S(1)}, bf16[4,2,2,768,64]{3,4,2,1,0:T(8,128)(2,1)S(1)}) %tuple.71, (s32[1]{0:T(128)}, bf16[2,768,64]{1,2,0:T(8,128)(2,1)S(1)}, ...), branch_computations={%region_1.2_spmd, %region_2.3_spmd} | conditional | bytes 4374580 | solution.py:223
  51.4 0.9 copy.205.q_ref
  52.3 2.7 %copy.206.k_ref.v_ref = bf16[4,2,2,768,64]{4,3,2,1,0:T(8,128)(2,1)} copy(bf16[4,2,2,768,64]{3,4,2,1,0:T(8,128)(2,1)S(1)} %get-tuple-element.103) | data formatting | bytes 3145728 | tf_op jit(solution)/shard_map
  55.1 23.5 %branch_1_fun.1 = (f32[2,768,64]{2,1,0:T(8,128)}, f32[2,768,1]{2,1,0:T(8,128)}, f32[2,768,1]{2,1,0:T(8,128)}) custom-call(s32[1]{0:T(128)} %get-tuple-element.21.flags_ref, bf16[2,768,64]{2,1,0:T(8,128)(2,1)} %copy.205.q_ref, bf16[4,2,2,768,64]{4,3,2,1,0:T(8,128)(2,1)} %copy.206.k_ref.v_ref, bf16[4,2,2,768,64]{4,3,2,1,0:T(8,128)(2,1)} %copy.206.k_ref.v_ref), custom_call_target="tpu_custom_call" | custom-call | tf_op jit(solution)/shard_map/cond/branch_1_fun/pallas_call | solution.py:96
  78.6 1.5 copy.232
  80.0 1.4 copy.234
  81.4 0.3 copy.236
  81.8 3.7 %collective-permute-done.3 = f32[2,768,1]{1,0,2:T(2,128)S(1)} collective-permute-done((f32[2,768,1]{1,0,2:T(2,128)S(1)}, f32[2,768,1]{1,0,2:T(2,128)S(1)}, u32[]{:S(2)}, u32[]{:S(2)}) %collective-permute-start.3) | collective-permute-done | bytes 6176 | tf_op jit(solution)/shard_map/ppermute | solution.py:229
  85.9 1.5 convolution_convert_fusion.2
  87.4 3.6 %all-to-all-start.1 = ((bf16[4,64,1536]{2,1,0:T(8,128)(2,1)}), bf16[4,64,1536]{2,1,0:T(8,128)(2,1)S(1)}, u32[]{:S(2)}, u32[]{:S(2)}) async-start(bf16[4,64,1536]{2,1,0:T(8,128)(2,1)} %bitcast.15), calls=%async_computation.1 | async-start | bytes 1572864 | tf_op jit(solution)/shard_map/all_to_all | solution.py:244
  91.6 11.1 %all-to-all-done.1 = bf16[4,64,1536]{2,1,0:T(8,128)(2,1)S(1)} async-done(((bf16[4,64,1536]{2,1,0:T(8,128)(2,1)}), bf16[4,64,1536]{2,1,0:T(8,128)(2,1)S(1)}, u32[]{:S(2)}, u32[]{:S(2)}) %all-to-all-start.1) | async-done | bytes 786464 | tf_op jit(solution)/shard_map/all_to_all | solution.py:244
  103.1 0.8 concatenate.7
  104.1 0.3 reshape_reshape.3
  104.4 0.8 copy.225
  105.2 16.4 %all-to-all-start.3 = ((bf16[4,8,2048]{2,0,1:T(4,128)(2,1)}), bf16[4,8,2048]{2,0,1:T(4,128)(2,1)S(1)}, u32[]{:S(2)}, u32[]{:S(2)}) async-start(bf16[4,8,2048]{2,0,1:T(4,128)(2,1)} %copy.225), calls=%async_computation.3 | async-start | bytes 262144 | tf_op jit(solution)/shard_map/all_to_all | solution.py:173
  121.7 38.5 %all-gather.2.cloned.1.call-done = bf16[512,1664]{1,0:T(8,128)(2,1)} async-done(((bf16[64,1664]{1,0:T(8,128)(2,1)}), bf16[512,1664]{1,0:T(8,128)(2,1)}) %all-gather.2.cloned.1.call-update) | async-done | bytes 1703952 | tf_op jit(solution)/shard_map/all_gather | solution.py:275
  160.2 0.9 slice.16
  161.9 6.3 %fusion.42 = s32[8,64,4]{2,0,1:T(8,128)S(1)} fusion(s32[8,64,4]{2,0,1:T(8,128)S(1)} %copy.221), kind=kOutput, calls=%fused_computation.79 | output fusion | flops 129024 | bytes 16384 | tf_op jit(solution)/shard_map/jit(cumsum)/reduce_window_sum | solution.py:288
  168.5 10.2 %fusion.43 = f32[4,256,1024]{2,1,0:T(8,128)} fusion(bf16[4,1536,1024]{2,1,0:T(8,128)(2,1)} %param.25, bf16[512,1664]{1,0:T(8,128)(2,1)} %all-gather.2.cloned.1.call-done, s32[512,4]{0,1:T(4,128)S(1)} %subtract_add_fusion, pred[512,4]{0,1:T(4,128)(4,1)S(1)} %get-tuple-element.119), kind=kOutput, calls=%fused_computation.80 | convolution fusion | flops 4834459648 | bytes 18360320 | tf_op jit(solution)/shard_map/ecd,edf->ecf/dot_general | solution.py:300
  178.7 5.9 %convolution_convert_fusion.1 = bf16[4,256,1536]{2,1,0:T(8,128)(2,1)S(1)} fusion(bf16[4,512,1536]{2,1,0:T(8,128)(2,1)} %param.26, f32[4,256,1024]{2,1,0:T(8,128)} %fusion.43), kind=kOutput, calls=%fused_computation.2 | convolution fusion | flops 1615331328 | bytes 13631488 | tf_op jit(solution)/shard_map/ecf,efd->ecd/dot_general | solution.py:303
  184.6 2.1 convolution_bitcast_fusion
  186.7 3.7 %fusion.1 = bf16[512,1536]{1,0:T(8,128)(2,1)} fusion(f32[512,1536]{1,0:T(8,128)S(1)} %convolution_bitcast_fusion, bf16[4,256,1536]{2,1,0:T(8,128)(2,1)S(1)} %convolution_convert_fusion.1, s32[512,4]{0,1:T(4,128)S(1)} %subtract_add_fusion, pred[512,4]{0,1:T(4,128)(4,1)S(1)} %get-tuple-element.119, bf16[512,4]{0,1:T(4,128)(2,1)S(1)} %copy.240), kind=kOutput, calls=%fused_computation.7 | convolution fusion | flops 1613758464 | bytes 7878656 | tf_op jit(solution)/shard_map/nec,ecd->nd/dot_general | solution.py:308
  190.4 3.8 %all-to-all-start.2 = ((bf16[8,64,1536]{2,1,0:T(8,128)(2,1)}), bf16[8,64,1536]{2,1,0:T(8,128)(2,1)S(1)}, u32[]{:S(2)}, u32[]{:S(2)}) async-start(bf16[8,64,1536]{2,1,0:T(8,128)(2,1)} %bitcast.73), calls=%async_computation.2 | async-start | bytes 3145728 | tf_op jit(solution)/shard_map/all_to_all | solution.py:311
  194.6 0.9 scatter_custom_fusion
  195.8 0.7 copy.230
  196.5 1.8 reshape.142
  198.3 32.8 %all-to-all-done.2 = bf16[8,64,1536]{2,1,0:T(8,128)(2,1)S(1)} async-done(((bf16[8,64,1536]{2,1,0:T(8,128)(2,1)}), bf16[8,64,1536]{2,1,0:T(8,128)(2,1)S(1)}, u32[]{:S(2)}, u32[]{:S(2)}) %all-to-all-start.2) | async-done | bytes 1572896 | tf_op jit(solution)/shard_map/all_to_all | solution.py:311
  231.3 1.7 add_convert_fusion
  (76 shorter events, 3.6 us)
Async XLA Ops:
  7.2 78.8 %copy-start = (bf16[384,1536]{1,0:T(8,128)(2,1)S(1)}, bf16[384,1536]{1,0:T(8,128)(2,1)}, u32[]{:S(2)}) copy-start(bf16[384,1536]{1,0:T(8,128)(2,1)} %param.22) | copy-start | bytes 3538948
  7.2 3.3 %copy-start.2 = (bf16[256,1536]{1,0:T(8,128)(2,1)S(1)}, bf16[256,1536]{1,0:T(8,128)(2,1)}, u32[]{:S(2)}) copy-start(bf16[256,1536]{1,0:T(8,128)(2,1)} %param.17) | copy-start | bytes 2359300
  7.2 3.3 %copy-start.13 = (f32[1536]{0:T(1024)S(1)}, f32[1536]{0:T(1024)}, u32[]{:S(2)}) copy-start(f32[1536]{0:T(1024)} %param.18) | copy-start | bytes 18436
  7.2 3.3 %copy-start.12 = (bf16[1536,128]{1,0:T(8,128)(2,1)S(1)}, bf16[1536,128]{1,0:T(8,128)(2,1)}, u32[]{:S(2)}) copy-start(bf16[1536,128]{1,0:T(8,128)(2,1)} %param.21) | copy-start | bytes 1179652
  7.2 3.8 %copy-start.7 = (bf16[512,256]{1,0:T(8,128)(2,1)S(1)}, bf16[512,256]{1,0:T(8,128)(2,1)}, u32[]{:S(2)}) copy-start(bf16[512,256]{1,0:T(8,128)(2,1)} %param.23) | copy-start | bytes 786436
  13.2 26.5 %all-to-all-start = ((bf16[4,2,2,768,64]{3,4,2,1,0:T(8,128)(2,1)}), bf16[4,2,2,768,64]{3,4,2,1,0:T(8,128)(2,1)S(1)}, u32[]{:S(2)}, u32[]{:S(2)}) async-start(bf16[4,2,2,768,64]{3,4,2,1,0:T(8,128)(2,1)} %broadcast_in_dim.78), calls=%async_computation | async-start | bytes 3145728 | tf_op jit(solution)/shard_map/all_to_all | solution.py:196
  22.1 17.6 %collective-permute-start = (bf16[2,768,64]{1,2,0:T(8,128)(2,1)S(1)}, bf16[2,768,64]{1,2,0:T(8,128)(2,1)S(1)}, u32[]{:S(2)}, u32[]{:S(2)}) collective-permute-start(bf16[2,768,64]{1,2,0:T(8,128)(2,1)S(1)} %bitcast.70), channel_id=1, source_target_pairs={{0,16},{1,17},{2,18},{3,19},{4,20},{5,21},{6,22},{7,23},{8,24},{9,... | collective-permute-start | bytes 589832 | tf_op jit(solution)/shard_map/ppermute | solution.py:205
  44.7 41.0 %collective-permute-start.2 = (f32[2,768,64]{1,2,0:T(8,128)}, f32[2,768,64]{1,2,0:T(8,128)S(1)}, u32[]{:S(2)}, u32[]{:S(2)}) collective-permute-start(f32[2,768,64]{1,2,0:T(8,128)} %copy.213), channel_id=1, source_target_pairs={{16,0},{17,1},{18,2},{19,3},{20,4},{21,5},{22,6},{23,7},{24,8},{25... | collective-permute-start | bytes 1179656 | tf_op jit(solution)/shard_map/ppermute | solution.py:229
  48.8 36.8 %collective-permute-start.3 = (f32[2,768,1]{1,0,2:T(2,128)S(1)}, f32[2,768,1]{1,0,2:T(2,128)S(1)}, u32[]{:S(2)}, u32[]{:S(2)}) collective-permute-start(f32[2,768,1]{1,0,2:T(2,128)S(1)} %copy.215), channel_id=1, source_target_pairs={{16,0},{17,1},{18,2},{19,3},{20,4},{21,5},{22,6},{23,7},{24,8},{25... | collective-permute-start | bytes 18440 | tf_op jit(solution)/shard_map/ppermute | solution.py:229
  50.1 35.6 %collective-permute-start.1 = (f32[2,768,1]{1,0,2:T(2,128)S(1)}, f32[2,768,1]{1,0,2:T(2,128)S(1)}, u32[]{:S(2)}, u32[]{:S(2)}) collective-permute-start(f32[2,768,1]{1,0,2:T(2,128)S(1)} %copy.209), channel_id=1, source_target_pairs={{16,0},{17,1},{18,2},{19,3},{20,4},{21,5},{22,6},{23,7},{24,8},{25... | collective-permute-start | bytes 18440 | tf_op jit(solution)/shard_map/ppermute | solution.py:229
  78.6 2.9 %copy-start.5 = (f32[2,768,1]{2,1,0:T(8,128)S(1)}, f32[2,768,1]{2,1,0:T(8,128)}, u32[]{:S(2)}) copy-start(f32[2,768,1]{2,1,0:T(8,128)} %get-tuple-element.114) | copy-start | bytes 18436 | tf_op jit(solution)/shard_map/cond
  85.9 5.3 %copy-start.9 = (s32[64,8]{0,1:T(8,128)S(1)}, s32[64,8]{0,1:T(8,128)}, u32[]{:S(2)}) copy-start(s32[64,8]{0,1:T(8,128)} %param.27) | copy-start | bytes 6148
  85.9 5.4 %copy-start.8 = (f32[64,8]{0,1:T(8,128)S(1)}, f32[64,8]{0,1:T(8,128)}, u32[]{:S(2)}) copy-start(f32[64,8]{0,1:T(8,128)} %param.28) | copy-start | bytes 6148
  85.9 16.9 %copy-start.3 = (bf16[256,1536]{1,0:T(8,128)(2,1)S(1)}, bf16[256,1536]{1,0:T(8,128)(2,1)}, u32[]{:S(2)}) copy-start(bf16[256,1536]{1,0:T(8,128)(2,1)} %param.17) | copy-start | bytes 2359300
  87.4 15.6 %copy-start.10 = (f32[1536]{0:T(1024)S(1)}, f32[1536]{0:T(1024)}, u32[]{:S(2)}) copy-start(f32[1536]{0:T(1024)} %param.24) | copy-start | bytes 18436
  87.4 15.3 %all-to-all-start.1 = ((bf16[4,64,1536]{2,1,0:T(8,128)(2,1)}), bf16[4,64,1536]{2,1,0:T(8,128)(2,1)S(1)}, u32[]{:S(2)}, u32[]{:S(2)}) async-start(bf16[4,64,1536]{2,1,0:T(8,128)(2,1)} %bitcast.15), calls=%async_computation.1 | async-start | bytes 1572864 | tf_op jit(solution)/shard_map/all_to_all | solution.py:244
  91.1 12.9 %copy-start.6 = (bf16[256,2,2,64]{0,3,2,1:T(8,128)(2,1)S(1)}, bf16[256,2,2,64]{0,3,2,1:T(8,128)(2,1)}, u32[]{:S(2)}) copy-start(bf16[256,2,2,64]{0,3,2,1:T(8,128)(2,1)} %get-tuple-element.122) | copy-start | bytes 393220
  91.1 69.1 %all-gather.2.cloned.1.call-start = ((), (), s32[]{:S(2)}) async-start(), calls=%async_computation.4 | async-start | bytes 1916928 | tf_op jit(solution)/shard_map/all_gather | solution.py:275
  105.2 85.2 %all-to-all-start.3 = ((bf16[4,8,2048]{2,0,1:T(4,128)(2,1)}), bf16[4,8,2048]{2,0,1:T(4,128)(2,1)S(1)}, u32[]{:S(2)}, u32[]{:S(2)}) async-start(bf16[4,8,2048]{2,0,1:T(4,128)(2,1)} %copy.225), calls=%async_computation.3 | async-start | bytes 262144 | tf_op jit(solution)/shard_map/all_to_all | solution.py:173
  190.4 4.0 %copy-start.11 = (s32[256]{0:T(256)S(1)}, s32[256]{0:T(256)}, u32[]{:S(2)}) copy-start(s32[256]{0:T(256)} %param.29) | copy-start | bytes 3076
  190.4 40.7 %all-to-all-start.2 = ((bf16[8,64,1536]{2,1,0:T(8,128)(2,1)}), bf16[8,64,1536]{2,1,0:T(8,128)(2,1)S(1)}, u32[]{:S(2)}, u32[]{:S(2)}) async-start(bf16[8,64,1536]{2,1,0:T(8,128)(2,1)} %bitcast.73), calls=%async_computation.2 | async-start | bytes 3145728 | tf_op jit(solution)/shard_map/all_to_all | solution.py:311
  195.5 37.5 %copy-start.1 = (bf16[384,1536]{1,0:T(8,128)(2,1)S(1)}, bf16[384,1536]{1,0:T(8,128)(2,1)}, u32[]{:S(2)}) copy-start(bf16[384,1536]{1,0:T(8,128)(2,1)} %param.22) | copy-start | bytes 3538948
Sparse Core Ops, SparseCore 0:
  104.1 56.0 all-gather.1

commit v9 on v8

--- a/solution.py
+++ b/solution.py
@@ -169,26 +169,8 @@
     pairs_new = split_new.reshape(tokens_here, pair_width)
     blocks_here = tokens_here // PAGE
     rounds = blocks_here // seq_count
-    outgoing = pairs_new.reshape(rounds, seq_count, PAGE * pair_width)
-    received = lax.all_to_all(outgoing, SEQ_AXES, split_axis=1, concat_axis=1, tiled=True)
-    block_ids = (
-        jnp.arange(seq_count, dtype=jnp.int32)[None, :] * blocks_here
-        + jnp.arange(rounds, dtype=jnp.int32)[:, None] * seq_count
-        + seq_index
-    ).reshape(-1)
-    table_ids = jnp.arange(page_slot.shape[0], dtype=jnp.int32)
-    page_slots = jnp.sum(
-        jnp.where(block_ids[:, None] == table_ids[None, :], page_slot[None, :], 0), axis=1
-    )
-    local_pages = (
-        jnp.zeros((blocks_here, PAGE * pair_width), jnp.bfloat16)
-        .at[page_slots]
-        .set(received.reshape(blocks_here, -1))
-    )
-    page_rows = local_pages.reshape(blocks_here, PAGE, kv_local, 2, head_dim).transpose(
-        0, 2, 3, 1, 4
-    )
-    page_rows = page_rows.reshape(blocks_here, kv_local, 2, PAGE * head_dim)
+    outgoing = pairs_new.reshape(rounds, seq_count, PAGE * pair_width).transpose(1, 0, 2)
+    outgoing = outgoing.reshape(seq_count, -1)
     kv_own = split_new.transpose(2, 1, 0, 3)
     cache_rows = cache_kv.shape[0]
     cache_own = cache_kv.reshape(cache_rows, kv_local, 2, head_dim).transpose(2, 1, 0, 3)
@@ -214,17 +196,18 @@
             jnp.zeros((heads, rows, 1), jnp.float32),
         )
 
+    own_part = lax.cond(
+        holds_first,
+        lambda rows_in: attend_partial(flags, rows_in, kv_all, "all", **shapes),
+        lambda rows_in: attend_partial(flags, rows_in, kv_all, "new", **shapes),
+        query_rows,
+    )
+    partner_rows, own_part = lax.optimization_barrier((partner_rows, own_part))
     far_part = lax.cond(
         holds_first,
         empty_partial,
         lambda rows_in: attend_partial(flags, rows_in, kv_all, "cache", **shapes),
         partner_rows,
-    )
-    own_part = lax.cond(
-        holds_first,
-        lambda rows_in: attend_partial(flags, rows_in, kv_all, "all", **shapes),
-        lambda rows_in: attend_partial(flags, rows_in, kv_all, "new", **shapes),
-        query_rows,
     )
     back_acc, back_best, back_total = lax.ppermute(far_part, "half", perm=[(1, 0)])
     back_best = jnp.where(holds_first, back_best, masked_score)
@@ -261,7 +244,7 @@
     full_hi = full_weight.astype(jnp.bfloat16)
     full_lo = (full_weight - full_hi.astype(jnp.float32)).astype(jnp.bfloat16)
     full_named = jnp.any(route_hits, axis=1).astype(jnp.bfloat16)
-    model_width = moe_in.shape[1]
+    moe_width = moe_in.shape[1]
     side_width = 128 * pl_cdiv(3 * EXPERTS, 128)
     side = jnp.concatenate(
         [
@@ -275,10 +258,10 @@
     packed_all = lax.all_gather(
         jnp.concatenate([moe_in, side], axis=1), SEQ_AXES, axis=0, tiled=True
     )
-    rows_all = packed_all[:, :model_width]
+    rows_all = packed_all[:, :moe_width]
     total_rows = rows_all.shape[0]
     local_first = seq_index * experts_here
-    side_all = packed_all[:, model_width:]
+    side_all = packed_all[:, moe_width:]
     named = (
         lax.dynamic_slice_in_dim(side_all, local_first, experts_here, 1) > 0
     )
@@ -308,14 +291,38 @@
     partial = jnp.einsum(
         "nec,ecd->nd", scaled_hi, produced, preferred_element_type=jnp.float32
     ) + jnp.einsum("nec,ecd->nd", scaled_lo, produced, preferred_element_type=jnp.float32)
-    returned = lax.all_to_all(
-        partial.astype(jnp.bfloat16).reshape(seq_count, moe_rows, -1),
-        SEQ_AXES,
-        split_axis=0,
-        concat_axis=0,
-        tiled=True,
-    )
-    moe = jnp.sum(returned.astype(jnp.float32), axis=0)
+    model_width = partial.shape[1]
+    page_lines = pl_cdiv(outgoing.shape[1], model_width)
+    page_part = jnp.pad(outgoing, ((0, 0), (0, page_lines * model_width - outgoing.shape[1])))
+    both = jnp.concatenate(
+        [
+            partial.astype(jnp.bfloat16).reshape(seq_count, moe_rows, model_width),
+            page_part.reshape(seq_count, page_lines, model_width),
+        ],
+        axis=1,
+    )
+    returned = lax.all_to_all(both, SEQ_AXES, split_axis=0, concat_axis=0, tiled=True)
+    moe = jnp.sum(returned[:, :moe_rows].astype(jnp.float32), axis=0)
+    received = returned[:, moe_rows:].reshape(seq_count, -1)[:, : outgoing.shape[1]]
+    received = received.reshape(seq_count, rounds, -1).transpose(1, 0, 2)
+    block_ids = (
+        jnp.arange(seq_count, dtype=jnp.int32)[None, :] * blocks_here
+        + jnp.arange(rounds, dtype=jnp.int32)[:, None] * seq_count
+        + seq_index
+    ).reshape(-1)
+    table_ids = jnp.arange(page_slot.shape[0], dtype=jnp.int32)
+    page_slots = jnp.sum(
+        jnp.where(block_ids[:, None] == table_ids[None, :], page_slot[None, :], 0), axis=1
+    )
+    local_pages = (
+        jnp.zeros((blocks_here, PAGE * pair_width), jnp.bfloat16)
+        .at[page_slots]
+        .set(received.reshape(blocks_here, -1))
+    )
+    page_rows = local_pages.reshape(blocks_here, PAGE, kv_local, 2, head_dim).transpose(
+        0, 2, 3, 1, 4
+    )
+    page_rows = page_rows.reshape(blocks_here, kv_local, 2, PAGE * head_dim)
     hidden_out = (residual + residual_scale * moe).astype(jnp.bfloat16)
     return (hidden_out, page_rows)
 

time: 241 us -> 251 us (1.041)
  waiting for transfers between devices: 99.3 us -> 127 us
  starting transfers between devices: 37.5 us -> 21.8 us
  local copies, waits for them, and re-layouts: 25.4 us -> 22.3 us
    ppermute x3, waiting for transfers between devices: 3.81 us -> 22.2 us  [body(): lax.ppermute(far_part, 'half', perm=[(1, 0)])]
    all_to_all x2 -> x1, starting transfers between devices: 20.2 us -> 3.72 us  [body(): lax.all_to_all(both, SEQ_AXES, split_axis=0, concat_axis=0, tiled=True)]
    ppermute x1, waiting for transfers between devices: 13.1 us -> 0.01 us  [body(): partner_rows = lax.ppermute(query_rows, 'half', perm=[(0, 1)])]
    all_to_all x1, waiting for transfers between devices: 0.01 us -> 8.15 us  [body(): lax.all_to_all(jnp.broadcast_to(kv_piece[None], (half_size,) + kv_piece.s...]
    all_to_all x2 -> x1, waiting for transfers between devices: 32.8 us -> 40.8 us  [body(): lax.all_to_all(both, SEQ_AXES, split_axis=0, concat_axis=0, tiled=True)]
    all_gather x1, waiting for transfers between devices: 38.5 us -> 44.6 us  [body(): lax.all_gather(jnp.concatenate([moe_in, side], axis=1), SEQ_AXES, axis=0,...]
    cond x5 -> x0, local copies, waits for them, and re-layouts: 3.11 us -> none  [the longest x3 3.11 us: body(): lax.cond(holds_first, lambda rows_in: attend_partial(flags, rows_in, kv_a...]
    optimization_barrier x0 -> x3, local copies, waits for them, and re-layouts: none -> 3.03 us  [body(): partner_rows, own_part = lax.optimization_barrier((partner_rows, own_part))]
  transfers between devices with their start and end apart: 9 -> 8, of which waited for: 6 -> 5; matrix products, arithmetic and copies ran while one was open for 20% -> 7% of each run, Pallas kernels for 10% -> 9%
where the time goes in v9:
time: 251 us; the launch traced here: 250 us
  waiting for transfers between devices  127 us (51%)
  matrix products  26.9 us (11%)
  Pallas kernels  23.5 us (9%)
  local copies, waits for them, and re-layouts  22.3 us (9%)
  starting transfers between devices  21.8 us (9%)
  between operations  14.5 us (6%)
  other arithmetic  13.9 us (6%)
    all_gather x1, waiting for transfers between devices, body(): lax.all_gather(jnp.concatenate([moe_in, side], axis=1), SEQ_AXES, axis=0,...  44.6 us
    all_to_all x1, waiting for transfers between devices, body(): lax.all_to_all(both, SEQ_AXES, split_axis=0, concat_axis=0, tiled=True)  40.8 us
    pallas_call x1, Pallas kernels, attend_partial(): pl.pallas_call(kernel, out_shape=(jax.ShapeDtypeStruct((heads, rows, dim)...  23.5 us
    ppermute x3, waiting for transfers between devices, body(): lax.ppermute(far_part, 'half', perm=[(1, 0)])  22.2 us
    all_to_all x1, waiting for transfers between devices, body(): lax.all_to_all(projected.reshape(exp_count, -1, projected.shape[1]), 'exp...  10.9 us
    dot_general x1, matrix products, body(): jnp.einsum('ecd,edf->ecf', rows_in, expert_in, preferred_element_type=jnp...  9.73 us
    all_to_all x1, waiting for transfers between devices, body(): lax.all_to_all(jnp.broadcast_to(kv_piece[None], (half_size,) + kv_piece.s...  8.15 us
    another operation x1, other arithmetic, body(): rank = jnp.cumsum(named_blocks, axis=1) - named_blocks  6.33 us
  transfers between devices with their start and end apart: 8, of which 5 were waited for; matrix products, arithmetic and copies ran while one was open for 7% of the time, Pallas kernels for 9%

profile of v9, /device:TPU:0, one launch (start us, length us, event | category | flops | bytes accessed | tf_op | source)
XLA Modules:
  0.0 249.7 jit_solution(6898687693518975194)
XLA Ops:
  7.2 1.5 fusion.7
  8.8 1.7 convolution_convert_fusion.5
  10.5 0.5 convolution_convert_fusion.4
  11.2 0.7 fusion.35
  11.9 1.3 broadcast_in_dim.78
  13.2 5.2 %all-to-all-start = ((bf16[4,2,2,768,64]{3,4,2,1,0:T(8,128)(2,1)}), bf16[4,2,2,768,64]{3,4,2,1,0:T(8,128)(2,1)S(1)}, u32[]{:S(2)}, u32[]{:S(2)}) async-start(bf16[4,2,2,768,64]{3,4,2,1,0:T(8,128)(2,1)} %broadcast_in_dim.78), calls=%async_computation | async-start | bytes 3145728 | tf_op jit(solution)/shard_map/all_to_all | solution.py:178
  18.4 2.6 %convolution_convert_fusion.3 = bf16[256,384]{1,0:T(8,128)(2,1)} fusion(bf16[1536,384]{1,0:T(8,128)(2,1)} %param.19, bf16[256,1536]{1,0:T(8,128)(2,1)S(1)} %copy-done.2, f32[1536]{0:T(1024)S(1)} %copy-done.12, f32[256]{0:T(256)S(1)} %add_rsqrt_fusion), kind=kOutput, calls=%fused_computation.23 | convolution fusion | flops 303661056 | bytes 2169856 | tf_op jit(solution)/shard_map/dot_general | solution.py:158
  21.0 1.7 copy.165
  22.8 1.6 copy.205
  24.4 5.2 %collective-permute-start = (bf16[2,768,64]{1,2,0:T(8,128)(2,1)}, bf16[2,768,64]{1,2,0:T(8,128)(2,1)}, u32[]{:S(2)}, u32[]{:S(2)}) collective-permute-start(bf16[2,768,64]{1,2,0:T(8,128)(2,1)} %bitcast.38), channel_id=1, source_target_pairs={{0,16},{1,17},{2,18},{3,19},{4,20},{5,21},{6,22},{7,23},{8,24},{9,... | collective-permute-start | bytes 589832 | tf_op jit(solution)/shard_map/ppermute | solution.py:187
  29.5 8.2 %all-to-all-done = bf16[4,2,2,768,64]{3,4,2,1,0:T(8,128)(2,1)S(1)} async-done(((bf16[4,2,2,768,64]{3,4,2,1,0:T(8,128)(2,1)}), bf16[4,2,2,768,64]{3,4,2,1,0:T(8,128)(2,1)S(1)}, u32[]{:S(2)}, u32[]{:S(2)}) %all-to-all-start) | async-done | bytes 1572896 | tf_op jit(solution)/shard_map/all_to_all | solution.py:178
  37.7 28.1 %conditional.2 = ((f32[2,768,64]{2,1,0:T(8,128)}, f32[2,768,1]{2,1,0:T(8,128)}, f32[2,768,1]{2,1,0:T(8,128)})) conditional(s32[]{:T(128)} %convert_element_type.81, (s32[1]{0:T(128)}, bf16[2,768,64]{1,2,0:T(8,128)(2,1)}, bf16[4,2,2,768,64]{3,4,2,1,0:T(8,128)(2,1)S(1)}) %tuple.22, (s32[1]{0:T(128)}, bf16[2,768,64]{1,2,0:T(8,128)(2,1)}, ...), branch_computations={%region_1.0_spmd, %region_2.0_spmd} | conditional | bytes 3538952 | solution.py:199
  37.7 1.9 copy.173.q_ref
  39.6 2.8 %copy.174.k_ref.v_ref = bf16[4,2,2,768,64]{4,3,2,1,0:T(8,128)(2,1)} copy(bf16[4,2,2,768,64]{3,4,2,1,0:T(8,128)(2,1)S(1)} %get-tuple-element.100) | data formatting | bytes 3145728 | tf_op jit(solution)/shard_map
  42.3 23.5 %branch_1_fun.1 = (f32[2,768,64]{2,1,0:T(8,128)}, f32[2,768,1]{2,1,0:T(8,128)}, f32[2,768,1]{2,1,0:T(8,128)}) custom-call(s32[1]{0:T(128)} %get-tuple-element.21.flags_ref, bf16[2,768,64]{2,1,0:T(8,128)(2,1)} %copy.173.q_ref, bf16[4,2,2,768,64]{4,3,2,1,0:T(8,128)(2,1)} %copy.174.k_ref.v_ref, bf16[4,2,2,768,64]{4,3,2,1,0:T(8,128)(2,1)} %copy.174.k_ref.v_ref), custom_call_target="tpu_custom_call" | custom-call | tf_op jit(solution)/shard_map/cond/branch_1_fun/pallas_call | solution.py:96
  65.8 1.1 conditional.3
  65.8 0.9 broadcast.94
  66.9 1.0 copy.181
  67.9 1.3 collective-permute-start.2
  69.2 0.3 copy.177
  69.4 1.5 copy.183
  70.9 1.3 collective-permute-start.3
  72.2 1.3 collective-permute-start.1
  73.5 1.4 copy.180
  74.9 0.3 copy.179
  75.1 1.4 copy.182
  76.5 22.1 %collective-permute-done.3 = f32[2,768,1]{1,0,2:T(2,128)S(1)} collective-permute-done((f32[2,768,1]{1,0,2:T(2,128)S(1)}, f32[2,768,1]{1,0,2:T(2,128)S(1)}, u32[]{:S(2)}, u32[]{:S(2)}) %collective-permute-start.3) | collective-permute-done | bytes 6176 | tf_op jit(solution)/shard_map/ppermute | solution.py:212
  98.8 1.1 divide_convert_fusion
  100.0 1.5 convolution_convert_fusion.2
  101.5 3.6 %all-to-all-start.1 = ((bf16[4,64,1536]{2,1,0:T(8,128)(2,1)}), bf16[4,64,1536]{2,1,0:T(8,128)(2,1)S(1)}, u32[]{:S(2)}, u32[]{:S(2)}) async-start(bf16[4,64,1536]{2,1,0:T(8,128)(2,1)} %bitcast.15), calls=%async_computation.1 | async-start | bytes 1572864 | tf_op jit(solution)/shard_map/all_to_all | solution.py:227
  105.1 0.2 all-gather.2.cloned.1.call-start
  105.8 10.9 %all-to-all-done.1 = bf16[4,64,1536]{2,1,0:T(8,128)(2,1)S(1)} async-done(((bf16[4,64,1536]{2,1,0:T(8,128)(2,1)}), bf16[4,64,1536]{2,1,0:T(8,128)(2,1)S(1)}, u32[]{:S(2)}, u32[]{:S(2)}) %all-to-all-start.1) | async-done | bytes 786464 | tf_op jit(solution)/shard_map/all_to_all | solution.py:227
  117.2 0.8 concatenate.10
  118.3 0.3 reshape_reshape.3
  118.7 44.6 %all-gather.2.cloned.1.call-done = bf16[512,1664]{1,0:T(8,128)(2,1)} async-done(((bf16[64,1664]{1,0:T(8,128)(2,1)}), bf16[512,1664]{1,0:T(8,128)(2,1)}) %all-gather.2.cloned.1.call-update) | async-done | bytes 1703952 | tf_op jit(solution)/shard_map/all_gather | solution.py:258
  163.3 1.0 slice.28
  165.2 6.3 %fusion.40 = s32[8,64,4]{2,0,1:T(8,128)S(1)} fusion(s32[8,64,4]{2,0,1:T(8,128)S(1)} %copy.189), kind=kOutput, calls=%fused_computation.78 | output fusion | flops 129024 | bytes 16384 | tf_op jit(solution)/shard_map/jit(cumsum)/reduce_window_sum | solution.py:271
  171.8 9.7 %fusion.41 = f32[4,256,1024]{2,1,0:T(8,128)} fusion(bf16[4,1536,1024]{2,1,0:T(8,128)(2,1)} %param.25, bf16[512,1664]{1,0:T(8,128)(2,1)S(1)} %copy-done.8, s32[512,4]{0,1:T(4,128)S(1)} %subtract_add_fusion, pred[512,4]{0,1:T(4,128)(4,1)S(1)} %get-tuple-element.107), kind=kOutput, calls=%fused_computation.79 | convolution fusion | flops 4834459648 | bytes 18360320 | tf_op jit(solution)/shard_map/ecd,edf->ecf/dot_general | solution.py:283
  181.5 5.9 %convolution_convert_fusion.1 = bf16[4,256,1536]{2,1,0:T(8,128)(2,1)S(1)} fusion(bf16[4,512,1536]{2,1,0:T(8,128)(2,1)} %param.26, f32[4,256,1024]{2,1,0:T(8,128)} %fusion.41), kind=kOutput, calls=%fused_computation.2 | convolution fusion | flops 1615331328 | bytes 13631488 | tf_op jit(solution)/shard_map/ecf,efd->ecd/dot_general | solution.py:286
  187.4 2.1 convolution_bitcast_fusion
  189.5 2.9 %fusion.1 = bf16[512,1536]{1,0:T(8,128)(2,1)S(1)} fusion(f32[512,1536]{1,0:T(8,128)S(1)} %convolution_bitcast_fusion, bf16[4,256,1536]{2,1,0:T(8,128)(2,1)S(1)} %convolution_convert_fusion.1, s32[512,4]{0,1:T(4,128)S(1)} %subtract_add_fusion, pred[512,4]{0,1:T(4,128)(4,1)S(1)} %get-tuple-element.107, bf16[512,4]{0,1:T(4,128)(2,1)S(1)} %copy.202), kind=kOutput, calls=%fused_computation.7 | convolution fusion | flops 1613758464 | bytes 7878656 | tf_op jit(solution)/shard_map/nec,ecd->nd/dot_general | solution.py:291
  192.5 1.4 pad_maximum_fusion
  193.9 3.7 %all-to-all-start.2 = ((bf16[8,70,1536]{2,1,0:T(8,128)(2,1)}), bf16[8,70,1536]{2,1,0:T(8,128)(2,1)S(1)}, u32[]{:S(2)}, u32[]{:S(2)}) async-start(bf16[8,70,1536]{2,1,0:T(8,128)(2,1)} %pad_maximum_fusion), calls=%async_computation.2 | async-start | bytes 3538944 | tf_op jit(solution)/shard_map/all_to_all | solution.py:304
  197.9 40.8 %all-to-all-done.2 = bf16[8,70,1536]{2,1,0:T(8,128)(2,1)S(1)} async-done(((bf16[8,70,1536]{2,1,0:T(8,128)(2,1)}), bf16[8,70,1536]{2,1,0:T(8,128)(2,1)S(1)}, u32[]{:S(2)}, u32[]{:S(2)}) %all-to-all-start.2) | async-done | bytes 1720352 | tf_op jit(solution)/shard_map/all_to_all | solution.py:304
  239.0 1.8 add_convert_fusion
  240.9 0.8 scatter_custom_fusion
  241.7 0.2 reshape.144
  242.0 0.8 reshape.158
  (79 shorter events, 3.4 us)
Async XLA Ops:
  7.2 92.8 %copy-start = (bf16[384,1536]{1,0:T(8,128)(2,1)S(1)}, bf16[384,1536]{1,0:T(8,128)(2,1)}, u32[]{:S(2)}) copy-start(bf16[384,1536]{1,0:T(8,128)(2,1)} %param.22) | copy-start | bytes 3538948
  7.2 3.3 %copy-start.2 = (bf16[256,1536]{1,0:T(8,128)(2,1)S(1)}, bf16[256,1536]{1,0:T(8,128)(2,1)}, u32[]{:S(2)}) copy-start(bf16[256,1536]{1,0:T(8,128)(2,1)} %param.17) | copy-start | bytes 2359300
  7.2 3.3 %copy-start.12 = (f32[1536]{0:T(1024)S(1)}, f32[1536]{0:T(1024)}, u32[]{:S(2)}) copy-start(f32[1536]{0:T(1024)} %param.18) | copy-start | bytes 18436
  7.2 3.3 %copy-start.11 = (bf16[1536,128]{1,0:T(8,128)(2,1)S(1)}, bf16[1536,128]{1,0:T(8,128)(2,1)}, u32[]{:S(2)}) copy-start(bf16[1536,128]{1,0:T(8,128)(2,1)} %param.21) | copy-start | bytes 1179652
  7.2 3.8 %copy-start.5 = (bf16[512,256]{1,0:T(8,128)(2,1)S(1)}, bf16[512,256]{1,0:T(8,128)(2,1)}, u32[]{:S(2)}) copy-start(bf16[512,256]{1,0:T(8,128)(2,1)} %param.23) | copy-start | bytes 786436
  13.2 24.5 %all-to-all-start = ((bf16[4,2,2,768,64]{3,4,2,1,0:T(8,128)(2,1)}), bf16[4,2,2,768,64]{3,4,2,1,0:T(8,128)(2,1)S(1)}, u32[]{:S(2)}, u32[]{:S(2)}) async-start(bf16[4,2,2,768,64]{3,4,2,1,0:T(8,128)(2,1)} %broadcast_in_dim.78), calls=%async_computation | async-start | bytes 3145728 | tf_op jit(solution)/shard_map/all_to_all | solution.py:178
  24.4 41.4 %collective-permute-start = (bf16[2,768,64]{1,2,0:T(8,128)(2,1)}, bf16[2,768,64]{1,2,0:T(8,128)(2,1)}, u32[]{:S(2)}, u32[]{:S(2)}) collective-permute-start(bf16[2,768,64]{1,2,0:T(8,128)(2,1)} %bitcast.38), channel_id=1, source_target_pairs={{0,16},{1,17},{2,18},{3,19},{4,20},{5,21},{6,22},{7,23},{8,24},{9,... | collective-permute-start | bytes 589832 | tf_op jit(solution)/shard_map/ppermute | solution.py:187
  67.9 30.9 %collective-permute-start.2 = (f32[2,768,64]{1,2,0:T(8,128)}, f32[2,768,64]{1,2,0:T(8,128)}, u32[]{:S(2)}, u32[]{:S(2)}) collective-permute-start(f32[2,768,64]{1,2,0:T(8,128)} %copy.181), channel_id=1, source_target_pairs={{16,0},{17,1},{18,2},{19,3},{20,4},{21,5},{22,6},{23,7},{24,8},{25... | collective-permute-start | bytes 1179656 | tf_op jit(solution)/shard_map/ppermute | solution.py:212
  69.4 5.5 %copy-start.3 = (f32[2,768,1]{2,1,0:T(8,128)S(1)}, f32[2,768,1]{2,1,0:T(8,128)}, u32[]{:S(2)}) copy-start(f32[2,768,1]{2,1,0:T(8,128)} %get-tuple-element.43) | copy-start | bytes 18436
  70.9 27.8 %collective-permute-start.3 = (f32[2,768,1]{1,0,2:T(2,128)S(1)}, f32[2,768,1]{1,0,2:T(2,128)S(1)}, u32[]{:S(2)}, u32[]{:S(2)}) collective-permute-start(f32[2,768,1]{1,0,2:T(2,128)S(1)} %copy.183), channel_id=1, source_target_pairs={{16,0},{17,1},{18,2},{19,3},{20,4},{21,5},{22,6},{23,7},{24,8},{25... | collective-permute-start | bytes 18440 | tf_op jit(solution)/shard_map/ppermute | solution.py:212
  72.2 26.5 %collective-permute-start.1 = (f32[2,768,1]{1,0,2:T(2,128)S(1)}, f32[2,768,1]{1,0,2:T(2,128)S(1)}, u32[]{:S(2)}, u32[]{:S(2)}) collective-permute-start(f32[2,768,1]{1,0,2:T(2,128)S(1)} %copy.177), channel_id=1, source_target_pairs={{16,0},{17,1},{18,2},{19,3},{20,4},{21,5},{22,6},{23,7},{24,8},{25... | collective-permute-start | bytes 18440 | tf_op jit(solution)/shard_map/ppermute | solution.py:212
  99.9 5.4 %copy-start.7 = (s32[64,8]{0,1:T(8,128)S(1)}, s32[64,8]{0,1:T(8,128)}, u32[]{:S(2)}) copy-start(s32[64,8]{0,1:T(8,128)} %param.27) | copy-start | bytes 6148
  99.9 5.6 %copy-start.6 = (f32[64,8]{0,1:T(8,128)S(1)}, f32[64,8]{0,1:T(8,128)}, u32[]{:S(2)}) copy-start(f32[64,8]{0,1:T(8,128)} %param.28) | copy-start | bytes 6148
  101.5 15.6 %copy-start.9 = (f32[1536]{0:T(1024)S(1)}, f32[1536]{0:T(1024)}, u32[]{:S(2)}) copy-start(f32[1536]{0:T(1024)} %param.24) | copy-start | bytes 18436
  101.5 15.3 %all-to-all-start.1 = ((bf16[4,64,1536]{2,1,0:T(8,128)(2,1)}), bf16[4,64,1536]{2,1,0:T(8,128)(2,1)S(1)}, u32[]{:S(2)}, u32[]{:S(2)}) async-start(bf16[4,64,1536]{2,1,0:T(8,128)(2,1)} %bitcast.15), calls=%async_computation.1 | async-start | bytes 1572864 | tf_op jit(solution)/shard_map/all_to_all | solution.py:227
  105.1 13.0 %copy-start.4 = (bf16[256,2,2,64]{0,3,2,1:T(8,128)(2,1)S(1)}, bf16[256,2,2,64]{0,3,2,1:T(8,128)(2,1)}, u32[]{:S(2)}) copy-start(bf16[256,2,2,64]{0,3,2,1:T(8,128)(2,1)} %get-tuple-element.114) | copy-start | bytes 393220
  105.1 58.2 %all-gather.2.cloned.1.call-start = ((), (), s32[]{:S(2)}) async-start(), calls=%async_computation.3 | async-start | bytes 1916928 | tf_op jit(solution)/shard_map/all_gather | solution.py:258
  163.3 8.4 %copy-start.8 = (bf16[512,1664]{1,0:T(8,128)(2,1)S(1)}, bf16[512,1664]{1,0:T(8,128)(2,1)}, u32[]{:S(2)}) copy-start(bf16[512,1664]{1,0:T(8,128)(2,1)} %all-gather.2.cloned.1.call-done) | copy-start | bytes 5111812
  193.9 3.9 %copy-start.10 = (s32[256]{0:T(256)S(1)}, s32[256]{0:T(256)}, u32[]{:S(2)}) copy-start(s32[256]{0:T(256)} %param.29) | copy-start | bytes 3076
  193.9 44.9 %all-to-all-start.2 = ((bf16[8,70,1536]{2,1,0:T(8,128)(2,1)}), bf16[8,70,1536]{2,1,0:T(8,128)(2,1)S(1)}, u32[]{:S(2)}, u32[]{:S(2)}) async-start(bf16[8,70,1536]{2,1,0:T(8,128)(2,1)} %pad_maximum_fusion), calls=%async_computation.2 | async-start | bytes 3538944 | tf_op jit(solution)/shard_map/all_to_all | solution.py:304
  238.8 4.1 %copy-start.1 = (bf16[384,1536]{1,0:T(8,128)(2,1)S(1)}, bf16[384,1536]{1,0:T(8,128)(2,1)}, u32[]{:S(2)}) copy-start(bf16[384,1536]{1,0:T(8,128)(2,1)} %param.22) | copy-start | bytes 3538948
Sparse Core Ops, SparseCore 0:
  118.1 45.1 all-gather.1

commit v10 on v9

--- a/solution.py
+++ b/solution.py
@@ -196,18 +196,17 @@
             jnp.zeros((heads, rows, 1), jnp.float32),
         )
 
+    far_part = lax.cond(
+        holds_first,
+        empty_partial,
+        lambda rows_in: attend_partial(flags, rows_in, kv_all, "cache", **shapes),
+        partner_rows,
+    )
     own_part = lax.cond(
         holds_first,
         lambda rows_in: attend_partial(flags, rows_in, kv_all, "all", **shapes),
         lambda rows_in: attend_partial(flags, rows_in, kv_all, "new", **shapes),
         query_rows,
-    )
-    partner_rows, own_part = lax.optimization_barrier((partner_rows, own_part))
-    far_part = lax.cond(
-        holds_first,
-        empty_partial,
-        lambda rows_in: attend_partial(flags, rows_in, kv_all, "cache", **shapes),
-        partner_rows,
     )
     back_acc, back_best, back_total = lax.ppermute(far_part, "half", perm=[(1, 0)])
     back_best = jnp.where(holds_first, back_best, masked_score)

time: 251 us -> 253 us (level)
  local copies, waits for them, and re-layouts: 22.3 us -> 27.6 us
  waiting for transfers between devices: 127 us -> 123 us
    ppermute x3, waiting for transfers between devices: 22.2 us -> 2.73 us  [body(): lax.ppermute(far_part, 'half', perm=[(1, 0)])]
    all_gather x1, waiting for transfers between devices: 44.6 us -> 57.7 us  [body(): lax.all_gather(jnp.concatenate([moe_in, side], axis=1), SEQ_AXES, axis=0,...]
    ppermute x1, waiting for transfers between devices: 0.01 us -> 10.3 us  [body(): partner_rows = lax.ppermute(query_rows, 'half', perm=[(0, 1)])]
    all_to_all x1, waiting for transfers between devices: 8.15 us -> 0.01 us  [body(): lax.all_to_all(jnp.broadcast_to(kv_piece[None], (half_size,) + kv_piece.s...]
    cond x3, local copies, waits for them, and re-layouts: 2.72 us -> 6.11 us  [body(): lax.cond(holds_first, empty_partial, lambda rows_in: attend_partial(flags...]
    cond x0 -> x5, local copies, waits for them, and re-layouts: none -> 3.11 us  [the longest x3 3.11 us: body(): lax.cond(holds_first, lambda rows_in: attend_partial(flags, rows_in, kv_a...]
    optimization_barrier x3 -> x0, local copies, waits for them, and re-layouts: 3.03 us -> none  [body(): partner_rows, own_part = lax.optimization_barrier((partner_rows, own_part))]
  transfers between devices with their start and end apart: 8 -> 8, of which waited for: 5 -> 6; matrix products, arithmetic and copies ran while one was open for 7% -> 8% of each run, Pallas kernels for 9% -> 9%
where the time goes in v10:
time: 253 us; the launch traced here: 252 us
  waiting for transfers between devices  123 us (49%)
  local copies, waits for them, and re-layouts  27.6 us (11%)
  matrix products  26.9 us (11%)
  Pallas kernels  23.5 us (9%)
  starting transfers between devices  21.7 us (9%)
  other arithmetic  14.6 us (6%)
  between operations  14.5 us (6%)
    all_gather x1, waiting for transfers between devices, body(): lax.all_gather(jnp.concatenate([moe_in, side], axis=1), SEQ_AXES, axis=0,...  57.7 us
    all_to_all x1, waiting for transfers between devices, body(): lax.all_to_all(both, SEQ_AXES, split_axis=0, concat_axis=0, tiled=True)  40.8 us
    pallas_call x1, Pallas kernels, attend_partial(): pl.pallas_call(kernel, out_shape=(jax.ShapeDtypeStruct((heads, rows, dim)...  23.5 us
    all_to_all x1, waiting for transfers between devices, body(): lax.all_to_all(projected.reshape(exp_count, -1, projected.shape[1]), 'exp...  11.1 us
    ppermute x1, waiting for transfers between devices, body(): partner_rows = lax.ppermute(query_rows, 'half', perm=[(0, 1)])  10.3 us
    dot_general x1, matrix products, body(): jnp.einsum('ecd,edf->ecf', rows_in, expert_in, preferred_element_type=jnp...  9.75 us
    another operation x5, local copies, waits for them, and re-layouts  7.51 us
    another operation x1, other arithmetic, body(): rank = jnp.cumsum(named_blocks, axis=1) - named_blocks  6.33 us
  transfers between devices with their start and end apart: 8, of which 6 were waited for; matrix products, arithmetic and copies ran while one was open for 8% of the time, Pallas kernels for 9%

profile of v10, /device:TPU:0, one launch (start us, length us, event | category | flops | bytes accessed | tf_op | source)
XLA Modules:
  0.0 251.7 jit_solution(12499194634165577197)
XLA Ops:
  7.2 1.5 fusion.7
  8.8 1.7 convolution_convert_fusion.5
  10.5 0.5 convolution_convert_fusion.4
  11.2 0.7 fusion.35
  11.9 1.3 broadcast_in_dim.78
  13.2 5.2 %all-to-all-start = ((bf16[4,2,2,768,64]{3,4,2,1,0:T(8,128)(2,1)}), bf16[4,2,2,768,64]{3,4,2,1,0:T(8,128)(2,1)S(1)}, u32[]{:S(2)}, u32[]{:S(2)}) async-start(bf16[4,2,2,768,64]{3,4,2,1,0:T(8,128)(2,1)} %broadcast_in_dim.78), calls=%async_computation | async-start | bytes 3145728 | tf_op jit(solution)/shard_map/all_to_all | solution.py:178
  18.4 2.6 %convolution_convert_fusion.3 = bf16[256,384]{1,0:T(8,128)(2,1)} fusion(bf16[1536,384]{1,0:T(8,128)(2,1)} %param.19, bf16[256,1536]{1,0:T(8,128)(2,1)S(1)} %copy-done.2, f32[1536]{0:T(1024)S(1)} %copy-done.13, f32[256]{0:T(256)S(1)} %add_rsqrt_fusion), kind=kOutput, calls=%fused_computation.23 | convolution fusion | flops 303661056 | bytes 2169856 | tf_op jit(solution)/shard_map/dot_general | solution.py:158
  21.0 1.7 copy.165
  22.7 1.6 copy.211
  24.3 5.2 %collective-permute-start = (bf16[2,768,64]{1,2,0:T(8,128)(2,1)}, bf16[2,768,64]{1,2,0:T(8,128)(2,1)}, u32[]{:S(2)}, u32[]{:S(2)}) collective-permute-start(bf16[2,768,64]{1,2,0:T(8,128)(2,1)} %bitcast.38), channel_id=1, source_target_pairs={{0,16},{1,17},{2,18},{3,19},{4,20},{5,21},{6,22},{7,23},{8,24},{9,... | collective-permute-start | bytes 589832 | tf_op jit(solution)/shard_map/ppermute | solution.py:187
  29.5 10.3 %collective-permute-done = bf16[2,768,64]{1,2,0:T(8,128)(2,1)} collective-permute-done((bf16[2,768,64]{1,2,0:T(8,128)(2,1)}, bf16[2,768,64]{1,2,0:T(8,128)(2,1)}, u32[]{:S(2)}, u32[]{:S(2)}) %collective-permute-start) | collective-permute-done | bytes 196640 | tf_op jit(solution)/shard_map/ppermute | solution.py:187
  39.8 2.8 %conditional.3 = ((f32[2,768,64]{2,1,0:T(8,128)}, f32[2,768,1]{2,1,0:T(8,128)}, f32[2,768,1]{2,1,0:T(8,128)})) conditional(s32[]{:T(128)} %convert_element_type.78, (s32[1]{0:T(128)}, bf16[2,768,64]{1,2,0:T(8,128)(2,1)}, bf16[4,2,2,768,64]{3,4,2,1,0:T(8,128)(2,1)S(1)}) %tuple.22, () %tuple.23), branch_computations={%region_3.0_spmd, %region_4.0_spmd} | conditional | bytes 3538952 | solution.py:199
  39.8 1.0 broadcast.94
  40.8 0.9 broadcast.92
  41.7 0.9 broadcast.93
  42.7 2.1 copy.181
  44.8 1.3 collective-permute-start.2
  46.1 2.0 copy.177
  48.1 2.0 copy.183
  50.1 1.3 collective-permute-start.3
  51.3 1.3 collective-permute-start.1
  52.6 31.5 %conditional.2 = (f32[2,768,64]{1,2,0:T(8,128)S(1)}, f32[2,768,1]{1,0,2:T(2,128)S(1)}, f32[2,768,1]{1,0,2:T(2,128)S(1)}) conditional(s32[]{:T(128)} %convert_element_type.78, (s32[1]{0:T(128)}, bf16[2,768,64]{1,2,0:T(8,128)(2,1)}, bf16[4,2,2,768,64]{3,4,2,1,0:T(8,128)(2,1)S(1)}) %tuple.21, (s32[1]{0:T(128)}, bf16[2,768,64]{1,2,0:T(8,128)(2,1)}, ...), branch_computations={%region_1.0_spmd, %region_2.0_spmd} | conditional | bytes 4374580 | solution.py:205
  52.7 1.9 copy.173.q_ref
  54.5 2.8 %copy.174.k_ref.v_ref = bf16[4,2,2,768,64]{4,3,2,1,0:T(8,128)(2,1)} copy(bf16[4,2,2,768,64]{3,4,2,1,0:T(8,128)(2,1)S(1)} %get-tuple-element.92) | data formatting | bytes 3145728 | tf_op jit(solution)/shard_map
  57.3 23.5 %branch_1_fun.1 = (f32[2,768,64]{2,1,0:T(8,128)}, f32[2,768,1]{2,1,0:T(8,128)}, f32[2,768,1]{2,1,0:T(8,128)}) custom-call(s32[1]{0:T(128)} %get-tuple-element.21.flags_ref, bf16[2,768,64]{2,1,0:T(8,128)(2,1)} %copy.173.q_ref, bf16[4,2,2,768,64]{4,3,2,1,0:T(8,128)(2,1)} %copy.174.k_ref.v_ref, bf16[4,2,2,768,64]{4,3,2,1,0:T(8,128)(2,1)} %copy.174.k_ref.v_ref), custom_call_target="tpu_custom_call" | custom-call | tf_op jit(solution)/shard_map/cond/branch_1_fun/pallas_call | solution.py:96
  80.9 1.5 copy.200
  82.3 1.4 copy.202
  84.1 2.7 %collective-permute-done.3 = f32[2,768,1]{1,0,2:T(2,128)} collective-permute-done((f32[2,768,1]{1,0,2:T(2,128)}, f32[2,768,1]{1,0,2:T(2,128)}, u32[]{:S(2)}, u32[]{:S(2)}) %collective-permute-start.3) | collective-permute-done | bytes 6176 | tf_op jit(solution)/shard_map/ppermute | solution.py:211
  86.9 0.7 fusion.34
  87.6 1.1 divide_convert_fusion
  88.9 1.5 convolution_convert_fusion.2
  90.3 3.6 %all-to-all-start.1 = ((bf16[4,64,1536]{2,1,0:T(8,128)(2,1)}), bf16[4,64,1536]{2,1,0:T(8,128)(2,1)S(1)}, u32[]{:S(2)}, u32[]{:S(2)}) async-start(bf16[4,64,1536]{2,1,0:T(8,128)(2,1)} %bitcast.15), calls=%async_computation.1 | async-start | bytes 1572864 | tf_op jit(solution)/shard_map/all_to_all | solution.py:226
  94.5 11.1 %all-to-all-done.1 = bf16[4,64,1536]{2,1,0:T(8,128)(2,1)S(1)} async-done(((bf16[4,64,1536]{2,1,0:T(8,128)(2,1)}), bf16[4,64,1536]{2,1,0:T(8,128)(2,1)S(1)}, u32[]{:S(2)}, u32[]{:S(2)}) %all-to-all-start.1) | async-done | bytes 786464 | tf_op jit(solution)/shard_map/all_to_all | solution.py:226
  106.0 0.8 concatenate.10
  107.2 0.3 reshape_reshape.3
  107.5 57.7 %all-gather.2.cloned.1.call-done = bf16[512,1664]{1,0:T(8,128)(2,1)} async-done(((bf16[64,1664]{1,0:T(8,128)(2,1)}), bf16[512,1664]{1,0:T(8,128)(2,1)}) %all-gather.2.cloned.1.call-update) | async-done | bytes 1703952 | tf_op jit(solution)/shard_map/all_gather | solution.py:257
  165.3 1.0 slice.28
  167.1 6.3 %fusion.40 = s32[8,64,4]{2,0,1:T(8,128)S(1)} fusion(s32[8,64,4]{2,0,1:T(8,128)S(1)} %copy.189), kind=kOutput, calls=%fused_computation.78 | output fusion | flops 129024 | bytes 16384 | tf_op jit(solution)/shard_map/jit(cumsum)/reduce_window_sum | solution.py:270
  173.7 9.7 %fusion.41 = f32[4,256,1024]{2,1,0:T(8,128)} fusion(bf16[4,1536,1024]{2,1,0:T(8,128)(2,1)} %param.25, bf16[512,1664]{1,0:T(8,128)(2,1)S(1)} %copy-done.9, s32[512,4]{0,1:T(4,128)S(1)} %subtract_add_fusion, pred[512,4]{0,1:T(4,128)(4,1)S(1)} %get-tuple-element.108), kind=kOutput, calls=%fused_computation.79 | convolution fusion | flops 4834459648 | bytes 18360320 | tf_op jit(solution)/shard_map/ecd,edf->ecf/dot_general | solution.py:282
  183.5 5.9 %convolution_convert_fusion.1 = bf16[4,256,1536]{2,1,0:T(8,128)(2,1)S(1)} fusion(bf16[4,512,1536]{2,1,0:T(8,128)(2,1)} %param.26, f32[4,256,1024]{2,1,0:T(8,128)} %fusion.41), kind=kOutput, calls=%fused_computation.2 | convolution fusion | flops 1615331328 | bytes 13631488 | tf_op jit(solution)/shard_map/ecf,efd->ecd/dot_general | solution.py:285
  189.4 2.1 convolution_bitcast_fusion
  191.5 2.9 %fusion.1 = bf16[512,1536]{1,0:T(8,128)(2,1)S(1)} fusion(f32[512,1536]{1,0:T(8,128)S(1)} %convolution_bitcast_fusion, bf16[4,256,1536]{2,1,0:T(8,128)(2,1)S(1)} %convolution_convert_fusion.1, s32[512,4]{0,1:T(4,128)S(1)} %subtract_add_fusion, pred[512,4]{0,1:T(4,128)(4,1)S(1)} %get-tuple-element.108, bf16[512,4]{0,1:T(4,128)(2,1)S(1)} %copy.208), kind=kOutput, calls=%fused_computation.7 | convolution fusion | flops 1613758464 | bytes 7878656 | tf_op jit(solution)/shard_map/nec,ecd->nd/dot_general | solution.py:290
  194.4 1.4 pad_maximum_fusion
  195.8 3.7 %all-to-all-start.2 = ((bf16[8,70,1536]{2,1,0:T(8,128)(2,1)}), bf16[8,70,1536]{2,1,0:T(8,128)(2,1)S(1)}, u32[]{:S(2)}, u32[]{:S(2)}) async-start(bf16[8,70,1536]{2,1,0:T(8,128)(2,1)} %pad_maximum_fusion), calls=%async_computation.2 | async-start | bytes 3538944 | tf_op jit(solution)/shard_map/all_to_all | solution.py:303
  199.9 40.8 %all-to-all-done.2 = bf16[8,70,1536]{2,1,0:T(8,128)(2,1)S(1)} async-done(((bf16[8,70,1536]{2,1,0:T(8,128)(2,1)}), bf16[8,70,1536]{2,1,0:T(8,128)(2,1)S(1)}, u32[]{:S(2)}, u32[]{:S(2)}) %all-to-all-start.2) | async-done | bytes 1720352 | tf_op jit(solution)/shard_map/all_to_all | solution.py:303
  240.9 1.8 add_convert_fusion
  242.8 0.8 scatter_custom_fusion
  244.0 0.8 reshape.158
  (79 shorter events, 3.9 us)
Async XLA Ops:
  7.2 81.7 %copy-start = (bf16[384,1536]{1,0:T(8,128)(2,1)S(1)}, bf16[384,1536]{1,0:T(8,128)(2,1)}, u32[]{:S(2)}) copy-start(bf16[384,1536]{1,0:T(8,128)(2,1)} %param.22) | copy-start | bytes 3538948
  7.2 3.3 %copy-start.2 = (bf16[256,1536]{1,0:T(8,128)(2,1)S(1)}, bf16[256,1536]{1,0:T(8,128)(2,1)}, u32[]{:S(2)}) copy-start(bf16[256,1536]{1,0:T(8,128)(2,1)} %param.17) | copy-start | bytes 2359300
  7.2 3.3 %copy-start.13 = (f32[1536]{0:T(1024)S(1)}, f32[1536]{0:T(1024)}, u32[]{:S(2)}) copy-start(f32[1536]{0:T(1024)} %param.18) | copy-start | bytes 18436
  7.2 3.3 %copy-start.12 = (bf16[1536,128]{1,0:T(8,128)(2,1)S(1)}, bf16[1536,128]{1,0:T(8,128)(2,1)}, u32[]{:S(2)}) copy-start(bf16[1536,128]{1,0:T(8,128)(2,1)} %param.21) | copy-start | bytes 1179652
  7.2 3.8 %copy-start.6 = (bf16[512,256]{1,0:T(8,128)(2,1)S(1)}, bf16[512,256]{1,0:T(8,128)(2,1)}, u32[]{:S(2)}) copy-start(bf16[512,256]{1,0:T(8,128)(2,1)} %param.23) | copy-start | bytes 786436
  13.2 26.6 %all-to-all-start = ((bf16[4,2,2,768,64]{3,4,2,1,0:T(8,128)(2,1)}), bf16[4,2,2,768,64]{3,4,2,1,0:T(8,128)(2,1)S(1)}, u32[]{:S(2)}, u32[]{:S(2)}) async-start(bf16[4,2,2,768,64]{3,4,2,1,0:T(8,128)(2,1)} %broadcast_in_dim.78), calls=%async_computation | async-start | bytes 3145728 | tf_op jit(solution)/shard_map/all_to_all | solution.py:178
  24.3 15.5 %collective-permute-start = (bf16[2,768,64]{1,2,0:T(8,128)(2,1)}, bf16[2,768,64]{1,2,0:T(8,128)(2,1)}, u32[]{:S(2)}, u32[]{:S(2)}) collective-permute-start(bf16[2,768,64]{1,2,0:T(8,128)(2,1)} %bitcast.38), channel_id=1, source_target_pairs={{0,16},{1,17},{2,18},{3,19},{4,20},{5,21},{6,22},{7,23},{8,24},{9,... | collective-permute-start | bytes 589832 | tf_op jit(solution)/shard_map/ppermute | solution.py:187
  44.8 42.8 %collective-permute-start.2 = (f32[2,768,64]{1,2,0:T(8,128)}, f32[2,768,64]{1,2,0:T(8,128)}, u32[]{:S(2)}, u32[]{:S(2)}) collective-permute-start(f32[2,768,64]{1,2,0:T(8,128)} %copy.181), channel_id=1, source_target_pairs={{16,0},{17,1},{18,2},{19,3},{20,4},{21,5},{22,6},{23,7},{24,8},{25... | collective-permute-start | bytes 1179656 | tf_op jit(solution)/shard_map/ppermute | solution.py:211
  50.1 36.7 %collective-permute-start.3 = (f32[2,768,1]{1,0,2:T(2,128)}, f32[2,768,1]{1,0,2:T(2,128)}, u32[]{:S(2)}, u32[]{:S(2)}) collective-permute-start(f32[2,768,1]{1,0,2:T(2,128)} %copy.183), channel_id=1, source_target_pairs={{16,0},{17,1},{18,2},{19,3},{20,4},{21,5},{22,6},{23,7},{24,8},{25... | collective-permute-start | bytes 18440 | tf_op jit(solution)/shard_map/ppermute | solution.py:211
  51.3 35.5 %collective-permute-start.1 = (f32[2,768,1]{1,0,2:T(2,128)}, f32[2,768,1]{1,0,2:T(2,128)}, u32[]{:S(2)}, u32[]{:S(2)}) collective-permute-start(f32[2,768,1]{1,0,2:T(2,128)} %copy.177), channel_id=1, source_target_pairs={{16,0},{17,1},{18,2},{19,3},{20,4},{21,5},{22,6},{23,7},{24,8},{25... | collective-permute-start | bytes 18440 | tf_op jit(solution)/shard_map/ppermute | solution.py:211
  80.9 2.9 %copy-start.4 = (f32[2,768,1]{2,1,0:T(8,128)S(1)}, f32[2,768,1]{2,1,0:T(8,128)}, u32[]{:S(2)}) copy-start(f32[2,768,1]{2,1,0:T(8,128)} %get-tuple-element.103) | copy-start | bytes 18436 | tf_op jit(solution)/shard_map/cond
  88.8 5.2 %copy-start.8 = (s32[64,8]{0,1:T(8,128)S(1)}, s32[64,8]{0,1:T(8,128)}, u32[]{:S(2)}) copy-start(s32[64,8]{0,1:T(8,128)} %param.27) | copy-start | bytes 6148
  88.8 5.4 %copy-start.7 = (f32[64,8]{0,1:T(8,128)S(1)}, f32[64,8]{0,1:T(8,128)}, u32[]{:S(2)}) copy-start(f32[64,8]{0,1:T(8,128)} %param.28) | copy-start | bytes 6148
  90.3 15.6 %copy-start.10 = (f32[1536]{0:T(1024)S(1)}, f32[1536]{0:T(1024)}, u32[]{:S(2)}) copy-start(f32[1536]{0:T(1024)} %param.24) | copy-start | bytes 18436
  90.3 15.3 %all-to-all-start.1 = ((bf16[4,64,1536]{2,1,0:T(8,128)(2,1)}), bf16[4,64,1536]{2,1,0:T(8,128)(2,1)S(1)}, u32[]{:S(2)}, u32[]{:S(2)}) async-start(bf16[4,64,1536]{2,1,0:T(8,128)(2,1)} %bitcast.15), calls=%async_computation.1 | async-start | bytes 1572864 | tf_op jit(solution)/shard_map/all_to_all | solution.py:226
  94.0 13.0 %copy-start.5 = (bf16[256,2,2,64]{0,3,2,1:T(8,128)(2,1)S(1)}, bf16[256,2,2,64]{0,3,2,1:T(8,128)(2,1)}, u32[]{:S(2)}) copy-start(bf16[256,2,2,64]{0,3,2,1:T(8,128)(2,1)} %get-tuple-element.115) | copy-start | bytes 393220
  94.0 71.3 %all-gather.2.cloned.1.call-start = ((), (), s32[]{:S(2)}) async-start(), calls=%async_computation.3 | async-start | bytes 1916928 | tf_op jit(solution)/shard_map/all_gather | solution.py:257
  165.3 8.4 %copy-start.9 = (bf16[512,1664]{1,0:T(8,128)(2,1)S(1)}, bf16[512,1664]{1,0:T(8,128)(2,1)}, u32[]{:S(2)}) copy-start(bf16[512,1664]{1,0:T(8,128)(2,1)} %all-gather.2.cloned.1.call-done) | copy-start | bytes 5111812
  195.8 3.9 %copy-start.11 = (s32[256]{0:T(256)S(1)}, s32[256]{0:T(256)}, u32[]{:S(2)}) copy-start(s32[256]{0:T(256)} %param.29) | copy-start | bytes 3076
  195.8 44.9 %all-to-all-start.2 = ((bf16[8,70,1536]{2,1,0:T(8,128)(2,1)}), bf16[8,70,1536]{2,1,0:T(8,128)(2,1)S(1)}, u32[]{:S(2)}, u32[]{:S(2)}) async-start(bf16[8,70,1536]{2,1,0:T(8,128)(2,1)} %pad_maximum_fusion), calls=%async_computation.2 | async-start | bytes 3538944 | tf_op jit(solution)/shard_map/all_to_all | solution.py:303
  240.7 4.1 %copy-start.1 = (bf16[384,1536]{1,0:T(8,128)(2,1)S(1)}, bf16[384,1536]{1,0:T(8,128)(2,1)}, u32[]{:S(2)}) copy-start(bf16[384,1536]{1,0:T(8,128)(2,1)} %param.22) | copy-start | bytes 3538948
Sparse Core Ops, SparseCore 0:
  107.0 58.2 all-gather.1

commit v11 on v8

--- a/solution.py
+++ b/solution.py
@@ -272,9 +272,19 @@
         ],
         axis=1,
     )
-    packed_all = lax.all_gather(
-        jnp.concatenate([moe_in, side], axis=1), SEQ_AXES, axis=0, tiled=True
-    )
+    packed = jnp.concatenate([moe_in, side], axis=1)
+    crossed = lax.ppermute(packed, "half", perm=[(0, 1), (1, 0)])
+    pair = jnp.where(
+        holds_first, jnp.stack([packed, crossed]), jnp.stack([crossed, packed])
+    )
+    fanned = lax.all_to_all(
+        jnp.broadcast_to(pair[None], (half_size,) + pair.shape),
+        "hseq",
+        split_axis=0,
+        concat_axis=0,
+        tiled=True,
+    )
+    packed_all = fanned.transpose(1, 0, 2, 3).reshape(seq_count * moe_rows, -1)
     rows_all = packed_all[:, :model_width]
     total_rows = rows_all.shape[0]
     local_first = seq_index * experts_here

time: 241 us -> 221 us (0.917)
  waiting for transfers between devices: 99.3 us -> 84.3 us
  between operations: 14.5 us -> 1.08 us
  starting transfers between devices: 37.5 us -> 45.1 us
    all_gather x1 -> x0, waiting for transfers between devices: 38.5 us -> none  [body(): lax.all_gather(jnp.concatenate([moe_in, side], axis=1), SEQ_AXES, axis=0,...]
    all_to_all x0 -> x1, waiting for transfers between devices: none -> 18.5 us  [body(): lax.all_to_all(jnp.broadcast_to(pair[None], (half_size,) + pair.shape), '...]
    all_to_all x0 -> x1, starting transfers between devices: none -> 12.5 us  [body(): lax.all_to_all(jnp.broadcast_to(pair[None], (half_size,) + pair.shape), '...]
    all_to_all x1, starting transfers between devices: 16.4 us -> 4.49 us  [body(): lax.all_to_all(outgoing, SEQ_AXES, split_axis=1, concat_axis=1, tiled=True)]
    ppermute x0 -> x1, waiting for transfers between devices: none -> 5.06 us  [body(): crossed = lax.ppermute(packed, 'half', perm=[(0, 1), (1, 0)])]
    ppermute x0 -> x1, starting transfers between devices: none -> 4.6 us  [body(): crossed = lax.ppermute(packed, 'half', perm=[(0, 1), (1, 0)])]
  transfers between devices with their start and end apart: 9 -> 10, of which waited for: 6 -> 7; matrix products, arithmetic and copies ran while one was open for 20% -> 22% of each run, Pallas kernels for 10% -> 11%
where the time goes in v11:
time: 221 us; the launch traced here: 220 us
  waiting for transfers between devices  84.3 us (38%)
  starting transfers between devices  45.1 us (20%)
  matrix products  28.2 us (13%)
  local copies, waits for them, and re-layouts  26.4 us (12%)
  Pallas kernels  23.5 us (11%)
  other arithmetic  11.4 us (5%)
    all_to_all x1, waiting for transfers between devices, body(): lax.all_to_all(partial.astype(jnp.bfloat16).reshape(seq_count, moe_rows,...  32.5 us
    pallas_call x1, Pallas kernels, attend_partial(): pl.pallas_call(kernel, out_shape=(jax.ShapeDtypeStruct((heads, rows, dim)...  23.5 us
    all_to_all x1, waiting for transfers between devices, body(): lax.all_to_all(jnp.broadcast_to(pair[None], (half_size,) + pair.shape), '...  18.5 us
    ppermute x1, waiting for transfers between devices, body(): partner_rows = lax.ppermute(query_rows, 'half', perm=[(0, 1)])  13.1 us
    all_to_all x1, starting transfers between devices, body(): lax.all_to_all(jnp.broadcast_to(pair[None], (half_size,) + pair.shape), '...  12.5 us
    all_to_all x1, waiting for transfers between devices, body(): lax.all_to_all(projected.reshape(exp_count, -1, projected.shape[1]), 'exp...  11.2 us
    dot_general x1, matrix products, body(): jnp.einsum('ecd,edf->ecf', rows_in, expert_in, preferred_element_type=jnp...  10.2 us
    another operation x5, local copies, waits for them, and re-layouts  6.62 us
  transfers between devices with their start and end apart: 10, of which 7 were waited for; matrix products, arithmetic and copies ran while one was open for 22% of the time, Pallas kernels for 11%

profile of v11, /device:TPU:0, one launch (start us, length us, event | category | flops | bytes accessed | tf_op | source)
XLA Modules:
  0.0 220.1 jit_solution(639613894698175590)
XLA Ops:
  0.7 1.5 fusion.7
  2.2 1.7 convolution_convert_fusion.5
  4.6 0.7 pad_maximum_fusion.1
  5.4 1.3 broadcast_in_dim.84
  6.7 5.2 %all-to-all-start = ((bf16[4,2,2,768,64]{3,4,2,1,0:T(8,128)(2,1)}), bf16[4,2,2,768,64]{3,4,2,1,0:T(8,128)(2,1)S(1)}, u32[]{:S(2)}, u32[]{:S(2)}) async-start(bf16[4,2,2,768,64]{3,4,2,1,0:T(8,128)(2,1)} %broadcast_in_dim.84), calls=%async_computation | async-start | bytes 3145728 | tf_op jit(solution)/shard_map/all_to_all | solution.py:196
  11.9 2.6 %convolution_convert_fusion.3 = bf16[256,384]{1,0:T(8,128)(2,1)} fusion(bf16[1536,384]{1,0:T(8,128)(2,1)} %param.19, bf16[256,1536]{1,0:T(8,128)(2,1)S(1)} %copy-done.2, f32[1536]{0:T(1024)S(1)} %copy-done.14, f32[256]{0:T(256)S(1)} %add_rsqrt_fusion), kind=kOutput, calls=%fused_computation.22 | convolution fusion | flops 303661056 | bytes 2169856 | tf_op jit(solution)/shard_map/dot_general | solution.py:158
  14.5 1.1 copy.173
  15.6 4.5 %collective-permute-start = (bf16[2,768,64]{1,2,0:T(8,128)(2,1)S(1)}, bf16[2,768,64]{1,2,0:T(8,128)(2,1)S(1)}, u32[]{:S(2)}, u32[]{:S(2)}) collective-permute-start(bf16[2,768,64]{1,2,0:T(8,128)(2,1)S(1)} %bitcast.77), channel_id=1, source_target_pairs={{0,16},{1,17},{2,18},{3,19},{4,20},{5,21},{6,22},{7,23},{8,24},{9,... | collective-permute-start | bytes 589832 | tf_op jit(solution)/shard_map/ppermute | solution.py:205
  20.1 13.1 %collective-permute-done = bf16[2,768,64]{1,2,0:T(8,128)(2,1)S(1)} collective-permute-done((bf16[2,768,64]{1,2,0:T(8,128)(2,1)S(1)}, bf16[2,768,64]{1,2,0:T(8,128)(2,1)S(1)}, u32[]{:S(2)}, u32[]{:S(2)}) %collective-permute-start) | collective-permute-done | bytes 196640 | tf_op jit(solution)/shard_map/ppermute | solution.py:205
  33.2 2.8 %conditional.3 = ((f32[2,768,64]{2,1,0:T(8,128)}, f32[2,768,1]{2,1,0:T(8,128)}, f32[2,768,1]{2,1,0:T(8,128)})) conditional(s32[]{:T(128)} %convert_element_type.76, (s32[1]{0:T(128)}, bf16[2,768,64]{1,2,0:T(8,128)(2,1)S(1)}, bf16[4,2,2,768,64]{3,4,2,1,0:T(8,128)(2,1)S(1)}) %tuple.22, () %tuple.23), branch_computations={%region_3.4_spmd, %region_4.5_spmd} | conditional | bytes 3538952 | solution.py:217
  33.2 1.0 broadcast.98
  34.1 0.9 broadcast.96
  35.1 0.9 broadcast.97
  36.0 2.1 copy.189
  38.2 1.3 collective-permute-start.2
  39.5 1.4 copy.185
  40.8 1.4 copy.191
  42.2 1.3 collective-permute-start.3
  43.5 1.3 collective-permute-start.1
  44.8 30.5 %conditional.2 = (f32[2,768,64]{1,2,0:T(8,128)S(1)}, f32[2,768,1]{1,0,2:T(2,128)S(1)}, f32[2,768,1]{1,0,2:T(2,128)S(1)}) conditional(s32[]{:T(128)} %convert_element_type.76, (s32[1]{0:T(128)}, bf16[2,768,64]{1,2,0:T(8,128)(2,1)S(1)}, bf16[4,2,2,768,64]{3,4,2,1,0:T(8,128)(2,1)S(1)}) %tuple.64, (s32[1]{0:T(128)}, bf16[2,768,64]{1,2,0:T(8,128)(2,1)S(1)}, ...), branch_computations={%region_1.2_spmd, %region_2.3_spmd} | conditional | bytes 4374580 | solution.py:223
  44.9 0.9 copy.181.q_ref
  45.8 2.8 %copy.182.k_ref.v_ref = bf16[4,2,2,768,64]{4,3,2,1,0:T(8,128)(2,1)} copy(bf16[4,2,2,768,64]{3,4,2,1,0:T(8,128)(2,1)S(1)} %get-tuple-element.90) | data formatting | bytes 3145728 | tf_op jit(solution)/shard_map
  48.6 23.5 %branch_1_fun.1 = (f32[2,768,64]{2,1,0:T(8,128)}, f32[2,768,1]{2,1,0:T(8,128)}, f32[2,768,1]{2,1,0:T(8,128)}) custom-call(s32[1]{0:T(128)} %get-tuple-element.21.flags_ref, bf16[2,768,64]{2,1,0:T(8,128)(2,1)} %copy.181.q_ref, bf16[4,2,2,768,64]{4,3,2,1,0:T(8,128)(2,1)} %copy.182.k_ref.v_ref, bf16[4,2,2,768,64]{4,3,2,1,0:T(8,128)(2,1)} %copy.182.k_ref.v_ref), custom_call_target="tpu_custom_call" | custom-call | tf_op jit(solution)/shard_map/cond/branch_1_fun/pallas_call | solution.py:96
  72.2 1.5 copy.209
  73.6 1.4 copy.211
  75.3 3.9 %collective-permute-done.3 = f32[2,768,1]{1,0,2:T(2,128)S(1)} collective-permute-done((f32[2,768,1]{1,0,2:T(2,128)S(1)}, f32[2,768,1]{1,0,2:T(2,128)S(1)}, u32[]{:S(2)}, u32[]{:S(2)}) %collective-permute-start.3) | collective-permute-done | bytes 6176 | tf_op jit(solution)/shard_map/ppermute | solution.py:229
  79.5 1.5 convolution_convert_fusion.2
  81.0 3.8 %all-to-all-start.1 = ((bf16[4,64,1536]{2,1,0:T(8,128)(2,1)}), bf16[4,64,1536]{2,1,0:T(8,128)(2,1)S(1)}, u32[]{:S(2)}, u32[]{:S(2)}) async-start(bf16[4,64,1536]{2,1,0:T(8,128)(2,1)} %bitcast.15), calls=%async_computation.1 | async-start | bytes 1572864 | tf_op jit(solution)/shard_map/all_to_all | solution.py:244
  85.3 11.2 %all-to-all-done.1 = bf16[4,64,1536]{2,1,0:T(8,128)(2,1)S(1)} async-done(((bf16[4,64,1536]{2,1,0:T(8,128)(2,1)}), bf16[4,64,1536]{2,1,0:T(8,128)(2,1)S(1)}, u32[]{:S(2)}, u32[]{:S(2)}) %all-to-all-start.1) | async-done | bytes 786464 | tf_op jit(solution)/shard_map/all_to_all | solution.py:244
  97.0 4.6 %collective-permute-start.4 = (bf16[64,1664]{1,0:T(8,128)(2,1)S(1)}, bf16[64,1664]{1,0:T(8,128)(2,1)S(1)}, u32[]{:S(2)}, u32[]{:S(2)}) collective-permute-start(bf16[64,1664]{1,0:T(8,128)(2,1)S(1)} %concatenate.15), channel_id=1, source_target_pairs={{0,16},{16,0},{1,17},{17,1},{2,18},{18,2},{3,19},{19,3},{4,20},{20... | collective-permute-start | bytes 638984 | tf_op jit(solution)/shard_map/ppermute | solution.py:276
  101.6 5.1 %collective-permute-done.4 = bf16[64,1664]{1,0:T(8,128)(2,1)S(1)} collective-permute-done((bf16[64,1664]{1,0:T(8,128)(2,1)S(1)}, bf16[64,1664]{1,0:T(8,128)(2,1)S(1)}, u32[]{:S(2)}, u32[]{:S(2)}) %collective-permute-start.4) | collective-permute-done | bytes 213024 | tf_op jit(solution)/shard_map/ppermute | solution.py:276
  106.7 1.3 broadcast_in_dim.91
  108.1 12.5 %all-to-all-start.2 = ((bf16[4,2,64,1664]{3,2,1,0:T(8,128)(2,1)}), bf16[4,2,64,1664]{3,2,1,0:T(8,128)(2,1)S(1)}, u32[]{:S(2)}, u32[]{:S(2)}) async-start(bf16[4,2,64,1664]{3,2,1,0:T(8,128)(2,1)} %broadcast_in_dim.91), calls=%async_computation.2 | async-start | bytes 3407872 | tf_op jit(solution)/shard_map/all_to_all | solution.py:280
  121.2 0.8 copy.202
  121.9 18.5 %all-to-all-done.2 = bf16[4,2,64,1664]{3,2,1,0:T(8,128)(2,1)S(1)} async-done(((bf16[4,2,64,1664]{3,2,1,0:T(8,128)(2,1)}), bf16[4,2,64,1664]{3,2,1,0:T(8,128)(2,1)S(1)}, u32[]{:S(2)}, u32[]{:S(2)}) %all-to-all-start.2) | async-done | bytes 1703968 | tf_op jit(solution)/shard_map/all_to_all | solution.py:280
  140.4 4.5 %all-to-all-start.4 = ((bf16[4,8,2048]{2,0,1:T(4,128)(2,1)}), bf16[4,8,2048]{2,0,1:T(4,128)(2,1)S(1)}, u32[]{:S(2)}, u32[]{:S(2)}) async-start(bf16[4,8,2048]{2,0,1:T(4,128)(2,1)} %copy.202), calls=%async_computation.4 | async-start | bytes 262144 | tf_op jit(solution)/shard_map/all_to_all | solution.py:173
  145.3 1.0 copy-done.4
  146.9 6.3 %fusion.42 = s32[8,64,4]{2,0,1:T(8,128)S(1)} fusion(s32[8,64,4]{2,0,1:T(8,128)S(1)} %copy.198), kind=kOutput, calls=%fused_computation.80 | output fusion | flops 129024 | bytes 16384 | tf_op jit(solution)/shard_map/jit(cumsum)/reduce_window_sum | solution.py:298
  153.5 10.2 %fusion.43 = f32[4,256,1024]{2,1,0:T(8,128)} fusion(bf16[4,1536,1024]{2,1,0:T(8,128)(2,1)} %param.25, bf16[512,1664]{1,0:T(8,128)(2,1)} %bitcast.76, s32[512,4]{0,1:T(4,128)S(1)} %subtract_add_fusion, pred[512,4]{0,1:T(4,128)(4,1)S(1)} %get-tuple-element.106), kind=kOutput, calls=%fused_computation.81 | convolution fusion | flops 4834459648 | bytes 18360320 | tf_op jit(solution)/shard_map/ecd,edf->ecf/dot_general | solution.py:310
  163.7 5.9 %convolution_convert_fusion.1 = bf16[4,256,1536]{2,1,0:T(8,128)(2,1)S(1)} fusion(bf16[4,512,1536]{2,1,0:T(8,128)(2,1)} %param.26, f32[4,256,1024]{2,1,0:T(8,128)} %fusion.43), kind=kOutput, calls=%fused_computation.2 | convolution fusion | flops 1615331328 | bytes 13631488 | tf_op jit(solution)/shard_map/ecf,efd->ecd/dot_general | solution.py:313
  169.6 2.1 convolution_bitcast_fusion
  171.7 3.7 %fusion.1 = bf16[512,1536]{1,0:T(8,128)(2,1)} fusion(f32[512,1536]{1,0:T(8,128)S(1)} %convolution_bitcast_fusion, bf16[4,256,1536]{2,1,0:T(8,128)(2,1)S(1)} %convolution_convert_fusion.1, s32[512,4]{0,1:T(4,128)S(1)} %subtract_add_fusion, pred[512,4]{0,1:T(4,128)(4,1)S(1)} %get-tuple-element.106, bf16[512,4]{0,1:T(4,128)(2,1)S(1)} %copy.217), kind=kOutput, calls=%fused_computation.7 | convolution fusion | flops 1613758464 | bytes 7878656 | tf_op jit(solution)/shard_map/nec,ecd->nd/dot_general | solution.py:318
  175.4 6.1 %all-to-all-start.3 = ((bf16[8,64,1536]{2,1,0:T(8,128)(2,1)}), bf16[8,64,1536]{2,1,0:T(8,128)(2,1)S(1)}, u32[]{:S(2)}, u32[]{:S(2)}) async-start(bf16[8,64,1536]{2,1,0:T(8,128)(2,1)} %bitcast.80), calls=%async_computation.3 | async-start | bytes 3145728 | tf_op jit(solution)/shard_map/all_to_all | solution.py:321
  181.9 0.9 scatter_custom_fusion
  183.1 0.8 copy.207
  183.9 1.8 reshape.179
  185.6 32.5 %all-to-all-done.3 = bf16[8,64,1536]{2,1,0:T(8,128)(2,1)S(1)} async-done(((bf16[8,64,1536]{2,1,0:T(8,128)(2,1)}), bf16[8,64,1536]{2,1,0:T(8,128)(2,1)S(1)}, u32[]{:S(2)}, u32[]{:S(2)}) %all-to-all-start.3) | async-done | bytes 1572896 | tf_op jit(solution)/shard_map/all_to_all | solution.py:321
  218.4 1.7 add_convert_fusion
  (82 shorter events, 4.8 us)
Async XLA Ops:
  0.6 78.9 %copy-start = (bf16[384,1536]{1,0:T(8,128)(2,1)S(1)}, bf16[384,1536]{1,0:T(8,128)(2,1)}, u32[]{:S(2)}) copy-start(bf16[384,1536]{1,0:T(8,128)(2,1)} %param.22) | copy-start | bytes 3538948
  0.6 3.3 %copy-start.2 = (bf16[256,1536]{1,0:T(8,128)(2,1)S(1)}, bf16[256,1536]{1,0:T(8,128)(2,1)}, u32[]{:S(2)}) copy-start(bf16[256,1536]{1,0:T(8,128)(2,1)} %param.17) | copy-start | bytes 2359300
  0.7 3.3 %copy-start.14 = (f32[1536]{0:T(1024)S(1)}, f32[1536]{0:T(1024)}, u32[]{:S(2)}) copy-start(f32[1536]{0:T(1024)} %param.18) | copy-start | bytes 18436
  0.7 3.3 %copy-start.13 = (bf16[1536,128]{1,0:T(8,128)(2,1)S(1)}, bf16[1536,128]{1,0:T(8,128)(2,1)}, u32[]{:S(2)}) copy-start(bf16[1536,128]{1,0:T(8,128)(2,1)} %param.21) | copy-start | bytes 1179652
  0.7 3.8 %copy-start.8 = (bf16[512,256]{1,0:T(8,128)(2,1)S(1)}, bf16[512,256]{1,0:T(8,128)(2,1)}, u32[]{:S(2)}) copy-start(bf16[512,256]{1,0:T(8,128)(2,1)} %param.23) | copy-start | bytes 786436
  6.7 26.5 %all-to-all-start = ((bf16[4,2,2,768,64]{3,4,2,1,0:T(8,128)(2,1)}), bf16[4,2,2,768,64]{3,4,2,1,0:T(8,128)(2,1)S(1)}, u32[]{:S(2)}, u32[]{:S(2)}) async-start(bf16[4,2,2,768,64]{3,4,2,1,0:T(8,128)(2,1)} %broadcast_in_dim.84), calls=%async_computation | async-start | bytes 3145728 | tf_op jit(solution)/shard_map/all_to_all | solution.py:196
  15.6 17.6 %collective-permute-start = (bf16[2,768,64]{1,2,0:T(8,128)(2,1)S(1)}, bf16[2,768,64]{1,2,0:T(8,128)(2,1)S(1)}, u32[]{:S(2)}, u32[]{:S(2)}) collective-permute-start(bf16[2,768,64]{1,2,0:T(8,128)(2,1)S(1)} %bitcast.77), channel_id=1, source_target_pairs={{0,16},{1,17},{2,18},{3,19},{4,20},{5,21},{6,22},{7,23},{8,24},{9,... | collective-permute-start | bytes 589832 | tf_op jit(solution)/shard_map/ppermute | solution.py:205
  38.2 41.1 %collective-permute-start.2 = (f32[2,768,64]{1,2,0:T(8,128)}, f32[2,768,64]{1,2,0:T(8,128)S(1)}, u32[]{:S(2)}, u32[]{:S(2)}) collective-permute-start(f32[2,768,64]{1,2,0:T(8,128)} %copy.189), channel_id=1, source_target_pairs={{16,0},{17,1},{18,2},{19,3},{20,4},{21,5},{22,6},{23,7},{24,8},{25... | collective-permute-start | bytes 1179656 | tf_op jit(solution)/shard_map/ppermute | solution.py:229
  42.2 36.9 %collective-permute-start.3 = (f32[2,768,1]{1,0,2:T(2,128)S(1)}, f32[2,768,1]{1,0,2:T(2,128)S(1)}, u32[]{:S(2)}, u32[]{:S(2)}) collective-permute-start(f32[2,768,1]{1,0,2:T(2,128)S(1)} %copy.191), channel_id=1, source_target_pairs={{16,0},{17,1},{18,2},{19,3},{20,4},{21,5},{22,6},{23,7},{24,8},{25... | collective-permute-start | bytes 18440 | tf_op jit(solution)/shard_map/ppermute | solution.py:229
  43.5 35.7 %collective-permute-start.1 = (f32[2,768,1]{1,0,2:T(2,128)S(1)}, f32[2,768,1]{1,0,2:T(2,128)S(1)}, u32[]{:S(2)}, u32[]{:S(2)}) collective-permute-start(f32[2,768,1]{1,0,2:T(2,128)S(1)} %copy.185), channel_id=1, source_target_pairs={{16,0},{17,1},{18,2},{19,3},{20,4},{21,5},{22,6},{23,7},{24,8},{25... | collective-permute-start | bytes 18440 | tf_op jit(solution)/shard_map/ppermute | solution.py:229
  72.2 2.9 %copy-start.6 = (f32[2,768,1]{2,1,0:T(8,128)S(1)}, f32[2,768,1]{2,1,0:T(8,128)}, u32[]{:S(2)}) copy-start(f32[2,768,1]{2,1,0:T(8,128)} %get-tuple-element.101) | copy-start | bytes 18436 | tf_op jit(solution)/shard_map/cond
  79.4 5.4 %copy-start.10 = (s32[64,8]{0,1:T(8,128)S(1)}, s32[64,8]{0,1:T(8,128)}, u32[]{:S(2)}) copy-start(s32[64,8]{0,1:T(8,128)} %param.27) | copy-start | bytes 6148
  79.5 5.5 %copy-start.9 = (f32[64,8]{0,1:T(8,128)S(1)}, f32[64,8]{0,1:T(8,128)}, u32[]{:S(2)}) copy-start(f32[64,8]{0,1:T(8,128)} %param.28) | copy-start | bytes 6148
  79.5 17.1 %copy-start.3 = (bf16[256,1536]{1,0:T(8,128)(2,1)S(1)}, bf16[256,1536]{1,0:T(8,128)(2,1)}, u32[]{:S(2)}) copy-start(bf16[256,1536]{1,0:T(8,128)(2,1)} %param.17) | copy-start | bytes 2359300
  81.0 15.7 %copy-start.11 = (f32[1536]{0:T(1024)S(1)}, f32[1536]{0:T(1024)}, u32[]{:S(2)}) copy-start(f32[1536]{0:T(1024)} %param.24) | copy-start | bytes 18436
  81.0 15.4 %all-to-all-start.1 = ((bf16[4,64,1536]{2,1,0:T(8,128)(2,1)}), bf16[4,64,1536]{2,1,0:T(8,128)(2,1)S(1)}, u32[]{:S(2)}, u32[]{:S(2)}) async-start(bf16[4,64,1536]{2,1,0:T(8,128)(2,1)} %bitcast.15), calls=%async_computation.1 | async-start | bytes 1572864 | tf_op jit(solution)/shard_map/all_to_all | solution.py:244
  97.0 9.7 %collective-permute-start.4 = (bf16[64,1664]{1,0:T(8,128)(2,1)S(1)}, bf16[64,1664]{1,0:T(8,128)(2,1)S(1)}, u32[]{:S(2)}, u32[]{:S(2)}) collective-permute-start(bf16[64,1664]{1,0:T(8,128)(2,1)S(1)} %concatenate.15), channel_id=1, source_target_pairs={{0,16},{16,0},{1,17},{17,1},{2,18},{18,2},{3,19},{19,3},{4,20},{20... | collective-permute-start | bytes 638984 | tf_op jit(solution)/shard_map/ppermute | solution.py:276
  108.1 12.6 %copy-start.7 = (bf16[256,2,2,64]{0,3,2,1:T(8,128)(2,1)S(1)}, bf16[256,2,2,64]{0,3,2,1:T(8,128)(2,1)}, u32[]{:S(2)}) copy-start(bf16[256,2,2,64]{0,3,2,1:T(8,128)(2,1)} %get-tuple-element.109) | copy-start | bytes 393220
  108.1 32.4 %all-to-all-start.2 = ((bf16[4,2,64,1664]{3,2,1,0:T(8,128)(2,1)}), bf16[4,2,64,1664]{3,2,1,0:T(8,128)(2,1)S(1)}, u32[]{:S(2)}, u32[]{:S(2)}) async-start(bf16[4,2,64,1664]{3,2,1,0:T(8,128)(2,1)} %broadcast_in_dim.91), calls=%async_computation.2 | async-start | bytes 3407872 | tf_op jit(solution)/shard_map/all_to_all | solution.py:280
  140.4 35.0 %all-to-all-start.4 = ((bf16[4,8,2048]{2,0,1:T(4,128)(2,1)}), bf16[4,8,2048]{2,0,1:T(4,128)(2,1)S(1)}, u32[]{:S(2)}, u32[]{:S(2)}) async-start(bf16[4,8,2048]{2,0,1:T(4,128)(2,1)} %copy.202), calls=%async_computation.4 | async-start | bytes 262144 | tf_op jit(solution)/shard_map/all_to_all | solution.py:173
  145.1 1.2 copy-start.4
  175.4 6.3 %copy-start.12 = (s32[256]{0:T(256)S(1)}, s32[256]{0:T(256)}, u32[]{:S(2)}) copy-start(s32[256]{0:T(256)} %param.29) | copy-start | bytes 3076
  175.4 42.7 %all-to-all-start.3 = ((bf16[8,64,1536]{2,1,0:T(8,128)(2,1)}), bf16[8,64,1536]{2,1,0:T(8,128)(2,1)S(1)}, u32[]{:S(2)}, u32[]{:S(2)}) async-start(bf16[8,64,1536]{2,1,0:T(8,128)(2,1)} %bitcast.80), calls=%async_computation.3 | async-start | bytes 3145728 | tf_op jit(solution)/shard_map/all_to_all | solution.py:321
  182.8 37.2 %copy-start.1 = (bf16[384,1536]{1,0:T(8,128)(2,1)S(1)}, bf16[384,1536]{1,0:T(8,128)(2,1)}, u32[]{:S(2)}) copy-start(bf16[384,1536]{1,0:T(8,128)(2,1)} %param.22) | copy-start | bytes 3538948

commit v12 on v11

--- a/solution.py
+++ b/solution.py
@@ -318,14 +318,15 @@
     partial = jnp.einsum(
         "nec,ecd->nd", scaled_hi, produced, preferred_element_type=jnp.float32
     ) + jnp.einsum("nec,ecd->nd", scaled_lo, produced, preferred_element_type=jnp.float32)
-    returned = lax.all_to_all(
-        partial.astype(jnp.bfloat16).reshape(seq_count, moe_rows, -1),
-        SEQ_AXES,
-        split_axis=0,
-        concat_axis=0,
-        tiled=True,
-    )
-    moe = jnp.sum(returned.astype(jnp.float32), axis=0)
+    by_dest = partial.astype(jnp.bfloat16).reshape(halves, half_size, moe_rows, -1)
+    from_half = lax.all_to_all(
+        by_dest.transpose(1, 0, 2, 3), "hseq", split_axis=0, concat_axis=0, tiled=True
+    )
+    half_sums = jnp.sum(from_half.astype(jnp.float32), axis=0)
+    own_sum = jnp.where(holds_first, half_sums[0], half_sums[1])
+    other_sum = jnp.where(holds_first, half_sums[1], half_sums[0])
+    from_partner = lax.ppermute(other_sum.astype(jnp.bfloat16), "half", perm=[(0, 1), (1, 0)])
+    moe = own_sum + from_partner.astype(jnp.float32)
     hidden_out = (residual + residual_scale * moe).astype(jnp.bfloat16)
     return (hidden_out, page_rows)
 

time: 221 us -> 216 us (0.977)
  waiting for transfers between devices: 84.3 us -> 79.5 us
    all_to_all x1, waiting for transfers between devices: 32.5 us -> 17.8 us  [body(): lax.all_to_all(by_dest.transpose(1, 0, 2, 3), 'hseq', split_axis=0, conca...]
    all_to_all x1, waiting for transfers between devices: 0.01 us -> 7.42 us  [body(): lax.all_to_all(outgoing, SEQ_AXES, split_axis=1, concat_axis=1, tiled=True)]
    ppermute x0 -> x1, starting transfers between devices: none -> 2.98 us  [body(): lax.ppermute(other_sum.astype(jnp.bfloat16), 'half', perm=[(0, 1), (1, 0)])]
    all_to_all x1, starting transfers between devices: 6.13 us -> 3.69 us  [body(): lax.all_to_all(by_dest.transpose(1, 0, 2, 3), 'hseq', split_axis=0, conca...]
  transfers between devices with their start and end apart: 10 -> 11, of which waited for: 7 -> 9; matrix products, arithmetic and copies ran while one was open for 22% -> 8% of each run, Pallas kernels for 11% -> 11%
where the time goes in v12:
time: 216 us; the launch traced here: 215 us
  waiting for transfers between devices  79.5 us (37%)
  starting transfers between devices  44.7 us (21%)
  matrix products  27.4 us (13%)
  local copies, waits for them, and re-layouts  26.9 us (12%)
  Pallas kernels  23.5 us (11%)
  other arithmetic  11.5 us (5%)
    pallas_call x1, Pallas kernels, attend_partial(): pl.pallas_call(kernel, out_shape=(jax.ShapeDtypeStruct((heads, rows, dim)...  23.5 us
    all_to_all x1, waiting for transfers between devices, body(): lax.all_to_all(jnp.broadcast_to(pair[None], (half_size,) + pair.shape), '...  19.7 us
    all_to_all x1, waiting for transfers between devices, body(): lax.all_to_all(by_dest.transpose(1, 0, 2, 3), 'hseq', split_axis=0, conca...  17.8 us
    ppermute x1, waiting for transfers between devices, body(): partner_rows = lax.ppermute(query_rows, 'half', perm=[(0, 1)])  13.1 us
    all_to_all x1, starting transfers between devices, body(): lax.all_to_all(jnp.broadcast_to(pair[None], (half_size,) + pair.shape), '...  12.4 us
    all_to_all x1, waiting for transfers between devices, body(): lax.all_to_all(projected.reshape(exp_count, -1, projected.shape[1]), 'exp...  11.2 us
    dot_general x1, matrix products, body(): jnp.einsum('ecd,edf->ecf', rows_in, expert_in, preferred_element_type=jnp...  10.2 us
    all_to_all x1, waiting for transfers between devices, body(): lax.all_to_all(outgoing, SEQ_AXES, split_axis=1, concat_axis=1, tiled=True)  7.42 us
  transfers between devices with their start and end apart: 11, of which 9 were waited for; matrix products, arithmetic and copies ran while one was open for 8% of the time, Pallas kernels for 11%

profile of v12, /device:TPU:0, one launch (start us, length us, event | category | flops | bytes accessed | tf_op | source)
XLA Modules:
  0.0 214.7 jit_solution(899612643755240067)
XLA Ops:
  0.7 1.5 fusion.7
  2.2 1.7 convolution_convert_fusion.5
  5.4 1.3 broadcast_in_dim.84
  6.7 5.2 %all-to-all-start = ((bf16[4,2,2,768,64]{3,4,2,1,0:T(8,128)(2,1)}), bf16[4,2,2,768,64]{3,4,2,1,0:T(8,128)(2,1)S(1)}, u32[]{:S(2)}, u32[]{:S(2)}) async-start(bf16[4,2,2,768,64]{3,4,2,1,0:T(8,128)(2,1)} %broadcast_in_dim.84), calls=%async_computation | async-start | bytes 3145728 | tf_op jit(solution)/shard_map/all_to_all | solution.py:196
  11.9 2.6 %convolution_convert_fusion.3 = bf16[256,384]{1,0:T(8,128)(2,1)} fusion(bf16[1536,384]{1,0:T(8,128)(2,1)} %param.19, bf16[256,1536]{1,0:T(8,128)(2,1)S(1)} %copy-done.4, f32[1536]{0:T(1024)S(1)} %copy-done.16, f32[256]{0:T(256)S(1)} %add_rsqrt_fusion), kind=kOutput, calls=%fused_computation.23 | convolution fusion | flops 303661056 | bytes 2169856 | tf_op jit(solution)/shard_map/dot_general | solution.py:158
  14.5 1.1 copy.176
  15.6 4.5 %collective-permute-start = (bf16[2,768,64]{1,2,0:T(8,128)(2,1)S(1)}, bf16[2,768,64]{1,2,0:T(8,128)(2,1)S(1)}, u32[]{:S(2)}, u32[]{:S(2)}) collective-permute-start(bf16[2,768,64]{1,2,0:T(8,128)(2,1)S(1)} %bitcast.91), channel_id=1, source_target_pairs={{0,16},{1,17},{2,18},{3,19},{4,20},{5,21},{6,22},{7,23},{8,24},{9,... | collective-permute-start | bytes 589832 | tf_op jit(solution)/shard_map/ppermute | solution.py:205
  20.1 13.1 %collective-permute-done = bf16[2,768,64]{1,2,0:T(8,128)(2,1)S(1)} collective-permute-done((bf16[2,768,64]{1,2,0:T(8,128)(2,1)S(1)}, bf16[2,768,64]{1,2,0:T(8,128)(2,1)S(1)}, u32[]{:S(2)}, u32[]{:S(2)}) %collective-permute-start) | collective-permute-done | bytes 196640 | tf_op jit(solution)/shard_map/ppermute | solution.py:205
  33.2 2.8 %conditional.3 = ((f32[2,768,64]{2,1,0:T(8,128)}, f32[2,768,1]{2,1,0:T(8,128)}, f32[2,768,1]{2,1,0:T(8,128)})) conditional(s32[]{:T(128)} %convert_element_type.85, (s32[1]{0:T(128)}, bf16[2,768,64]{1,2,0:T(8,128)(2,1)S(1)}, bf16[4,2,2,768,64]{3,4,2,1,0:T(8,128)(2,1)S(1)}) %tuple.22, () %tuple.23), branch_computations={%region_3.4_spmd, %region_4.5_spmd} | conditional | bytes 3538952 | solution.py:217
  33.2 1.0 broadcast.101
  34.2 1.0 broadcast.99
  35.1 0.9 broadcast.100
  36.0 2.1 copy.192
  38.2 1.3 collective-permute-start.2
  39.5 1.4 copy.188
  40.9 1.4 copy.194
  42.3 1.3 collective-permute-start.3
  43.6 1.3 collective-permute-start.1
  44.9 30.4 %conditional.2 = (f32[2,768,64]{1,2,0:T(8,128)S(1)}, f32[2,768,1]{1,0,2:T(2,128)S(1)}, f32[2,768,1]{1,0,2:T(2,128)S(1)}) conditional(s32[]{:T(128)} %convert_element_type.85, (s32[1]{0:T(128)}, bf16[2,768,64]{1,2,0:T(8,128)(2,1)S(1)}, bf16[4,2,2,768,64]{3,4,2,1,0:T(8,128)(2,1)S(1)}) %tuple.64, (s32[1]{0:T(128)}, bf16[2,768,64]{1,2,0:T(8,128)(2,1)S(1)}, ...), branch_computations={%region_1.2_spmd, %region_2.3_spmd} | conditional | bytes 4374580 | solution.py:223
  44.9 0.9 copy.184.q_ref
  45.8 2.8 %copy.185.k_ref.v_ref = bf16[4,2,2,768,64]{4,3,2,1,0:T(8,128)(2,1)} copy(bf16[4,2,2,768,64]{3,4,2,1,0:T(8,128)(2,1)S(1)} %get-tuple-element.90) | data formatting | bytes 3145728 | tf_op jit(solution)/shard_map
  48.6 23.5 %branch_1_fun.1 = (f32[2,768,64]{2,1,0:T(8,128)}, f32[2,768,1]{2,1,0:T(8,128)}, f32[2,768,1]{2,1,0:T(8,128)}) custom-call(s32[1]{0:T(128)} %get-tuple-element.21.flags_ref, bf16[2,768,64]{2,1,0:T(8,128)(2,1)} %copy.184.q_ref, bf16[4,2,2,768,64]{4,3,2,1,0:T(8,128)(2,1)} %copy.185.k_ref.v_ref, bf16[4,2,2,768,64]{4,3,2,1,0:T(8,128)(2,1)} %copy.185.k_ref.v_ref), custom_call_target="tpu_custom_call" | custom-call | tf_op jit(solution)/shard_map/cond/branch_1_fun/pallas_call | solution.py:96
  72.1 1.5 copy.213
  73.6 1.4 copy.215
  75.2 3.9 %collective-permute-done.3 = f32[2,768,1]{1,0,2:T(2,128)S(1)} collective-permute-done((f32[2,768,1]{1,0,2:T(2,128)S(1)}, f32[2,768,1]{1,0,2:T(2,128)S(1)}, u32[]{:S(2)}, u32[]{:S(2)}) %collective-permute-start.3) | collective-permute-done | bytes 6176 | tf_op jit(solution)/shard_map/ppermute | solution.py:229
  79.4 1.5 convolution_convert_fusion.2
  80.9 3.8 %all-to-all-start.1 = ((bf16[4,64,1536]{2,1,0:T(8,128)(2,1)}), bf16[4,64,1536]{2,1,0:T(8,128)(2,1)S(1)}, u32[]{:S(2)}, u32[]{:S(2)}) async-start(bf16[4,64,1536]{2,1,0:T(8,128)(2,1)} %bitcast.15), calls=%async_computation.1 | async-start | bytes 1572864 | tf_op jit(solution)/shard_map/all_to_all | solution.py:244
  85.2 11.2 %all-to-all-done.1 = bf16[4,64,1536]{2,1,0:T(8,128)(2,1)S(1)} async-done(((bf16[4,64,1536]{2,1,0:T(8,128)(2,1)}), bf16[4,64,1536]{2,1,0:T(8,128)(2,1)S(1)}, u32[]{:S(2)}, u32[]{:S(2)}) %all-to-all-start.1) | async-done | bytes 786464 | tf_op jit(solution)/shard_map/all_to_all | solution.py:244
  96.9 4.5 %collective-permute-start.4 = (bf16[64,1664]{1,0:T(8,128)(2,1)S(1)}, bf16[64,1664]{1,0:T(8,128)(2,1)S(1)}, u32[]{:S(2)}, u32[]{:S(2)}) collective-permute-start(bf16[64,1664]{1,0:T(8,128)(2,1)S(1)} %concatenate.15), channel_id=1, source_target_pairs={{0,16},{16,0},{1,17},{17,1},{2,18},{18,2},{3,19},{19,3},{4,20},{20... | collective-permute-start | bytes 638984 | tf_op jit(solution)/shard_map/ppermute | solution.py:276
  101.4 5.1 %collective-permute-done.4 = bf16[64,1664]{1,0:T(8,128)(2,1)S(1)} collective-permute-done((bf16[64,1664]{1,0:T(8,128)(2,1)S(1)}, bf16[64,1664]{1,0:T(8,128)(2,1)S(1)}, u32[]{:S(2)}, u32[]{:S(2)}) %collective-permute-start.4) | collective-permute-done | bytes 213024 | tf_op jit(solution)/shard_map/ppermute | solution.py:276
  106.5 1.3 broadcast_in_dim.91
  107.9 12.4 %all-to-all-start.2 = ((bf16[4,2,64,1664]{3,2,1,0:T(8,128)(2,1)}), bf16[4,2,64,1664]{3,2,1,0:T(8,128)(2,1)S(1)}, u32[]{:S(2)}, u32[]{:S(2)}) async-start(bf16[4,2,64,1664]{3,2,1,0:T(8,128)(2,1)} %broadcast_in_dim.91), calls=%async_computation.2 | async-start | bytes 3407872 | tf_op jit(solution)/shard_map/all_to_all | solution.py:280
  120.4 19.7 %all-to-all-done.2 = bf16[4,2,64,1664]{3,2,1,0:T(8,128)(2,1)S(1)} async-done(((bf16[4,2,64,1664]{3,2,1,0:T(8,128)(2,1)}), bf16[4,2,64,1664]{3,2,1,0:T(8,128)(2,1)S(1)}, u32[]{:S(2)}, u32[]{:S(2)}) %all-to-all-start.2) | async-done | bytes 1703968 | tf_op jit(solution)/shard_map/all_to_all | solution.py:280
  140.5 1.0 copy-done.6
  142.1 6.3 %fusion.46 = s32[8,64,4]{2,0,1:T(8,128)S(1)} fusion(s32[8,64,4]{2,0,1:T(8,128)S(1)} %copy.201), kind=kOutput, calls=%fused_computation.86 | output fusion | flops 129024 | bytes 16384 | tf_op jit(solution)/shard_map/jit(cumsum)/reduce_window_sum | solution.py:298
  148.7 10.2 %fusion.47 = f32[4,256,1024]{2,1,0:T(8,128)} fusion(bf16[4,1536,1024]{2,1,0:T(8,128)(2,1)} %param.25, bf16[512,1664]{1,0:T(8,128)(2,1)} %bitcast.90, s32[512,4]{0,1:T(4,128)S(1)} %subtract_add_fusion, pred[512,4]{0,1:T(4,128)(4,1)S(1)} %get-tuple-element.106), kind=kOutput, calls=%fused_computation.87 | convolution fusion | flops 4834459648 | bytes 18360320 | tf_op jit(solution)/shard_map/ecd,edf->ecf/dot_general | solution.py:310
  158.9 5.9 %convolution_convert_fusion.1 = bf16[4,256,1536]{2,1,0:T(8,128)(2,1)S(1)} fusion(bf16[4,512,1536]{2,1,0:T(8,128)(2,1)} %param.26, f32[4,256,1024]{2,1,0:T(8,128)} %fusion.47), kind=kOutput, calls=%fused_computation.2 | convolution fusion | flops 1615331328 | bytes 13631488 | tf_op jit(solution)/shard_map/ecf,efd->ecd/dot_general | solution.py:313
  164.8 2.1 convolution_bitcast_fusion
  166.9 2.9 %fusion.1 = bf16[512,1536]{1,0:T(8,128)(2,1)S(1)} fusion(f32[512,1536]{1,0:T(8,128)S(1)} %convolution_bitcast_fusion, bf16[4,256,1536]{2,1,0:T(8,128)(2,1)S(1)} %convolution_convert_fusion.1, s32[512,4]{0,1:T(4,128)S(1)} %subtract_add_fusion, pred[512,4]{0,1:T(4,128)(4,1)S(1)} %get-tuple-element.106, bf16[512,4]{0,1:T(4,128)(2,1)S(1)} %copy.221), kind=kOutput, calls=%fused_computation.7 | convolution fusion | flops 1613758464 | bytes 7878656 | tf_op jit(solution)/shard_map/nec,ecd->nd/dot_general | solution.py:318
  169.8 1.3 copy.229
  171.2 3.7 %all-to-all-start.3 = ((bf16[4,2,64,1536]{3,2,1,0:T(8,128)(2,1)}), bf16[4,2,64,1536]{3,2,1,0:T(8,128)(2,1)S(1)}, u32[]{:S(2)}, u32[]{:S(2)}) async-start(bf16[4,2,64,1536]{3,2,1,0:T(8,128)(2,1)} %bitcast.88), calls=%async_computation.3 | async-start | bytes 3145728 | tf_op jit(solution)/shard_map/all_to_all | solution.py:322
  176.4 17.8 %all-to-all-done.3 = bf16[4,2,64,1536]{3,2,1,0:T(8,128)(2,1)S(1)} async-done(((bf16[4,2,64,1536]{3,2,1,0:T(8,128)(2,1)}), bf16[4,2,64,1536]{3,2,1,0:T(8,128)(2,1)S(1)}, u32[]{:S(2)}, u32[]{:S(2)}) %all-to-all-start.3) | async-done | bytes 1572896 | tf_op jit(solution)/shard_map/all_to_all | solution.py:322
  194.2 3.8 %all-to-all-start.4 = ((bf16[4,8,2048]{2,0,1:T(4,128)(2,1)}), bf16[4,8,2048]{2,0,1:T(4,128)(2,1)S(1)}, u32[]{:S(2)}, u32[]{:S(2)}) async-start(bf16[4,8,2048]{2,0,1:T(4,128)(2,1)} %copy.206), calls=%async_computation.4 | async-start | bytes 262144 | tf_op jit(solution)/shard_map/all_to_all | solution.py:173
  198.3 0.9 copy-done.2
  199.2 3.0 %collective-permute-start.5 = (bf16[64,1536]{1,0:T(8,128)(2,1)S(1)}, bf16[64,1536]{1,0:T(8,128)(2,1)S(1)}, u32[]{:S(2)}, u32[]{:S(2)}) collective-permute-start(bf16[64,1536]{1,0:T(8,128)(2,1)S(1)} %fusion.27), channel_id=1, source_target_pairs={{0,16},{16,0},{1,17},{17,1},{2,18},{18,2},{3,19},{19,3},{4,20},{20... | collective-permute-start | bytes 589832 | tf_op jit(solution)/shard_map/ppermute | solution.py:328
  202.2 7.4 %all-to-all-done.4 = bf16[4,8,2048]{2,0,1:T(4,128)(2,1)S(1)} async-done(((bf16[4,8,2048]{2,0,1:T(4,128)(2,1)}), bf16[4,8,2048]{2,0,1:T(4,128)(2,1)S(1)}, u32[]{:S(2)}, u32[]{:S(2)}) %all-to-all-start.4) | async-done | bytes 131104 | tf_op jit(solution)/shard_map/all_to_all | solution.py:173
  211.7 1.3 collective-permute-done.5
  213.0 1.7 fusion.26
  (90 shorter events, 8.1 us)
Async XLA Ops:
  0.6 78.8 %copy-start = (bf16[384,1536]{1,0:T(8,128)(2,1)S(1)}, bf16[384,1536]{1,0:T(8,128)(2,1)}, u32[]{:S(2)}) copy-start(bf16[384,1536]{1,0:T(8,128)(2,1)} %param.22) | copy-start | bytes 3538948
  0.6 3.3 %copy-start.4 = (bf16[256,1536]{1,0:T(8,128)(2,1)S(1)}, bf16[256,1536]{1,0:T(8,128)(2,1)}, u32[]{:S(2)}) copy-start(bf16[256,1536]{1,0:T(8,128)(2,1)} %param.17) | copy-start | bytes 2359300
  0.7 3.3 %copy-start.16 = (f32[1536]{0:T(1024)S(1)}, f32[1536]{0:T(1024)}, u32[]{:S(2)}) copy-start(f32[1536]{0:T(1024)} %param.18) | copy-start | bytes 18436
  0.7 3.3 %copy-start.15 = (bf16[1536,128]{1,0:T(8,128)(2,1)S(1)}, bf16[1536,128]{1,0:T(8,128)(2,1)}, u32[]{:S(2)}) copy-start(bf16[1536,128]{1,0:T(8,128)(2,1)} %param.21) | copy-start | bytes 1179652
  0.7 3.8 %copy-start.10 = (bf16[512,256]{1,0:T(8,128)(2,1)S(1)}, bf16[512,256]{1,0:T(8,128)(2,1)}, u32[]{:S(2)}) copy-start(bf16[512,256]{1,0:T(8,128)(2,1)} %param.23) | copy-start | bytes 786436
  6.7 26.5 %all-to-all-start = ((bf16[4,2,2,768,64]{3,4,2,1,0:T(8,128)(2,1)}), bf16[4,2,2,768,64]{3,4,2,1,0:T(8,128)(2,1)S(1)}, u32[]{:S(2)}, u32[]{:S(2)}) async-start(bf16[4,2,2,768,64]{3,4,2,1,0:T(8,128)(2,1)} %broadcast_in_dim.84), calls=%async_computation | async-start | bytes 3145728 | tf_op jit(solution)/shard_map/all_to_all | solution.py:196
  15.6 17.6 %collective-permute-start = (bf16[2,768,64]{1,2,0:T(8,128)(2,1)S(1)}, bf16[2,768,64]{1,2,0:T(8,128)(2,1)S(1)}, u32[]{:S(2)}, u32[]{:S(2)}) collective-permute-start(bf16[2,768,64]{1,2,0:T(8,128)(2,1)S(1)} %bitcast.91), channel_id=1, source_target_pairs={{0,16},{1,17},{2,18},{3,19},{4,20},{5,21},{6,22},{7,23},{8,24},{9,... | collective-permute-start | bytes 589832 | tf_op jit(solution)/shard_map/ppermute | solution.py:205
  38.2 41.0 %collective-permute-start.2 = (f32[2,768,64]{1,2,0:T(8,128)}, f32[2,768,64]{1,2,0:T(8,128)S(1)}, u32[]{:S(2)}, u32[]{:S(2)}) collective-permute-start(f32[2,768,64]{1,2,0:T(8,128)} %copy.192), channel_id=1, source_target_pairs={{16,0},{17,1},{18,2},{19,3},{20,4},{21,5},{22,6},{23,7},{24,8},{25... | collective-permute-start | bytes 1179656 | tf_op jit(solution)/shard_map/ppermute | solution.py:229
  42.3 36.8 %collective-permute-start.3 = (f32[2,768,1]{1,0,2:T(2,128)S(1)}, f32[2,768,1]{1,0,2:T(2,128)S(1)}, u32[]{:S(2)}, u32[]{:S(2)}) collective-permute-start(f32[2,768,1]{1,0,2:T(2,128)S(1)} %copy.194), channel_id=1, source_target_pairs={{16,0},{17,1},{18,2},{19,3},{20,4},{21,5},{22,6},{23,7},{24,8},{25... | collective-permute-start | bytes 18440 | tf_op jit(solution)/shard_map/ppermute | solution.py:229
  43.6 35.6 %collective-permute-start.1 = (f32[2,768,1]{1,0,2:T(2,128)S(1)}, f32[2,768,1]{1,0,2:T(2,128)S(1)}, u32[]{:S(2)}, u32[]{:S(2)}) collective-permute-start(f32[2,768,1]{1,0,2:T(2,128)S(1)} %copy.188), channel_id=1, source_target_pairs={{16,0},{17,1},{18,2},{19,3},{20,4},{21,5},{22,6},{23,7},{24,8},{25... | collective-permute-start | bytes 18440 | tf_op jit(solution)/shard_map/ppermute | solution.py:229
  72.1 2.9 %copy-start.8 = (f32[2,768,1]{2,1,0:T(8,128)S(1)}, f32[2,768,1]{2,1,0:T(8,128)}, u32[]{:S(2)}) copy-start(f32[2,768,1]{2,1,0:T(8,128)} %get-tuple-element.101) | copy-start | bytes 18436 | tf_op jit(solution)/shard_map/cond
  79.3 5.4 %copy-start.12 = (s32[64,8]{0,1:T(8,128)S(1)}, s32[64,8]{0,1:T(8,128)}, u32[]{:S(2)}) copy-start(s32[64,8]{0,1:T(8,128)} %param.27) | copy-start | bytes 6148
  79.4 5.5 %copy-start.11 = (f32[64,8]{0,1:T(8,128)S(1)}, f32[64,8]{0,1:T(8,128)}, u32[]{:S(2)}) copy-start(f32[64,8]{0,1:T(8,128)} %param.28) | copy-start | bytes 6148
  79.4 17.1 %copy-start.5 = (bf16[256,1536]{1,0:T(8,128)(2,1)S(1)}, bf16[256,1536]{1,0:T(8,128)(2,1)}, u32[]{:S(2)}) copy-start(bf16[256,1536]{1,0:T(8,128)(2,1)} %param.17) | copy-start | bytes 2359300
  80.9 15.7 %copy-start.13 = (f32[1536]{0:T(1024)S(1)}, f32[1536]{0:T(1024)}, u32[]{:S(2)}) copy-start(f32[1536]{0:T(1024)} %param.24) | copy-start | bytes 18436
  80.9 15.4 %all-to-all-start.1 = ((bf16[4,64,1536]{2,1,0:T(8,128)(2,1)}), bf16[4,64,1536]{2,1,0:T(8,128)(2,1)S(1)}, u32[]{:S(2)}, u32[]{:S(2)}) async-start(bf16[4,64,1536]{2,1,0:T(8,128)(2,1)} %bitcast.15), calls=%async_computation.1 | async-start | bytes 1572864 | tf_op jit(solution)/shard_map/all_to_all | solution.py:244
  96.9 9.6 %collective-permute-start.4 = (bf16[64,1664]{1,0:T(8,128)(2,1)S(1)}, bf16[64,1664]{1,0:T(8,128)(2,1)S(1)}, u32[]{:S(2)}, u32[]{:S(2)}) collective-permute-start(bf16[64,1664]{1,0:T(8,128)(2,1)S(1)} %concatenate.15), channel_id=1, source_target_pairs={{0,16},{16,0},{1,17},{17,1},{2,18},{18,2},{3,19},{19,3},{4,20},{20... | collective-permute-start | bytes 638984 | tf_op jit(solution)/shard_map/ppermute | solution.py:276
  107.9 32.2 %all-to-all-start.2 = ((bf16[4,2,64,1664]{3,2,1,0:T(8,128)(2,1)}), bf16[4,2,64,1664]{3,2,1,0:T(8,128)(2,1)S(1)}, u32[]{:S(2)}, u32[]{:S(2)}) async-start(bf16[4,2,64,1664]{3,2,1,0:T(8,128)(2,1)} %broadcast_in_dim.91), calls=%async_computation.2 | async-start | bytes 3407872 | tf_op jit(solution)/shard_map/all_to_all | solution.py:280
  140.2 1.2 copy-start.6
  171.2 3.9 %copy-start.9 = (bf16[256,2,2,64]{0,3,2,1:T(8,128)(2,1)S(1)}, bf16[256,2,2,64]{0,3,2,1:T(8,128)(2,1)}, u32[]{:S(2)}) copy-start(bf16[256,2,2,64]{0,3,2,1:T(8,128)(2,1)} %get-tuple-element.109) | copy-start | bytes 393220
  171.2 5.1 %copy-start.14 = (s32[256]{0:T(256)S(1)}, s32[256]{0:T(256)}, u32[]{:S(2)}) copy-start(s32[256]{0:T(256)} %param.29) | copy-start | bytes 3076
  171.2 23.1 %all-to-all-start.3 = ((bf16[4,2,64,1536]{3,2,1,0:T(8,128)(2,1)}), bf16[4,2,64,1536]{3,2,1,0:T(8,128)(2,1)S(1)}, u32[]{:S(2)}, u32[]{:S(2)}) async-start(bf16[4,2,64,1536]{3,2,1,0:T(8,128)(2,1)} %bitcast.88), calls=%async_computation.3 | async-start | bytes 3145728 | tf_op jit(solution)/shard_map/all_to_all | solution.py:322
  194.2 15.4 %all-to-all-start.4 = ((bf16[4,8,2048]{2,0,1:T(4,128)(2,1)}), bf16[4,8,2048]{2,0,1:T(4,128)(2,1)S(1)}, u32[]{:S(2)}, u32[]{:S(2)}) async-start(bf16[4,8,2048]{2,0,1:T(4,128)(2,1)} %copy.206), calls=%async_computation.4 | async-start | bytes 262144 | tf_op jit(solution)/shard_map/all_to_all | solution.py:173
  198.0 16.7 %copy-start.1 = (bf16[384,1536]{1,0:T(8,128)(2,1)S(1)}, bf16[384,1536]{1,0:T(8,128)(2,1)}, u32[]{:S(2)}) copy-start(bf16[384,1536]{1,0:T(8,128)(2,1)} %param.22) | copy-start | bytes 3538948
  198.3 0.9 copy-start.2
  199.2 13.8 %copy-start.3 = (f32[2,64,1536]{2,1,0:T(8,128)S(1)}, f32[2,64,1536]{2,1,0:T(8,128)}, u32[]{:S(2)}) copy-start(f32[2,64,1536]{2,1,0:T(8,128)} %copy-done.2) | copy-start | bytes 2359300
  199.2 13.8 %collective-permute-start.5 = (bf16[64,1536]{1,0:T(8,128)(2,1)S(1)}, bf16[64,1536]{1,0:T(8,128)(2,1)S(1)}, u32[]{:S(2)}, u32[]{:S(2)}) collective-permute-start(bf16[64,1536]{1,0:T(8,128)(2,1)S(1)} %fusion.27), channel_id=1, source_target_pairs={{0,16},{16,0},{1,17},{17,1},{2,18},{18,2},{3,19},{19,3},{4,20},{20... | collective-permute-start | bytes 589832 | tf_op jit(solution)/shard_map/ppermute | solution.py:328

commit v13 on v12

--- a/solution.py
+++ b/solution.py
@@ -203,6 +203,7 @@
     query_rows = queries.reshape(tokens_here, kv_local, group_size, head_dim)
     query_rows = query_rows.transpose(1, 2, 0, 3).reshape(kv_local, group_size * tokens_here, head_dim)
     partner_rows = lax.ppermute(query_rows, "half", perm=[(0, 1)])
+    received, partner_rows = lax.optimization_barrier((received, partner_rows))
     flags = jnp.reshape(half_pos * tokens_here, (1,)).astype(jnp.int32)
     shapes = dict(cache_rows=cache_rows, group_rows=tokens_here)
 

time: 216 us -> 227 us (1.051)
  local copies, waits for them, and re-layouts: 26.9 us -> 32.4 us
  starting transfers between devices: 44.7 us -> 47.8 us
    ppermute x1, waiting for transfers between devices: 1.35 us -> 6.09 us  [body(): lax.ppermute(other_sum.astype(jnp.bfloat16), 'half', perm=[(0, 1), (1, 0)])]
    ppermute x1, starting transfers between devices: 4.51 us -> 8.72 us  [body(): crossed = lax.ppermute(packed, 'half', perm=[(0, 1), (1, 0)])]
    all_to_all x1, starting transfers between devices: 3.8 us -> 7.24 us  [body(): lax.all_to_all(outgoing, SEQ_AXES, split_axis=1, concat_axis=1, tiled=True)]
    ppermute x3, waiting for transfers between devices: 3.92 us -> 0.88 us  [body(): lax.ppermute(far_part, 'half', perm=[(1, 0)])]
  transfers between devices with their start and end apart: 11 -> 11, of which waited for: 9 -> 9; matrix products, arithmetic and copies ran while one was open for 8% -> 10% of each run, Pallas kernels for 11% -> 10%
where the time goes in v13:
time: 227 us; the launch traced here: 226 us
  waiting for transfers between devices  81 us (36%)
  starting transfers between devices  47.8 us (21%)
  local copies, waits for them, and re-layouts  32.4 us (14%)
  matrix products  27.4 us (12%)
  Pallas kernels  23.5 us (10%)
  other arithmetic  12.6 us (6%)
    pallas_call x1, Pallas kernels, attend_partial(): pl.pallas_call(kernel, out_shape=(jax.ShapeDtypeStruct((heads, rows, dim)...  23.5 us
    all_to_all x1, waiting for transfers between devices, body(): lax.all_to_all(jnp.broadcast_to(pair[None], (half_size,) + pair.shape), '...  20.4 us
    all_to_all x1, waiting for transfers between devices, body(): lax.all_to_all(by_dest.transpose(1, 0, 2, 3), 'hseq', split_axis=0, conca...  19 us
    ppermute x1, waiting for transfers between devices, body(): partner_rows = lax.ppermute(query_rows, 'half', perm=[(0, 1)])  11.3 us
    all_to_all x1, waiting for transfers between devices, body(): lax.all_to_all(projected.reshape(exp_count, -1, projected.shape[1]), 'exp...  11.2 us
    all_to_all x1, starting transfers between devices, body(): lax.all_to_all(jnp.broadcast_to(pair[None], (half_size,) + pair.shape), '...  10.5 us
    dot_general x1, matrix products, body(): jnp.einsum('ecd,edf->ecf', rows_in, expert_in, preferred_element_type=jnp...  10.2 us
    ppermute x1, starting transfers between devices, body(): crossed = lax.ppermute(packed, 'half', perm=[(0, 1), (1, 0)])  8.72 us
  transfers between devices with their start and end apart: 11, of which 9 were waited for; matrix products, arithmetic and copies ran while one was open for 10% of the time, Pallas kernels for 10%

profile of v13, /device:TPU:0, one launch (start us, length us, event | category | flops | bytes accessed | tf_op | source)
XLA Modules:
  0.0 226.0 jit_solution(10870278283436279785)
XLA Ops:
  0.7 1.5 fusion.7
  2.2 1.7 convolution_convert_fusion.5
  5.7 7.2 %all-to-all-start.1 = ((bf16[4,8,2048]{2,0,1:T(4,128)(2,1)}), bf16[4,8,2048]{2,0,1:T(4,128)(2,1)S(1)}, u32[]{:S(2)}, u32[]{:S(2)}) async-start(bf16[4,8,2048]{2,0,1:T(4,128)(2,1)} %copy.187), calls=%async_computation.1 | async-start | bytes 262144 | tf_op jit(solution)/shard_map/all_to_all | solution.py:173
  13.2 7.1 %all-to-all-done.1 = bf16[4,8,2048]{2,0,1:T(4,128)(2,1)S(1)} async-done(((bf16[4,8,2048]{2,0,1:T(4,128)(2,1)}), bf16[4,8,2048]{2,0,1:T(4,128)(2,1)S(1)}, u32[]{:S(2)}, u32[]{:S(2)}) %all-to-all-start.1) | async-done | bytes 131104 | tf_op jit(solution)/shard_map/all_to_all | solution.py:173
  20.3 1.3 broadcast_in_dim.84
  21.6 3.6 %all-to-all-start = ((bf16[4,2,2,768,64]{3,4,2,1,0:T(8,128)(2,1)}), bf16[4,2,2,768,64]{3,4,2,1,0:T(8,128)(2,1)S(1)}, u32[]{:S(2)}, u32[]{:S(2)}) async-start(bf16[4,2,2,768,64]{3,4,2,1,0:T(8,128)(2,1)} %broadcast_in_dim.84), calls=%async_computation | async-start | bytes 3145728 | tf_op jit(solution)/shard_map/all_to_all | solution.py:196
  25.2 2.6 %convolution_convert_fusion.3 = bf16[256,384]{1,0:T(8,128)(2,1)} fusion(bf16[1536,384]{1,0:T(8,128)(2,1)} %param.19, bf16[256,1536]{1,0:T(8,128)(2,1)S(1)} %copy-done.4, f32[1536]{0:T(1024)S(1)} %copy-done.15, f32[256]{0:T(256)S(1)} %add_rsqrt_fusion), kind=kOutput, calls=%fused_computation.23 | convolution fusion | flops 303661056 | bytes 2169856 | tf_op jit(solution)/shard_map/dot_general | solution.py:158
  27.8 1.7 copy.176
  29.5 1.6 copy.223
  31.1 3.0 %collective-permute-start = (bf16[2,768,64]{1,2,0:T(8,128)(2,1)}, bf16[2,768,64]{1,2,0:T(8,128)(2,1)}, u32[]{:S(2)}, u32[]{:S(2)}) collective-permute-start(bf16[2,768,64]{1,2,0:T(8,128)(2,1)} %bitcast.37), channel_id=1, source_target_pairs={{0,16},{1,17},{2,18},{3,19},{4,20},{5,21},{6,22},{7,23},{8,24},{9,... | collective-permute-start | bytes 589832 | tf_op jit(solution)/shard_map/ppermute | solution.py:205
  34.1 11.3 %collective-permute-done = bf16[2,768,64]{1,2,0:T(8,128)(2,1)} collective-permute-done((bf16[2,768,64]{1,2,0:T(8,128)(2,1)}, bf16[2,768,64]{1,2,0:T(8,128)(2,1)}, u32[]{:S(2)}, u32[]{:S(2)}) %collective-permute-start) | collective-permute-done | bytes 196640 | tf_op jit(solution)/shard_map/ppermute | solution.py:205
  45.4 2.8 %conditional.3 = ((f32[2,768,64]{2,1,0:T(8,128)}, f32[2,768,1]{2,1,0:T(8,128)}, f32[2,768,1]{2,1,0:T(8,128)})) conditional(s32[]{:T(128)} %convert_element_type.85, (s32[1]{0:T(128)}, bf16[2,768,64]{1,2,0:T(8,128)(2,1)}, bf16[4,2,2,768,64]{3,4,2,1,0:T(8,128)(2,1)S(1)}) %tuple.24, () %tuple.25), branch_computations={%region_3.4_spmd, %region_4.5_spmd} | conditional | bytes 3538952 | solution.py:218
  45.4 1.0 broadcast.101
  46.4 1.0 broadcast.99
  47.4 0.9 broadcast.100
  48.3 2.1 copy.194
  50.4 1.3 collective-permute-start.2
  51.7 2.0 copy.190
  53.7 2.0 copy.196
  55.7 1.3 collective-permute-start.3
  57.0 1.3 collective-permute-start.1
  58.3 31.5 %conditional.2 = (f32[2,768,64]{1,2,0:T(8,128)S(1)}, f32[2,768,1]{1,0,2:T(2,128)S(1)}, f32[2,768,1]{1,0,2:T(2,128)S(1)}) conditional(s32[]{:T(128)} %convert_element_type.85, (s32[1]{0:T(128)}, bf16[2,768,64]{1,2,0:T(8,128)(2,1)}, bf16[4,2,2,768,64]{3,4,2,1,0:T(8,128)(2,1)S(1)}) %tuple.22, (s32[1]{0:T(128)}, bf16[2,768,64]{1,2,0:T(8,128)(2,1)}, ...), branch_computations={%region_1.2_spmd, %region_2.3_spmd} | conditional | bytes 4374580 | solution.py:224
  58.3 1.9 copy.184.q_ref
  60.2 2.8 %copy.185.k_ref.v_ref = bf16[4,2,2,768,64]{4,3,2,1,0:T(8,128)(2,1)} copy(bf16[4,2,2,768,64]{3,4,2,1,0:T(8,128)(2,1)S(1)} %get-tuple-element.92) | data formatting | bytes 3145728 | tf_op jit(solution)/shard_map
  63.0 23.5 %branch_1_fun.1 = (f32[2,768,64]{2,1,0:T(8,128)}, f32[2,768,1]{2,1,0:T(8,128)}, f32[2,768,1]{2,1,0:T(8,128)}) custom-call(s32[1]{0:T(128)} %get-tuple-element.21.flags_ref, bf16[2,768,64]{2,1,0:T(8,128)(2,1)} %copy.184.q_ref, bf16[4,2,2,768,64]{4,3,2,1,0:T(8,128)(2,1)} %copy.185.k_ref.v_ref, bf16[4,2,2,768,64]{4,3,2,1,0:T(8,128)(2,1)} %copy.185.k_ref.v_ref), custom_call_target="tpu_custom_call" | custom-call | tf_op jit(solution)/shard_map/cond/branch_1_fun/pallas_call | solution.py:96
  86.5 1.5 copy.213
  88.0 1.4 copy.215
  91.4 1.1 divide_convert_fusion
  92.6 1.5 convolution_convert_fusion.2
  94.1 3.6 %all-to-all-start.2 = ((bf16[4,64,1536]{2,1,0:T(8,128)(2,1)}), bf16[4,64,1536]{2,1,0:T(8,128)(2,1)S(1)}, u32[]{:S(2)}, u32[]{:S(2)}) async-start(bf16[4,64,1536]{2,1,0:T(8,128)(2,1)} %bitcast.15), calls=%async_computation.2 | async-start | bytes 1572864 | tf_op jit(solution)/shard_map/all_to_all | solution.py:245
  98.2 11.2 %all-to-all-done.2 = bf16[4,64,1536]{2,1,0:T(8,128)(2,1)S(1)} async-done(((bf16[4,64,1536]{2,1,0:T(8,128)(2,1)}), bf16[4,64,1536]{2,1,0:T(8,128)(2,1)S(1)}, u32[]{:S(2)}, u32[]{:S(2)}) %all-to-all-start.2) | async-done | bytes 786464 | tf_op jit(solution)/shard_map/all_to_all | solution.py:245
  109.9 8.7 %collective-permute-start.4 = (bf16[64,1664]{1,0:T(8,128)(2,1)S(1)}, bf16[64,1664]{1,0:T(8,128)(2,1)S(1)}, u32[]{:S(2)}, u32[]{:S(2)}) collective-permute-start(bf16[64,1664]{1,0:T(8,128)(2,1)S(1)} %concatenate.15), channel_id=1, source_target_pairs={{0,16},{16,0},{1,17},{17,1},{2,18},{18,2},{3,19},{19,3},{4,20},{20... | collective-permute-start | bytes 638984 | tf_op jit(solution)/shard_map/ppermute | solution.py:277
  118.7 5.1 %collective-permute-done.4 = bf16[64,1664]{1,0:T(8,128)(2,1)S(1)} collective-permute-done((bf16[64,1664]{1,0:T(8,128)(2,1)S(1)}, bf16[64,1664]{1,0:T(8,128)(2,1)S(1)}, u32[]{:S(2)}, u32[]{:S(2)}) %collective-permute-start.4) | collective-permute-done | bytes 213024 | tf_op jit(solution)/shard_map/ppermute | solution.py:277
  123.8 1.3 broadcast_in_dim.91
  125.1 10.5 %all-to-all-start.3 = ((bf16[4,2,64,1664]{3,2,1,0:T(8,128)(2,1)}), bf16[4,2,64,1664]{3,2,1,0:T(8,128)(2,1)S(1)}, u32[]{:S(2)}, u32[]{:S(2)}) async-start(bf16[4,2,64,1664]{3,2,1,0:T(8,128)(2,1)} %broadcast_in_dim.91), calls=%async_computation.3 | async-start | bytes 3407872 | tf_op jit(solution)/shard_map/all_to_all | solution.py:281
  135.7 20.4 %all-to-all-done.3 = bf16[4,2,64,1664]{3,2,1,0:T(8,128)(2,1)S(1)} async-done(((bf16[4,2,64,1664]{3,2,1,0:T(8,128)(2,1)}), bf16[4,2,64,1664]{3,2,1,0:T(8,128)(2,1)S(1)}, u32[]{:S(2)}, u32[]{:S(2)}) %all-to-all-start.3) | async-done | bytes 1703968 | tf_op jit(solution)/shard_map/all_to_all | solution.py:281
  156.1 1.4 copy.201
  159.2 6.3 %fusion.46 = s32[8,64,4]{2,0,1:T(8,128)S(1)} fusion(s32[8,64,4]{2,0,1:T(8,128)S(1)} %copy.203), kind=kOutput, calls=%fused_computation.86 | output fusion | flops 129024 | bytes 16384 | tf_op jit(solution)/shard_map/jit(cumsum)/reduce_window_sum | solution.py:299
  165.8 10.2 %fusion.47 = f32[4,256,1024]{2,1,0:T(8,128)} fusion(bf16[4,1536,1024]{2,1,0:T(8,128)(2,1)} %param.25, bf16[512,1664]{1,0:T(8,128)(2,1)} %bitcast.19, s32[512,4]{0,1:T(4,128)S(1)} %subtract_add_fusion, pred[512,4]{0,1:T(4,128)(4,1)S(1)} %get-tuple-element.108), kind=kOutput, calls=%fused_computation.87 | convolution fusion | flops 4834459648 | bytes 18360320 | tf_op jit(solution)/shard_map/ecd,edf->ecf/dot_general | solution.py:311
  176.0 5.9 %convolution_convert_fusion.1 = bf16[4,256,1536]{2,1,0:T(8,128)(2,1)S(1)} fusion(bf16[4,512,1536]{2,1,0:T(8,128)(2,1)} %param.26, f32[4,256,1024]{2,1,0:T(8,128)} %fusion.47), kind=kOutput, calls=%fused_computation.2 | convolution fusion | flops 1615331328 | bytes 13631488 | tf_op jit(solution)/shard_map/ecf,efd->ecd/dot_general | solution.py:314
  181.9 2.1 convolution_bitcast_fusion
  184.0 2.9 %fusion.1 = bf16[512,1536]{1,0:T(8,128)(2,1)S(1)} fusion(f32[512,1536]{1,0:T(8,128)S(1)} %convolution_bitcast_fusion, bf16[4,256,1536]{2,1,0:T(8,128)(2,1)S(1)} %convolution_convert_fusion.1, s32[512,4]{0,1:T(4,128)S(1)} %subtract_add_fusion, pred[512,4]{0,1:T(4,128)(4,1)S(1)} %get-tuple-element.108, bf16[512,4]{0,1:T(4,128)(2,1)S(1)} %copy.221), kind=kOutput, calls=%fused_computation.7 | convolution fusion | flops 1613758464 | bytes 7878656 | tf_op jit(solution)/shard_map/nec,ecd->nd/dot_general | solution.py:319
  187.0 1.3 copy.229
  188.3 3.7 %all-to-all-start.4 = ((bf16[4,2,64,1536]{3,2,1,0:T(8,128)(2,1)}), bf16[4,2,64,1536]{3,2,1,0:T(8,128)(2,1)S(1)}, u32[]{:S(2)}, u32[]{:S(2)}) async-start(bf16[4,2,64,1536]{3,2,1,0:T(8,128)(2,1)} %bitcast.88), calls=%async_computation.4 | async-start | bytes 3145728 | tf_op jit(solution)/shard_map/all_to_all | solution.py:323
  192.4 19.0 %all-to-all-done.4 = bf16[4,2,64,1536]{3,2,1,0:T(8,128)(2,1)S(1)} async-done(((bf16[4,2,64,1536]{3,2,1,0:T(8,128)(2,1)}), bf16[4,2,64,1536]{3,2,1,0:T(8,128)(2,1)S(1)}, u32[]{:S(2)}, u32[]{:S(2)}) %all-to-all-start.4) | async-done | bytes 1572896 | tf_op jit(solution)/shard_map/all_to_all | solution.py:323
  212.5 3.6 %collective-permute-start.5 = (bf16[64,1536]{1,0:T(8,128)(2,1)S(1)}, bf16[64,1536]{1,0:T(8,128)(2,1)S(1)}, u32[]{:S(2)}, u32[]{:S(2)}) collective-permute-start(bf16[64,1536]{1,0:T(8,128)(2,1)S(1)} %fusion.27), channel_id=1, source_target_pairs={{0,16},{16,0},{1,17},{17,1},{2,18},{18,2},{3,19},{19,3},{4,20},{20... | collective-permute-start | bytes 589832 | tf_op jit(solution)/shard_map/ppermute | solution.py:329
  218.2 6.1 %collective-permute-done.5 = bf16[64,1536]{1,0:T(8,128)(2,1)S(1)} collective-permute-done((bf16[64,1536]{1,0:T(8,128)(2,1)S(1)}, bf16[64,1536]{1,0:T(8,128)(2,1)S(1)}, u32[]{:S(2)}, u32[]{:S(2)}) %collective-permute-start.5) | collective-permute-done | bytes 196640 | tf_op jit(solution)/shard_map/ppermute | solution.py:329
  224.3 1.7 fusion.26
  (88 shorter events, 10.5 us)
Async XLA Ops:
  0.6 92.0 %copy-start = (bf16[384,1536]{1,0:T(8,128)(2,1)S(1)}, bf16[384,1536]{1,0:T(8,128)(2,1)}, u32[]{:S(2)}) copy-start(bf16[384,1536]{1,0:T(8,128)(2,1)} %param.22) | copy-start | bytes 3538948
  0.6 3.3 %copy-start.4 = (bf16[256,1536]{1,0:T(8,128)(2,1)S(1)}, bf16[256,1536]{1,0:T(8,128)(2,1)}, u32[]{:S(2)}) copy-start(bf16[256,1536]{1,0:T(8,128)(2,1)} %param.17) | copy-start | bytes 2359300
  0.7 3.3 %copy-start.15 = (f32[1536]{0:T(1024)S(1)}, f32[1536]{0:T(1024)}, u32[]{:S(2)}) copy-start(f32[1536]{0:T(1024)} %param.18) | copy-start | bytes 18436
  0.7 3.3 %copy-start.14 = (bf16[1536,128]{1,0:T(8,128)(2,1)S(1)}, bf16[1536,128]{1,0:T(8,128)(2,1)}, u32[]{:S(2)}) copy-start(bf16[1536,128]{1,0:T(8,128)(2,1)} %param.21) | copy-start | bytes 1179652
  4.0 9.0 %copy-start.9 = (bf16[512,256]{1,0:T(8,128)(2,1)S(1)}, bf16[512,256]{1,0:T(8,128)(2,1)}, u32[]{:S(2)}) copy-start(bf16[512,256]{1,0:T(8,128)(2,1)} %param.23) | copy-start | bytes 786436
  5.7 14.6 %all-to-all-start.1 = ((bf16[4,8,2048]{2,0,1:T(4,128)(2,1)}), bf16[4,8,2048]{2,0,1:T(4,128)(2,1)S(1)}, u32[]{:S(2)}, u32[]{:S(2)}) async-start(bf16[4,8,2048]{2,0,1:T(4,128)(2,1)} %copy.187), calls=%async_computation.1 | async-start | bytes 262144 | tf_op jit(solution)/shard_map/all_to_all | solution.py:173
  20.3 1.3 copy-start.7
  21.6 23.8 %all-to-all-start = ((bf16[4,2,2,768,64]{3,4,2,1,0:T(8,128)(2,1)}), bf16[4,2,2,768,64]{3,4,2,1,0:T(8,128)(2,1)S(1)}, u32[]{:S(2)}, u32[]{:S(2)}) async-start(bf16[4,2,2,768,64]{3,4,2,1,0:T(8,128)(2,1)} %broadcast_in_dim.84), calls=%async_computation | async-start | bytes 3145728 | tf_op jit(solution)/shard_map/all_to_all | solution.py:196
  31.1 14.3 %collective-permute-start = (bf16[2,768,64]{1,2,0:T(8,128)(2,1)}, bf16[2,768,64]{1,2,0:T(8,128)(2,1)}, u32[]{:S(2)}, u32[]{:S(2)}) collective-permute-start(bf16[2,768,64]{1,2,0:T(8,128)(2,1)} %bitcast.37), channel_id=1, source_target_pairs={{0,16},{1,17},{2,18},{3,19},{4,20},{5,21},{6,22},{7,23},{8,24},{9,... | collective-permute-start | bytes 589832 | tf_op jit(solution)/shard_map/ppermute | solution.py:205
  50.4 41.0 %collective-permute-start.2 = (f32[2,768,64]{1,2,0:T(8,128)}, f32[2,768,64]{1,2,0:T(8,128)}, u32[]{:S(2)}, u32[]{:S(2)}) collective-permute-start(f32[2,768,64]{1,2,0:T(8,128)} %copy.194), channel_id=1, source_target_pairs={{16,0},{17,1},{18,2},{19,3},{20,4},{21,5},{22,6},{23,7},{24,8},{25... | collective-permute-start | bytes 1179656 | tf_op jit(solution)/shard_map/ppermute | solution.py:230
  55.7 34.9 %collective-permute-start.3 = (f32[2,768,1]{1,0,2:T(2,128)}, f32[2,768,1]{1,0,2:T(2,128)}, u32[]{:S(2)}, u32[]{:S(2)}) collective-permute-start(f32[2,768,1]{1,0,2:T(2,128)} %copy.196), channel_id=1, source_target_pairs={{16,0},{17,1},{18,2},{19,3},{20,4},{21,5},{22,6},{23,7},{24,8},{25... | collective-permute-start | bytes 18440 | tf_op jit(solution)/shard_map/ppermute | solution.py:230
  57.0 33.7 %collective-permute-start.1 = (f32[2,768,1]{1,0,2:T(2,128)}, f32[2,768,1]{1,0,2:T(2,128)}, u32[]{:S(2)}, u32[]{:S(2)}) collective-permute-start(f32[2,768,1]{1,0,2:T(2,128)} %copy.190), channel_id=1, source_target_pairs={{16,0},{17,1},{18,2},{19,3},{20,4},{21,5},{22,6},{23,7},{24,8},{25... | collective-permute-start | bytes 18440 | tf_op jit(solution)/shard_map/ppermute | solution.py:230
  86.5 2.9 %copy-start.6 = (f32[2,768,1]{2,1,0:T(8,128)S(1)}, f32[2,768,1]{2,1,0:T(8,128)}, u32[]{:S(2)}) copy-start(f32[2,768,1]{2,1,0:T(8,128)} %get-tuple-element.103) | copy-start | bytes 18436 | tf_op jit(solution)/shard_map/cond
  92.6 5.2 %copy-start.11 = (s32[64,8]{0,1:T(8,128)S(1)}, s32[64,8]{0,1:T(8,128)}, u32[]{:S(2)}) copy-start(s32[64,8]{0,1:T(8,128)} %param.27) | copy-start | bytes 6148
  92.6 5.3 %copy-start.10 = (f32[64,8]{0,1:T(8,128)S(1)}, f32[64,8]{0,1:T(8,128)}, u32[]{:S(2)}) copy-start(f32[64,8]{0,1:T(8,128)} %param.28) | copy-start | bytes 6148
  94.1 15.6 %copy-start.12 = (f32[1536]{0:T(1024)S(1)}, f32[1536]{0:T(1024)}, u32[]{:S(2)}) copy-start(f32[1536]{0:T(1024)} %param.24) | copy-start | bytes 18436
  94.1 15.3 %all-to-all-start.2 = ((bf16[4,64,1536]{2,1,0:T(8,128)(2,1)}), bf16[4,64,1536]{2,1,0:T(8,128)(2,1)S(1)}, u32[]{:S(2)}, u32[]{:S(2)}) async-start(bf16[4,64,1536]{2,1,0:T(8,128)(2,1)} %bitcast.15), calls=%async_computation.2 | async-start | bytes 1572864 | tf_op jit(solution)/shard_map/all_to_all | solution.py:245
  109.9 13.8 %collective-permute-start.4 = (bf16[64,1664]{1,0:T(8,128)(2,1)S(1)}, bf16[64,1664]{1,0:T(8,128)(2,1)S(1)}, u32[]{:S(2)}, u32[]{:S(2)}) collective-permute-start(bf16[64,1664]{1,0:T(8,128)(2,1)S(1)} %concatenate.15), channel_id=1, source_target_pairs={{0,16},{16,0},{1,17},{17,1},{2,18},{18,2},{3,19},{19,3},{4,20},{20... | collective-permute-start | bytes 638984 | tf_op jit(solution)/shard_map/ppermute | solution.py:277
  125.1 31.0 %all-to-all-start.3 = ((bf16[4,2,64,1664]{3,2,1,0:T(8,128)(2,1)}), bf16[4,2,64,1664]{3,2,1,0:T(8,128)(2,1)S(1)}, u32[]{:S(2)}, u32[]{:S(2)}) async-start(bf16[4,2,64,1664]{3,2,1,0:T(8,128)(2,1)} %broadcast_in_dim.91), calls=%async_computation.3 | async-start | bytes 3407872 | tf_op jit(solution)/shard_map/all_to_all | solution.py:281
  188.3 3.9 %copy-start.13 = (s32[256]{0:T(256)S(1)}, s32[256]{0:T(256)}, u32[]{:S(2)}) copy-start(s32[256]{0:T(256)} %param.29) | copy-start | bytes 3076
  188.3 23.1 %all-to-all-start.4 = ((bf16[4,2,64,1536]{3,2,1,0:T(8,128)(2,1)}), bf16[4,2,64,1536]{3,2,1,0:T(8,128)(2,1)S(1)}, u32[]{:S(2)}, u32[]{:S(2)}) async-start(bf16[4,2,64,1536]{3,2,1,0:T(8,128)(2,1)} %bitcast.88), calls=%async_computation.4 | async-start | bytes 3145728 | tf_op jit(solution)/shard_map/all_to_all | solution.py:323
  192.0 24.2 %copy-start.8 = (bf16[4,8,2048]{2,0,1:T(4,128)(2,1)S(1)}, bf16[4,8,2048]{2,0,1:T(4,128)(2,1)}, u32[]{:S(2)}) copy-start(bf16[4,8,2048]{2,0,1:T(4,128)(2,1)} %copy-done.7) | copy-start | bytes 393220
  211.4 14.7 %copy-start.1 = (bf16[384,1536]{1,0:T(8,128)(2,1)S(1)}, bf16[384,1536]{1,0:T(8,128)(2,1)}, u32[]{:S(2)}) copy-start(bf16[384,1536]{1,0:T(8,128)(2,1)} %param.22) | copy-start | bytes 3538948
  211.6 0.9 copy-start.2
  212.5 11.8 %copy-start.3 = (f32[2,64,1536]{2,1,0:T(8,128)S(1)}, f32[2,64,1536]{2,1,0:T(8,128)}, u32[]{:S(2)}) copy-start(f32[2,64,1536]{2,1,0:T(8,128)} %copy-done.2) | copy-start | bytes 2359300
  212.5 11.7 %collective-permute-start.5 = (bf16[64,1536]{1,0:T(8,128)(2,1)S(1)}, bf16[64,1536]{1,0:T(8,128)(2,1)S(1)}, u32[]{:S(2)}, u32[]{:S(2)}) collective-permute-start(bf16[64,1536]{1,0:T(8,128)(2,1)S(1)} %fusion.27), channel_id=1, source_target_pairs={{0,16},{16,0},{1,17},{17,1},{2,18},{18,2},{3,19},{19,3},{4,20},{20... | collective-permute-start | bytes 589832 | tf_op jit(solution)/shard_map/ppermute | solution.py:329

commit v14 on v12

--- a/solution.py
+++ b/solution.py
@@ -295,7 +295,12 @@
     weight_hi = lax.dynamic_slice_in_dim(side_all, EXPERTS + local_first, experts_here, 1)
     weight_lo = lax.dynamic_slice_in_dim(side_all, 2 * EXPERTS + local_first, experts_here, 1)
     named_blocks = named.reshape(seq_count, moe_rows, experts_here).astype(jnp.int32)
-    rank = jnp.cumsum(named_blocks, axis=1) - named_blocks
+    earlier_rows = (
+        jnp.arange(moe_rows, dtype=jnp.int32)[None, :] < jnp.arange(moe_rows, dtype=jnp.int32)[:, None]
+    ).astype(jnp.bfloat16)
+    rank = jnp.einsum(
+        "ij,bjx->bix", earlier_rows, named_blocks.astype(jnp.bfloat16), preferred_element_type=jnp.float32
+    ).astype(jnp.int32)
     slot = (jnp.arange(seq_count, dtype=jnp.int32)[:, None, None] * capacity + rank).reshape(
         total_rows, experts_here
     )

time: 216 us -> 209 us (0.968)
  other arithmetic: 11.5 us -> 5.15 us
    another operation x1 -> x0, other arithmetic: 6.33 us -> none  [body(): rank = jnp.cumsum(named_blocks, axis=1) - named_blocks]
    another operation x7 -> x5, local copies, waits for them, and re-layouts: 6.77 us -> 6.5 us
where the time goes in v14:
time: 209 us; the launch traced here: 208 us
  waiting for transfers between devices  79.7 us (38%)
  starting transfers between devices  44.7 us (21%)
  matrix products  27.6 us (13%)
  local copies, waits for them, and re-layouts  26.4 us (13%)
  Pallas kernels  23.5 us (11%)
  other arithmetic  5.15 us (2%)
    pallas_call x1, Pallas kernels, attend_partial(): pl.pallas_call(kernel, out_shape=(jax.ShapeDtypeStruct((heads, rows, dim)...  23.5 us
    all_to_all x1, waiting for transfers between devices, body(): lax.all_to_all(jnp.broadcast_to(pair[None], (half_size,) + pair.shape), '...  19.9 us
    all_to_all x1, waiting for transfers between devices, body(): lax.all_to_all(by_dest.transpose(1, 0, 2, 3), 'hseq', split_axis=0, conca...  17.8 us
    ppermute x1, waiting for transfers between devices, body(): partner_rows = lax.ppermute(query_rows, 'half', perm=[(0, 1)])  13.1 us
    all_to_all x1, starting transfers between devices, body(): lax.all_to_all(jnp.broadcast_to(pair[None], (half_size,) + pair.shape), '...  12.4 us
    all_to_all x1, waiting for transfers between devices, body(): lax.all_to_all(projected.reshape(exp_count, -1, projected.shape[1]), 'exp...  11.2 us
    dot_general x1, matrix products, body(): jnp.einsum('ecd,edf->ecf', rows_in, expert_in, preferred_element_type=jnp...  10.2 us
    all_to_all x1, waiting for transfers between devices, body(): lax.all_to_all(outgoing, SEQ_AXES, split_axis=1, concat_axis=1, tiled=True)  7.43 us
  transfers between devices with their start and end apart: 11, of which 9 were waited for; matrix products, arithmetic and copies ran while one was open for 8% of the time, Pallas kernels for 11%

profile of v14, /device:TPU:0, one launch (start us, length us, event | category | flops | bytes accessed | tf_op | source)
XLA Modules:
  0.0 208.1 jit_solution(16511913940884207116)
XLA Ops:
  0.7 1.5 fusion.7
  2.2 1.7 convolution_convert_fusion.5
  5.4 1.3 broadcast_in_dim.86
  6.7 5.2 %all-to-all-start = ((bf16[4,2,2,768,64]{3,4,2,1,0:T(8,128)(2,1)}), bf16[4,2,2,768,64]{3,4,2,1,0:T(8,128)(2,1)S(1)}, u32[]{:S(2)}, u32[]{:S(2)}) async-start(bf16[4,2,2,768,64]{3,4,2,1,0:T(8,128)(2,1)} %broadcast_in_dim.86), calls=%async_computation | async-start | bytes 3145728 | tf_op jit(solution)/shard_map/all_to_all | solution.py:196
  11.9 2.6 %convolution_convert_fusion.3 = bf16[256,384]{1,0:T(8,128)(2,1)} fusion(bf16[1536,384]{1,0:T(8,128)(2,1)} %param.19, bf16[256,1536]{1,0:T(8,128)(2,1)S(1)} %copy-done.4, f32[1536]{0:T(1024)S(1)} %copy-done.16, f32[256]{0:T(256)S(1)} %add_rsqrt_fusion), kind=kOutput, calls=%fused_computation.23 | convolution fusion | flops 303661056 | bytes 2169856 | tf_op jit(solution)/shard_map/dot_general | solution.py:158
  14.5 1.1 copy.156
  15.6 4.5 %collective-permute-start = (bf16[2,768,64]{1,2,0:T(8,128)(2,1)S(1)}, bf16[2,768,64]{1,2,0:T(8,128)(2,1)S(1)}, u32[]{:S(2)}, u32[]{:S(2)}) collective-permute-start(bf16[2,768,64]{1,2,0:T(8,128)(2,1)S(1)} %bitcast.96), channel_id=1, source_target_pairs={{0,16},{1,17},{2,18},{3,19},{4,20},{5,21},{6,22},{7,23},{8,24},{9,... | collective-permute-start | bytes 589832 | tf_op jit(solution)/shard_map/ppermute | solution.py:205
  20.1 13.1 %collective-permute-done = bf16[2,768,64]{1,2,0:T(8,128)(2,1)S(1)} collective-permute-done((bf16[2,768,64]{1,2,0:T(8,128)(2,1)S(1)}, bf16[2,768,64]{1,2,0:T(8,128)(2,1)S(1)}, u32[]{:S(2)}, u32[]{:S(2)}) %collective-permute-start) | collective-permute-done | bytes 196640 | tf_op jit(solution)/shard_map/ppermute | solution.py:205
  33.2 2.8 %conditional.3 = ((f32[2,768,64]{2,1,0:T(8,128)}, f32[2,768,1]{2,1,0:T(8,128)}, f32[2,768,1]{2,1,0:T(8,128)})) conditional(s32[]{:T(128)} %convert_element_type.90, (s32[1]{0:T(128)}, bf16[2,768,64]{1,2,0:T(8,128)(2,1)S(1)}, bf16[4,2,2,768,64]{3,4,2,1,0:T(8,128)(2,1)S(1)}) %tuple.22, () %tuple.23), branch_computations={%region_3.4_spmd, %region_4.5_spmd} | conditional | bytes 3538952 | solution.py:217
  33.2 0.9 broadcast.98
  34.1 1.0 broadcast.96
  35.1 0.9 broadcast.97
  36.0 2.1 %copy.172 = f32[2,768,64]{1,2,0:T(8,128)} copy(f32[2,768,64]{2,1,0:T(8,128)} %get-tuple-element.38) | data formatting | bytes 786432 | tf_op jit(solution)/shard_map/cond | solution.py:217
  38.2 1.3 collective-permute-start.2
  39.5 1.4 copy.168
  40.9 1.4 copy.174
  42.3 1.3 collective-permute-start.3
  43.6 1.3 collective-permute-start.1
  44.9 30.3 %conditional.2 = (f32[2,768,64]{1,2,0:T(8,128)S(1)}, f32[2,768,1]{1,0,2:T(2,128)S(1)}, f32[2,768,1]{1,0,2:T(2,128)S(1)}) conditional(s32[]{:T(128)} %convert_element_type.90, (s32[1]{0:T(128)}, bf16[2,768,64]{1,2,0:T(8,128)(2,1)S(1)}, bf16[4,2,2,768,64]{3,4,2,1,0:T(8,128)(2,1)S(1)}) %tuple.64, (s32[1]{0:T(128)}, bf16[2,768,64]{1,2,0:T(8,128)(2,1)S(1)}, ...), branch_computations={%region_1.2_spmd, %region_2.3_spmd} | conditional | bytes 4374580 | solution.py:223
  44.9 0.9 copy.164.q_ref
  45.8 2.7 %copy.165.k_ref.v_ref = bf16[4,2,2,768,64]{4,3,2,1,0:T(8,128)(2,1)} copy(bf16[4,2,2,768,64]{3,4,2,1,0:T(8,128)(2,1)S(1)} %get-tuple-element.90) | data formatting | bytes 3145728 | tf_op jit(solution)/shard_map
  48.5 23.5 %branch_1_fun.1 = (f32[2,768,64]{2,1,0:T(8,128)}, f32[2,768,1]{2,1,0:T(8,128)}, f32[2,768,1]{2,1,0:T(8,128)}) custom-call(s32[1]{0:T(128)} %get-tuple-element.21.flags_ref, bf16[2,768,64]{2,1,0:T(8,128)(2,1)} %copy.164.q_ref, bf16[4,2,2,768,64]{4,3,2,1,0:T(8,128)(2,1)} %copy.165.k_ref.v_ref, bf16[4,2,2,768,64]{4,3,2,1,0:T(8,128)(2,1)} %copy.165.k_ref.v_ref), custom_call_target="tpu_custom_call" | custom-call | tf_op jit(solution)/shard_map/cond/branch_1_fun/pallas_call | solution.py:96
  72.1 1.5 copy.191
  73.5 1.4 copy.193
  75.2 3.9 %collective-permute-done.3 = f32[2,768,1]{1,0,2:T(2,128)S(1)} collective-permute-done((f32[2,768,1]{1,0,2:T(2,128)S(1)}, f32[2,768,1]{1,0,2:T(2,128)S(1)}, u32[]{:S(2)}, u32[]{:S(2)}) %collective-permute-start.3) | collective-permute-done | bytes 6176 | tf_op jit(solution)/shard_map/ppermute | solution.py:229
  79.4 1.5 convolution_convert_fusion.2
  80.9 3.8 %all-to-all-start.1 = ((bf16[4,64,1536]{2,1,0:T(8,128)(2,1)}), bf16[4,64,1536]{2,1,0:T(8,128)(2,1)S(1)}, u32[]{:S(2)}, u32[]{:S(2)}) async-start(bf16[4,64,1536]{2,1,0:T(8,128)(2,1)} %bitcast.15), calls=%async_computation.1 | async-start | bytes 1572864 | tf_op jit(solution)/shard_map/all_to_all | solution.py:244
  85.2 11.2 %all-to-all-done.1 = bf16[4,64,1536]{2,1,0:T(8,128)(2,1)S(1)} async-done(((bf16[4,64,1536]{2,1,0:T(8,128)(2,1)}), bf16[4,64,1536]{2,1,0:T(8,128)(2,1)S(1)}, u32[]{:S(2)}, u32[]{:S(2)}) %all-to-all-start.1) | async-done | bytes 786464 | tf_op jit(solution)/shard_map/all_to_all | solution.py:244
  96.9 4.5 %collective-permute-start.4 = (bf16[64,1664]{1,0:T(8,128)(2,1)S(1)}, bf16[64,1664]{1,0:T(8,128)(2,1)S(1)}, u32[]{:S(2)}, u32[]{:S(2)}) collective-permute-start(bf16[64,1664]{1,0:T(8,128)(2,1)S(1)} %concatenate.15), channel_id=1, source_target_pairs={{0,16},{16,0},{1,17},{17,1},{2,18},{18,2},{3,19},{19,3},{4,20},{20... | collective-permute-start | bytes 638984 | tf_op jit(solution)/shard_map/ppermute | solution.py:276
  101.4 5.1 %collective-permute-done.4 = bf16[64,1664]{1,0:T(8,128)(2,1)S(1)} collective-permute-done((bf16[64,1664]{1,0:T(8,128)(2,1)S(1)}, bf16[64,1664]{1,0:T(8,128)(2,1)S(1)}, u32[]{:S(2)}, u32[]{:S(2)}) %collective-permute-start.4) | collective-permute-done | bytes 213024 | tf_op jit(solution)/shard_map/ppermute | solution.py:276
  106.5 1.3 broadcast_in_dim.93
  107.8 12.4 %all-to-all-start.2 = ((bf16[4,2,64,1664]{3,2,1,0:T(8,128)(2,1)}), bf16[4,2,64,1664]{3,2,1,0:T(8,128)(2,1)S(1)}, u32[]{:S(2)}, u32[]{:S(2)}) async-start(bf16[4,2,64,1664]{3,2,1,0:T(8,128)(2,1)} %broadcast_in_dim.93), calls=%async_computation.2 | async-start | bytes 3407872 | tf_op jit(solution)/shard_map/all_to_all | solution.py:280
  120.2 19.9 %all-to-all-done.2 = bf16[4,2,64,1664]{3,2,1,0:T(8,128)(2,1)S(1)} async-done(((bf16[4,2,64,1664]{3,2,1,0:T(8,128)(2,1)}), bf16[4,2,64,1664]{3,2,1,0:T(8,128)(2,1)S(1)}, u32[]{:S(2)}, u32[]{:S(2)}) %all-to-all-start.2) | async-done | bytes 1703968 | tf_op jit(solution)/shard_map/all_to_all | solution.py:280
  140.4 1.0 copy-done.6
  142.1 10.2 %fusion.49 = f32[4,256,1024]{2,1,0:T(8,128)} fusion(bf16[4,1536,1024]{2,1,0:T(8,128)(2,1)} %param.25, bf16[512,1664]{1,0:T(8,128)(2,1)} %bitcast.95, s32[512,4]{0,1:T(4,128)S(1)} %eq.48, pred[512,4]{0,1:T(4,128)(4,1)S(1)} %get-tuple-element.106), kind=kOutput, calls=%fused_computation.90 | convolution fusion | flops 4834459648 | bytes 18360320 | tf_op jit(solution)/shard_map/ecd,edf->ecf/dot_general | solution.py:315
  152.3 5.9 %convolution_convert_fusion.1 = bf16[4,256,1536]{2,1,0:T(8,128)(2,1)S(1)} fusion(bf16[4,512,1536]{2,1,0:T(8,128)(2,1)} %param.26, f32[4,256,1024]{2,1,0:T(8,128)} %fusion.49), kind=kOutput, calls=%fused_computation.2 | convolution fusion | flops 1615331328 | bytes 13631488 | tf_op jit(solution)/shard_map/ecf,efd->ecd/dot_general | solution.py:318
  158.2 2.1 %convolution_bitcast_fusion = f32[512,1536]{1,0:T(8,128)S(1)} fusion(bf16[4,256,1536]{2,1,0:T(8,128)(2,1)S(1)} %convolution_convert_fusion.1, s32[512,4]{0,1:T(4,128)S(1)} %eq.48, pred[512,4]{0,1:T(4,128)(4,1)S(1)} %get-tuple-element.106, bf16[512,4]{0,1:T(4,128)(2,1)S(1)} %copy.200), kind=kOutput, calls=%fused_computation.3 | convolution fusion | flops 1612185600 | bytes 6305792 | tf_op jit(solution)/shard_map/nec,ecd->nd/dot_general | solution.py:325
  160.3 3.0 %fusion.1 = bf16[512,1536]{1,0:T(8,128)(2,1)S(1)} fusion(f32[512,1536]{1,0:T(8,128)S(1)} %convolution_bitcast_fusion, bf16[4,256,1536]{2,1,0:T(8,128)(2,1)S(1)} %convolution_convert_fusion.1, s32[512,4]{0,1:T(4,128)S(1)} %eq.48, pred[512,4]{0,1:T(4,128)(4,1)S(1)} %get-tuple-element.106, bf16[512,4]{0,1:T(4,128)(2,1)S(1)} %copy.199), kind=kOutput, calls=%fused_computation.7 | convolution fusion | flops 1613758464 | bytes 7878656 | tf_op jit(solution)/shard_map/nec,ecd->nd/dot_general | solution.py:323
  163.3 1.3 copy.207
  164.6 3.7 %all-to-all-start.3 = ((bf16[4,2,64,1536]{3,2,1,0:T(8,128)(2,1)}), bf16[4,2,64,1536]{3,2,1,0:T(8,128)(2,1)S(1)}, u32[]{:S(2)}, u32[]{:S(2)}) async-start(bf16[4,2,64,1536]{3,2,1,0:T(8,128)(2,1)} %bitcast.93), calls=%async_computation.3 | async-start | bytes 3145728 | tf_op jit(solution)/shard_map/all_to_all | solution.py:327
  169.9 17.8 %all-to-all-done.3 = bf16[4,2,64,1536]{3,2,1,0:T(8,128)(2,1)S(1)} async-done(((bf16[4,2,64,1536]{3,2,1,0:T(8,128)(2,1)}), bf16[4,2,64,1536]{3,2,1,0:T(8,128)(2,1)S(1)}, u32[]{:S(2)}, u32[]{:S(2)}) %all-to-all-start.3) | async-done | bytes 1572896 | tf_op jit(solution)/shard_map/all_to_all | solution.py:327
  187.7 3.8 %all-to-all-start.4 = ((bf16[4,8,2048]{2,0,1:T(4,128)(2,1)}), bf16[4,8,2048]{2,0,1:T(4,128)(2,1)S(1)}, u32[]{:S(2)}, u32[]{:S(2)}) async-start(bf16[4,8,2048]{2,0,1:T(4,128)(2,1)} %copy.184), calls=%async_computation.4 | async-start | bytes 262144 | tf_op jit(solution)/shard_map/all_to_all | solution.py:173
  191.7 0.9 copy-done.2
  192.6 3.0 %collective-permute-start.5 = (bf16[64,1536]{1,0:T(8,128)(2,1)S(1)}, bf16[64,1536]{1,0:T(8,128)(2,1)S(1)}, u32[]{:S(2)}, u32[]{:S(2)}) collective-permute-start(bf16[64,1536]{1,0:T(8,128)(2,1)S(1)} %fusion.29), channel_id=1, source_target_pairs={{0,16},{16,0},{1,17},{17,1},{2,18},{18,2},{3,19},{19,3},{4,20},{20... | collective-permute-start | bytes 589832 | tf_op jit(solution)/shard_map/ppermute | solution.py:333
  195.6 7.4 %all-to-all-done.4 = bf16[4,8,2048]{2,0,1:T(4,128)(2,1)S(1)} async-done(((bf16[4,8,2048]{2,0,1:T(4,128)(2,1)}), bf16[4,8,2048]{2,0,1:T(4,128)(2,1)S(1)}, u32[]{:S(2)}, u32[]{:S(2)}) %all-to-all-start.4) | async-done | bytes 131104 | tf_op jit(solution)/shard_map/all_to_all | solution.py:173
  203.0 0.9 scatter_custom_fusion
  205.1 1.3 collective-permute-done.5
  206.4 1.7 fusion.28
  (85 shorter events, 6.8 us)
Async XLA Ops:
  0.6 78.8 %copy-start = (bf16[384,1536]{1,0:T(8,128)(2,1)S(1)}, bf16[384,1536]{1,0:T(8,128)(2,1)}, u32[]{:S(2)}) copy-start(bf16[384,1536]{1,0:T(8,128)(2,1)} %param.22) | copy-start | bytes 3538948
  0.6 3.3 %copy-start.4 = (bf16[256,1536]{1,0:T(8,128)(2,1)S(1)}, bf16[256,1536]{1,0:T(8,128)(2,1)}, u32[]{:S(2)}) copy-start(bf16[256,1536]{1,0:T(8,128)(2,1)} %param.17) | copy-start | bytes 2359300
  0.7 3.3 %copy-start.16 = (f32[1536]{0:T(1024)S(1)}, f32[1536]{0:T(1024)}, u32[]{:S(2)}) copy-start(f32[1536]{0:T(1024)} %param.18) | copy-start | bytes 18436
  0.7 3.3 %copy-start.15 = (bf16[1536,128]{1,0:T(8,128)(2,1)S(1)}, bf16[1536,128]{1,0:T(8,128)(2,1)}, u32[]{:S(2)}) copy-start(bf16[1536,128]{1,0:T(8,128)(2,1)} %param.21) | copy-start | bytes 1179652
  0.7 3.8 %copy-start.10 = (bf16[512,256]{1,0:T(8,128)(2,1)S(1)}, bf16[512,256]{1,0:T(8,128)(2,1)}, u32[]{:S(2)}) copy-start(bf16[512,256]{1,0:T(8,128)(2,1)} %param.23) | copy-start | bytes 786436
  6.7 26.5 %all-to-all-start = ((bf16[4,2,2,768,64]{3,4,2,1,0:T(8,128)(2,1)}), bf16[4,2,2,768,64]{3,4,2,1,0:T(8,128)(2,1)S(1)}, u32[]{:S(2)}, u32[]{:S(2)}) async-start(bf16[4,2,2,768,64]{3,4,2,1,0:T(8,128)(2,1)} %broadcast_in_dim.86), calls=%async_computation | async-start | bytes 3145728 | tf_op jit(solution)/shard_map/all_to_all | solution.py:196
  15.6 17.6 %collective-permute-start = (bf16[2,768,64]{1,2,0:T(8,128)(2,1)S(1)}, bf16[2,768,64]{1,2,0:T(8,128)(2,1)S(1)}, u32[]{:S(2)}, u32[]{:S(2)}) collective-permute-start(bf16[2,768,64]{1,2,0:T(8,128)(2,1)S(1)} %bitcast.96), channel_id=1, source_target_pairs={{0,16},{1,17},{2,18},{3,19},{4,20},{5,21},{6,22},{7,23},{8,24},{9,... | collective-permute-start | bytes 589832 | tf_op jit(solution)/shard_map/ppermute | solution.py:205
  38.2 41.0 %collective-permute-start.2 = (f32[2,768,64]{1,2,0:T(8,128)}, f32[2,768,64]{1,2,0:T(8,128)S(1)}, u32[]{:S(2)}, u32[]{:S(2)}) collective-permute-start(f32[2,768,64]{1,2,0:T(8,128)} %copy.172), channel_id=1, source_target_pairs={{16,0},{17,1},{18,2},{19,3},{20,4},{21,5},{22,6},{23,7},{24,8},{25... | collective-permute-start | bytes 1179656 | tf_op jit(solution)/shard_map/ppermute | solution.py:229
  42.3 36.8 %collective-permute-start.3 = (f32[2,768,1]{1,0,2:T(2,128)S(1)}, f32[2,768,1]{1,0,2:T(2,128)S(1)}, u32[]{:S(2)}, u32[]{:S(2)}) collective-permute-start(f32[2,768,1]{1,0,2:T(2,128)S(1)} %copy.174), channel_id=1, source_target_pairs={{16,0},{17,1},{18,2},{19,3},{20,4},{21,5},{22,6},{23,7},{24,8},{25... | collective-permute-start | bytes 18440 | tf_op jit(solution)/shard_map/ppermute | solution.py:229
  43.6 35.6 %collective-permute-start.1 = (f32[2,768,1]{1,0,2:T(2,128)S(1)}, f32[2,768,1]{1,0,2:T(2,128)S(1)}, u32[]{:S(2)}, u32[]{:S(2)}) collective-permute-start(f32[2,768,1]{1,0,2:T(2,128)S(1)} %copy.168), channel_id=1, source_target_pairs={{16,0},{17,1},{18,2},{19,3},{20,4},{21,5},{22,6},{23,7},{24,8},{25... | collective-permute-start | bytes 18440 | tf_op jit(solution)/shard_map/ppermute | solution.py:229
  72.1 2.9 %copy-start.8 = (f32[2,768,1]{2,1,0:T(8,128)S(1)}, f32[2,768,1]{2,1,0:T(8,128)}, u32[]{:S(2)}) copy-start(f32[2,768,1]{2,1,0:T(8,128)} %get-tuple-element.101) | copy-start | bytes 18436 | tf_op jit(solution)/shard_map/cond
  79.3 5.4 %copy-start.12 = (s32[64,8]{0,1:T(8,128)S(1)}, s32[64,8]{0,1:T(8,128)}, u32[]{:S(2)}) copy-start(s32[64,8]{0,1:T(8,128)} %param.27) | copy-start | bytes 6148
  79.4 5.5 %copy-start.11 = (f32[64,8]{0,1:T(8,128)S(1)}, f32[64,8]{0,1:T(8,128)}, u32[]{:S(2)}) copy-start(f32[64,8]{0,1:T(8,128)} %param.28) | copy-start | bytes 6148
  79.4 17.0 %copy-start.5 = (bf16[256,1536]{1,0:T(8,128)(2,1)S(1)}, bf16[256,1536]{1,0:T(8,128)(2,1)}, u32[]{:S(2)}) copy-start(bf16[256,1536]{1,0:T(8,128)(2,1)} %param.17) | copy-start | bytes 2359300
  80.9 15.7 %copy-start.13 = (f32[1536]{0:T(1024)S(1)}, f32[1536]{0:T(1024)}, u32[]{:S(2)}) copy-start(f32[1536]{0:T(1024)} %param.24) | copy-start | bytes 18436
  80.9 15.4 %all-to-all-start.1 = ((bf16[4,64,1536]{2,1,0:T(8,128)(2,1)}), bf16[4,64,1536]{2,1,0:T(8,128)(2,1)S(1)}, u32[]{:S(2)}, u32[]{:S(2)}) async-start(bf16[4,64,1536]{2,1,0:T(8,128)(2,1)} %bitcast.15), calls=%async_computation.1 | async-start | bytes 1572864 | tf_op jit(solution)/shard_map/all_to_all | solution.py:244
  96.9 9.5 %collective-permute-start.4 = (bf16[64,1664]{1,0:T(8,128)(2,1)S(1)}, bf16[64,1664]{1,0:T(8,128)(2,1)S(1)}, u32[]{:S(2)}, u32[]{:S(2)}) collective-permute-start(bf16[64,1664]{1,0:T(8,128)(2,1)S(1)} %concatenate.15), channel_id=1, source_target_pairs={{0,16},{16,0},{1,17},{17,1},{2,18},{18,2},{3,19},{19,3},{4,20},{20... | collective-permute-start | bytes 638984 | tf_op jit(solution)/shard_map/ppermute | solution.py:276
  107.8 32.2 %all-to-all-start.2 = ((bf16[4,2,64,1664]{3,2,1,0:T(8,128)(2,1)}), bf16[4,2,64,1664]{3,2,1,0:T(8,128)(2,1)S(1)}, u32[]{:S(2)}, u32[]{:S(2)}) async-start(bf16[4,2,64,1664]{3,2,1,0:T(8,128)(2,1)} %broadcast_in_dim.93), calls=%async_computation.2 | async-start | bytes 3407872 | tf_op jit(solution)/shard_map/all_to_all | solution.py:280
  140.2 1.2 copy-start.6
  164.6 3.9 %copy-start.9 = (bf16[256,2,2,64]{0,3,2,1:T(8,128)(2,1)S(1)}, bf16[256,2,2,64]{0,3,2,1:T(8,128)(2,1)}, u32[]{:S(2)}) copy-start(bf16[256,2,2,64]{0,3,2,1:T(8,128)(2,1)} %get-tuple-element.109) | copy-start | bytes 393220
  164.6 5.1 %copy-start.14 = (s32[256]{0:T(256)S(1)}, s32[256]{0:T(256)}, u32[]{:S(2)}) copy-start(s32[256]{0:T(256)} %param.29) | copy-start | bytes 3076
  164.6 23.1 %all-to-all-start.3 = ((bf16[4,2,64,1536]{3,2,1,0:T(8,128)(2,1)}), bf16[4,2,64,1536]{3,2,1,0:T(8,128)(2,1)S(1)}, u32[]{:S(2)}, u32[]{:S(2)}) async-start(bf16[4,2,64,1536]{3,2,1,0:T(8,128)(2,1)} %bitcast.93), calls=%async_computation.3 | async-start | bytes 3145728 | tf_op jit(solution)/shard_map/all_to_all | solution.py:327
  187.7 15.4 %all-to-all-start.4 = ((bf16[4,8,2048]{2,0,1:T(4,128)(2,1)}), bf16[4,8,2048]{2,0,1:T(4,128)(2,1)S(1)}, u32[]{:S(2)}, u32[]{:S(2)}) async-start(bf16[4,8,2048]{2,0,1:T(4,128)(2,1)} %copy.184), calls=%async_computation.4 | async-start | bytes 262144 | tf_op jit(solution)/shard_map/all_to_all | solution.py:173
  191.5 16.7 %copy-start.1 = (bf16[384,1536]{1,0:T(8,128)(2,1)S(1)}, bf16[384,1536]{1,0:T(8,128)(2,1)}, u32[]{:S(2)}) copy-start(bf16[384,1536]{1,0:T(8,128)(2,1)} %param.22) | copy-start | bytes 3538948
  191.7 0.9 copy-start.2
  192.6 13.8 %copy-start.3 = (f32[2,64,1536]{2,1,0:T(8,128)S(1)}, f32[2,64,1536]{2,1,0:T(8,128)}, u32[]{:S(2)}) copy-start(f32[2,64,1536]{2,1,0:T(8,128)} %copy-done.2) | copy-start | bytes 2359300
  192.6 13.8 %collective-permute-start.5 = (bf16[64,1536]{1,0:T(8,128)(2,1)S(1)}, bf16[64,1536]{1,0:T(8,128)(2,1)S(1)}, u32[]{:S(2)}, u32[]{:S(2)}) collective-permute-start(bf16[64,1536]{1,0:T(8,128)(2,1)S(1)} %fusion.29), channel_id=1, source_target_pairs={{0,16},{16,0},{1,17},{17,1},{2,18},{18,2},{3,19},{19,3},{4,20},{20... | collective-permute-start | bytes 589832 | tf_op jit(solution)/shard_map/ppermute | solution.py:333

commit v15 on v10

--- a/solution.py
+++ b/solution.py
@@ -243,7 +243,7 @@
     full_hi = full_weight.astype(jnp.bfloat16)
     full_lo = (full_weight - full_hi.astype(jnp.float32)).astype(jnp.bfloat16)
     full_named = jnp.any(route_hits, axis=1).astype(jnp.bfloat16)
-    moe_width = moe_in.shape[1]
+    model_width = moe_in.shape[1]
     side_width = 128 * pl_cdiv(3 * EXPERTS, 128)
     side = jnp.concatenate(
         [
@@ -254,20 +254,35 @@
         ],
         axis=1,
     )
-    packed_all = lax.all_gather(
-        jnp.concatenate([moe_in, side], axis=1), SEQ_AXES, axis=0, tiled=True
-    )
-    rows_all = packed_all[:, :moe_width]
+    packed = jnp.concatenate([moe_in, side], axis=1)
+    crossed = lax.ppermute(packed, "half", perm=[(0, 1), (1, 0)])
+    pair = jnp.where(
+        holds_first, jnp.stack([packed, crossed]), jnp.stack([crossed, packed])
+    )
+    fanned = lax.all_to_all(
+        jnp.broadcast_to(pair[None], (half_size,) + pair.shape),
+        "hseq",
+        split_axis=0,
+        concat_axis=0,
+        tiled=True,
+    )
+    packed_all = fanned.transpose(1, 0, 2, 3).reshape(seq_count * moe_rows, -1)
+    rows_all = packed_all[:, :model_width]
     total_rows = rows_all.shape[0]
     local_first = seq_index * experts_here
-    side_all = packed_all[:, moe_width:]
+    side_all = packed_all[:, model_width:]
     named = (
         lax.dynamic_slice_in_dim(side_all, local_first, experts_here, 1) > 0
     )
     weight_hi = lax.dynamic_slice_in_dim(side_all, EXPERTS + local_first, experts_here, 1)
     weight_lo = lax.dynamic_slice_in_dim(side_all, 2 * EXPERTS + local_first, experts_here, 1)
     named_blocks = named.reshape(seq_count, moe_rows, experts_here).astype(jnp.int32)
-    rank = jnp.cumsum(named_blocks, axis=1) - named_blocks
+    earlier_rows = (
+        jnp.arange(moe_rows, dtype=jnp.int32)[None, :] < jnp.arange(moe_rows, dtype=jnp.int32)[:, None]
+    ).astype(jnp.bfloat16)
+    rank = jnp.einsum(
+        "ij,bjx->bix", earlier_rows, named_blocks.astype(jnp.bfloat16), preferred_element_type=jnp.float32
+    ).astype(jnp.int32)
     slot = (jnp.arange(seq_count, dtype=jnp.int32)[:, None, None] * capacity + rank).reshape(
         total_rows, experts_here
     )
@@ -293,16 +308,35 @@
     model_width = partial.shape[1]
     page_lines = pl_cdiv(outgoing.shape[1], model_width)
     page_part = jnp.pad(outgoing, ((0, 0), (0, page_lines * model_width - outgoing.shape[1])))
-    both = jnp.concatenate(
+    page_part = page_part.reshape(halves, half_size, page_lines, model_width)
+    by_dest = jnp.concatenate(
         [
-            partial.astype(jnp.bfloat16).reshape(seq_count, moe_rows, model_width),
-            page_part.reshape(seq_count, page_lines, model_width),
+            partial.astype(jnp.bfloat16).reshape(halves, half_size, moe_rows, model_width),
+            page_part,
         ],
-        axis=1,
-    )
-    returned = lax.all_to_all(both, SEQ_AXES, split_axis=0, concat_axis=0, tiled=True)
-    moe = jnp.sum(returned[:, :moe_rows].astype(jnp.float32), axis=0)
-    received = returned[:, moe_rows:].reshape(seq_count, -1)[:, : outgoing.shape[1]]
+        axis=2,
+    )
+    from_half = lax.all_to_all(
+        by_dest.transpose(1, 0, 2, 3), "hseq", split_axis=0, concat_axis=0, tiled=True
+    )
+    half_sums = jnp.sum(from_half[:, :, :moe_rows].astype(jnp.float32), axis=0)
+    pages_in = from_half[:, :, moe_rows:]
+    own_sum = jnp.where(holds_first, half_sums[0], half_sums[1])
+    other_sum = jnp.where(holds_first, half_sums[1], half_sums[0])
+    own_pages = jnp.where(holds_first, pages_in[:, 0], pages_in[:, 1])
+    other_pages = jnp.where(holds_first, pages_in[:, 1], pages_in[:, 0])
+    forward = jnp.concatenate(
+        [other_sum.astype(jnp.bfloat16), other_pages.reshape(-1, model_width)], axis=0
+    )
+    from_partner = lax.ppermute(forward, "half", perm=[(0, 1), (1, 0)])
+    moe = own_sum + from_partner[:moe_rows].astype(jnp.float32)
+    partner_pages = from_partner[moe_rows:].reshape(half_size, page_lines, model_width)
+    pages_by_source = jnp.where(
+        holds_first,
+        jnp.concatenate([own_pages, partner_pages], axis=0),
+        jnp.concatenate([partner_pages, own_pages], axis=0),
+    )
+    received = pages_by_source.reshape(seq_count, -1)[:, : outgoing.shape[1]]
     received = received.reshape(seq_count, rounds, -1).transpose(1, 0, 2)
     block_ids = (
         jnp.arange(seq_count, dtype=jnp.int32)[None, :] * blocks_here

time: 253 us -> 217 us (0.86)
  waiting for transfers between devices: 123 us -> 84.3 us
  starting transfers between devices: 21.7 us -> 40.5 us
  between operations: 14.5 us -> 1.14 us
    all_gather x1 -> x0, waiting for transfers between devices: 57.7 us -> none  [body(): lax.all_gather(jnp.concatenate([moe_in, side], axis=1), SEQ_AXES, axis=0,...]
    ppermute x0 -> x2, waiting for transfers between devices: none -> 16.5 us  [the longest x1 11.4 us: body(): from_partner = lax.ppermute(forward, 'half', perm=[(0, 1), (1, 0)])]
    all_to_all x1 -> x2, starting transfers between devices: 3.72 us -> 16.4 us  [the longest x1 12.5 us: body(): lax.all_to_all(jnp.broadcast_to(pair[None], (half_size,) + pair.shape), '...]
    ppermute x0 -> x2, starting transfers between devices: none -> 6.68 us  [the longest x1 4.3 us: body(): crossed = lax.ppermute(packed, 'half', perm=[(0, 1), (1, 0)])]
    another operation x1 -> x0, other arithmetic: 6.33 us -> none  [body(): rank = jnp.cumsum(named_blocks, axis=1) - named_blocks]
    transpose x0 -> x1, other arithmetic: none -> 3.44 us  [body(): by_dest.transpose(1, 0, 2, 3)]
    ppermute x1, waiting for transfers between devices: 10.3 us -> 13.1 us  [body(): partner_rows = lax.ppermute(query_rows, 'half', perm=[(0, 1)])]
    all_to_all x1 -> x2, waiting for transfers between devices: 40.8 us -> 39.6 us  [the longest x1 20.6 us: body(): lax.all_to_all(by_dest.transpose(1, 0, 2, 3), 'hseq', split_axis=0, conca...]
  transfers between devices with their start and end apart: 8 -> 10, of which waited for: 6 -> 7; matrix products, arithmetic and copies ran while one was open for 8% -> 7% of each run, Pallas kernels for 9% -> 11%
where the time goes in v15:
time: 217 us; the launch traced here: 216 us
  waiting for transfers between devices  84.3 us (39%)
  starting transfers between devices  40.5 us (19%)
  matrix products  27.6 us (13%)
  local copies, waits for them, and re-layouts  26.7 us (12%)
  Pallas kernels  23.5 us (11%)
  other arithmetic  12.6 us (6%)
    pallas_call x1, Pallas kernels, attend_partial(): pl.pallas_call(kernel, out_shape=(jax.ShapeDtypeStruct((heads, rows, dim)...  23.5 us
    all_to_all x1, waiting for transfers between devices, body(): lax.all_to_all(by_dest.transpose(1, 0, 2, 3), 'hseq', split_axis=0, conca...  20.6 us
    all_to_all x1, waiting for transfers between devices, body(): lax.all_to_all(jnp.broadcast_to(pair[None], (half_size,) + pair.shape), '...  19 us
    ppermute x1, waiting for transfers between devices, body(): partner_rows = lax.ppermute(query_rows, 'half', perm=[(0, 1)])  13.1 us
    all_to_all x1, starting transfers between devices, body(): lax.all_to_all(jnp.broadcast_to(pair[None], (half_size,) + pair.shape), '...  12.5 us
    ppermute x1, waiting for transfers between devices, body(): from_partner = lax.ppermute(forward, 'half', perm=[(0, 1), (1, 0)])  11.4 us
    all_to_all x1, waiting for transfers between devices, body(): lax.all_to_all(projected.reshape(exp_count, -1, projected.shape[1]), 'exp...  11.2 us
    dot_general x1, matrix products, body(): jnp.einsum('ecd,edf->ecf', rows_in, expert_in, preferred_element_type=jnp...  10.2 us
  transfers between devices with their start and end apart: 10, of which 7 were waited for; matrix products, arithmetic and copies ran while one was open for 7% of the time, Pallas kernels for 11%

profile of v15, /device:TPU:0, one launch (start us, length us, event | category | flops | bytes accessed | tf_op | source)
XLA Modules:
  0.0 216.3 jit_solution(16075037115242005425)
XLA Ops:
  0.7 1.5 fusion.7
  2.2 1.8 convolution_convert_fusion.5
  5.4 1.3 broadcast_in_dim.86
  6.7 5.2 %all-to-all-start = ((bf16[4,2,2,768,64]{3,4,2,1,0:T(8,128)(2,1)}), bf16[4,2,2,768,64]{3,4,2,1,0:T(8,128)(2,1)S(1)}, u32[]{:S(2)}, u32[]{:S(2)}) async-start(bf16[4,2,2,768,64]{3,4,2,1,0:T(8,128)(2,1)} %broadcast_in_dim.86), calls=%async_computation | async-start | bytes 3145728 | tf_op jit(solution)/shard_map/all_to_all | solution.py:178
  11.9 2.6 %convolution_convert_fusion.3 = bf16[256,384]{1,0:T(8,128)(2,1)} fusion(bf16[1536,384]{1,0:T(8,128)(2,1)} %param.19, bf16[256,1536]{1,0:T(8,128)(2,1)S(1)} %copy-done.2, f32[1536]{0:T(1024)S(1)} %copy-done.13, f32[256]{0:T(256)S(1)} %add_rsqrt_fusion), kind=kOutput, calls=%fused_computation.23 | convolution fusion | flops 303661056 | bytes 2169856 | tf_op jit(solution)/shard_map/dot_general | solution.py:158
  14.5 1.1 copy.191
  15.6 4.5 %collective-permute-start = (bf16[2,768,64]{1,2,0:T(8,128)(2,1)S(1)}, bf16[2,768,64]{1,2,0:T(8,128)(2,1)S(1)}, u32[]{:S(2)}, u32[]{:S(2)}) collective-permute-start(bf16[2,768,64]{1,2,0:T(8,128)(2,1)S(1)} %bitcast.100), channel_id=1, source_target_pairs={{0,16},{1,17},{2,18},{3,19},{4,20},{5,21},{6,22},{7,23},{8,24},{9,... | collective-permute-start | bytes 589832 | tf_op jit(solution)/shard_map/ppermute | solution.py:187
  20.1 13.1 %collective-permute-done = bf16[2,768,64]{1,2,0:T(8,128)(2,1)S(1)} collective-permute-done((bf16[2,768,64]{1,2,0:T(8,128)(2,1)S(1)}, bf16[2,768,64]{1,2,0:T(8,128)(2,1)S(1)}, u32[]{:S(2)}, u32[]{:S(2)}) %collective-permute-start) | collective-permute-done | bytes 196640 | tf_op jit(solution)/shard_map/ppermute | solution.py:187
  33.2 2.8 %conditional.3 = ((f32[2,768,64]{2,1,0:T(8,128)}, f32[2,768,1]{2,1,0:T(8,128)}, f32[2,768,1]{2,1,0:T(8,128)})) conditional(s32[]{:T(128)} %convert_element_type.92, (s32[1]{0:T(128)}, bf16[2,768,64]{1,2,0:T(8,128)(2,1)S(1)}, bf16[4,2,2,768,64]{3,4,2,1,0:T(8,128)(2,1)S(1)}) %tuple.22, () %tuple.23), branch_computations={%region_3.0_spmd, %region_4.0_spmd} | conditional | bytes 3538952 | solution.py:199
  33.2 1.0 broadcast.105
  34.2 0.9 broadcast.103
  35.1 0.9 broadcast.104
  36.1 2.1 copy.207
  38.2 1.3 collective-permute-start.2
  39.5 1.4 copy.203
  40.9 1.4 copy.209
  42.3 1.3 collective-permute-start.3
  43.6 1.3 collective-permute-start.1
  44.9 30.4 %conditional.2 = (f32[2,768,64]{1,2,0:T(8,128)S(1)}, f32[2,768,1]{1,0,2:T(2,128)S(1)}, f32[2,768,1]{1,0,2:T(2,128)S(1)}) conditional(s32[]{:T(128)} %convert_element_type.92, (s32[1]{0:T(128)}, bf16[2,768,64]{1,2,0:T(8,128)(2,1)S(1)}, bf16[4,2,2,768,64]{3,4,2,1,0:T(8,128)(2,1)S(1)}) %tuple.69, (s32[1]{0:T(128)}, bf16[2,768,64]{1,2,0:T(8,128)(2,1)S(1)}, ...), branch_computations={%region_1.0_spmd, %region_2.0_spmd} | conditional | bytes 4374580 | solution.py:205
  44.9 0.9 copy.199.q_ref
  45.8 2.8 %copy.200.k_ref.v_ref = bf16[4,2,2,768,64]{4,3,2,1,0:T(8,128)(2,1)} copy(bf16[4,2,2,768,64]{3,4,2,1,0:T(8,128)(2,1)S(1)} %get-tuple-element.101) | data formatting | bytes 3145728 | tf_op jit(solution)/shard_map
  48.6 23.5 %branch_1_fun.1 = (f32[2,768,64]{2,1,0:T(8,128)}, f32[2,768,1]{2,1,0:T(8,128)}, f32[2,768,1]{2,1,0:T(8,128)}) custom-call(s32[1]{0:T(128)} %get-tuple-element.21.flags_ref, bf16[2,768,64]{2,1,0:T(8,128)(2,1)} %copy.199.q_ref, bf16[4,2,2,768,64]{4,3,2,1,0:T(8,128)(2,1)} %copy.200.k_ref.v_ref, bf16[4,2,2,768,64]{4,3,2,1,0:T(8,128)(2,1)} %copy.200.k_ref.v_ref), custom_call_target="tpu_custom_call" | custom-call | tf_op jit(solution)/shard_map/cond/branch_1_fun/pallas_call | solution.py:96
  72.2 1.5 copy.225
  73.6 1.4 copy.227
  75.3 3.9 %collective-permute-done.3 = f32[2,768,1]{1,0,2:T(2,128)S(1)} collective-permute-done((f32[2,768,1]{1,0,2:T(2,128)S(1)}, f32[2,768,1]{1,0,2:T(2,128)S(1)}, u32[]{:S(2)}, u32[]{:S(2)}) %collective-permute-start.3) | collective-permute-done | bytes 6176 | tf_op jit(solution)/shard_map/ppermute | solution.py:211
  79.3 1.1 divide_convert_fusion
  80.5 1.5 convolution_convert_fusion.2
  82.0 3.8 %all-to-all-start.1 = ((bf16[4,64,1536]{2,1,0:T(8,128)(2,1)}), bf16[4,64,1536]{2,1,0:T(8,128)(2,1)S(1)}, u32[]{:S(2)}, u32[]{:S(2)}) async-start(bf16[4,64,1536]{2,1,0:T(8,128)(2,1)} %bitcast.15), calls=%async_computation.1 | async-start | bytes 1572864 | tf_op jit(solution)/shard_map/all_to_all | solution.py:226
  86.2 11.2 %all-to-all-done.1 = bf16[4,64,1536]{2,1,0:T(8,128)(2,1)S(1)} async-done(((bf16[4,64,1536]{2,1,0:T(8,128)(2,1)}), bf16[4,64,1536]{2,1,0:T(8,128)(2,1)S(1)}, u32[]{:S(2)}, u32[]{:S(2)}) %all-to-all-start.1) | async-done | bytes 786464 | tf_op jit(solution)/shard_map/all_to_all | solution.py:226
  98.0 4.3 %collective-permute-start.4 = (bf16[64,1664]{1,0:T(8,128)(2,1)S(1)}, bf16[64,1664]{1,0:T(8,128)(2,1)S(1)}, u32[]{:S(2)}, u32[]{:S(2)}) collective-permute-start(bf16[64,1664]{1,0:T(8,128)(2,1)S(1)} %concatenate.31), channel_id=1, source_target_pairs={{0,16},{16,0},{1,17},{17,1},{2,18},{18,2},{3,19},{19,3},{4,20},{20... | collective-permute-start | bytes 638984 | tf_op jit(solution)/shard_map/ppermute | solution.py:258
  102.3 5.1 %collective-permute-done.4 = bf16[64,1664]{1,0:T(8,128)(2,1)S(1)} collective-permute-done((bf16[64,1664]{1,0:T(8,128)(2,1)S(1)}, bf16[64,1664]{1,0:T(8,128)(2,1)S(1)}, u32[]{:S(2)}, u32[]{:S(2)}) %collective-permute-start.4) | collective-permute-done | bytes 213024 | tf_op jit(solution)/shard_map/ppermute | solution.py:258
  107.4 1.3 broadcast_in_dim.93
  108.7 12.5 %all-to-all-start.2 = ((bf16[4,2,64,1664]{3,2,1,0:T(8,128)(2,1)}), bf16[4,2,64,1664]{3,2,1,0:T(8,128)(2,1)S(1)}, u32[]{:S(2)}, u32[]{:S(2)}) async-start(bf16[4,2,64,1664]{3,2,1,0:T(8,128)(2,1)} %broadcast_in_dim.93), calls=%async_computation.2 | async-start | bytes 3407872 | tf_op jit(solution)/shard_map/all_to_all | solution.py:262
  122.1 19.0 %all-to-all-done.2 = bf16[4,2,64,1664]{3,2,1,0:T(8,128)(2,1)S(1)} async-done(((bf16[4,2,64,1664]{3,2,1,0:T(8,128)(2,1)}), bf16[4,2,64,1664]{3,2,1,0:T(8,128)(2,1)S(1)}, u32[]{:S(2)}, u32[]{:S(2)}) %all-to-all-start.2) | async-done | bytes 1703968 | tf_op jit(solution)/shard_map/all_to_all | solution.py:262
  141.1 1.4 copy.214
  142.5 0.9 slice.55
  144.2 10.2 %fusion.50 = f32[4,256,1024]{2,1,0:T(8,128)} fusion(bf16[4,1536,1024]{2,1,0:T(8,128)(2,1)} %param.25, bf16[512,1664]{1,0:T(8,128)(2,1)} %bitcast.19, s32[512,4]{0,1:T(4,128)S(1)} %eq.48, pred[512,4]{0,1:T(4,128)(4,1)S(1)} %get-tuple-element.119), kind=kOutput, calls=%fused_computation.98 | convolution fusion | flops 4834459648 | bytes 18360320 | tf_op jit(solution)/shard_map/ecd,edf->ecf/dot_general | solution.py:297
  154.4 5.9 %convolution_convert_fusion.1 = bf16[4,256,1536]{2,1,0:T(8,128)(2,1)S(1)} fusion(bf16[4,512,1536]{2,1,0:T(8,128)(2,1)} %param.26, f32[4,256,1024]{2,1,0:T(8,128)} %fusion.50), kind=kOutput, calls=%fused_computation.2 | convolution fusion | flops 1615331328 | bytes 13631488 | tf_op jit(solution)/shard_map/ecf,efd->ecd/dot_general | solution.py:300
  160.3 2.1 convolution_bitcast_fusion
  162.4 2.9 %fusion.1 = bf16[512,1536]{1,0:T(8,128)(2,1)S(1)} fusion(f32[512,1536]{1,0:T(8,128)S(1)} %convolution_bitcast_fusion, bf16[4,256,1536]{2,1,0:T(8,128)(2,1)S(1)} %convolution_convert_fusion.1, s32[512,4]{0,1:T(4,128)S(1)} %eq.48, pred[512,4]{0,1:T(4,128)(4,1)S(1)} %get-tuple-element.119, bf16[512,4]{0,1:T(4,128)(2,1)S(1)} %copy.236), kind=kOutput, calls=%fused_computation.7 | convolution fusion | flops 1613758464 | bytes 7878656 | tf_op jit(solution)/shard_map/nec,ecd->nd/dot_general | solution.py:305
  165.4 1.6 copy.218
  167.0 3.4 %maximum_bitcast_fusion = bf16[4,2,70,1536]{3,1,2,0:T(2,128)(2,1)} fusion(bf16[2,4,6,1536]{3,0,2,1:T(2,128)(2,1)S(1)} %copy.219, bf16[2,4,64,1536]{3,0,2,1:T(2,128)(2,1)S(1)} %copy.218), kind=kLoop, calls=%fused_computation.17 | loop fusion | flops 860160 | bytes 3440640 | tf_op jit(solution)/shard_map/transpose | solution.py:320
  170.5 3.9 %all-to-all-start.3 = ((bf16[4,2,70,1536]{3,1,2,0:T(2,128)(2,1)}), bf16[4,2,70,1536]{3,1,2,0:T(2,128)(2,1)S(1)}, u32[]{:S(2)}, u32[]{:S(2)}) async-start(bf16[4,2,70,1536]{3,1,2,0:T(2,128)(2,1)} %maximum_bitcast_fusion), calls=%async_computation.3 | async-start | bytes 3440640 | tf_op jit(solution)/shard_map/all_to_all | solution.py:319
  174.8 20.6 %all-to-all-done.3 = bf16[4,2,70,1536]{3,1,2,0:T(2,128)(2,1)S(1)} async-done(((bf16[4,2,70,1536]{3,1,2,0:T(2,128)(2,1)}), bf16[4,2,70,1536]{3,1,2,0:T(2,128)(2,1)S(1)}, u32[]{:S(2)}, u32[]{:S(2)}) %all-to-all-start.3) | async-done | bytes 1720352 | tf_op jit(solution)/shard_map/all_to_all | solution.py:319
  196.1 1.5 convert_reduce_fusion
  198.2 2.4 %collective-permute-start.5 = (bf16[88,1536]{1,0:T(8,128)(2,1)S(1)}, bf16[88,1536]{1,0:T(8,128)(2,1)S(1)}, u32[]{:S(2)}, u32[]{:S(2)}) collective-permute-start(bf16[88,1536]{1,0:T(8,128)(2,1)S(1)} %pad_maximum_fusion.1), channel_id=1, source_target_pairs={{0,16},{16,0},{1,17},{17,1},{2,18},{18,2},{3,19},{19,3},{4,20},{20... | collective-permute-start | bytes 811016 | tf_op jit(solution)/shard_map/ppermute | solution.py:331
  201.0 11.4 %collective-permute-done.5 = bf16[88,1536]{1,0:T(8,128)(2,1)S(1)} collective-permute-done((bf16[88,1536]{1,0:T(8,128)(2,1)S(1)}, bf16[88,1536]{1,0:T(8,128)(2,1)S(1)}, u32[]{:S(2)}, u32[]{:S(2)}) %collective-permute-start.5) | collective-permute-done | bytes 270368 | tf_op jit(solution)/shard_map/ppermute | solution.py:331
  214.6 1.7 fusion.29
  (89 shorter events, 8.7 us)
Async XLA Ops:
  0.6 79.9 %copy-start = (bf16[384,1536]{1,0:T(8,128)(2,1)S(1)}, bf16[384,1536]{1,0:T(8,128)(2,1)}, u32[]{:S(2)}) copy-start(bf16[384,1536]{1,0:T(8,128)(2,1)} %param.22) | copy-start | bytes 3538948
  0.6 3.3 %copy-start.2 = (bf16[256,1536]{1,0:T(8,128)(2,1)S(1)}, bf16[256,1536]{1,0:T(8,128)(2,1)}, u32[]{:S(2)}) copy-start(bf16[256,1536]{1,0:T(8,128)(2,1)} %param.17) | copy-start | bytes 2359300
  0.7 3.3 %copy-start.13 = (f32[1536]{0:T(1024)S(1)}, f32[1536]{0:T(1024)}, u32[]{:S(2)}) copy-start(f32[1536]{0:T(1024)} %param.18) | copy-start | bytes 18436
  0.7 3.3 %copy-start.12 = (bf16[1536,128]{1,0:T(8,128)(2,1)S(1)}, bf16[1536,128]{1,0:T(8,128)(2,1)}, u32[]{:S(2)}) copy-start(bf16[1536,128]{1,0:T(8,128)(2,1)} %param.21) | copy-start | bytes 1179652
  2.2 2.3 %copy-start.7 = (bf16[512,256]{1,0:T(8,128)(2,1)S(1)}, bf16[512,256]{1,0:T(8,128)(2,1)}, u32[]{:S(2)}) copy-start(bf16[512,256]{1,0:T(8,128)(2,1)} %param.23) | copy-start | bytes 786436
  6.7 26.5 %all-to-all-start = ((bf16[4,2,2,768,64]{3,4,2,1,0:T(8,128)(2,1)}), bf16[4,2,2,768,64]{3,4,2,1,0:T(8,128)(2,1)S(1)}, u32[]{:S(2)}, u32[]{:S(2)}) async-start(bf16[4,2,2,768,64]{3,4,2,1,0:T(8,128)(2,1)} %broadcast_in_dim.86), calls=%async_computation | async-start | bytes 3145728 | tf_op jit(solution)/shard_map/all_to_all | solution.py:178
  15.6 17.6 %collective-permute-start = (bf16[2,768,64]{1,2,0:T(8,128)(2,1)S(1)}, bf16[2,768,64]{1,2,0:T(8,128)(2,1)S(1)}, u32[]{:S(2)}, u32[]{:S(2)}) collective-permute-start(bf16[2,768,64]{1,2,0:T(8,128)(2,1)S(1)} %bitcast.100), channel_id=1, source_target_pairs={{0,16},{1,17},{2,18},{3,19},{4,20},{5,21},{6,22},{7,23},{8,24},{9,... | collective-permute-start | bytes 589832 | tf_op jit(solution)/shard_map/ppermute | solution.py:187
  38.2 41.1 %collective-permute-start.2 = (f32[2,768,64]{1,2,0:T(8,128)}, f32[2,768,64]{1,2,0:T(8,128)}, u32[]{:S(2)}, u32[]{:S(2)}) collective-permute-start(f32[2,768,64]{1,2,0:T(8,128)} %copy.207), channel_id=1, source_target_pairs={{16,0},{17,1},{18,2},{19,3},{20,4},{21,5},{22,6},{23,7},{24,8},{25... | collective-permute-start | bytes 1179656 | tf_op jit(solution)/shard_map/ppermute | solution.py:211
  42.3 36.9 %collective-permute-start.3 = (f32[2,768,1]{1,0,2:T(2,128)S(1)}, f32[2,768,1]{1,0,2:T(2,128)S(1)}, u32[]{:S(2)}, u32[]{:S(2)}) collective-permute-start(f32[2,768,1]{1,0,2:T(2,128)S(1)} %copy.209), channel_id=1, source_target_pairs={{16,0},{17,1},{18,2},{19,3},{20,4},{21,5},{22,6},{23,7},{24,8},{25... | collective-permute-start | bytes 18440 | tf_op jit(solution)/shard_map/ppermute | solution.py:211
  43.6 35.7 %collective-permute-start.1 = (f32[2,768,1]{1,0,2:T(2,128)S(1)}, f32[2,768,1]{1,0,2:T(2,128)S(1)}, u32[]{:S(2)}, u32[]{:S(2)}) collective-permute-start(f32[2,768,1]{1,0,2:T(2,128)S(1)} %copy.203), channel_id=1, source_target_pairs={{16,0},{17,1},{18,2},{19,3},{20,4},{21,5},{22,6},{23,7},{24,8},{25... | collective-permute-start | bytes 18440 | tf_op jit(solution)/shard_map/ppermute | solution.py:211
  72.2 2.9 %copy-start.5 = (f32[2,768,1]{2,1,0:T(8,128)S(1)}, f32[2,768,1]{2,1,0:T(8,128)}, u32[]{:S(2)}) copy-start(f32[2,768,1]{2,1,0:T(8,128)} %get-tuple-element.112) | copy-start | bytes 18436 | tf_op jit(solution)/shard_map/cond
  80.5 5.3 %copy-start.9 = (s32[64,8]{0,1:T(8,128)S(1)}, s32[64,8]{0,1:T(8,128)}, u32[]{:S(2)}) copy-start(s32[64,8]{0,1:T(8,128)} %param.27) | copy-start | bytes 6148
  80.5 5.5 %copy-start.8 = (f32[64,8]{0,1:T(8,128)S(1)}, f32[64,8]{0,1:T(8,128)}, u32[]{:S(2)}) copy-start(f32[64,8]{0,1:T(8,128)} %param.28) | copy-start | bytes 6148
  82.0 15.6 %copy-start.3 = (bf16[256,1536]{1,0:T(8,128)(2,1)S(1)}, bf16[256,1536]{1,0:T(8,128)(2,1)}, u32[]{:S(2)}) copy-start(bf16[256,1536]{1,0:T(8,128)(2,1)} %param.17) | copy-start | bytes 2359300
  82.0 15.7 %copy-start.10 = (f32[1536]{0:T(1024)S(1)}, f32[1536]{0:T(1024)}, u32[]{:S(2)}) copy-start(f32[1536]{0:T(1024)} %param.24) | copy-start | bytes 18436
  82.0 15.4 %all-to-all-start.1 = ((bf16[4,64,1536]{2,1,0:T(8,128)(2,1)}), bf16[4,64,1536]{2,1,0:T(8,128)(2,1)S(1)}, u32[]{:S(2)}, u32[]{:S(2)}) async-start(bf16[4,64,1536]{2,1,0:T(8,128)(2,1)} %bitcast.15), calls=%async_computation.1 | async-start | bytes 1572864 | tf_op jit(solution)/shard_map/all_to_all | solution.py:226
  98.0 9.4 %collective-permute-start.4 = (bf16[64,1664]{1,0:T(8,128)(2,1)S(1)}, bf16[64,1664]{1,0:T(8,128)(2,1)S(1)}, u32[]{:S(2)}, u32[]{:S(2)}) collective-permute-start(bf16[64,1664]{1,0:T(8,128)(2,1)S(1)} %concatenate.31), channel_id=1, source_target_pairs={{0,16},{16,0},{1,17},{17,1},{2,18},{18,2},{3,19},{19,3},{4,20},{20... | collective-permute-start | bytes 638984 | tf_op jit(solution)/shard_map/ppermute | solution.py:258
  108.7 12.5 %copy-start.6 = (bf16[256,2,2,64]{0,3,2,1:T(8,128)(2,1)S(1)}, bf16[256,2,2,64]{0,3,2,1:T(8,128)(2,1)}, u32[]{:S(2)}) copy-start(bf16[256,2,2,64]{0,3,2,1:T(8,128)(2,1)} %get-tuple-element.126) | copy-start | bytes 393220
  108.7 32.4 %all-to-all-start.2 = ((bf16[4,2,64,1664]{3,2,1,0:T(8,128)(2,1)}), bf16[4,2,64,1664]{3,2,1,0:T(8,128)(2,1)S(1)}, u32[]{:S(2)}, u32[]{:S(2)}) async-start(bf16[4,2,64,1664]{3,2,1,0:T(8,128)(2,1)} %broadcast_in_dim.93), calls=%async_computation.2 | async-start | bytes 3407872 | tf_op jit(solution)/shard_map/all_to_all | solution.py:262
  170.5 4.1 %copy-start.11 = (s32[256]{0:T(256)S(1)}, s32[256]{0:T(256)}, u32[]{:S(2)}) copy-start(s32[256]{0:T(256)} %param.29) | copy-start | bytes 3076
  170.5 24.9 %all-to-all-start.3 = ((bf16[4,2,70,1536]{3,1,2,0:T(2,128)(2,1)}), bf16[4,2,70,1536]{3,1,2,0:T(2,128)(2,1)S(1)}, u32[]{:S(2)}, u32[]{:S(2)}) async-start(bf16[4,2,70,1536]{3,1,2,0:T(2,128)(2,1)} %maximum_bitcast_fusion), calls=%async_computation.3 | async-start | bytes 3440640 | tf_op jit(solution)/shard_map/all_to_all | solution.py:319
  198.2 14.2 %collective-permute-start.5 = (bf16[88,1536]{1,0:T(8,128)(2,1)S(1)}, bf16[88,1536]{1,0:T(8,128)(2,1)S(1)}, u32[]{:S(2)}, u32[]{:S(2)}) collective-permute-start(bf16[88,1536]{1,0:T(8,128)(2,1)S(1)} %pad_maximum_fusion.1), channel_id=1, source_target_pairs={{0,16},{16,0},{1,17},{17,1},{2,18},{18,2},{3,19},{19,3},{4,20},{20... | collective-permute-start | bytes 811016 | tf_op jit(solution)/shard_map/ppermute | solution.py:331
  200.6 15.7 %copy-start.1 = (bf16[384,1536]{1,0:T(8,128)(2,1)S(1)}, bf16[384,1536]{1,0:T(8,128)(2,1)}, u32[]{:S(2)}) copy-start(bf16[384,1536]{1,0:T(8,128)(2,1)} %param.22) | copy-start | bytes 3538948

commit v16 on v14

--- a/solution.py
+++ b/solution.py
@@ -323,6 +323,7 @@
     partial = jnp.einsum(
         "nec,ecd->nd", scaled_hi, produced, preferred_element_type=jnp.float32
     ) + jnp.einsum("nec,ecd->nd", scaled_lo, produced, preferred_element_type=jnp.float32)
+    received, partial = lax.optimization_barrier((received, partial))
     by_dest = partial.astype(jnp.bfloat16).reshape(halves, half_size, moe_rows, -1)
     from_half = lax.all_to_all(
         by_dest.transpose(1, 0, 2, 3), "hseq", split_axis=0, concat_axis=0, tiled=True

time: 209 us -> 213 us (1.019)
  waiting for transfers between devices: 79.7 us -> 72.8 us
  local copies, waits for them, and re-layouts: 26.4 us -> 31.9 us
  starting transfers between devices: 44.7 us -> 48.6 us
    all_to_all x1, waiting for transfers between devices: 7.43 us -> 0.01 us  [body(): lax.all_to_all(outgoing, SEQ_AXES, split_axis=1, concat_axis=1, tiled=True)]
    ppermute x1, waiting for transfers between devices: 1.33 us -> 6.33 us  [body(): lax.ppermute(other_sum.astype(jnp.bfloat16), 'half', perm=[(0, 1), (1, 0)])]
    ppermute x1, waiting for transfers between devices: 13.1 us -> 10.3 us  [body(): partner_rows = lax.ppermute(query_rows, 'half', perm=[(0, 1)])]
    ppermute x1, starting transfers between devices: 4.48 us -> 6.71 us  [body(): crossed = lax.ppermute(packed, 'half', perm=[(0, 1), (1, 0)])]
  transfers between devices with their start and end apart: 11 -> 11, of which waited for: 9 -> 8; matrix products, arithmetic and copies ran while one was open for 8% -> 22% of each run, Pallas kernels for 11% -> 11%
where the time goes in v16:
time: 213 us; the launch traced here: 212 us
  waiting for transfers between devices  72.8 us (34%)
  starting transfers between devices  48.6 us (23%)
  local copies, waits for them, and re-layouts  31.9 us (15%)
  matrix products  27.6 us (13%)
  Pallas kernels  23.5 us (11%)
  other arithmetic  6.86 us (3%)
    pallas_call x1, Pallas kernels, attend_partial(): pl.pallas_call(kernel, out_shape=(jax.ShapeDtypeStruct((heads, rows, dim)...  23.5 us
    all_to_all x1, waiting for transfers between devices, body(): lax.all_to_all(jnp.broadcast_to(pair[None], (half_size,) + pair.shape), '...  18.7 us
    all_to_all x1, waiting for transfers between devices, body(): lax.all_to_all(by_dest.transpose(1, 0, 2, 3), 'hseq', split_axis=0, conca...  18.4 us
    all_to_all x1, starting transfers between devices, body(): lax.all_to_all(jnp.broadcast_to(pair[None], (half_size,) + pair.shape), '...  12.4 us
    all_to_all x1, waiting for transfers between devices, body(): lax.all_to_all(projected.reshape(exp_count, -1, projected.shape[1]), 'exp...  11.2 us
    ppermute x1, waiting for transfers between devices, body(): partner_rows = lax.ppermute(query_rows, 'half', perm=[(0, 1)])  10.3 us
    dot_general x1, matrix products, body(): jnp.einsum('ecd,edf->ecf', rows_in, expert_in, preferred_element_type=jnp...  10.2 us
    another operation x5, local copies, waits for them, and re-layouts  7.49 us
  transfers between devices with their start and end apart: 11, of which 8 were waited for; matrix products, arithmetic and copies ran while one was open for 22% of the time, Pallas kernels for 11%

profile of v16, /device:TPU:0, one launch (start us, length us, event | category | flops | bytes accessed | tf_op | source)
XLA Modules:
  0.0 212.3 jit_solution(18109983654951430369)
XLA Ops:
  0.7 1.5 fusion.6
  2.2 1.7 convolution_convert_fusion.5
  5.4 1.3 broadcast_in_dim.86
  6.7 5.2 %all-to-all-start = ((bf16[4,2,2,768,64]{3,4,2,1,0:T(8,128)(2,1)}), bf16[4,2,2,768,64]{3,4,2,1,0:T(8,128)(2,1)S(1)}, u32[]{:S(2)}, u32[]{:S(2)}) async-start(bf16[4,2,2,768,64]{3,4,2,1,0:T(8,128)(2,1)} %broadcast_in_dim.86), calls=%async_computation | async-start | bytes 3145728 | tf_op jit(solution)/shard_map/all_to_all | solution.py:196
  11.9 2.6 %convolution_convert_fusion.3 = bf16[256,384]{1,0:T(8,128)(2,1)} fusion(bf16[1536,384]{1,0:T(8,128)(2,1)} %param.19, bf16[256,1536]{1,0:T(8,128)(2,1)S(1)} %copy-done.4, f32[1536]{0:T(1024)S(1)} %copy-done.14, f32[256]{0:T(256)S(1)} %add_rsqrt_fusion), kind=kOutput, calls=%fused_computation.22 | convolution fusion | flops 303661056 | bytes 2169856 | tf_op jit(solution)/shard_map/dot_general | solution.py:158
  14.5 1.7 copy.156
  16.3 1.6 copy.201
  17.9 5.1 %collective-permute-start = (bf16[2,768,64]{1,2,0:T(8,128)(2,1)}, bf16[2,768,64]{1,2,0:T(8,128)(2,1)}, u32[]{:S(2)}, u32[]{:S(2)}) collective-permute-start(bf16[2,768,64]{1,2,0:T(8,128)(2,1)} %bitcast.39), channel_id=1, source_target_pairs={{0,16},{1,17},{2,18},{3,19},{4,20},{5,21},{6,22},{7,23},{8,24},{9,... | collective-permute-start | bytes 589832 | tf_op jit(solution)/shard_map/ppermute | solution.py:205
  23.0 10.3 %collective-permute-done = bf16[2,768,64]{1,2,0:T(8,128)(2,1)} collective-permute-done((bf16[2,768,64]{1,2,0:T(8,128)(2,1)}, bf16[2,768,64]{1,2,0:T(8,128)(2,1)}, u32[]{:S(2)}, u32[]{:S(2)}) %collective-permute-start) | collective-permute-done | bytes 196640 | tf_op jit(solution)/shard_map/ppermute | solution.py:205
  33.3 2.8 %conditional.3 = ((f32[2,768,64]{2,1,0:T(8,128)}, f32[2,768,1]{2,1,0:T(8,128)}, f32[2,768,1]{2,1,0:T(8,128)})) conditional(s32[]{:T(128)} %convert_element_type.90, (s32[1]{0:T(128)}, bf16[2,768,64]{1,2,0:T(8,128)(2,1)}, bf16[4,2,2,768,64]{3,4,2,1,0:T(8,128)(2,1)S(1)}) %tuple.23, () %tuple.24), branch_computations={%region_3.4_spmd, %region_4.5_spmd} | conditional | bytes 3538952 | solution.py:217
  33.3 1.0 broadcast.98
  34.3 1.0 broadcast.96
  35.2 0.9 broadcast.97
  36.1 2.1 %copy.172 = f32[2,768,64]{1,2,0:T(8,128)} copy(f32[2,768,64]{2,1,0:T(8,128)} %get-tuple-element.39) | data formatting | bytes 786432 | tf_op jit(solution)/shard_map/cond | solution.py:217
  38.3 1.3 collective-permute-start.2
  39.6 2.0 copy.168
  41.6 2.0 copy.174
  43.5 1.3 collective-permute-start.3
  44.8 1.3 collective-permute-start.1
  46.1 31.3 %conditional.2 = (f32[2,768,64]{1,2,0:T(8,128)S(1)}, f32[2,768,1]{1,0,2:T(2,128)S(1)}, f32[2,768,1]{1,0,2:T(2,128)S(1)}) conditional(s32[]{:T(128)} %convert_element_type.90, (s32[1]{0:T(128)}, bf16[2,768,64]{1,2,0:T(8,128)(2,1)}, bf16[4,2,2,768,64]{3,4,2,1,0:T(8,128)(2,1)S(1)}) %tuple.22, (s32[1]{0:T(128)}, bf16[2,768,64]{1,2,0:T(8,128)(2,1)}, ...), branch_computations={%region_1.2_spmd, %region_2.3_spmd} | conditional | bytes 4374580 | solution.py:223
  46.2 1.9 copy.164.q_ref
  48.0 2.8 %copy.165.k_ref.v_ref = bf16[4,2,2,768,64]{4,3,2,1,0:T(8,128)(2,1)} copy(bf16[4,2,2,768,64]{3,4,2,1,0:T(8,128)(2,1)S(1)} %get-tuple-element.92) | data formatting | bytes 3145728 | tf_op jit(solution)/shard_map
  50.8 23.5 %branch_1_fun.1 = (f32[2,768,64]{2,1,0:T(8,128)}, f32[2,768,1]{2,1,0:T(8,128)}, f32[2,768,1]{2,1,0:T(8,128)}) custom-call(s32[1]{0:T(128)} %get-tuple-element.21.flags_ref, bf16[2,768,64]{2,1,0:T(8,128)(2,1)} %copy.164.q_ref, bf16[4,2,2,768,64]{4,3,2,1,0:T(8,128)(2,1)} %copy.165.k_ref.v_ref, bf16[4,2,2,768,64]{4,3,2,1,0:T(8,128)(2,1)} %copy.165.k_ref.v_ref), custom_call_target="tpu_custom_call" | custom-call | tf_op jit(solution)/shard_map/cond/branch_1_fun/pallas_call | solution.py:96
  74.3 1.5 copy.191
  75.8 1.4 copy.193
  77.4 2.8 %collective-permute-done.3 = f32[2,768,1]{1,0,2:T(2,128)} collective-permute-done((f32[2,768,1]{1,0,2:T(2,128)}, f32[2,768,1]{1,0,2:T(2,128)}, u32[]{:S(2)}, u32[]{:S(2)}) %collective-permute-start.3) | collective-permute-done | bytes 6176 | tf_op jit(solution)/shard_map/ppermute | solution.py:229
  81.0 1.1 divide_convert_fusion
  82.3 1.5 convolution_convert_fusion.2
  83.7 3.8 %all-to-all-start.1 = ((bf16[4,64,1536]{2,1,0:T(8,128)(2,1)}), bf16[4,64,1536]{2,1,0:T(8,128)(2,1)S(1)}, u32[]{:S(2)}, u32[]{:S(2)}) async-start(bf16[4,64,1536]{2,1,0:T(8,128)(2,1)} %bitcast.15), calls=%async_computation.1 | async-start | bytes 1572864 | tf_op jit(solution)/shard_map/all_to_all | solution.py:244
  88.0 11.2 %all-to-all-done.1 = bf16[4,64,1536]{2,1,0:T(8,128)(2,1)S(1)} async-done(((bf16[4,64,1536]{2,1,0:T(8,128)(2,1)}), bf16[4,64,1536]{2,1,0:T(8,128)(2,1)S(1)}, u32[]{:S(2)}, u32[]{:S(2)}) %all-to-all-start.1) | async-done | bytes 786464 | tf_op jit(solution)/shard_map/all_to_all | solution.py:244
  99.7 6.7 %collective-permute-start.4 = (bf16[64,1664]{1,0:T(8,128)(2,1)S(1)}, bf16[64,1664]{1,0:T(8,128)(2,1)S(1)}, u32[]{:S(2)}, u32[]{:S(2)}) collective-permute-start(bf16[64,1664]{1,0:T(8,128)(2,1)S(1)} %concatenate.15), channel_id=1, source_target_pairs={{0,16},{16,0},{1,17},{17,1},{2,18},{18,2},{3,19},{19,3},{4,20},{20... | collective-permute-start | bytes 638984 | tf_op jit(solution)/shard_map/ppermute | solution.py:276
  106.4 5.1 %collective-permute-done.4 = bf16[64,1664]{1,0:T(8,128)(2,1)S(1)} collective-permute-done((bf16[64,1664]{1,0:T(8,128)(2,1)S(1)}, bf16[64,1664]{1,0:T(8,128)(2,1)S(1)}, u32[]{:S(2)}, u32[]{:S(2)}) %collective-permute-start.4) | collective-permute-done | bytes 213024 | tf_op jit(solution)/shard_map/ppermute | solution.py:276
  111.6 1.3 broadcast_in_dim.93
  112.9 12.4 %all-to-all-start.3 = ((bf16[4,2,64,1664]{3,2,1,0:T(8,128)(2,1)}), bf16[4,2,64,1664]{3,2,1,0:T(8,128)(2,1)S(1)}, u32[]{:S(2)}, u32[]{:S(2)}) async-start(bf16[4,2,64,1664]{3,2,1,0:T(8,128)(2,1)} %broadcast_in_dim.93), calls=%async_computation.3 | async-start | bytes 3407872 | tf_op jit(solution)/shard_map/all_to_all | solution.py:280
  126.5 18.7 %all-to-all-done.3 = bf16[4,2,64,1664]{3,2,1,0:T(8,128)(2,1)S(1)} async-done(((bf16[4,2,64,1664]{3,2,1,0:T(8,128)(2,1)}), bf16[4,2,64,1664]{3,2,1,0:T(8,128)(2,1)S(1)}, u32[]{:S(2)}, u32[]{:S(2)}) %all-to-all-start.3) | async-done | bytes 1703968 | tf_op jit(solution)/shard_map/all_to_all | solution.py:280
  145.2 4.5 %all-to-all-start.2 = ((bf16[4,8,2048]{2,0,1:T(4,128)(2,1)}), bf16[4,8,2048]{2,0,1:T(4,128)(2,1)S(1)}, u32[]{:S(2)}, u32[]{:S(2)}) async-start(bf16[4,8,2048]{2,0,1:T(4,128)(2,1)} %copy.177), calls=%async_computation.2 | async-start | bytes 262144 | tf_op jit(solution)/shard_map/all_to_all | solution.py:173
  149.7 1.4 copy.181
  151.0 0.9 slice.26
  152.7 10.2 %fusion.48 = f32[4,256,1024]{2,1,0:T(8,128)} fusion(bf16[4,1536,1024]{2,1,0:T(8,128)(2,1)} %param.25, bf16[512,1664]{1,0:T(8,128)(2,1)} %bitcast.19, s32[512,4]{0,1:T(4,128)S(1)} %eq.48, pred[512,4]{0,1:T(4,128)(4,1)S(1)} %get-tuple-element.108), kind=kOutput, calls=%fused_computation.89 | convolution fusion | flops 4834459648 | bytes 18360320 | tf_op jit(solution)/shard_map/ecd,edf->ecf/dot_general | solution.py:315
  163.0 5.9 %convolution_convert_fusion.1 = bf16[4,256,1536]{2,1,0:T(8,128)(2,1)S(1)} fusion(bf16[4,512,1536]{2,1,0:T(8,128)(2,1)} %param.26, f32[4,256,1024]{2,1,0:T(8,128)} %fusion.48), kind=kOutput, calls=%fused_computation.2 | convolution fusion | flops 1615331328 | bytes 13631488 | tf_op jit(solution)/shard_map/ecf,efd->ecd/dot_general | solution.py:318
  168.9 2.1 %convolution_bitcast_fusion = f32[512,1536]{1,0:T(8,128)S(1)} fusion(bf16[4,256,1536]{2,1,0:T(8,128)(2,1)S(1)} %convolution_convert_fusion.1, s32[512,4]{0,1:T(4,128)S(1)} %eq.48, pred[512,4]{0,1:T(4,128)(4,1)S(1)} %get-tuple-element.108, bf16[512,4]{0,1:T(4,128)(2,1)S(1)} %copy.200), kind=kOutput, calls=%fused_computation.3 | convolution fusion | flops 1612185600 | bytes 6305792 | tf_op jit(solution)/shard_map/nec,ecd->nd/dot_general | solution.py:325
  171.0 3.0 %fusion = bf16[512,1536]{1,0:T(8,128)(2,1)S(1)} fusion(f32[512,1536]{1,0:T(8,128)S(1)} %convolution_bitcast_fusion, bf16[4,256,1536]{2,1,0:T(8,128)(2,1)S(1)} %convolution_convert_fusion.1, s32[512,4]{0,1:T(4,128)S(1)} %eq.48, pred[512,4]{0,1:T(4,128)(4,1)S(1)} %get-tuple-element.108, bf16[512,4]{0,1:T(4,128)(2,1)S(1)} %copy.199), kind=kOutput, calls=%fused_computation.5 | convolution fusion | flops 1613758464 | bytes 7878656 | tf_op jit(solution)/shard_map/nec,ecd->nd/dot_general | solution.py:323
  174.0 1.3 copy.207
  175.3 4.4 %all-to-all-start.4 = ((bf16[4,2,64,1536]{3,2,1,0:T(8,128)(2,1)}), bf16[4,2,64,1536]{3,2,1,0:T(8,128)(2,1)S(1)}, u32[]{:S(2)}, u32[]{:S(2)}) async-start(bf16[4,2,64,1536]{3,2,1,0:T(8,128)(2,1)} %bitcast.91), calls=%async_computation.4 | async-start | bytes 3145728 | tf_op jit(solution)/shard_map/all_to_all | solution.py:328
  180.0 18.4 %all-to-all-done.4 = bf16[4,2,64,1536]{3,2,1,0:T(8,128)(2,1)S(1)} async-done(((bf16[4,2,64,1536]{3,2,1,0:T(8,128)(2,1)}), bf16[4,2,64,1536]{3,2,1,0:T(8,128)(2,1)S(1)}, u32[]{:S(2)}, u32[]{:S(2)}) %all-to-all-start.4) | async-done | bytes 1572896 | tf_op jit(solution)/shard_map/all_to_all | solution.py:328
  199.6 2.6 %collective-permute-start.5 = (bf16[64,1536]{1,0:T(8,128)(2,1)S(1)}, bf16[64,1536]{1,0:T(8,128)(2,1)S(1)}, u32[]{:S(2)}, u32[]{:S(2)}) collective-permute-start(bf16[64,1536]{1,0:T(8,128)(2,1)S(1)} %fusion.28), channel_id=1, source_target_pairs={{0,16},{16,0},{1,17},{17,1},{2,18},{18,2},{3,19},{19,3},{4,20},{20... | collective-permute-start | bytes 589832 | tf_op jit(solution)/shard_map/ppermute | solution.py:334
  204.3 6.3 %collective-permute-done.5 = bf16[64,1536]{1,0:T(8,128)(2,1)S(1)} collective-permute-done((bf16[64,1536]{1,0:T(8,128)(2,1)S(1)}, bf16[64,1536]{1,0:T(8,128)(2,1)S(1)}, u32[]{:S(2)}, u32[]{:S(2)}) %collective-permute-start.5) | collective-permute-done | bytes 196640 | tf_op jit(solution)/shard_map/ppermute | solution.py:334
  210.6 1.7 fusion.27
  (81 shorter events, 9.1 us)
Async XLA Ops:
  0.6 81.6 %copy-start = (bf16[384,1536]{1,0:T(8,128)(2,1)S(1)}, bf16[384,1536]{1,0:T(8,128)(2,1)}, u32[]{:S(2)}) copy-start(bf16[384,1536]{1,0:T(8,128)(2,1)} %param.22) | copy-start | bytes 3538948
  0.6 3.3 %copy-start.4 = (bf16[256,1536]{1,0:T(8,128)(2,1)S(1)}, bf16[256,1536]{1,0:T(8,128)(2,1)}, u32[]{:S(2)}) copy-start(bf16[256,1536]{1,0:T(8,128)(2,1)} %param.17) | copy-start | bytes 2359300
  0.7 3.3 %copy-start.14 = (f32[1536]{0:T(1024)S(1)}, f32[1536]{0:T(1024)}, u32[]{:S(2)}) copy-start(f32[1536]{0:T(1024)} %param.18) | copy-start | bytes 18436
  0.7 3.3 %copy-start.13 = (bf16[1536,128]{1,0:T(8,128)(2,1)S(1)}, bf16[1536,128]{1,0:T(8,128)(2,1)}, u32[]{:S(2)}) copy-start(bf16[1536,128]{1,0:T(8,128)(2,1)} %param.21) | copy-start | bytes 1179652
  0.7 3.8 %copy-start.8 = (bf16[512,256]{1,0:T(8,128)(2,1)S(1)}, bf16[512,256]{1,0:T(8,128)(2,1)}, u32[]{:S(2)}) copy-start(bf16[512,256]{1,0:T(8,128)(2,1)} %param.23) | copy-start | bytes 786436
  6.7 26.6 %all-to-all-start = ((bf16[4,2,2,768,64]{3,4,2,1,0:T(8,128)(2,1)}), bf16[4,2,2,768,64]{3,4,2,1,0:T(8,128)(2,1)S(1)}, u32[]{:S(2)}, u32[]{:S(2)}) async-start(bf16[4,2,2,768,64]{3,4,2,1,0:T(8,128)(2,1)} %broadcast_in_dim.86), calls=%async_computation | async-start | bytes 3145728 | tf_op jit(solution)/shard_map/all_to_all | solution.py:196
  17.9 15.4 %collective-permute-start = (bf16[2,768,64]{1,2,0:T(8,128)(2,1)}, bf16[2,768,64]{1,2,0:T(8,128)(2,1)}, u32[]{:S(2)}, u32[]{:S(2)}) collective-permute-start(bf16[2,768,64]{1,2,0:T(8,128)(2,1)} %bitcast.39), channel_id=1, source_target_pairs={{0,16},{1,17},{2,18},{3,19},{4,20},{5,21},{6,22},{7,23},{8,24},{9,... | collective-permute-start | bytes 589832 | tf_op jit(solution)/shard_map/ppermute | solution.py:205
  38.3 42.7 %collective-permute-start.2 = (f32[2,768,64]{1,2,0:T(8,128)}, f32[2,768,64]{1,2,0:T(8,128)}, u32[]{:S(2)}, u32[]{:S(2)}) collective-permute-start(f32[2,768,64]{1,2,0:T(8,128)} %copy.172), channel_id=1, source_target_pairs={{16,0},{17,1},{18,2},{19,3},{20,4},{21,5},{22,6},{23,7},{24,8},{25... | collective-permute-start | bytes 1179656 | tf_op jit(solution)/shard_map/ppermute | solution.py:229
  43.5 36.7 %collective-permute-start.3 = (f32[2,768,1]{1,0,2:T(2,128)}, f32[2,768,1]{1,0,2:T(2,128)}, u32[]{:S(2)}, u32[]{:S(2)}) collective-permute-start(f32[2,768,1]{1,0,2:T(2,128)} %copy.174), channel_id=1, source_target_pairs={{16,0},{17,1},{18,2},{19,3},{20,4},{21,5},{22,6},{23,7},{24,8},{25... | collective-permute-start | bytes 18440 | tf_op jit(solution)/shard_map/ppermute | solution.py:229
  44.8 35.4 %collective-permute-start.1 = (f32[2,768,1]{1,0,2:T(2,128)}, f32[2,768,1]{1,0,2:T(2,128)}, u32[]{:S(2)}, u32[]{:S(2)}) collective-permute-start(f32[2,768,1]{1,0,2:T(2,128)} %copy.168), channel_id=1, source_target_pairs={{16,0},{17,1},{18,2},{19,3},{20,4},{21,5},{22,6},{23,7},{24,8},{25... | collective-permute-start | bytes 18440 | tf_op jit(solution)/shard_map/ppermute | solution.py:229
  74.3 2.9 %copy-start.6 = (f32[2,768,1]{2,1,0:T(8,128)S(1)}, f32[2,768,1]{2,1,0:T(8,128)}, u32[]{:S(2)}) copy-start(f32[2,768,1]{2,1,0:T(8,128)} %get-tuple-element.103) | copy-start | bytes 18436 | tf_op jit(solution)/shard_map/cond
  82.2 5.4 %copy-start.10 = (s32[64,8]{0,1:T(8,128)S(1)}, s32[64,8]{0,1:T(8,128)}, u32[]{:S(2)}) copy-start(s32[64,8]{0,1:T(8,128)} %param.27) | copy-start | bytes 6148
  82.2 5.5 %copy-start.9 = (f32[64,8]{0,1:T(8,128)S(1)}, f32[64,8]{0,1:T(8,128)}, u32[]{:S(2)}) copy-start(f32[64,8]{0,1:T(8,128)} %param.28) | copy-start | bytes 6148
  83.7 15.7 %copy-start.11 = (f32[1536]{0:T(1024)S(1)}, f32[1536]{0:T(1024)}, u32[]{:S(2)}) copy-start(f32[1536]{0:T(1024)} %param.24) | copy-start | bytes 18436
  83.7 15.4 %all-to-all-start.1 = ((bf16[4,64,1536]{2,1,0:T(8,128)(2,1)}), bf16[4,64,1536]{2,1,0:T(8,128)(2,1)S(1)}, u32[]{:S(2)}, u32[]{:S(2)}) async-start(bf16[4,64,1536]{2,1,0:T(8,128)(2,1)} %bitcast.15), calls=%async_computation.1 | async-start | bytes 1572864 | tf_op jit(solution)/shard_map/all_to_all | solution.py:244
  99.7 11.8 %collective-permute-start.4 = (bf16[64,1664]{1,0:T(8,128)(2,1)S(1)}, bf16[64,1664]{1,0:T(8,128)(2,1)S(1)}, u32[]{:S(2)}, u32[]{:S(2)}) collective-permute-start(bf16[64,1664]{1,0:T(8,128)(2,1)S(1)} %concatenate.15), channel_id=1, source_target_pairs={{0,16},{16,0},{1,17},{17,1},{2,18},{18,2},{3,19},{19,3},{4,20},{20... | collective-permute-start | bytes 638984 | tf_op jit(solution)/shard_map/ppermute | solution.py:276
  112.9 12.4 %copy-start.7 = (bf16[256,2,2,64]{0,3,2,1:T(8,128)(2,1)S(1)}, bf16[256,2,2,64]{0,3,2,1:T(8,128)(2,1)}, u32[]{:S(2)}) copy-start(bf16[256,2,2,64]{0,3,2,1:T(8,128)(2,1)} %get-tuple-element.115) | copy-start | bytes 393220
  112.9 32.3 %all-to-all-start.3 = ((bf16[4,2,64,1664]{3,2,1,0:T(8,128)(2,1)}), bf16[4,2,64,1664]{3,2,1,0:T(8,128)(2,1)S(1)}, u32[]{:S(2)}, u32[]{:S(2)}) async-start(bf16[4,2,64,1664]{3,2,1,0:T(8,128)(2,1)} %broadcast_in_dim.93), calls=%async_computation.3 | async-start | bytes 3407872 | tf_op jit(solution)/shard_map/all_to_all | solution.py:280
  145.2 28.8 %all-to-all-start.2 = ((bf16[4,8,2048]{2,0,1:T(4,128)(2,1)}), bf16[4,8,2048]{2,0,1:T(4,128)(2,1)S(1)}, u32[]{:S(2)}, u32[]{:S(2)}) async-start(bf16[4,8,2048]{2,0,1:T(4,128)(2,1)} %copy.177), calls=%async_computation.2 | async-start | bytes 262144 | tf_op jit(solution)/shard_map/all_to_all | solution.py:173
  175.3 4.5 %copy-start.12 = (s32[256]{0:T(256)S(1)}, s32[256]{0:T(256)}, u32[]{:S(2)}) copy-start(s32[256]{0:T(256)} %param.29) | copy-start | bytes 3076
  175.3 23.1 %all-to-all-start.4 = ((bf16[4,2,64,1536]{3,2,1,0:T(8,128)(2,1)}), bf16[4,2,64,1536]{3,2,1,0:T(8,128)(2,1)S(1)}, u32[]{:S(2)}, u32[]{:S(2)}) async-start(bf16[4,2,64,1536]{3,2,1,0:T(8,128)(2,1)} %bitcast.91), calls=%async_computation.4 | async-start | bytes 3145728 | tf_op jit(solution)/shard_map/all_to_all | solution.py:328
  198.4 13.9 %copy-start.1 = (bf16[384,1536]{1,0:T(8,128)(2,1)S(1)}, bf16[384,1536]{1,0:T(8,128)(2,1)}, u32[]{:S(2)}) copy-start(bf16[384,1536]{1,0:T(8,128)(2,1)} %param.22) | copy-start | bytes 3538948
  198.7 0.9 copy-start.2
  199.6 11.0 %copy-start.3 = (f32[2,64,1536]{2,1,0:T(8,128)S(1)}, f32[2,64,1536]{2,1,0:T(8,128)}, u32[]{:S(2)}) copy-start(f32[2,64,1536]{2,1,0:T(8,128)} %copy-done.2) | copy-start | bytes 2359300
  199.6 11.0 %collective-permute-start.5 = (bf16[64,1536]{1,0:T(8,128)(2,1)S(1)}, bf16[64,1536]{1,0:T(8,128)(2,1)S(1)}, u32[]{:S(2)}, u32[]{:S(2)}) collective-permute-start(bf16[64,1536]{1,0:T(8,128)(2,1)S(1)} %fusion.28), channel_id=1, source_target_pairs={{0,16},{16,0},{1,17},{17,1},{2,18},{18,2},{3,19},{19,3},{4,20},{20... | collective-permute-start | bytes 589832 | tf_op jit(solution)/shard_map/ppermute | solution.py:334

commit v17 on v14

--- a/solution.py
+++ b/solution.py
@@ -208,16 +208,21 @@
 
     def empty_partial(rows_in):
         heads, rows, _ = rows_in.shape
-        return (
-            jnp.zeros((heads, rows, head_dim), jnp.float32),
-            jnp.full((heads, rows, 1), masked_score, jnp.float32),
-            jnp.zeros((heads, rows, 1), jnp.float32),
+        return jnp.concatenate(
+            [
+                jnp.zeros((heads, rows, head_dim), jnp.float32),
+                jnp.full((heads, rows, 1), masked_score, jnp.float32),
+                jnp.zeros((heads, rows, 1), jnp.float32),
+            ],
+            axis=2,
         )
 
     far_part = lax.cond(
         holds_first,
         empty_partial,
-        lambda rows_in: attend_partial(flags, rows_in, kv_all, "cache", **shapes),
+        lambda rows_in: jnp.concatenate(
+            attend_partial(flags, rows_in, kv_all, "cache", **shapes), axis=2
+        ),
         partner_rows,
     )
     own_part = lax.cond(
@@ -226,7 +231,10 @@
         lambda rows_in: attend_partial(flags, rows_in, kv_all, "new", **shapes),
         query_rows,
     )
-    back_acc, back_best, back_total = lax.ppermute(far_part, "half", perm=[(1, 0)])
+    back = lax.ppermute(far_part, "half", perm=[(1, 0)])
+    back_acc = back[..., :head_dim]
+    back_best = back[..., head_dim : head_dim + 1]
+    back_total = back[..., head_dim + 1 :]
     back_best = jnp.where(holds_first, back_best, masked_score)
     back_total = jnp.where(holds_first, back_total, 0.0)
     back_acc = jnp.where(holds_first, back_acc, 0.0)

time: 209 us -> 206 us (0.986)
  waiting for transfers between devices: 79.7 us -> 96.1 us
  starting transfers between devices: 44.7 us -> 30.5 us
  local copies, waits for them, and re-layouts: 26.4 us -> 20.7 us
    ppermute x3 -> x1, waiting for transfers between devices: 3.93 us -> 13.2 us  [body(): back = lax.ppermute(far_part, 'half', perm=[(1, 0)])]
    all_to_all x1, starting transfers between devices: 12.4 us -> 5.15 us  [body(): lax.all_to_all(jnp.broadcast_to(pair[None], (half_size,) + pair.shape), '...]
    ppermute x1, waiting for transfers between devices: 5.06 us -> 12.2 us  [body(): crossed = lax.ppermute(packed, 'half', perm=[(0, 1), (1, 0)])]
    ppermute x1, starting transfers between devices: 4.48 us -> 0.07 us  [body(): crossed = lax.ppermute(packed, 'half', perm=[(0, 1), (1, 0)])]
    cond x5 -> x3, local copies, waits for them, and re-layouts: 4.94 us -> 1.05 us  [the longest x1 1.04 us: body(): lax.cond(holds_first, empty_partial, lambda rows_in: jnp.concatenate(atte...]
    ppermute x3 -> x1, starting transfers between devices: 3.87 us -> 1.28 us  [body(): back = lax.ppermute(far_part, 'half', perm=[(1, 0)])]
    another operation x5 -> x3, local copies, waits for them, and re-layouts: 6.5 us -> 4.64 us
  transfers between devices with their start and end apart: 11 -> 9, of which waited for: 9 -> 8; matrix products, arithmetic and copies ran while one was open for 8% -> 8% of each run, Pallas kernels for 11% -> 11%
where the time goes in v17:
time: 206 us; the launch traced here: 205 us
  waiting for transfers between devices  96.1 us (47%)
  starting transfers between devices  30.5 us (15%)
  matrix products  27.6 us (13%)
  Pallas kernels  23.5 us (11%)
  local copies, waits for them, and re-layouts  20.7 us (10%)
  other arithmetic  5.23 us (3%)
    pallas_call x1, Pallas kernels, attend_partial(): pl.pallas_call(kernel, out_shape=(jax.ShapeDtypeStruct((heads, rows, dim)...  23.5 us
    all_to_all x1, waiting for transfers between devices, body(): lax.all_to_all(jnp.broadcast_to(pair[None], (half_size,) + pair.shape), '...  19.9 us
    all_to_all x1, waiting for transfers between devices, body(): lax.all_to_all(by_dest.transpose(1, 0, 2, 3), 'hseq', split_axis=0, conca...  17.8 us
    ppermute x1, waiting for transfers between devices, body(): back = lax.ppermute(far_part, 'half', perm=[(1, 0)])  13.2 us
    ppermute x1, waiting for transfers between devices, body(): partner_rows = lax.ppermute(query_rows, 'half', perm=[(0, 1)])  13.1 us
    ppermute x1, waiting for transfers between devices, body(): crossed = lax.ppermute(packed, 'half', perm=[(0, 1), (1, 0)])  12.2 us
    all_to_all x1, waiting for transfers between devices, body(): lax.all_to_all(projected.reshape(exp_count, -1, projected.shape[1]), 'exp...  11.2 us
    dot_general x1, matrix products, body(): jnp.einsum('ecd,edf->ecf', rows_in, expert_in, preferred_element_type=jnp...  10.2 us
  transfers between devices with their start and end apart: 9, of which 8 were waited for; matrix products, arithmetic and copies ran while one was open for 8% of the time, Pallas kernels for 11%

profile of v17, /device:TPU:0, one launch (start us, length us, event | category | flops | bytes accessed | tf_op | source)
XLA Modules:
  0.0 204.8 jit_solution(16931923219972659934)
XLA Ops:
  0.7 1.5 fusion.7
  2.2 1.7 convolution_convert_fusion.5
  4.0 0.5 convolution_convert_fusion.4
  4.6 0.7 pad_maximum_fusion.2
  5.4 1.3 broadcast_in_dim.86
  6.7 5.2 %all-to-all-start = ((bf16[4,2,2,768,64]{3,4,2,1,0:T(8,128)(2,1)}), bf16[4,2,2,768,64]{3,4,2,1,0:T(8,128)(2,1)S(1)}, u32[]{:S(2)}, u32[]{:S(2)}) async-start(bf16[4,2,2,768,64]{3,4,2,1,0:T(8,128)(2,1)} %broadcast_in_dim.86), calls=%async_computation | async-start | bytes 3145728 | tf_op jit(solution)/shard_map/all_to_all | solution.py:196
  11.9 2.6 %convolution_convert_fusion.3 = bf16[256,384]{1,0:T(8,128)(2,1)} fusion(bf16[1536,384]{1,0:T(8,128)(2,1)} %param.19, bf16[256,1536]{1,0:T(8,128)(2,1)S(1)} %copy-done.4, f32[1536]{0:T(1024)S(1)} %copy-done.17, f32[256]{0:T(256)S(1)} %add_rsqrt_fusion), kind=kOutput, calls=%fused_computation.25 | convolution fusion | flops 303661056 | bytes 2169856 | tf_op jit(solution)/shard_map/dot_general | solution.py:158
  14.5 1.1 copy.153
  15.6 4.5 %collective-permute-start = (bf16[2,768,64]{1,2,0:T(8,128)(2,1)S(1)}, bf16[2,768,64]{1,2,0:T(8,128)(2,1)S(1)}, u32[]{:S(2)}, u32[]{:S(2)}) collective-permute-start(bf16[2,768,64]{1,2,0:T(8,128)(2,1)S(1)} %bitcast.98), channel_id=1, source_target_pairs={{0,16},{1,17},{2,18},{3,19},{4,20},{5,21},{6,22},{7,23},{8,24},{9,... | collective-permute-start | bytes 589832 | tf_op jit(solution)/shard_map/ppermute | solution.py:205
  20.1 13.1 %collective-permute-done = bf16[2,768,64]{1,2,0:T(8,128)(2,1)S(1)} collective-permute-done((bf16[2,768,64]{1,2,0:T(8,128)(2,1)S(1)}, bf16[2,768,64]{1,2,0:T(8,128)(2,1)S(1)}, u32[]{:S(2)}, u32[]{:S(2)}) %collective-permute-start) | collective-permute-done | bytes 196640 | tf_op jit(solution)/shard_map/ppermute | solution.py:205
  33.3 1.0 copy.165
  34.4 1.3 collective-permute-start.1
  35.7 31.3 %conditional.2 = (f32[2,768,64]{1,2,0:T(8,128)S(1)}, f32[2,768,1]{1,0,2:T(2,128)S(1)}, f32[2,768,1]{1,0,2:T(2,128)S(1)}) conditional(s32[]{:T(128)} %convert_element_type.90, (s32[1]{0:T(128)}, bf16[2,768,64]{1,2,0:T(8,128)(2,1)}, bf16[4,2,2,768,64]{3,4,2,1,0:T(8,128)(2,1)S(1)}) %tuple.61, (s32[1]{0:T(128)}, bf16[2,768,64]{1,2,0:T(8,128)(2,1)}, ...), branch_computations={%region_1.2_spmd, %region_2.3_spmd} | conditional | bytes 4374580 | solution.py:228
  35.7 1.9 copy.161.q_ref
  37.6 2.8 %copy.162.k_ref.v_ref = bf16[4,2,2,768,64]{4,3,2,1,0:T(8,128)(2,1)} copy(bf16[4,2,2,768,64]{3,4,2,1,0:T(8,128)(2,1)S(1)} %get-tuple-element.90) | data formatting | bytes 3145728 | tf_op jit(solution)/shard_map
  40.3 23.5 %branch_1_fun.1 = (f32[2,768,64]{2,1,0:T(8,128)}, f32[2,768,1]{2,1,0:T(8,128)}, f32[2,768,1]{2,1,0:T(8,128)}) custom-call(s32[1]{0:T(128)} %get-tuple-element.24.flags_ref, bf16[2,768,64]{2,1,0:T(8,128)(2,1)} %copy.161.q_ref, bf16[4,2,2,768,64]{4,3,2,1,0:T(8,128)(2,1)} %copy.162.k_ref.v_ref, bf16[4,2,2,768,64]{4,3,2,1,0:T(8,128)(2,1)} %copy.162.k_ref.v_ref), custom_call_target="tpu_custom_call" | custom-call | tf_op jit(solution)/shard_map/cond/branch_1_fun/pallas_call | solution.py:96
  63.9 1.5 copy.187
  65.3 1.4 copy.189
  66.7 0.3 copy.191
  67.0 13.2 %collective-permute-done.1 = f32[2,768,66]{1,0,2:T(2,128)S(1)} collective-permute-done((f32[2,768,66]{1,0,2:T(2,128)}, f32[2,768,66]{1,0,2:T(2,128)S(1)}, u32[]{:S(2)}, u32[]{:S(2)}) %collective-permute-start.1) | collective-permute-done | bytes 405536 | tf_op jit(solution)/shard_map/ppermute | solution.py:234
  80.5 1.5 convolution_convert_fusion.2
  82.0 3.8 %all-to-all-start.1 = ((bf16[4,64,1536]{2,1,0:T(8,128)(2,1)}), bf16[4,64,1536]{2,1,0:T(8,128)(2,1)S(1)}, u32[]{:S(2)}, u32[]{:S(2)}) async-start(bf16[4,64,1536]{2,1,0:T(8,128)(2,1)} %bitcast.15), calls=%async_computation.1 | async-start | bytes 1572864 | tf_op jit(solution)/shard_map/all_to_all | solution.py:252
  86.2 11.2 %all-to-all-done.1 = bf16[4,64,1536]{2,1,0:T(8,128)(2,1)S(1)} async-done(((bf16[4,64,1536]{2,1,0:T(8,128)(2,1)}), bf16[4,64,1536]{2,1,0:T(8,128)(2,1)S(1)}, u32[]{:S(2)}, u32[]{:S(2)}) %all-to-all-start.1) | async-done | bytes 786464 | tf_op jit(solution)/shard_map/all_to_all | solution.py:252
  98.0 12.2 %collective-permute-done.2 = bf16[64,1664]{1,0:T(8,128)(2,1)S(1)} collective-permute-done((bf16[64,1664]{1,0:T(8,128)(2,1)S(1)}, bf16[64,1664]{1,0:T(8,128)(2,1)S(1)}, u32[]{:S(2)}, u32[]{:S(2)}) %collective-permute-start.2) | collective-permute-done | bytes 213024 | tf_op jit(solution)/shard_map/ppermute | solution.py:284
  110.4 1.3 broadcast_in_dim.93
  111.7 5.1 %all-to-all-start.2 = ((bf16[4,2,64,1664]{3,2,1,0:T(8,128)(2,1)}), bf16[4,2,64,1664]{3,2,1,0:T(8,128)(2,1)S(1)}, u32[]{:S(2)}, u32[]{:S(2)}) async-start(bf16[4,2,64,1664]{3,2,1,0:T(8,128)(2,1)} %broadcast_in_dim.93), calls=%async_computation.2 | async-start | bytes 3407872 | tf_op jit(solution)/shard_map/all_to_all | solution.py:288
  116.9 19.9 %all-to-all-done.2 = bf16[4,2,64,1664]{3,2,1,0:T(8,128)(2,1)S(1)} async-done(((bf16[4,2,64,1664]{3,2,1,0:T(8,128)(2,1)}), bf16[4,2,64,1664]{3,2,1,0:T(8,128)(2,1)S(1)}, u32[]{:S(2)}, u32[]{:S(2)}) %all-to-all-start.2) | async-done | bytes 1703968 | tf_op jit(solution)/shard_map/all_to_all | solution.py:288
  136.9 0.2 constant_dynamic-slice_fusion.1
  137.1 1.0 copy-done.6
  138.7 10.2 %fusion.56 = f32[4,256,1024]{2,1,0:T(8,128)} fusion(bf16[4,1536,1024]{2,1,0:T(8,128)(2,1)} %param.25, bf16[512,1664]{1,0:T(8,128)(2,1)} %bitcast.97, s32[512,4]{0,1:T(4,128)S(1)} %eq.48, pred[512,4]{0,1:T(4,128)(4,1)S(1)} %get-tuple-element.106), kind=kOutput, calls=%fused_computation.99 | convolution fusion | flops 4834459648 | bytes 18360320 | tf_op jit(solution)/shard_map/ecd,edf->ecf/dot_general | solution.py:323
  148.9 5.9 %convolution_convert_fusion.1 = bf16[4,256,1536]{2,1,0:T(8,128)(2,1)S(1)} fusion(bf16[4,512,1536]{2,1,0:T(8,128)(2,1)} %param.26, f32[4,256,1024]{2,1,0:T(8,128)} %fusion.56), kind=kOutput, calls=%fused_computation.4 | convolution fusion | flops 1615331328 | bytes 13631488 | tf_op jit(solution)/shard_map/ecf,efd->ecd/dot_general | solution.py:326
  154.8 2.1 %convolution_bitcast_fusion = f32[512,1536]{1,0:T(8,128)S(1)} fusion(bf16[4,256,1536]{2,1,0:T(8,128)(2,1)S(1)} %convolution_convert_fusion.1, s32[512,4]{0,1:T(4,128)S(1)} %eq.48, pred[512,4]{0,1:T(4,128)(4,1)S(1)} %get-tuple-element.106, bf16[512,4]{0,1:T(4,128)(2,1)S(1)} %copy.197), kind=kOutput, calls=%fused_computation.5 | convolution fusion | flops 1612185600 | bytes 6305792 | tf_op jit(solution)/shard_map/nec,ecd->nd/dot_general | solution.py:333
  157.0 3.0 %fusion.1 = bf16[512,1536]{1,0:T(8,128)(2,1)S(1)} fusion(f32[512,1536]{1,0:T(8,128)S(1)} %convolution_bitcast_fusion, bf16[4,256,1536]{2,1,0:T(8,128)(2,1)S(1)} %convolution_convert_fusion.1, s32[512,4]{0,1:T(4,128)S(1)} %eq.48, pred[512,4]{0,1:T(4,128)(4,1)S(1)} %get-tuple-element.106, bf16[512,4]{0,1:T(4,128)(2,1)S(1)} %copy.196), kind=kOutput, calls=%fused_computation.9 | convolution fusion | flops 1613758464 | bytes 7878656 | tf_op jit(solution)/shard_map/nec,ecd->nd/dot_general | solution.py:331
  159.9 1.3 copy.213
  161.3 3.7 %all-to-all-start.3 = ((bf16[4,2,64,1536]{3,2,1,0:T(8,128)(2,1)}), bf16[4,2,64,1536]{3,2,1,0:T(8,128)(2,1)S(1)}, u32[]{:S(2)}, u32[]{:S(2)}) async-start(bf16[4,2,64,1536]{3,2,1,0:T(8,128)(2,1)} %bitcast.95), calls=%async_computation.3 | async-start | bytes 3145728 | tf_op jit(solution)/shard_map/all_to_all | solution.py:335
  165.3 0.3 reshape_reshape.3
  165.6 0.8 copy.180
  166.5 17.8 %all-to-all-done.3 = bf16[4,2,64,1536]{3,2,1,0:T(8,128)(2,1)S(1)} async-done(((bf16[4,2,64,1536]{3,2,1,0:T(8,128)(2,1)}), bf16[4,2,64,1536]{3,2,1,0:T(8,128)(2,1)S(1)}, u32[]{:S(2)}, u32[]{:S(2)}) %all-to-all-start.3) | async-done | bytes 1572896 | tf_op jit(solution)/shard_map/all_to_all | solution.py:335
  184.3 3.8 %all-to-all-start.4 = ((bf16[4,8,2048]{2,0,1:T(4,128)(2,1)}), bf16[4,8,2048]{2,0,1:T(4,128)(2,1)S(1)}, u32[]{:S(2)}, u32[]{:S(2)}) async-start(bf16[4,8,2048]{2,0,1:T(4,128)(2,1)} %copy.180), calls=%async_computation.4 | async-start | bytes 262144 | tf_op jit(solution)/shard_map/all_to_all | solution.py:173
  188.1 0.2 convert_reduce_fusion
  188.4 0.9 copy-done.2
  189.3 3.0 %collective-permute-start.3 = (bf16[64,1536]{1,0:T(8,128)(2,1)S(1)}, bf16[64,1536]{1,0:T(8,128)(2,1)S(1)}, u32[]{:S(2)}, u32[]{:S(2)}) collective-permute-start(bf16[64,1536]{1,0:T(8,128)(2,1)S(1)} %fusion.33), channel_id=1, source_target_pairs={{0,16},{16,0},{1,17},{17,1},{2,18},{18,2},{3,19},{19,3},{4,20},{20... | collective-permute-start | bytes 589832 | tf_op jit(solution)/shard_map/ppermute | solution.py:341
  192.3 7.4 %all-to-all-done.4 = bf16[4,8,2048]{2,0,1:T(4,128)(2,1)S(1)} async-done(((bf16[4,8,2048]{2,0,1:T(4,128)(2,1)}), bf16[4,8,2048]{2,0,1:T(4,128)(2,1)S(1)}, u32[]{:S(2)}, u32[]{:S(2)}) %all-to-all-start.4) | async-done | bytes 131104 | tf_op jit(solution)/shard_map/all_to_all | solution.py:173
  199.7 0.9 scatter_custom_fusion
  200.6 0.2 reshape.163
  200.9 0.8 reshape.177
  201.7 1.3 collective-permute-done.3
  203.1 1.7 fusion.31
  (82 shorter events, 3.2 us)
Async XLA Ops:
  0.6 79.8 %copy-start = (bf16[384,1536]{1,0:T(8,128)(2,1)S(1)}, bf16[384,1536]{1,0:T(8,128)(2,1)}, u32[]{:S(2)}) copy-start(bf16[384,1536]{1,0:T(8,128)(2,1)} %param.22) | copy-start | bytes 3538948
  0.6 3.3 %copy-start.4 = (bf16[256,1536]{1,0:T(8,128)(2,1)S(1)}, bf16[256,1536]{1,0:T(8,128)(2,1)}, u32[]{:S(2)}) copy-start(bf16[256,1536]{1,0:T(8,128)(2,1)} %param.17) | copy-start | bytes 2359300
  0.7 3.3 %copy-start.17 = (f32[1536]{0:T(1024)S(1)}, f32[1536]{0:T(1024)}, u32[]{:S(2)}) copy-start(f32[1536]{0:T(1024)} %param.18) | copy-start | bytes 18436
  0.7 3.3 %copy-start.16 = (bf16[1536,128]{1,0:T(8,128)(2,1)S(1)}, bf16[1536,128]{1,0:T(8,128)(2,1)}, u32[]{:S(2)}) copy-start(bf16[1536,128]{1,0:T(8,128)(2,1)} %param.21) | copy-start | bytes 1179652
  0.7 3.8 %copy-start.11 = (bf16[512,256]{1,0:T(8,128)(2,1)S(1)}, bf16[512,256]{1,0:T(8,128)(2,1)}, u32[]{:S(2)}) copy-start(bf16[512,256]{1,0:T(8,128)(2,1)} %param.23) | copy-start | bytes 786436
  6.7 26.5 %all-to-all-start = ((bf16[4,2,2,768,64]{3,4,2,1,0:T(8,128)(2,1)}), bf16[4,2,2,768,64]{3,4,2,1,0:T(8,128)(2,1)S(1)}, u32[]{:S(2)}, u32[]{:S(2)}) async-start(bf16[4,2,2,768,64]{3,4,2,1,0:T(8,128)(2,1)} %broadcast_in_dim.86), calls=%async_computation | async-start | bytes 3145728 | tf_op jit(solution)/shard_map/all_to_all | solution.py:196
  15.6 17.6 %copy-start.7 = (bf16[2,3,8,8,256]{4,3,1,2,0:T(8,128)(2,1)}, bf16[2,3,8,8,256]{4,3,1,2,0:T(8,128)(2,1)S(1)}, u32[]{:S(2)}) copy-start(bf16[2,3,8,8,256]{4,3,1,2,0:T(8,128)(2,1)S(1)} %copy.198) | copy-start | bytes 589828
  15.6 17.6 %collective-permute-start = (bf16[2,768,64]{1,2,0:T(8,128)(2,1)S(1)}, bf16[2,768,64]{1,2,0:T(8,128)(2,1)S(1)}, u32[]{:S(2)}, u32[]{:S(2)}) collective-permute-start(bf16[2,768,64]{1,2,0:T(8,128)(2,1)S(1)} %bitcast.98), channel_id=1, source_target_pairs={{0,16},{1,17},{2,18},{3,19},{4,20},{5,21},{6,22},{7,23},{8,24},{9,... | collective-permute-start | bytes 589832 | tf_op jit(solution)/shard_map/ppermute | solution.py:205
  34.4 45.8 %collective-permute-start.1 = (f32[2,768,66]{1,0,2:T(2,128)}, f32[2,768,66]{1,0,2:T(2,128)S(1)}, u32[]{:S(2)}, u32[]{:S(2)}) collective-permute-start(f32[2,768,66]{1,0,2:T(2,128)} %copy.165), channel_id=1, source_target_pairs={{16,0},{17,1},{18,2},{19,3},{20,4},{21,5},{22,6},{23,7},{24,8},{25... | collective-permute-start | bytes 1216520 | tf_op jit(solution)/shard_map/ppermute | solution.py:234
  63.9 2.9 %copy-start.9 = (f32[2,768,1]{2,1,0:T(8,128)S(1)}, f32[2,768,1]{2,1,0:T(8,128)}, u32[]{:S(2)}) copy-start(f32[2,768,1]{2,1,0:T(8,128)} %get-tuple-element.101) | copy-start | bytes 18436 | tf_op jit(solution)/shard_map/cond
  80.4 5.4 %copy-start.13 = (s32[64,8]{0,1:T(8,128)S(1)}, s32[64,8]{0,1:T(8,128)}, u32[]{:S(2)}) copy-start(s32[64,8]{0,1:T(8,128)} %param.27) | copy-start | bytes 6148
  80.4 5.5 %copy-start.12 = (f32[64,8]{0,1:T(8,128)S(1)}, f32[64,8]{0,1:T(8,128)}, u32[]{:S(2)}) copy-start(f32[64,8]{0,1:T(8,128)} %param.28) | copy-start | bytes 6148
  80.5 17.1 %copy-start.5 = (bf16[256,1536]{1,0:T(8,128)(2,1)S(1)}, bf16[256,1536]{1,0:T(8,128)(2,1)}, u32[]{:S(2)}) copy-start(bf16[256,1536]{1,0:T(8,128)(2,1)} %param.17) | copy-start | bytes 2359300
  82.0 15.7 %copy-start.14 = (f32[1536]{0:T(1024)S(1)}, f32[1536]{0:T(1024)}, u32[]{:S(2)}) copy-start(f32[1536]{0:T(1024)} %param.24) | copy-start | bytes 18436
  82.0 15.4 %all-to-all-start.1 = ((bf16[4,64,1536]{2,1,0:T(8,128)(2,1)}), bf16[4,64,1536]{2,1,0:T(8,128)(2,1)S(1)}, u32[]{:S(2)}, u32[]{:S(2)}) async-start(bf16[4,64,1536]{2,1,0:T(8,128)(2,1)} %bitcast.15), calls=%async_computation.1 | async-start | bytes 1572864 | tf_op jit(solution)/shard_map/all_to_all | solution.py:252
  98.0 12.3 %collective-permute-start.2 = (bf16[64,1664]{1,0:T(8,128)(2,1)S(1)}, bf16[64,1664]{1,0:T(8,128)(2,1)S(1)}, u32[]{:S(2)}, u32[]{:S(2)}) collective-permute-start(bf16[64,1664]{1,0:T(8,128)(2,1)S(1)} %concatenate.21), channel_id=1, source_target_pairs={{0,16},{16,0},{1,17},{17,1},{2,18},{18,2},{3,19},{19,3},{4,20},{20... | collective-permute-start | bytes 638984 | tf_op jit(solution)/shard_map/ppermute | solution.py:284
  111.7 25.0 %all-to-all-start.2 = ((bf16[4,2,64,1664]{3,2,1,0:T(8,128)(2,1)}), bf16[4,2,64,1664]{3,2,1,0:T(8,128)(2,1)S(1)}, u32[]{:S(2)}, u32[]{:S(2)}) async-start(bf16[4,2,64,1664]{3,2,1,0:T(8,128)(2,1)} %broadcast_in_dim.93), calls=%async_computation.2 | async-start | bytes 3407872 | tf_op jit(solution)/shard_map/all_to_all | solution.py:288
  136.9 1.2 copy-start.6
  161.3 3.9 %copy-start.10 = (bf16[256,2,2,64]{0,3,2,1:T(8,128)(2,1)S(1)}, bf16[256,2,2,64]{0,3,2,1:T(8,128)(2,1)}, u32[]{:S(2)}) copy-start(bf16[256,2,2,64]{0,3,2,1:T(8,128)(2,1)} %get-tuple-element.112) | copy-start | bytes 393220
  161.3 5.1 %copy-start.15 = (s32[256]{0:T(256)S(1)}, s32[256]{0:T(256)}, u32[]{:S(2)}) copy-start(s32[256]{0:T(256)} %param.29) | copy-start | bytes 3076
  161.3 23.1 %all-to-all-start.3 = ((bf16[4,2,64,1536]{3,2,1,0:T(8,128)(2,1)}), bf16[4,2,64,1536]{3,2,1,0:T(8,128)(2,1)S(1)}, u32[]{:S(2)}, u32[]{:S(2)}) async-start(bf16[4,2,64,1536]{3,2,1,0:T(8,128)(2,1)} %bitcast.95), calls=%async_computation.3 | async-start | bytes 3145728 | tf_op jit(solution)/shard_map/all_to_all | solution.py:335
  184.3 15.4 %all-to-all-start.4 = ((bf16[4,8,2048]{2,0,1:T(4,128)(2,1)}), bf16[4,8,2048]{2,0,1:T(4,128)(2,1)S(1)}, u32[]{:S(2)}, u32[]{:S(2)}) async-start(bf16[4,8,2048]{2,0,1:T(4,128)(2,1)} %copy.180), calls=%async_computation.4 | async-start | bytes 262144 | tf_op jit(solution)/shard_map/all_to_all | solution.py:173
  188.1 16.7 %copy-start.1 = (bf16[384,1536]{1,0:T(8,128)(2,1)S(1)}, bf16[384,1536]{1,0:T(8,128)(2,1)}, u32[]{:S(2)}) copy-start(bf16[384,1536]{1,0:T(8,128)(2,1)} %param.22) | copy-start | bytes 3538948
  188.4 0.9 copy-start.2
  189.3 13.8 %copy-start.3 = (f32[2,64,1536]{2,1,0:T(8,128)S(1)}, f32[2,64,1536]{2,1,0:T(8,128)}, u32[]{:S(2)}) copy-start(f32[2,64,1536]{2,1,0:T(8,128)} %copy-done.2) | copy-start | bytes 2359300
  189.3 13.8 %collective-permute-start.3 = (bf16[64,1536]{1,0:T(8,128)(2,1)S(1)}, bf16[64,1536]{1,0:T(8,128)(2,1)S(1)}, u32[]{:S(2)}, u32[]{:S(2)}) collective-permute-start(bf16[64,1536]{1,0:T(8,128)(2,1)S(1)} %fusion.33), channel_id=1, source_target_pairs={{0,16},{16,0},{1,17},{17,1},{2,18},{18,2},{3,19},{19,3},{4,20},{20... | collective-permute-start | bytes 589832 | tf_op jit(solution)/shard_map/ppermute | solution.py:341

commit v18 on v17

--- a/solution.py
+++ b/solution.py
@@ -206,23 +206,31 @@
     flags = jnp.reshape(half_pos * tokens_here, (1,)).astype(jnp.int32)
     shapes = dict(cache_rows=cache_rows, group_rows=tokens_here)
 
+    def pack_partial(part):
+        acc, best, total = part
+        pieces = [acc.astype(jnp.bfloat16)]
+        for value in (best, total):
+            high = value.astype(jnp.bfloat16)
+            rest = value - high.astype(jnp.float32)
+            middle = rest.astype(jnp.bfloat16)
+            low = (rest - middle.astype(jnp.float32)).astype(jnp.bfloat16)
+            pieces += [high, middle, low]
+        return jnp.concatenate(pieces, axis=2)
+
     def empty_partial(rows_in):
         heads, rows, _ = rows_in.shape
-        return jnp.concatenate(
-            [
+        return pack_partial(
+            (
                 jnp.zeros((heads, rows, head_dim), jnp.float32),
                 jnp.full((heads, rows, 1), masked_score, jnp.float32),
                 jnp.zeros((heads, rows, 1), jnp.float32),
-            ],
-            axis=2,
+            )
         )
 
     far_part = lax.cond(
         holds_first,
         empty_partial,
-        lambda rows_in: jnp.concatenate(
-            attend_partial(flags, rows_in, kv_all, "cache", **shapes), axis=2
-        ),
+        lambda rows_in: pack_partial(attend_partial(flags, rows_in, kv_all, "cache", **shapes)),
         partner_rows,
     )
     own_part = lax.cond(
@@ -231,10 +239,10 @@
         lambda rows_in: attend_partial(flags, rows_in, kv_all, "new", **shapes),
         query_rows,
     )
-    back = lax.ppermute(far_part, "half", perm=[(1, 0)])
+    back = lax.ppermute(far_part, "half", perm=[(1, 0)]).astype(jnp.float32)
     back_acc = back[..., :head_dim]
-    back_best = back[..., head_dim : head_dim + 1]
-    back_total = back[..., head_dim + 1 :]
+    back_best = jnp.sum(back[..., head_dim : head_dim + 3], axis=2, keepdims=True)
+    back_total = jnp.sum(back[..., head_dim + 3 : head_dim + 6], axis=2, keepdims=True)
     back_best = jnp.where(holds_first, back_best, masked_score)
     back_total = jnp.where(holds_first, back_total, 0.0)
     back_acc = jnp.where(holds_first, back_acc, 0.0)

time: 206 us -> 212 us (1.029)
  local copies, waits for them, and re-layouts: 20.7 us -> 26.1 us
    concatenate x1, local copies, waits for them, and re-layouts: 0.06 us -> 3.61 us  [pack_partial(): return jnp.concatenate(pieces, axis=2)]
    another operation x3 -> x8, local copies, waits for them, and re-layouts: 4.64 us -> 7.72 us
  transfers between devices with their start and end apart: 9 -> 9, of which waited for: 8 -> 8; matrix products, arithmetic and copies ran while one was open for 8% -> 7% of each run, Pallas kernels for 11% -> 11%
where the time goes in v18:
time: 212 us; the launch traced here: 210 us
  waiting for transfers between devices  95.4 us (45%)
  starting transfers between devices  29.8 us (14%)
  matrix products  27.6 us (13%)
  local copies, waits for them, and re-layouts  26.1 us (12%)
  Pallas kernels  23.5 us (11%)
  other arithmetic  6.83 us (3%)
    pallas_call x1, Pallas kernels, attend_partial(): pl.pallas_call(kernel, out_shape=(jax.ShapeDtypeStruct((heads, rows, dim)...  23.5 us
    all_to_all x1, waiting for transfers between devices, body(): lax.all_to_all(jnp.broadcast_to(pair[None], (half_size,) + pair.shape), '...  19.9 us
    all_to_all x1, waiting for transfers between devices, body(): lax.all_to_all(by_dest.transpose(1, 0, 2, 3), 'hseq', split_axis=0, conca...  17.8 us
    ppermute x1, waiting for transfers between devices, body(): partner_rows = lax.ppermute(query_rows, 'half', perm=[(0, 1)])  13.1 us
    ppermute x1, waiting for transfers between devices, body(): back = lax.ppermute(far_part, 'half', perm=[(1, 0)]).astype(jnp.float32)  12.5 us
    ppermute x1, waiting for transfers between devices, body(): crossed = lax.ppermute(packed, 'half', perm=[(0, 1), (1, 0)])  12.2 us
    all_to_all x1, waiting for transfers between devices, body(): lax.all_to_all(projected.reshape(exp_count, -1, projected.shape[1]), 'exp...  11.2 us
    dot_general x1, matrix products, body(): jnp.einsum('ecd,edf->ecf', rows_in, expert_in, preferred_element_type=jnp...  10.2 us
  transfers between devices with their start and end apart: 9, of which 8 were waited for; matrix products, arithmetic and copies ran while one was open for 7% of the time, Pallas kernels for 11%

profile of v18, /device:TPU:0, one launch (start us, length us, event | category | flops | bytes accessed | tf_op | source)
XLA Modules:
  0.0 210.5 jit_solution(10503754524028155947)
XLA Ops:
  0.7 1.5 fusion.9
  2.2 1.7 convolution_convert_fusion.5
  5.4 1.3 broadcast_in_dim.53
  6.7 5.2 %all-to-all-start = ((bf16[4,2,2,768,64]{3,4,2,1,0:T(8,128)(2,1)}), bf16[4,2,2,768,64]{3,4,2,1,0:T(8,128)(2,1)S(1)}, u32[]{:S(2)}, u32[]{:S(2)}) async-start(bf16[4,2,2,768,64]{3,4,2,1,0:T(8,128)(2,1)} %broadcast_in_dim.53), calls=%async_computation | async-start | bytes 3145728 | tf_op jit(solution)/shard_map/all_to_all | solution.py:196
  11.9 2.6 %convolution_convert_fusion.3 = bf16[256,384]{1,0:T(8,128)(2,1)} fusion(bf16[1536,384]{1,0:T(8,128)(2,1)} %param.19, bf16[256,1536]{1,0:T(8,128)(2,1)S(1)} %copy-done.4, f32[1536]{0:T(1024)S(1)} %copy-done.15, f32[256]{0:T(256)S(1)} %add_rsqrt_fusion), kind=kOutput, calls=%fused_computation.29 | convolution fusion | flops 303661056 | bytes 2169856 | tf_op jit(solution)/shard_map/dot_general | solution.py:158
  14.5 1.1 copy.154
  15.6 4.5 %collective-permute-start = (bf16[2,768,64]{1,2,0:T(8,128)(2,1)S(1)}, bf16[2,768,64]{1,2,0:T(8,128)(2,1)S(1)}, u32[]{:S(2)}, u32[]{:S(2)}) collective-permute-start(bf16[2,768,64]{1,2,0:T(8,128)(2,1)S(1)} %bitcast.112), channel_id=1, source_target_pairs={{0,16},{1,17},{2,18},{3,19},{4,20},{5,21},{6,22},{7,23},{8,24},{9,... | collective-permute-start | bytes 589832 | tf_op jit(solution)/shard_map/ppermute | solution.py:205
  20.1 13.1 %collective-permute-done = bf16[2,768,64]{1,2,0:T(8,128)(2,1)S(1)} collective-permute-done((bf16[2,768,64]{1,2,0:T(8,128)(2,1)S(1)}, bf16[2,768,64]{1,2,0:T(8,128)(2,1)S(1)}, u32[]{:S(2)}, u32[]{:S(2)}) %collective-permute-start) | collective-permute-done | bytes 196640 | tf_op jit(solution)/shard_map/ppermute | solution.py:205
  33.2 7.7 %conditional.3 = (bf16[2,768,70]{2,1,0:T(8,128)(2,1)}) conditional(s32[]{:T(128)} %convert_element_type.128, (s32[1]{0:T(128)}, bf16[2,768,64]{1,2,0:T(8,128)(2,1)S(1)}, bf16[4,2,2,768,64]{3,4,2,1,0:T(8,128)(2,1)S(1)}) %tuple.21, () %tuple.22), branch_computations={%region_3.4_spmd, %region_4.5_spmd} | conditional | flops 119808 | bytes 4589576 | solution.py:230
  33.2 0.8 broadcast.147
  34.0 0.8 broadcast.143
  34.8 0.8 broadcast.144
  35.6 0.8 broadcast.145
  36.4 0.8 broadcast.146
  37.2 3.6 %concatenate.17 = bf16[2,768,70]{2,1,0:T(8,128)(2,1)} concatenate(bf16[2,768,64]{2,1,0:T(8,128)(2,1)} %broadcast.143, bf16[2,768,1]{2,1,0:T(8,128)(2,1)} %broadcast.144, bf16[2,768,1]{2,1,0:T(8,128)(2,1)} %broadcast.145, bf16[2,768,1]{2,1,0:T(8,128)(2,1)} %broadcast.146, bf16[2,768,2]{2,1,0:T(8,128)(2,1)} %broadcast.147, bf16[2,768,1]{2,1,0:T(8,128)(2,1)S(1)} %broadcast.148), dimensions={2} | concatenate | bytes 430080 | tf_op jit(solution)/shard_map/cond/branch_1_fun/concatenate | solution.py:218
  40.9 1.3 collective-permute-start.1
  42.1 30.1 %conditional.2 = (f32[2,768,64]{2,1,0:T(8,128)}, f32[2,768,1]{1,0,2:T(2,128)S(1)}, f32[2,768,1]{1,0,2:T(2,128)S(1)}) conditional(s32[]{:T(128)} %convert_element_type.128, (s32[1]{0:T(128)}, bf16[2,768,64]{1,2,0:T(8,128)(2,1)S(1)}, bf16[4,2,2,768,64]{3,4,2,1,0:T(8,128)(2,1)S(1)}) %tuple.67, (s32[1]{0:T(128)}, bf16[2,768,64]{1,2,0:T(8,128)(2,1)S(1)}, ...), branch_computations={%region_1.2_spmd, %region_2.3_spmd} | conditional | bytes 3563544 | solution.py:236
  42.2 0.9 copy.162.q_ref
  43.1 2.7 %copy.163.k_ref.v_ref = bf16[4,2,2,768,64]{4,3,2,1,0:T(8,128)(2,1)} copy(bf16[4,2,2,768,64]{3,4,2,1,0:T(8,128)(2,1)S(1)} %get-tuple-element.90) | data formatting | bytes 3145728 | tf_op jit(solution)/shard_map
  45.8 23.5 %branch_1_fun.1 = (f32[2,768,64]{2,1,0:T(8,128)}, f32[2,768,1]{2,1,0:T(8,128)}, f32[2,768,1]{2,1,0:T(8,128)}) custom-call(s32[1]{0:T(128)} %get-tuple-element.24.flags_ref, bf16[2,768,64]{2,1,0:T(8,128)(2,1)} %copy.162.q_ref, bf16[4,2,2,768,64]{4,3,2,1,0:T(8,128)(2,1)} %copy.163.k_ref.v_ref, bf16[4,2,2,768,64]{4,3,2,1,0:T(8,128)(2,1)} %copy.163.k_ref.v_ref), custom_call_target="tpu_custom_call" | custom-call | tf_op jit(solution)/shard_map/cond/branch_1_fun/pallas_call | solution.py:96
  69.3 1.4 copy.187
  70.7 1.4 copy.189
  72.3 12.5 %collective-permute-done.1 = bf16[2,768,70]{2,1,0:T(8,128)(2,1)S(1)} collective-permute-done((bf16[2,768,70]{2,1,0:T(8,128)(2,1)}, bf16[2,768,70]{2,1,0:T(8,128)(2,1)S(1)}, u32[]{:S(2)}, u32[]{:S(2)}) %collective-permute-start.1) | collective-permute-done | bytes 215072 | tf_op jit(solution)/shard_map/ppermute | solution.py:242
  84.8 0.9 slice_reduce_fusion.1
  85.8 0.8 fusion.27
  86.9 1.5 convolution_convert_fusion.2
  88.4 3.6 %all-to-all-start.1 = ((bf16[4,64,1536]{2,1,0:T(8,128)(2,1)}), bf16[4,64,1536]{2,1,0:T(8,128)(2,1)S(1)}, u32[]{:S(2)}, u32[]{:S(2)}) async-start(bf16[4,64,1536]{2,1,0:T(8,128)(2,1)} %bitcast.18), calls=%async_computation.1 | async-start | bytes 1572864 | tf_op jit(solution)/shard_map/all_to_all | solution.py:260
  92.4 11.2 %all-to-all-done.1 = bf16[4,64,1536]{2,1,0:T(8,128)(2,1)S(1)} async-done(((bf16[4,64,1536]{2,1,0:T(8,128)(2,1)}), bf16[4,64,1536]{2,1,0:T(8,128)(2,1)S(1)}, u32[]{:S(2)}, u32[]{:S(2)}) %all-to-all-start.1) | async-done | bytes 786464 | tf_op jit(solution)/shard_map/all_to_all | solution.py:260
  104.3 12.2 %collective-permute-done.2 = bf16[64,1664]{1,0:T(8,128)(2,1)S(1)} collective-permute-done((bf16[64,1664]{1,0:T(8,128)(2,1)S(1)}, bf16[64,1664]{1,0:T(8,128)(2,1)S(1)}, u32[]{:S(2)}, u32[]{:S(2)}) %collective-permute-start.2) | collective-permute-done | bytes 213024 | tf_op jit(solution)/shard_map/ppermute | solution.py:292
  116.6 1.3 broadcast_in_dim.95
  117.9 4.6 %all-to-all-start.2 = ((bf16[4,2,64,1664]{3,2,1,0:T(8,128)(2,1)}), bf16[4,2,64,1664]{3,2,1,0:T(8,128)(2,1)S(1)}, u32[]{:S(2)}, u32[]{:S(2)}) async-start(bf16[4,2,64,1664]{3,2,1,0:T(8,128)(2,1)} %broadcast_in_dim.95), calls=%async_computation.2 | async-start | bytes 3407872 | tf_op jit(solution)/shard_map/all_to_all | solution.py:296
  122.5 19.9 %all-to-all-done.2 = bf16[4,2,64,1664]{3,2,1,0:T(8,128)(2,1)S(1)} async-done(((bf16[4,2,64,1664]{3,2,1,0:T(8,128)(2,1)}), bf16[4,2,64,1664]{3,2,1,0:T(8,128)(2,1)S(1)}, u32[]{:S(2)}, u32[]{:S(2)}) %all-to-all-start.2) | async-done | bytes 1703968 | tf_op jit(solution)/shard_map/all_to_all | solution.py:296
  142.7 1.0 copy-done.6
  144.4 10.2 %fusion.57 = f32[4,256,1024]{2,1,0:T(8,128)} fusion(bf16[4,1536,1024]{2,1,0:T(8,128)(2,1)} %param.25, bf16[512,1664]{1,0:T(8,128)(2,1)} %bitcast.111, s32[512,4]{0,1:T(4,128)S(1)} %eq.48, pred[512,4]{0,1:T(4,128)(4,1)S(1)} %get-tuple-element.107), kind=kOutput, calls=%fused_computation.104 | convolution fusion | flops 4834459648 | bytes 18360320 | tf_op jit(solution)/shard_map/ecd,edf->ecf/dot_general | solution.py:331
  154.6 5.9 %convolution_convert_fusion.1 = bf16[4,256,1536]{2,1,0:T(8,128)(2,1)S(1)} fusion(bf16[4,512,1536]{2,1,0:T(8,128)(2,1)} %param.26, f32[4,256,1024]{2,1,0:T(8,128)} %fusion.57), kind=kOutput, calls=%fused_computation.8 | convolution fusion | flops 1615331328 | bytes 13631488 | tf_op jit(solution)/shard_map/ecf,efd->ecd/dot_general | solution.py:334
  160.5 2.2 %convolution_bitcast_fusion = f32[512,1536]{1,0:T(8,128)S(1)} fusion(bf16[4,256,1536]{2,1,0:T(8,128)(2,1)S(1)} %convolution_convert_fusion.1, s32[512,4]{0,1:T(4,128)S(1)} %eq.48, pred[512,4]{0,1:T(4,128)(4,1)S(1)} %get-tuple-element.107, bf16[512,4]{0,1:T(4,128)(2,1)S(1)} %copy.194), kind=kOutput, calls=%fused_computation.9 | convolution fusion | flops 1612185600 | bytes 6305792 | tf_op jit(solution)/shard_map/nec,ecd->nd/dot_general | solution.py:341
  162.7 3.0 %fusion.3 = bf16[512,1536]{1,0:T(8,128)(2,1)S(1)} fusion(f32[512,1536]{1,0:T(8,128)S(1)} %convolution_bitcast_fusion, bf16[4,256,1536]{2,1,0:T(8,128)(2,1)S(1)} %convolution_convert_fusion.1, s32[512,4]{0,1:T(4,128)S(1)} %eq.48, pred[512,4]{0,1:T(4,128)(4,1)S(1)} %get-tuple-element.107, bf16[512,4]{0,1:T(4,128)(2,1)S(1)} %copy.193), kind=kOutput, calls=%fused_computation.13 | convolution fusion | flops 1613758464 | bytes 7878656 | tf_op jit(solution)/shard_map/nec,ecd->nd/dot_general | solution.py:339
  165.6 1.3 copy.201
  166.9 3.7 %all-to-all-start.3 = ((bf16[4,2,64,1536]{3,2,1,0:T(8,128)(2,1)}), bf16[4,2,64,1536]{3,2,1,0:T(8,128)(2,1)S(1)}, u32[]{:S(2)}, u32[]{:S(2)}) async-start(bf16[4,2,64,1536]{3,2,1,0:T(8,128)(2,1)} %bitcast.109), calls=%async_computation.3 | async-start | bytes 3145728 | tf_op jit(solution)/shard_map/all_to_all | solution.py:343
  172.2 17.8 %all-to-all-done.3 = bf16[4,2,64,1536]{3,2,1,0:T(8,128)(2,1)S(1)} async-done(((bf16[4,2,64,1536]{3,2,1,0:T(8,128)(2,1)}), bf16[4,2,64,1536]{3,2,1,0:T(8,128)(2,1)S(1)}, u32[]{:S(2)}, u32[]{:S(2)}) %all-to-all-start.3) | async-done | bytes 1572896 | tf_op jit(solution)/shard_map/all_to_all | solution.py:343
  190.0 3.8 %all-to-all-start.4 = ((bf16[4,8,2048]{2,0,1:T(4,128)(2,1)}), bf16[4,8,2048]{2,0,1:T(4,128)(2,1)S(1)}, u32[]{:S(2)}, u32[]{:S(2)}) async-start(bf16[4,8,2048]{2,0,1:T(4,128)(2,1)} %copy.179), calls=%async_computation.4 | async-start | bytes 262144 | tf_op jit(solution)/shard_map/all_to_all | solution.py:173
  194.1 0.9 copy-done.2
  195.0 3.0 %collective-permute-start.3 = (bf16[64,1536]{1,0:T(8,128)(2,1)S(1)}, bf16[64,1536]{1,0:T(8,128)(2,1)S(1)}, u32[]{:S(2)}, u32[]{:S(2)}) collective-permute-start(bf16[64,1536]{1,0:T(8,128)(2,1)S(1)} %fusion.35), channel_id=1, source_target_pairs={{0,16},{16,0},{1,17},{17,1},{2,18},{18,2},{3,19},{19,3},{4,20},{20... | collective-permute-start | bytes 589832 | tf_op jit(solution)/shard_map/ppermute | solution.py:349
  198.0 7.4 %all-to-all-done.4 = bf16[4,8,2048]{2,0,1:T(4,128)(2,1)S(1)} async-done(((bf16[4,8,2048]{2,0,1:T(4,128)(2,1)}), bf16[4,8,2048]{2,0,1:T(4,128)(2,1)S(1)}, u32[]{:S(2)}, u32[]{:S(2)}) %all-to-all-start.4) | async-done | bytes 131104 | tf_op jit(solution)/shard_map/all_to_all | solution.py:173
  205.4 0.9 scatter_custom_fusion
  206.6 0.8 reshape.199
  207.4 1.3 collective-permute-done.3
  208.8 1.7 fusion.34
  (83 shorter events, 5.9 us)
Async XLA Ops:
  0.6 86.2 %copy-start = (bf16[384,1536]{1,0:T(8,128)(2,1)S(1)}, bf16[384,1536]{1,0:T(8,128)(2,1)}, u32[]{:S(2)}) copy-start(bf16[384,1536]{1,0:T(8,128)(2,1)} %param.22) | copy-start | bytes 3538948
  0.6 3.3 %copy-start.4 = (bf16[256,1536]{1,0:T(8,128)(2,1)S(1)}, bf16[256,1536]{1,0:T(8,128)(2,1)}, u32[]{:S(2)}) copy-start(bf16[256,1536]{1,0:T(8,128)(2,1)} %param.17) | copy-start | bytes 2359300
  0.7 3.3 %copy-start.15 = (f32[1536]{0:T(1024)S(1)}, f32[1536]{0:T(1024)}, u32[]{:S(2)}) copy-start(f32[1536]{0:T(1024)} %param.18) | copy-start | bytes 18436
  0.7 3.3 %copy-start.14 = (bf16[1536,128]{1,0:T(8,128)(2,1)S(1)}, bf16[1536,128]{1,0:T(8,128)(2,1)}, u32[]{:S(2)}) copy-start(bf16[1536,128]{1,0:T(8,128)(2,1)} %param.21) | copy-start | bytes 1179652
  0.7 3.8 %copy-start.9 = (bf16[512,256]{1,0:T(8,128)(2,1)S(1)}, bf16[512,256]{1,0:T(8,128)(2,1)}, u32[]{:S(2)}) copy-start(bf16[512,256]{1,0:T(8,128)(2,1)} %param.23) | copy-start | bytes 786436
  6.7 26.5 %all-to-all-start = ((bf16[4,2,2,768,64]{3,4,2,1,0:T(8,128)(2,1)}), bf16[4,2,2,768,64]{3,4,2,1,0:T(8,128)(2,1)S(1)}, u32[]{:S(2)}, u32[]{:S(2)}) async-start(bf16[4,2,2,768,64]{3,4,2,1,0:T(8,128)(2,1)} %broadcast_in_dim.53), calls=%async_computation | async-start | bytes 3145728 | tf_op jit(solution)/shard_map/all_to_all | solution.py:196
  15.6 17.6 %collective-permute-start = (bf16[2,768,64]{1,2,0:T(8,128)(2,1)S(1)}, bf16[2,768,64]{1,2,0:T(8,128)(2,1)S(1)}, u32[]{:S(2)}, u32[]{:S(2)}) collective-permute-start(bf16[2,768,64]{1,2,0:T(8,128)(2,1)S(1)} %bitcast.112), channel_id=1, source_target_pairs={{0,16},{1,17},{2,18},{3,19},{4,20},{5,21},{6,22},{7,23},{8,24},{9,... | collective-permute-start | bytes 589832 | tf_op jit(solution)/shard_map/ppermute | solution.py:205
  40.9 43.9 %collective-permute-start.1 = (bf16[2,768,70]{2,1,0:T(8,128)(2,1)}, bf16[2,768,70]{2,1,0:T(8,128)(2,1)S(1)}, u32[]{:S(2)}, u32[]{:S(2)}) collective-permute-start(bf16[2,768,70]{2,1,0:T(8,128)(2,1)} %get-tuple-element.133), channel_id=1, source_target_pairs={{16,0},{17,1},{18,2},{19,3},{20,4},{21,5},{22,6},{23,7},{24,8},{25... | collective-permute-start | bytes 645128 | tf_op jit(solution)/shard_map/ppermute | solution.py:242
  72.3 13.5 %copy-start.7 = (f32[2,768,64]{2,1,0:T(8,128)S(1)}, f32[2,768,64]{2,1,0:T(8,128)}, u32[]{:S(2)}) copy-start(f32[2,768,64]{2,1,0:T(8,128)} %get-tuple-element.38) | copy-start | bytes 1179652
  86.8 5.2 %copy-start.11 = (s32[64,8]{0,1:T(8,128)S(1)}, s32[64,8]{0,1:T(8,128)}, u32[]{:S(2)}) copy-start(s32[64,8]{0,1:T(8,128)} %param.27) | copy-start | bytes 6148
  86.8 5.4 %copy-start.10 = (f32[64,8]{0,1:T(8,128)S(1)}, f32[64,8]{0,1:T(8,128)}, u32[]{:S(2)}) copy-start(f32[64,8]{0,1:T(8,128)} %param.28) | copy-start | bytes 6148
  86.9 16.9 %copy-start.5 = (bf16[256,1536]{1,0:T(8,128)(2,1)S(1)}, bf16[256,1536]{1,0:T(8,128)(2,1)}, u32[]{:S(2)}) copy-start(bf16[256,1536]{1,0:T(8,128)(2,1)} %param.17) | copy-start | bytes 2359300
  88.4 15.6 %copy-start.12 = (f32[1536]{0:T(1024)S(1)}, f32[1536]{0:T(1024)}, u32[]{:S(2)}) copy-start(f32[1536]{0:T(1024)} %param.24) | copy-start | bytes 18436
  88.4 15.3 %all-to-all-start.1 = ((bf16[4,64,1536]{2,1,0:T(8,128)(2,1)}), bf16[4,64,1536]{2,1,0:T(8,128)(2,1)S(1)}, u32[]{:S(2)}, u32[]{:S(2)}) async-start(bf16[4,64,1536]{2,1,0:T(8,128)(2,1)} %bitcast.18), calls=%async_computation.1 | async-start | bytes 1572864 | tf_op jit(solution)/shard_map/all_to_all | solution.py:260
  104.2 12.3 %collective-permute-start.2 = (bf16[64,1664]{1,0:T(8,128)(2,1)S(1)}, bf16[64,1664]{1,0:T(8,128)(2,1)S(1)}, u32[]{:S(2)}, u32[]{:S(2)}) collective-permute-start(bf16[64,1664]{1,0:T(8,128)(2,1)S(1)} %concatenate.21), channel_id=1, source_target_pairs={{0,16},{16,0},{1,17},{17,1},{2,18},{18,2},{3,19},{19,3},{4,20},{20... | collective-permute-start | bytes 638984 | tf_op jit(solution)/shard_map/ppermute | solution.py:292
  117.9 24.5 %all-to-all-start.2 = ((bf16[4,2,64,1664]{3,2,1,0:T(8,128)(2,1)}), bf16[4,2,64,1664]{3,2,1,0:T(8,128)(2,1)S(1)}, u32[]{:S(2)}, u32[]{:S(2)}) async-start(bf16[4,2,64,1664]{3,2,1,0:T(8,128)(2,1)} %broadcast_in_dim.95), calls=%async_computation.2 | async-start | bytes 3407872 | tf_op jit(solution)/shard_map/all_to_all | solution.py:296
  142.5 1.2 copy-start.6
  166.9 3.9 %copy-start.8 = (bf16[256,2,2,64]{0,3,2,1:T(8,128)(2,1)S(1)}, bf16[256,2,2,64]{0,3,2,1:T(8,128)(2,1)}, u32[]{:S(2)}) copy-start(bf16[256,2,2,64]{0,3,2,1:T(8,128)(2,1)} %get-tuple-element.119) | copy-start | bytes 393220
  166.9 5.1 %copy-start.13 = (s32[256]{0:T(256)S(1)}, s32[256]{0:T(256)}, u32[]{:S(2)}) copy-start(s32[256]{0:T(256)} %param.29) | copy-start | bytes 3076
  166.9 23.1 %all-to-all-start.3 = ((bf16[4,2,64,1536]{3,2,1,0:T(8,128)(2,1)}), bf16[4,2,64,1536]{3,2,1,0:T(8,128)(2,1)S(1)}, u32[]{:S(2)}, u32[]{:S(2)}) async-start(bf16[4,2,64,1536]{3,2,1,0:T(8,128)(2,1)} %bitcast.109), calls=%async_computation.3 | async-start | bytes 3145728 | tf_op jit(solution)/shard_map/all_to_all | solution.py:343
  190.0 15.4 %all-to-all-start.4 = ((bf16[4,8,2048]{2,0,1:T(4,128)(2,1)}), bf16[4,8,2048]{2,0,1:T(4,128)(2,1)S(1)}, u32[]{:S(2)}, u32[]{:S(2)}) async-start(bf16[4,8,2048]{2,0,1:T(4,128)(2,1)} %copy.179), calls=%async_computation.4 | async-start | bytes 262144 | tf_op jit(solution)/shard_map/all_to_all | solution.py:173
  193.8 16.7 %copy-start.1 = (bf16[384,1536]{1,0:T(8,128)(2,1)S(1)}, bf16[384,1536]{1,0:T(8,128)(2,1)}, u32[]{:S(2)}) copy-start(bf16[384,1536]{1,0:T(8,128)(2,1)} %param.22) | copy-start | bytes 3538948
  194.0 0.9 copy-start.2
  195.0 13.8 %copy-start.3 = (f32[2,64,1536]{2,1,0:T(8,128)S(1)}, f32[2,64,1536]{2,1,0:T(8,128)}, u32[]{:S(2)}) copy-start(f32[2,64,1536]{2,1,0:T(8,128)} %copy-done.2) | copy-start | bytes 2359300
  195.0 13.8 %collective-permute-start.3 = (bf16[64,1536]{1,0:T(8,128)(2,1)S(1)}, bf16[64,1536]{1,0:T(8,128)(2,1)S(1)}, u32[]{:S(2)}, u32[]{:S(2)}) collective-permute-start(bf16[64,1536]{1,0:T(8,128)(2,1)S(1)} %fusion.35), channel_id=1, source_target_pairs={{0,16},{16,0},{1,17},{17,1},{2,18},{18,2},{3,19},{19,3},{4,20},{20... | collective-permute-start | bytes 589832 | tf_op jit(solution)/shard_map/ppermute | solution.py:349

commit v19 on v17

--- a/solution.py
+++ b/solution.py
@@ -193,6 +193,10 @@
     cache_rows = cache_kv.shape[0]
     cache_own = cache_kv.reshape(cache_rows, kv_local, 2, head_dim).transpose(2, 1, 0, 3)
     kv_piece = jnp.concatenate([cache_own, kv_own], axis=2)
+    query_rows = queries.reshape(tokens_here, kv_local, group_size, head_dim)
+    query_rows = query_rows.transpose(1, 2, 0, 3).reshape(kv_local, group_size * tokens_here, head_dim)
+    partner_rows = lax.ppermute(query_rows, "half", perm=[(0, 1)])
+    partner_rows, kv_piece = lax.optimization_barrier((partner_rows, kv_piece))
     kv_all = lax.all_to_all(
         jnp.broadcast_to(kv_piece[None], (half_size,) + kv_piece.shape),
         "hseq",
@@ -200,9 +204,6 @@
         concat_axis=0,
         tiled=True,
     )
-    query_rows = queries.reshape(tokens_here, kv_local, group_size, head_dim)
-    query_rows = query_rows.transpose(1, 2, 0, 3).reshape(kv_local, group_size * tokens_here, head_dim)
-    partner_rows = lax.ppermute(query_rows, "half", perm=[(0, 1)])
     flags = jnp.reshape(half_pos * tokens_here, (1,)).astype(jnp.int32)
     shapes = dict(cache_rows=cache_rows, group_rows=tokens_here)
 

time: 206 us -> 214 us (1.039)
  waiting for transfers between devices: 96.1 us -> 104 us
  starting transfers between devices: 30.5 us -> 33.2 us
    all_to_all x1, waiting for transfers between devices: 0.01 us -> 19.4 us  [body(): lax.all_to_all(jnp.broadcast_to(kv_piece[None], (half_size,) + kv_piece.s...]
    ppermute x1, waiting for transfers between devices: 13.1 us -> 1.3 us  [body(): partner_rows = lax.ppermute(query_rows, 'half', perm=[(0, 1)])]
    all_to_all x1, starting transfers between devices: 5.22 us -> 7.83 us  [body(): lax.all_to_all(jnp.broadcast_to(kv_piece[None], (half_size,) + kv_piece.s...]
  transfers between devices with their start and end apart: 9 -> 9, of which waited for: 8 -> 9; matrix products, arithmetic and copies ran while one was open for 8% -> 7% of each run, Pallas kernels for 11% -> 11%
where the time goes in v19:
time: 214 us
  waiting for transfers between devices  104 us (49%)
  starting transfers between devices  33.2 us (16%)
  matrix products  26.9 us (13%)
  Pallas kernels  23.5 us (11%)
  local copies, waits for them, and re-layouts  19.8 us (9%)
  other arithmetic  5.23 us (2%)
    pallas_call x1, Pallas kernels, attend_partial(): pl.pallas_call(kernel, out_shape=(jax.ShapeDtypeStruct((heads, rows, dim)...  23.5 us
    all_to_all x1, waiting for transfers between devices, body(): lax.all_to_all(jnp.broadcast_to(pair[None], (half_size,) + pair.shape), '...  19.9 us
    all_to_all x1, waiting for transfers between devices, body(): lax.all_to_all(jnp.broadcast_to(kv_piece[None], (half_size,) + kv_piece.s...  19.4 us
    all_to_all x1, waiting for transfers between devices, body(): lax.all_to_all(by_dest.transpose(1, 0, 2, 3), 'hseq', split_axis=0, conca...  17.8 us
    ppermute x1, waiting for transfers between devices, body(): back = lax.ppermute(far_part, 'half', perm=[(1, 0)])  13.3 us
    ppermute x1, waiting for transfers between devices, body(): crossed = lax.ppermute(packed, 'half', perm=[(0, 1), (1, 0)])  12.2 us
    all_to_all x1, waiting for transfers between devices, body(): lax.all_to_all(projected.reshape(exp_count, -1, projected.shape[1]), 'exp...  11.2 us
    dot_general x1, matrix products, body(): jnp.einsum('ecd,edf->ecf', rows_in, expert_in, preferred_element_type=jnp...  10.2 us
  transfers between devices with their start and end apart: 9, of which 9 were waited for; matrix products, arithmetic and copies ran while one was open for 7% of the time, Pallas kernels for 11%

profile of v19, /device:TPU:0, one launch (start us, length us, event | category | flops | bytes accessed | tf_op | source)
XLA Modules:
  0.0 213.6 jit_solution(467916156928630965)
XLA Ops:
  0.7 1.5 fusion.7
  2.2 2.2 %convolution_convert_fusion.3 = bf16[256,384]{1,0:T(8,128)(2,1)S(1)} fusion(bf16[1536,384]{1,0:T(8,128)(2,1)} %param.19, bf16[256,1536]{1,0:T(8,128)(2,1)} %param.17, f32[1536]{0:T(1024)} %param.18, f32[256]{0:T(256)S(1)} %add_rsqrt_fusion), kind=kOutput, calls=%fused_computation.25 | convolution fusion | flops 303661056 | bytes 2169856 | tf_op jit(solution)/shard_map/dot_general | solution.py:158
  4.6 5.9 %collective-permute-start = (bf16[2,768,64]{1,2,0:T(8,128)(2,1)S(1)}, bf16[2,768,64]{1,2,0:T(8,128)(2,1)S(1)}, u32[]{:S(2)}, u32[]{:S(2)}) collective-permute-start(bf16[2,768,64]{1,2,0:T(8,128)(2,1)S(1)} %bitcast.98), channel_id=1, source_target_pairs={{0,16},{1,17},{2,18},{3,19},{4,20},{5,21},{6,22},{7,23},{8,24},{9,... | collective-permute-start | bytes 589832 | tf_op jit(solution)/shard_map/ppermute | solution.py:198
  10.6 0.5 convolution_convert_fusion.5
  11.1 1.5 convolution_convert_fusion.4
  12.7 0.7 pad_maximum_fusion.2
  13.4 1.3 collective-permute-done
  14.7 1.3 broadcast_in_dim.86
  16.1 7.8 %all-to-all-start = ((bf16[4,2,2,768,64]{3,4,2,1,0:T(8,128)(2,1)}), bf16[4,2,2,768,64]{3,4,2,1,0:T(8,128)(2,1)S(1)}, u32[]{:S(2)}, u32[]{:S(2)}) async-start(bf16[4,2,2,768,64]{3,4,2,1,0:T(8,128)(2,1)} %broadcast_in_dim.86), calls=%async_computation | async-start | bytes 3145728 | tf_op jit(solution)/shard_map/all_to_all | solution.py:200
  23.9 19.4 %all-to-all-done = bf16[4,2,2,768,64]{3,4,2,1,0:T(8,128)(2,1)S(1)} async-done(((bf16[4,2,2,768,64]{3,4,2,1,0:T(8,128)(2,1)}), bf16[4,2,2,768,64]{3,4,2,1,0:T(8,128)(2,1)S(1)}, u32[]{:S(2)}, u32[]{:S(2)}) %all-to-all-start) | async-done | bytes 1572896 | tf_op jit(solution)/shard_map/all_to_all | solution.py:200
  43.5 1.0 copy.165
  44.5 1.3 collective-permute-start.1
  45.8 31.3 %conditional.2 = (f32[2,768,64]{1,2,0:T(8,128)S(1)}, f32[2,768,1]{1,0,2:T(2,128)S(1)}, f32[2,768,1]{1,0,2:T(2,128)S(1)}) conditional(s32[]{:T(128)} %convert_element_type.90, (s32[1]{0:T(128)}, bf16[2,768,64]{1,2,0:T(8,128)(2,1)}, bf16[4,2,2,768,64]{3,4,2,1,0:T(8,128)(2,1)S(1)}) %tuple.63, (s32[1]{0:T(128)}, bf16[2,768,64]{1,2,0:T(8,128)(2,1)}, ...), branch_computations={%region_1.2_spmd, %region_2.3_spmd} | conditional | bytes 4374580 | solution.py:229
  45.8 1.9 copy.161.q_ref
  47.7 2.8 %copy.162.k_ref.v_ref = bf16[4,2,2,768,64]{4,3,2,1,0:T(8,128)(2,1)} copy(bf16[4,2,2,768,64]{3,4,2,1,0:T(8,128)(2,1)S(1)} %get-tuple-element.94) | data formatting | bytes 3145728 | tf_op jit(solution)/shard_map
  50.5 23.5 %branch_1_fun.1 = (f32[2,768,64]{2,1,0:T(8,128)}, f32[2,768,1]{2,1,0:T(8,128)}, f32[2,768,1]{2,1,0:T(8,128)}) custom-call(s32[1]{0:T(128)} %get-tuple-element.24.flags_ref, bf16[2,768,64]{2,1,0:T(8,128)(2,1)} %copy.161.q_ref, bf16[4,2,2,768,64]{4,3,2,1,0:T(8,128)(2,1)} %copy.162.k_ref.v_ref, bf16[4,2,2,768,64]{4,3,2,1,0:T(8,128)(2,1)} %copy.162.k_ref.v_ref), custom_call_target="tpu_custom_call" | custom-call | tf_op jit(solution)/shard_map/cond/branch_1_fun/pallas_call | solution.py:96
  74.0 1.5 copy.187
  75.5 1.4 copy.189
  76.8 0.3 copy.191
  77.1 13.3 %collective-permute-done.1 = f32[2,768,66]{1,0,2:T(2,128)S(1)} collective-permute-done((f32[2,768,66]{1,0,2:T(2,128)}, f32[2,768,66]{1,0,2:T(2,128)S(1)}, u32[]{:S(2)}, u32[]{:S(2)}) %collective-permute-start.1) | collective-permute-done | bytes 405536 | tf_op jit(solution)/shard_map/ppermute | solution.py:235
  90.7 1.5 convolution_convert_fusion.2
  92.2 3.8 %all-to-all-start.1 = ((bf16[4,64,1536]{2,1,0:T(8,128)(2,1)}), bf16[4,64,1536]{2,1,0:T(8,128)(2,1)S(1)}, u32[]{:S(2)}, u32[]{:S(2)}) async-start(bf16[4,64,1536]{2,1,0:T(8,128)(2,1)} %bitcast.15), calls=%async_computation.1 | async-start | bytes 1572864 | tf_op jit(solution)/shard_map/all_to_all | solution.py:253
  96.4 11.2 %all-to-all-done.1 = bf16[4,64,1536]{2,1,0:T(8,128)(2,1)S(1)} async-done(((bf16[4,64,1536]{2,1,0:T(8,128)(2,1)}), bf16[4,64,1536]{2,1,0:T(8,128)(2,1)S(1)}, u32[]{:S(2)}, u32[]{:S(2)}) %all-to-all-start.1) | async-done | bytes 786464 | tf_op jit(solution)/shard_map/all_to_all | solution.py:253
  108.3 12.2 %collective-permute-done.2 = bf16[64,1664]{1,0:T(8,128)(2,1)S(1)} collective-permute-done((bf16[64,1664]{1,0:T(8,128)(2,1)S(1)}, bf16[64,1664]{1,0:T(8,128)(2,1)S(1)}, u32[]{:S(2)}, u32[]{:S(2)}) %collective-permute-start.2) | collective-permute-done | bytes 213024 | tf_op jit(solution)/shard_map/ppermute | solution.py:285
  120.6 1.3 broadcast_in_dim.93
  121.9 3.6 %all-to-all-start.2 = ((bf16[4,2,64,1664]{3,2,1,0:T(8,128)(2,1)}), bf16[4,2,64,1664]{3,2,1,0:T(8,128)(2,1)S(1)}, u32[]{:S(2)}, u32[]{:S(2)}) async-start(bf16[4,2,64,1664]{3,2,1,0:T(8,128)(2,1)} %broadcast_in_dim.93), calls=%async_computation.2 | async-start | bytes 3407872 | tf_op jit(solution)/shard_map/all_to_all | solution.py:289
  125.5 19.9 %all-to-all-done.2 = bf16[4,2,64,1664]{3,2,1,0:T(8,128)(2,1)S(1)} async-done(((bf16[4,2,64,1664]{3,2,1,0:T(8,128)(2,1)}), bf16[4,2,64,1664]{3,2,1,0:T(8,128)(2,1)S(1)}, u32[]{:S(2)}, u32[]{:S(2)}) %all-to-all-start.2) | async-done | bytes 1703968 | tf_op jit(solution)/shard_map/all_to_all | solution.py:289
  145.6 0.2 constant_dynamic-slice_fusion.1
  145.8 1.0 copy-done.6
  147.4 10.2 %fusion.56 = f32[4,256,1024]{2,1,0:T(8,128)} fusion(bf16[4,1536,1024]{2,1,0:T(8,128)(2,1)} %param.25, bf16[512,1664]{1,0:T(8,128)(2,1)} %bitcast.97, s32[512,4]{0,1:T(4,128)S(1)} %eq.48, pred[512,4]{0,1:T(4,128)(4,1)S(1)} %get-tuple-element.110), kind=kOutput, calls=%fused_computation.99 | convolution fusion | flops 4834459648 | bytes 18360320 | tf_op jit(solution)/shard_map/ecd,edf->ecf/dot_general | solution.py:324
  157.6 5.9 %convolution_convert_fusion.1 = bf16[4,256,1536]{2,1,0:T(8,128)(2,1)S(1)} fusion(bf16[4,512,1536]{2,1,0:T(8,128)(2,1)} %param.26, f32[4,256,1024]{2,1,0:T(8,128)} %fusion.56), kind=kOutput, calls=%fused_computation.4 | convolution fusion | flops 1615331328 | bytes 13631488 | tf_op jit(solution)/shard_map/ecf,efd->ecd/dot_general | solution.py:327
  163.5 2.1 convolution_bitcast_fusion
  165.6 3.0 %fusion.1 = bf16[512,1536]{1,0:T(8,128)(2,1)S(1)} fusion(f32[512,1536]{1,0:T(8,128)S(1)} %convolution_bitcast_fusion, bf16[4,256,1536]{2,1,0:T(8,128)(2,1)S(1)} %convolution_convert_fusion.1, s32[512,4]{0,1:T(4,128)S(1)} %eq.48, pred[512,4]{0,1:T(4,128)(4,1)S(1)} %get-tuple-element.110, bf16[512,4]{0,1:T(4,128)(2,1)S(1)} %copy.196), kind=kOutput, calls=%fused_computation.9 | convolution fusion | flops 1613758464 | bytes 7878656 | tf_op jit(solution)/shard_map/nec,ecd->nd/dot_general | solution.py:332
  168.6 1.3 copy.213
  169.9 3.7 %all-to-all-start.3 = ((bf16[4,2,64,1536]{3,2,1,0:T(8,128)(2,1)}), bf16[4,2,64,1536]{3,2,1,0:T(8,128)(2,1)S(1)}, u32[]{:S(2)}, u32[]{:S(2)}) async-start(bf16[4,2,64,1536]{3,2,1,0:T(8,128)(2,1)} %bitcast.95), calls=%async_computation.3 | async-start | bytes 3145728 | tf_op jit(solution)/shard_map/all_to_all | solution.py:336
  174.0 0.3 reshape_reshape.3
  174.3 0.8 copy.180
  175.2 17.8 %all-to-all-done.3 = bf16[4,2,64,1536]{3,2,1,0:T(8,128)(2,1)S(1)} async-done(((bf16[4,2,64,1536]{3,2,1,0:T(8,128)(2,1)}), bf16[4,2,64,1536]{3,2,1,0:T(8,128)(2,1)S(1)}, u32[]{:S(2)}, u32[]{:S(2)}) %all-to-all-start.3) | async-done | bytes 1572896 | tf_op jit(solution)/shard_map/all_to_all | solution.py:336
  193.0 3.9 %all-to-all-start.4 = ((bf16[4,8,2048]{2,0,1:T(4,128)(2,1)}), bf16[4,8,2048]{2,0,1:T(4,128)(2,1)S(1)}, u32[]{:S(2)}, u32[]{:S(2)}) async-start(bf16[4,8,2048]{2,0,1:T(4,128)(2,1)} %copy.180), calls=%async_computation.4 | async-start | bytes 262144 | tf_op jit(solution)/shard_map/all_to_all | solution.py:173
  196.9 0.2 convert_reduce_fusion
  197.2 0.9 copy-done.2
  198.1 3.0 %collective-permute-start.3 = (bf16[64,1536]{1,0:T(8,128)(2,1)S(1)}, bf16[64,1536]{1,0:T(8,128)(2,1)S(1)}, u32[]{:S(2)}, u32[]{:S(2)}) collective-permute-start(bf16[64,1536]{1,0:T(8,128)(2,1)S(1)} %fusion.33), channel_id=1, source_target_pairs={{0,16},{16,0},{1,17},{17,1},{2,18},{18,2},{3,19},{19,3},{4,20},{20... | collective-permute-start | bytes 589832 | tf_op jit(solution)/shard_map/ppermute | solution.py:342
  201.1 7.4 %all-to-all-done.4 = bf16[4,8,2048]{2,0,1:T(4,128)(2,1)S(1)} async-done(((bf16[4,8,2048]{2,0,1:T(4,128)(2,1)}), bf16[4,8,2048]{2,0,1:T(4,128)(2,1)S(1)}, u32[]{:S(2)}, u32[]{:S(2)}) %all-to-all-start.4) | async-done | bytes 131104 | tf_op jit(solution)/shard_map/all_to_all | solution.py:173
  208.5 0.9 scatter_custom_fusion
  209.4 0.2 reshape.163
  209.7 0.8 reshape.177
  210.6 1.3 collective-permute-done.3
  211.9 1.7 fusion.31
  (82 shorter events, 3.3 us)
Async XLA Ops:
  0.6 90.1 %copy-start = (bf16[384,1536]{1,0:T(8,128)(2,1)S(1)}, bf16[384,1536]{1,0:T(8,128)(2,1)}, u32[]{:S(2)}) copy-start(bf16[384,1536]{1,0:T(8,128)(2,1)} %param.22) | copy-start | bytes 3538948
  0.6 9.9 %copy-start.4 = (bf16[256,1536]{1,0:T(8,128)(2,1)S(1)}, bf16[256,1536]{1,0:T(8,128)(2,1)}, u32[]{:S(2)}) copy-start(bf16[256,1536]{1,0:T(8,128)(2,1)} %param.17) | copy-start | bytes 2359300
  0.7 9.9 %copy-start.17 = (f32[1536]{0:T(1024)S(1)}, f32[1536]{0:T(1024)}, u32[]{:S(2)}) copy-start(f32[1536]{0:T(1024)} %param.18) | copy-start | bytes 18436
  0.7 9.9 %copy-start.16 = (bf16[1536,128]{1,0:T(8,128)(2,1)S(1)}, bf16[1536,128]{1,0:T(8,128)(2,1)}, u32[]{:S(2)}) copy-start(bf16[1536,128]{1,0:T(8,128)(2,1)} %param.20) | copy-start | bytes 1179652
  4.4 8.2 %copy-start.11 = (bf16[512,256]{1,0:T(8,128)(2,1)S(1)}, bf16[512,256]{1,0:T(8,128)(2,1)}, u32[]{:S(2)}) copy-start(bf16[512,256]{1,0:T(8,128)(2,1)} %param.23) | copy-start | bytes 786436
  4.6 8.8 %copy-start.7 = (bf16[2,3,8,8,256]{4,3,1,2,0:T(8,128)(2,1)}, bf16[2,3,8,8,256]{4,3,1,2,0:T(8,128)(2,1)S(1)}, u32[]{:S(2)}) copy-start(bf16[2,3,8,8,256]{4,3,1,2,0:T(8,128)(2,1)S(1)} %copy.198) | copy-start | bytes 589828
  4.6 10.1 %collective-permute-start = (bf16[2,768,64]{1,2,0:T(8,128)(2,1)S(1)}, bf16[2,768,64]{1,2,0:T(8,128)(2,1)S(1)}, u32[]{:S(2)}, u32[]{:S(2)}) collective-permute-start(bf16[2,768,64]{1,2,0:T(8,128)(2,1)S(1)} %bitcast.98), channel_id=1, source_target_pairs={{0,16},{1,17},{2,18},{3,19},{4,20},{5,21},{6,22},{7,23},{8,24},{9,... | collective-permute-start | bytes 589832 | tf_op jit(solution)/shard_map/ppermute | solution.py:198
  16.1 27.3 %all-to-all-start = ((bf16[4,2,2,768,64]{3,4,2,1,0:T(8,128)(2,1)}), bf16[4,2,2,768,64]{3,4,2,1,0:T(8,128)(2,1)S(1)}, u32[]{:S(2)}, u32[]{:S(2)}) async-start(bf16[4,2,2,768,64]{3,4,2,1,0:T(8,128)(2,1)} %broadcast_in_dim.86), calls=%async_computation | async-start | bytes 3145728 | tf_op jit(solution)/shard_map/all_to_all | solution.py:200
  44.5 45.8 %collective-permute-start.1 = (f32[2,768,66]{1,0,2:T(2,128)}, f32[2,768,66]{1,0,2:T(2,128)S(1)}, u32[]{:S(2)}, u32[]{:S(2)}) collective-permute-start(f32[2,768,66]{1,0,2:T(2,128)} %copy.165), channel_id=1, source_target_pairs={{16,0},{17,1},{18,2},{19,3},{20,4},{21,5},{22,6},{23,7},{24,8},{25... | collective-permute-start | bytes 1216520 | tf_op jit(solution)/shard_map/ppermute | solution.py:235
  74.0 2.9 %copy-start.9 = (f32[2,768,1]{2,1,0:T(8,128)S(1)}, f32[2,768,1]{2,1,0:T(8,128)}, u32[]{:S(2)}) copy-start(f32[2,768,1]{2,1,0:T(8,128)} %get-tuple-element.105) | copy-start | bytes 18436 | tf_op jit(solution)/shard_map/cond
  90.6 5.4 %copy-start.13 = (s32[64,8]{0,1:T(8,128)S(1)}, s32[64,8]{0,1:T(8,128)}, u32[]{:S(2)}) copy-start(s32[64,8]{0,1:T(8,128)} %param.27) | copy-start | bytes 6148
  90.6 5.5 %copy-start.12 = (f32[64,8]{0,1:T(8,128)S(1)}, f32[64,8]{0,1:T(8,128)}, u32[]{:S(2)}) copy-start(f32[64,8]{0,1:T(8,128)} %param.28) | copy-start | bytes 6148
  90.7 17.1 %copy-start.5 = (bf16[256,1536]{1,0:T(8,128)(2,1)S(1)}, bf16[256,1536]{1,0:T(8,128)(2,1)}, u32[]{:S(2)}) copy-start(bf16[256,1536]{1,0:T(8,128)(2,1)} %param.17) | copy-start | bytes 2359300
  92.2 15.8 %copy-start.14 = (f32[1536]{0:T(1024)S(1)}, f32[1536]{0:T(1024)}, u32[]{:S(2)}) copy-start(f32[1536]{0:T(1024)} %param.24) | copy-start | bytes 18436
  92.2 15.4 %all-to-all-start.1 = ((bf16[4,64,1536]{2,1,0:T(8,128)(2,1)}), bf16[4,64,1536]{2,1,0:T(8,128)(2,1)S(1)}, u32[]{:S(2)}, u32[]{:S(2)}) async-start(bf16[4,64,1536]{2,1,0:T(8,128)(2,1)} %bitcast.15), calls=%async_computation.1 | async-start | bytes 1572864 | tf_op jit(solution)/shard_map/all_to_all | solution.py:253
  108.2 12.3 %collective-permute-start.2 = (bf16[64,1664]{1,0:T(8,128)(2,1)S(1)}, bf16[64,1664]{1,0:T(8,128)(2,1)S(1)}, u32[]{:S(2)}, u32[]{:S(2)}) collective-permute-start(bf16[64,1664]{1,0:T(8,128)(2,1)S(1)} %concatenate.21), channel_id=1, source_target_pairs={{0,16},{16,0},{1,17},{17,1},{2,18},{18,2},{3,19},{19,3},{4,20},{20... | collective-permute-start | bytes 638984 | tf_op jit(solution)/shard_map/ppermute | solution.py:285
  121.9 23.5 %all-to-all-start.2 = ((bf16[4,2,64,1664]{3,2,1,0:T(8,128)(2,1)}), bf16[4,2,64,1664]{3,2,1,0:T(8,128)(2,1)S(1)}, u32[]{:S(2)}, u32[]{:S(2)}) async-start(bf16[4,2,64,1664]{3,2,1,0:T(8,128)(2,1)} %broadcast_in_dim.93), calls=%async_computation.2 | async-start | bytes 3407872 | tf_op jit(solution)/shard_map/all_to_all | solution.py:289
  145.6 1.2 copy-start.6
  169.9 3.9 %copy-start.10 = (bf16[256,2,2,64]{0,3,2,1:T(8,128)(2,1)S(1)}, bf16[256,2,2,64]{0,3,2,1:T(8,128)(2,1)}, u32[]{:S(2)}) copy-start(bf16[256,2,2,64]{0,3,2,1:T(8,128)(2,1)} %get-tuple-element.116) | copy-start | bytes 393220
  169.9 5.1 %copy-start.15 = (s32[256]{0:T(256)S(1)}, s32[256]{0:T(256)}, u32[]{:S(2)}) copy-start(s32[256]{0:T(256)} %param.29) | copy-start | bytes 3076
  169.9 23.1 %all-to-all-start.3 = ((bf16[4,2,64,1536]{3,2,1,0:T(8,128)(2,1)}), bf16[4,2,64,1536]{3,2,1,0:T(8,128)(2,1)S(1)}, u32[]{:S(2)}, u32[]{:S(2)}) async-start(bf16[4,2,64,1536]{3,2,1,0:T(8,128)(2,1)} %bitcast.95), calls=%async_computation.3 | async-start | bytes 3145728 | tf_op jit(solution)/shard_map/all_to_all | solution.py:336
  193.0 15.5 %all-to-all-start.4 = ((bf16[4,8,2048]{2,0,1:T(4,128)(2,1)}), bf16[4,8,2048]{2,0,1:T(4,128)(2,1)S(1)}, u32[]{:S(2)}, u32[]{:S(2)}) async-start(bf16[4,8,2048]{2,0,1:T(4,128)(2,1)} %copy.180), calls=%async_computation.4 | async-start | bytes 262144 | tf_op jit(solution)/shard_map/all_to_all | solution.py:173
  196.9 16.7 %copy-start.1 = (bf16[384,1536]{1,0:T(8,128)(2,1)S(1)}, bf16[384,1536]{1,0:T(8,128)(2,1)}, u32[]{:S(2)}) copy-start(bf16[384,1536]{1,0:T(8,128)(2,1)} %param.22) | copy-start | bytes 3538948
  197.2 0.9 copy-start.2
  198.1 13.8 %copy-start.3 = (f32[2,64,1536]{2,1,0:T(8,128)S(1)}, f32[2,64,1536]{2,1,0:T(8,128)}, u32[]{:S(2)}) copy-start(f32[2,64,1536]{2,1,0:T(8,128)} %copy-done.2) | copy-start | bytes 2359300
  198.1 13.8 %collective-permute-start.3 = (bf16[64,1536]{1,0:T(8,128)(2,1)S(1)}, bf16[64,1536]{1,0:T(8,128)(2,1)S(1)}, u32[]{:S(2)}, u32[]{:S(2)}) collective-permute-start(bf16[64,1536]{1,0:T(8,128)(2,1)S(1)} %fusion.33), channel_id=1, source_target_pairs={{0,16},{16,0},{1,17},{17,1},{2,18},{18,2},{3,19},{19,3},{4,20},{20... | collective-permute-start | bytes 589832 | tf_op jit(solution)/shard_map/ppermute | solution.py:342
